TPU v7x, 32 devices: a whole 2x2x4 slice. The times are simulated.
32 devices in a mesh: track: 4 (over z), cross: 8 (over y, x, core).
Axes of the slice: x: 2, y: 2, z: 4, core: 2. Of those that a mesh axis runs over, the one named last changes fastest.
Arguments:
- cube: bfloat16 [1024, 256, 224], P('track', 'cross'), may hold values from -60 to 113, as said below
Outputs:
- scores: float32 [1024, 256], P('track', 'cross')
Inputs may be any that keep to these rules, and one draw needn't show every extreme that they name: `cube`: A positive radiance level per band plus noise, scaled per band and by position.
All inputs are finite; a program needn't handle non-finite values.
Results may differ from a plain program's by a relative error of at most 0.0003.
Values may be sent and summed in bfloat16 or wider, within the bound.
No kernel may reach another device: no remote copies, remote signals or barrier semaphores. Data moves between devices by JAX's collectives and lax.ppermute only.
A program may use at most 64 MiB of HBM per device.

v0:
```python
import jax
import jax.numpy as jnp
from jax import lax
from jax.sharding import PartitionSpec as P

HALF = 15


LOAD = 0.02


def with_halo(block, sides, width):
    for axis, dim in sides:
        count = lax.axis_size(axis)
        forward = [(i, i + 1) for i in range(count - 1)]
        backward = [(target, source) for source, target in forward]
        low = lax.ppermute(
            lax.slice_in_dim(block, block.shape[dim] - width, None, axis=dim), axis, forward
        )
        high = lax.ppermute(lax.slice_in_dim(block, 0, width, axis=dim), axis, backward)
        block = jnp.concatenate([low, block, high], axis=dim)
    return block


def band_matrix(rows_in, rows_out, dtype):
    source = jnp.arange(rows_in)[:, None]
    target = jnp.arange(rows_out)[None, :]
    inside = (source >= target) & (source <= target + 2 * HALF)
    return inside.astype(dtype)


def window_count(first, local, total):
    index = first + jnp.arange(local)
    upper = jnp.minimum(index + HALF, total - 1)
    lower = jnp.maximum(index - HALF, 0)
    return (upper - lower + 1).astype(jnp.float32)


def sum_pixels(values, width, dtype):
    weights = band_matrix(width + 2 * HALF, width, dtype)
    return jnp.einsum(
        "lqb,qp->lpb", values, weights, precision=None, preferred_element_type=jnp.float32
    )


def sum_lines(values, height, dtype, precision):
    weights = band_matrix(height + 2 * HALF, height, dtype)
    return jnp.einsum(
        "kpb,kl->lpb", values, weights, precision=precision, preferred_element_type=jnp.float32
    )


def shards(cube):
    lines_dev, pix_dev, bands = cube.shape
    n_track = lax.axis_size("track")
    n_cross = lax.axis_size("cross")
    total_lines = lines_dev * n_track
    total_pix = pix_dev * n_cross
    highest = lax.Precision.HIGHEST
    extended = with_halo(cube, (("track", 0), ("cross", 1)), HALF)
    across = sum_pixels(extended, pix_dev, jnp.bfloat16)
    window = sum_lines(across, lines_dev, jnp.float32, highest)
    line_count = window_count(lax.axis_index("track") * lines_dev, lines_dev, total_lines)
    pixel_count = window_count(lax.axis_index("cross") * pix_dev, pix_dev, total_pix)
    count = line_count[:, None, None] * pixel_count[None, :, None]
    residual = cube.astype(jnp.float32) - window / count
    flat = residual.reshape(lines_dev * pix_dev, bands)
    flat_bf = flat.astype(jnp.bfloat16)
    partial_cov = jnp.dot(flat_bf.T, flat_bf, preferred_element_type=jnp.float32)
    covariance = lax.psum(partial_cov, ("track", "cross")) / (total_lines * total_pix)
    identity = jnp.eye(bands, dtype=jnp.float32)
    loaded = covariance + LOAD * (jnp.trace(covariance) / bands) * identity
    factor = jnp.linalg.cholesky(loaded)
    inverse = jax.scipy.linalg.solve_triangular(factor, identity, lower=True)
    whitened = jnp.dot(flat, inverse.T, precision=highest, preferred_element_type=jnp.float32)
    scores = jnp.sum(whitened * whitened, axis=1) / bands
    return scores.reshape(lines_dev, pix_dev)


def solution(mesh):
    return jax.shard_map(
        shards,
        mesh=mesh,
        in_specs=(P("track", "cross", None),),
        out_specs=P("track", "cross"),
        check_vma=False,
    )
```

profile of v0, /device:TPU:0, one launch (start us, length us, event | category | flops | bytes accessed | tf_op | source)
XLA Modules:
  0.0 328.9 jit_solution(2984762335970636967)
XLA Ops:
  6.5 0.0 all-reduce.5.cloned.1.call-start
  6.5 7.8 %copy.6 = bf16[256,32,224]{2,1,0:T(8,128)(2,1)} copy(bf16[256,32,224]{0,2,1:T(8,128)(2,1)} %param.1) | data formatting | bytes 7340032 | tf_op args[0]
  14.4 1.1 fusion.46
  15.5 4.9 %collective-permute-start = (bf16[15,32,224]{2,1,0:T(8,128)(2,1)S(1)}, bf16[15,32,224]{2,1,0:T(8,128)(2,1)S(1)}, u32[]{:S(2)}, u32[]{:S(2)}) collective-permute-start(bf16[15,32,224]{2,1,0:T(8,128)(2,1)S(1)} %get-tuple-element.27), channel_id=1, source_target_pairs={{0,8},{8,16},{16,24},{1,9},{9,17},{17,25},{2,10},{10,18},{18,26},{... | collective-permute-start | bytes 645128 | tf_op jit(solution)/shard_map/ppermute | solution.py:17
  20.4 1.3 collective-permute-start.1
  21.7 3.9 %collective-permute-done = bf16[15,32,224]{2,1,0:T(8,128)(2,1)S(1)} collective-permute-done((bf16[15,32,224]{2,1,0:T(8,128)(2,1)S(1)}, bf16[15,32,224]{2,1,0:T(8,128)(2,1)S(1)}, u32[]{:S(2)}, u32[]{:S(2)}) %collective-permute-start) | collective-permute-done | bytes 215072 | tf_op jit(solution)/shard_map/ppermute | solution.py:17
  25.6 4.1 %collective-permute-done.1 = bf16[15,32,224]{2,1,0:T(8,128)(2,1)S(1)} collective-permute-done((bf16[15,32,224]{2,1,0:T(8,128)(2,1)S(1)}, bf16[15,32,224]{2,1,0:T(8,128)(2,1)S(1)}, u32[]{:S(2)}, u32[]{:S(2)}) %collective-permute-start.1) | collective-permute-done | bytes 215072 | tf_op jit(solution)/shard_map/ppermute | solution.py:20
  29.7 2.7 pad_maximum_fusion
  32.5 1.0 fusion.45
  33.5 0.8 copy.9
  34.3 2.7 collective-permute-start.2
  37.1 2.1 copy.10
  39.2 1.3 collective-permute-start.3
  40.5 0.0 copy-start.1
  40.6 0.1 broadcast_multiply_fusion.1
  40.7 0.0 collective-permute-done.2
  40.7 3.0 copy.11
  43.7 2.4 collective-permute-done.3
  46.1 2.9 copy.12
  48.9 0.0 copy-done.1
  48.9 0.0 copy-start.2
  49.0 15.9 %fusion.14 = f32[286,32,224]{2,1,0:T(8,128)} fusion(bf16[286,15,224]{2,1,0:T(8,128)(2,1)S(1)} %copy.12, bf16[15,32,224]{2,1,0:T(8,128)(2,1)S(1)} %collective-permute-done.1, bf16[256,32,224]{2,1,0:T(8,128)(2,1)S(1)} %copy-done.1, bf16[15,32,224]{2,1,0:T(8,128)(2,1)S(1)} %collective-permute-done, bf16[286,15,224]{2,1,0:T(8,128)(2,1)S(1)} %copy.11, ...), kind=kOutput, calls=%fused_computation.17 | convolution fusion | flops 293931584 | bytes 16144256 | tf_op jit(solution)/shard_map/lqb,qp->lpb/dot_general | solution.py:41
  64.8 0.0 copy-done.2
  64.8 18.1 %divide_subtract_fusion = f32[256,32,224]{0,2,1:T(8,128)S(1)} fusion(bf16[256,32,224]{0,2,1:T(8,128)(2,1)S(1)} %copy-done.2, f32[256,32]{0,1:T(8,128)S(1)} %broadcast_multiply_fusion.1, f32[286,32,224]{2,1,0:T(8,128)} %fusion.14, s32[256]{0:T(256)S(1)} %iota_add_fusion), kind=kOutput, calls=%fused_computation.13 | convolution fusion | flops 6303472128 | bytes 19244032 | tf_op jit(solution)/shard_map/kpb,kl->lpb/dot_general | solution.py:48
  82.9 0.0 copy-start
  83.0 3.0 copy-done
  86.0 1.8 fusion.20
  87.8 0.0 all-reduce.5.cloned.1.call-update
  87.8 9.9 %copy.14 = f32[256,32,224]{2,1,0:T(8,128)} copy(f32[256,32,224]{0,2,1:T(8,128)} %copy-done) | data formatting | bytes 14680064 | tf_op jit(solution)/shard_map/sub | solution.py:66
  97.7 153.7 %all-reduce.5.cloned.1.call-done = f32[224,224]{1,0:T(8,128)} async-done(((f32[224,224]{1,0:T(8,128)}), f32[224,224]{1,0:T(8,128)}) %all-reduce.5.cloned.1.call-update) | async-done | bytes 200720 | tf_op jit(solution)/shard_map/psum | solution.py:70
  251.4 1.6 select_reduce_fusion
  253.7 1.0 select_add_fusion
  254.6 0.1 copy.15
  254.8 1.0 fusion.29
  255.8 11.7 %cholesky.50 = f32[128,128]{1,0:T(8,128)S(1)} custom-call(f32[128,128]{1,0:T(8,128)S(1)} %cholesky.121), custom_call_target="Cholesky" | custom-call | tf_op jit(solution)/shard_map/jit(cholesky)/cholesky | solution.py:73
  267.5 9.8 %custom-call.15 = f32[1,128,128]{1,2,0:T(8,128)S(1)} custom-call(f32[1,128,128]{2,1,0:T(8,128)S(1)} %get-tuple-element.30), custom_call_target="InvertDiagBlocksLowerTriangular" | custom-call | tf_op jit(solution)/shard_map/jit(cholesky)/cholesky | solution.py:73
  277.3 0.2 constant_dynamic-update-slice_fusion.1
  277.5 0.2 convolution_subtract_fusion.1
  277.8 8.8 %cholesky.108 = f32[96,96]{1,0:T(8,128)S(1)} custom-call(f32[96,96]{1,0:T(8,128)S(1)} %convolution_subtract_fusion.1), custom_call_target="Cholesky" | custom-call | tf_op jit(solution)/shard_map/jit(cholesky)/cholesky | solution.py:73
  286.6 0.6 compare_reduce_fusion
  287.2 0.6 compare_reduce_fusion.1
  289.1 0.1 fusion.33
  289.2 19.7 %custom-call.16 = f32[2,128,128]{1,2,0:T(8,128)S(1)} custom-call(f32[2,128,128]{2,1,0:T(8,128)S(1)} %pad_maximum_fusion.1), custom_call_target="InvertDiagBlocksLowerTriangular" | custom-call | tf_op jit(solution)/shard_map/jit(_solve_triangular)/triangular_solve | solution.py:74
  308.9 0.3 fusion.31
  309.2 0.4 convolution_subtract_fusion
  309.6 0.4 fusion.37
  309.9 11.4 %fusion.19 = f32[8192]{0:T(1024)S(1)} fusion(f32[8192,224]{1,0:T(8,128)} %bitcast.37, f32[96,224]{0,1:T(8,128)S(1)} %fusion.37, f32[128,224]{0,1:T(8,128)S(1)} %fusion.31), kind=kOutput, calls=%fused_computation.18 | convolution fusion | flops 4936213504 | bytes 7573504 | tf_op jit(solution)/shard_map/dot_general | solution.py:75
  321.3 0.1 div.39
  321.4 0.7 copy.17
  (15 shorter events, 0.2 us)
Async XLA Ops:
  6.5 244.9 %all-reduce.5.cloned.1.call-start = ((), (), s32[]{:S(2)}) async-start(), calls=%async_computation | async-start | bytes 458752 | tf_op jit(solution)/shard_map/psum | solution.py:70
  15.5 10.1 %collective-permute-start = (bf16[15,32,224]{2,1,0:T(8,128)(2,1)S(1)}, bf16[15,32,224]{2,1,0:T(8,128)(2,1)S(1)}, u32[]{:S(2)}, u32[]{:S(2)}) collective-permute-start(bf16[15,32,224]{2,1,0:T(8,128)(2,1)S(1)} %get-tuple-element.27), channel_id=1, source_target_pairs={{0,8},{8,16},{16,24},{1,9},{9,17},{17,25},{2,10},{10,18},{18,26},{... | collective-permute-start | bytes 645128 | tf_op jit(solution)/shard_map/ppermute | solution.py:17
  20.4 9.3 %collective-permute-start.1 = (bf16[15,32,224]{2,1,0:T(8,128)(2,1)S(1)}, bf16[15,32,224]{2,1,0:T(8,128)(2,1)S(1)}, u32[]{:S(2)}, u32[]{:S(2)}) collective-permute-start(bf16[15,32,224]{2,1,0:T(8,128)(2,1)S(1)} %get-tuple-element.28), channel_id=1, source_target_pairs={{8,0},{16,8},{24,16},{9,1},{17,9},{25,17},{10,2},{18,10},{26,18},{... | collective-permute-start | bytes 645128 | tf_op jit(solution)/shard_map/ppermute | solution.py:20
  34.3 6.3 %collective-permute-start.2 = (bf16[286,15,224]{2,0,1:T(8,128)(2,1)S(1)}, bf16[286,15,224]{2,0,1:T(8,128)(2,1)}, u32[]{:S(2)}, u32[]{:S(2)}) collective-permute-start(bf16[286,15,224]{2,0,1:T(8,128)(2,1)S(1)} %copy.9), channel_id=1, source_target_pairs={{0,1},{1,2},{2,3},{3,4},{4,5},{5,6},{6,7},{8,9},{9,10},{10,11},{11... | collective-permute-start | bytes 5765768 | tf_op jit(solution)/shard_map/ppermute | solution.py:17
  39.2 6.9 %collective-permute-start.3 = (bf16[286,15,224]{2,0,1:T(8,128)(2,1)}, bf16[286,15,224]{2,0,1:T(8,128)(2,1)}, u32[]{:S(2)}, u32[]{:S(2)}) collective-permute-start(bf16[286,15,224]{2,0,1:T(8,128)(2,1)} %copy.10), channel_id=1, source_target_pairs={{1,0},{2,1},{3,2},{4,3},{5,4},{6,5},{7,6},{9,8},{10,9},{11,10},{12... | collective-permute-start | bytes 5765768 | tf_op jit(solution)/shard_map/ppermute | solution.py:20
  40.5 8.4 %copy-start.1 = (bf16[256,32,224]{2,1,0:T(8,128)(2,1)S(1)}, bf16[256,32,224]{2,1,0:T(8,128)(2,1)}, u32[]{:S(2)}) copy-start(bf16[256,32,224]{2,1,0:T(8,128)(2,1)} %copy.6) | copy-start | bytes 11010052
  48.9 15.9 %copy-start.2 = (bf16[256,32,224]{0,2,1:T(8,128)(2,1)S(1)}, bf16[256,32,224]{0,2,1:T(8,128)(2,1)}, u32[]{:S(2)}) copy-start(bf16[256,32,224]{0,2,1:T(8,128)(2,1)} %param.1) | copy-start | bytes 11010052
  82.9 3.0 copy-start
Sparse Core Ops, SparseCore 0:
  87.9 163.4 all-reduce.4
where the time goes:
time: 330 us; the launch traced here: 329 us
  waiting for transfers between devices  164 us (50%)
  other arithmetic  57.8 us (18%)
  matrix products  48.6 us (15%)
  local copies, waits for them, and re-layouts  32.6 us (10%)
  between operations  15.6 us (5%)
  starting transfers between devices  10.2 us (3%)
    psum x1, waiting for transfers between devices, shards(): lax.psum(partial_cov, ('track', 'cross')) / (total_lines * total_pix)  154 us
    another operation x7, other arithmetic, shards(): factor = jnp.linalg.cholesky(loaded)  31.6 us
    another operation x6, other arithmetic, shards(): inverse = jax.scipy.linalg.solve_triangular(factor, identity, lower=True)  19.8 us
    dot_general x1, matrix products, sum_lines(): jnp.einsum('kpb,kl->lpb', values, weights, precision=precision, preferred...  18.1 us
    dot_general x1, matrix products, sum_pixels(): jnp.einsum('lqb,qp->lpb', values, weights, precision=None, preferred_elem...  15.9 us
    dot_general x1, matrix products, shards(): jnp.dot(flat, inverse.T, precision=highest, preferred_element_type=jnp.fl...  11.4 us
    unnamed x7, local copies, waits for them, and re-layouts  10.8 us
    sub x1, local copies, waits for them, and re-layouts, shards(): residual = cube.astype(jnp.float32) - window / count  9.86 us
  transfers between devices with their start and end apart: 5, of which 4 were waited for; matrix products, arithmetic and copies ran while one was open for 5% of the time, Pallas kernels for 0%

commit v1 on v0

--- a/solution.py
+++ b/solution.py
@@ -27,6 +27,38 @@
     target = jnp.arange(rows_out)[None, :]
     inside = (source >= target) & (source <= target + 2 * HALF)
     return inside.astype(dtype)
+
+
+def butterfly_sum(x, axis):
+    count = lax.axis_size(axis)
+    step = 1
+    while step < count:
+        pairs = [(i, i ^ step) for i in range(count)]
+        x = x + lax.ppermute(x, axis, pairs)
+        step *= 2
+    return x
+
+
+def pack_symmetric(c):
+    h = c.shape[0] // 2
+    row = jnp.arange(h)[:, None]
+    col = jnp.arange(h)[None, :]
+    c11, c12, c22 = c[:h, :h], c[:h, h:], c[h:, h:]
+    mixed = jnp.where(col >= row, c11, c22)
+    return jnp.concatenate([c12, mixed, jnp.diagonal(c22)[None, :]], axis=0)
+
+
+def unpack_symmetric(p):
+    h = p.shape[1]
+    row = jnp.arange(h)[:, None]
+    col = jnp.arange(h)[None, :]
+    c12, mixed, d22 = p[:h], p[h:2 * h], p[2 * h]
+    c11 = jnp.where(col >= row, mixed, mixed.T)
+    c22 = jnp.where(col < row, mixed, mixed.T)
+    c22 = jnp.where(col == row, d22[None, :], c22)
+    top = jnp.concatenate([c11, c12], axis=1)
+    bottom = jnp.concatenate([c12.T, c22], axis=1)
+    return jnp.concatenate([top, bottom], axis=0)
 
 
 def window_count(first, local, total):
@@ -67,7 +99,8 @@
     flat = residual.reshape(lines_dev * pix_dev, bands)
     flat_bf = flat.astype(jnp.bfloat16)
     partial_cov = jnp.dot(flat_bf.T, flat_bf, preferred_element_type=jnp.float32)
-    covariance = lax.psum(partial_cov, ("track", "cross")) / (total_lines * total_pix)
+    packed = butterfly_sum(butterfly_sum(pack_symmetric(partial_cov), "cross"), "track")
+    covariance = unpack_symmetric(packed) / (total_lines * total_pix)
     identity = jnp.eye(bands, dtype=jnp.float32)
     loaded = covariance + LOAD * (jnp.trace(covariance) / bands) * identity
     factor = jnp.linalg.cholesky(loaded)

time: 330 us -> 222 us (0.67)
  waiting for transfers between devices: 164 us -> 23.4 us
  starting transfers between devices: 10.2 us -> 57.8 us
  between operations: 15.6 us -> 2.3 us
    psum x1 -> x0, waiting for transfers between devices: 154 us -> none  [shards(): lax.psum(partial_cov, ('track', 'cross')) / (total_lines * total_pix)]
    ppermute x0 -> x5, starting transfers between devices: none -> 47.6 us  [butterfly_sum(): x = x + lax.ppermute(x, axis, pairs)]
    ppermute x0 -> x5, waiting for transfers between devices: none -> 13 us  [butterfly_sum(): x = x + lax.ppermute(x, axis, pairs)]
  transfers between devices with their start and end apart: 5 -> 9, of which waited for: 4 -> 7; matrix products, arithmetic and copies ran while one was open for 5% -> 7% of each run, Pallas kernels for 0% -> 0%
where the time goes in v1:
time: 222 us
  starting transfers between devices  57.8 us (26%)
  other arithmetic  55.7 us (25%)
  matrix products  47.7 us (21%)
  local copies, waits for them, and re-layouts  34.6 us (16%)
  waiting for transfers between devices  23.4 us (11%)
  between operations  2.3 us (1%)
    ppermute x5, starting transfers between devices, butterfly_sum(): x = x + lax.ppermute(x, axis, pairs)  47.6 us
    another operation x7, other arithmetic, shards(): factor = jnp.linalg.cholesky(loaded)  31.6 us
    another operation x6, other arithmetic, shards(): inverse = jax.scipy.linalg.solve_triangular(factor, identity, lower=True)  20.1 us
    dot_general x1, matrix products, sum_lines(): jnp.einsum('kpb,kl->lpb', values, weights, precision=precision, preferred...  18.1 us
    dot_general x1, matrix products, sum_pixels(): jnp.einsum('lqb,qp->lpb', values, weights, precision=None, preferred_elem...  15.9 us
    ppermute x5, waiting for transfers between devices, butterfly_sum(): x = x + lax.ppermute(x, axis, pairs)  13 us
    dot_general x1, matrix products, shards(): jnp.dot(flat, inverse.T, precision=highest, preferred_element_type=jnp.fl...  11.1 us
    unnamed x7, local copies, waits for them, and re-layouts  10.8 us
  transfers between devices with their start and end apart: 9, of which 7 were waited for; matrix products, arithmetic and copies ran while one was open for 7% of the time, Pallas kernels for 0%

profile of v1, /device:TPU:0, one launch (start us, length us, event | category | flops | bytes accessed | tf_op | source)
XLA Modules:
  0.0 221.6 jit_solution(16750601395316609438)
XLA Ops:
  0.0 7.8 %copy.16 = bf16[256,32,224]{2,1,0:T(8,128)(2,1)} copy(bf16[256,32,224]{0,2,1:T(8,128)(2,1)} %param.1) | data formatting | bytes 7340032 | tf_op args[0]
  7.8 1.1 fusion.48
  8.9 4.9 %collective-permute-start = (bf16[15,32,224]{2,1,0:T(8,128)(2,1)S(1)}, bf16[15,32,224]{2,1,0:T(8,128)(2,1)S(1)}, u32[]{:S(2)}, u32[]{:S(2)}) collective-permute-start(bf16[15,32,224]{2,1,0:T(8,128)(2,1)S(1)} %get-tuple-element.27), channel_id=1, source_target_pairs={{0,8},{8,16},{16,24},{1,9},{9,17},{17,25},{2,10},{10,18},{18,26},{... | collective-permute-start | bytes 645128 | tf_op jit(solution)/shard_map/ppermute | solution.py:17
  13.8 1.3 collective-permute-start.1
  15.1 3.9 %collective-permute-done = bf16[15,32,224]{2,1,0:T(8,128)(2,1)S(1)} collective-permute-done((bf16[15,32,224]{2,1,0:T(8,128)(2,1)S(1)}, bf16[15,32,224]{2,1,0:T(8,128)(2,1)S(1)}, u32[]{:S(2)}, u32[]{:S(2)}) %collective-permute-start) | collective-permute-done | bytes 215072 | tf_op jit(solution)/shard_map/ppermute | solution.py:17
  19.0 4.1 %collective-permute-done.1 = bf16[15,32,224]{2,1,0:T(8,128)(2,1)S(1)} collective-permute-done((bf16[15,32,224]{2,1,0:T(8,128)(2,1)S(1)}, bf16[15,32,224]{2,1,0:T(8,128)(2,1)S(1)}, u32[]{:S(2)}, u32[]{:S(2)}) %collective-permute-start.1) | collective-permute-done | bytes 215072 | tf_op jit(solution)/shard_map/ppermute | solution.py:20
  23.2 2.7 %pad_maximum_fusion = bf16[286,32,224]{2,1,0:T(8,128)(2,1)S(1)} fusion(bf16[15,32,224]{2,1,0:T(8,128)(2,1)S(1)} %collective-permute-done.1, bf16[256,32,224]{2,1,0:T(8,128)(2,1)} %copy.16, bf16[15,32,224]{2,1,0:T(8,128)(2,1)S(1)} %collective-permute-done), kind=kLoop, calls=%fused_computation.15 | loop fusion | flops 4100096 | bytes 8200192 | tf_op jit(solution)/shard_map/concatenate | solution.py:21
  25.9 1.0 fusion.47
  27.0 0.8 copy.19
  27.8 2.7 %collective-permute-start.2 = (bf16[286,15,224]{2,0,1:T(8,128)(2,1)S(1)}, bf16[286,15,224]{2,0,1:T(8,128)(2,1)}, u32[]{:S(2)}, u32[]{:S(2)}) collective-permute-start(bf16[286,15,224]{2,0,1:T(8,128)(2,1)S(1)} %copy.19), channel_id=1, source_target_pairs={{0,1},{1,2},{2,3},{3,4},{4,5},{5,6},{6,7},{8,9},{9,10},{10,11},{11... | collective-permute-start | bytes 5765768 | tf_op jit(solution)/shard_map/ppermute | solution.py:17
  30.5 2.1 copy.20
  32.7 1.3 collective-permute-start.3
  33.9 0.0 copy-start.1
  34.0 0.1 broadcast_multiply_fusion.1
  34.1 0.0 collective-permute-done.2
  34.1 3.0 %copy.21 = bf16[286,15,224]{2,1,0:T(8,128)(2,1)S(1)} copy(bf16[286,15,224]{2,0,1:T(8,128)(2,1)} %collective-permute-done.2) | data formatting | bytes 3843840 | tf_op jit(solution)/shard_map/ppermute | solution.py:17
  37.1 2.4 %collective-permute-done.3 = bf16[286,15,224]{2,0,1:T(8,128)(2,1)} collective-permute-done((bf16[286,15,224]{2,0,1:T(8,128)(2,1)}, bf16[286,15,224]{2,0,1:T(8,128)(2,1)}, u32[]{:S(2)}, u32[]{:S(2)}) %collective-permute-start.3) | collective-permute-done | bytes 1921952 | tf_op jit(solution)/shard_map/ppermute | solution.py:20
  39.5 2.9 %copy.22 = bf16[286,15,224]{2,1,0:T(8,128)(2,1)S(1)} copy(bf16[286,15,224]{2,0,1:T(8,128)(2,1)} %collective-permute-done.3) | data formatting | bytes 3843840 | tf_op jit(solution)/shard_map/ppermute | solution.py:20
  42.4 0.0 copy-done.1
  42.4 0.0 copy-start.2
  42.4 15.9 %fusion.14 = f32[286,32,224]{2,1,0:T(8,128)} fusion(bf16[286,15,224]{2,1,0:T(8,128)(2,1)S(1)} %copy.22, bf16[15,32,224]{2,1,0:T(8,128)(2,1)S(1)} %collective-permute-done.1, bf16[256,32,224]{2,1,0:T(8,128)(2,1)S(1)} %copy-done.1, bf16[15,32,224]{2,1,0:T(8,128)(2,1)S(1)} %collective-permute-done, bf16[286,15,224]{2,1,0:T(8,128)(2,1)S(1)} %copy.21, ...), kind=kOutput, calls=%fused_computation.18 | convolution fusion | flops 293931584 | bytes 16144256 | tf_op jit(solution)/shard_map/lqb,qp->lpb/dot_general | solution.py:73
  58.3 0.0 copy-done.2
  58.3 18.1 %divide_subtract_fusion = f32[256,32,224]{0,2,1:T(8,128)S(1)} fusion(bf16[256,32,224]{0,2,1:T(8,128)(2,1)S(1)} %copy-done.2, f32[256,32]{0,1:T(8,128)S(1)} %broadcast_multiply_fusion.1, f32[286,32,224]{2,1,0:T(8,128)} %fusion.14, s32[256]{0:T(256)S(1)} %iota_add_fusion), kind=kOutput, calls=%fused_computation.14 | convolution fusion | flops 6303472128 | bytes 19244032 | tf_op jit(solution)/shard_map/kpb,kl->lpb/dot_general | solution.py:80
  76.4 0.0 copy-start
  76.4 3.0 %copy-done = f32[256,32,224]{0,2,1:T(8,128)} copy-done((f32[256,32,224]{0,2,1:T(8,128)}, f32[256,32,224]{0,2,1:T(8,128)S(1)}, u32[]{:S(2)}) %copy-start) | copy-done | bytes 7340056
  79.4 1.1 fusion.20
  80.6 0.1 fusion.49
  80.7 1.9 gather_fusion
  82.6 41.5 %collective-permute-start.4 = (f32[225,112]{1,0:T(8,128)S(1)}, f32[225,112]{1,0:T(8,128)S(1)}, u32[]{:S(2)}, u32[]{:S(2)}) collective-permute-start(f32[225,112]{1,0:T(8,128)S(1)} %pad_maximum_fusion.2), channel_id=1, source_target_pairs={{0,1},{1,0},{2,3},{3,2},{4,5},{5,4},{6,7},{7,6},{8,9},{9,8},{10,11... | collective-permute-start | bytes 302408 | tf_op jit(solution)/shard_map/ppermute | solution.py:37
  124.1 1.0 collective-permute-done.4
  125.1 1.6 collective-permute-start.5
  126.6 4.0 %collective-permute-done.5 = f32[225,112]{1,0:T(8,128)S(1)} collective-permute-done((f32[225,112]{1,0:T(8,128)S(1)}, f32[225,112]{1,0:T(8,128)S(1)}, u32[]{:S(2)}, u32[]{:S(2)}) %collective-permute-start.5) | collective-permute-done | bytes 100832 | tf_op jit(solution)/shard_map/ppermute | solution.py:37
  130.7 0.1 collective-permute-start.6
  130.8 4.8 %collective-permute-done.6 = f32[225,112]{1,0:T(8,128)S(1)} collective-permute-done((f32[225,112]{1,0:T(8,128)S(1)}, f32[225,112]{1,0:T(8,128)S(1)}, u32[]{:S(2)}, u32[]{:S(2)}) %collective-permute-start.6) | collective-permute-done | bytes 100832 | tf_op jit(solution)/shard_map/ppermute | solution.py:37
  135.6 1.6 collective-permute-start.7
  137.2 3.3 %collective-permute-done.7 = f32[225,112]{1,0:T(8,128)S(1)} collective-permute-done((f32[225,112]{1,0:T(8,128)S(1)}, f32[225,112]{1,0:T(8,128)S(1)}, u32[]{:S(2)}, u32[]{:S(2)}) %collective-permute-start.7) | collective-permute-done | bytes 100832 | tf_op jit(solution)/shard_map/ppermute | solution.py:37
  140.5 2.8 %collective-permute-start.8 = (f32[225,112]{1,0:T(8,128)S(1)}, f32[225,112]{1,0:T(8,128)S(1)}, u32[]{:S(2)}, u32[]{:S(2)}) collective-permute-start(f32[225,112]{1,0:T(8,128)S(1)} %add.150), channel_id=1, source_target_pairs={{0,16},{8,24},{16,0},{24,8},{1,17},{9,25},{17,1},{25,9},{2,18},{10... | collective-permute-start | bytes 302408 | tf_op jit(solution)/shard_map/ppermute | solution.py:37
  143.3 9.8 %copy.24 = f32[256,32,224]{2,1,0:T(8,128)} copy(f32[256,32,224]{0,2,1:T(8,128)} %copy-done) | data formatting | bytes 14680064 | tf_op jit(solution)/shard_map/sub | solution.py:98
  153.2 0.0 collective-permute-done.8
  153.2 0.1 copy.28
  153.4 0.1 copy.29
  153.5 0.7 select_reduce_fusion
  154.8 0.1 select_add_fusion
  154.9 0.1 copy.30
  155.1 11.7 %cholesky.50 = f32[128,128]{1,0:T(8,128)S(1)} custom-call(f32[128,128]{1,0:T(8,128)S(1)} %cholesky.121), custom_call_target="Cholesky" | custom-call | tf_op jit(solution)/shard_map/jit(cholesky)/cholesky | solution.py:106
  166.9 9.8 %custom-call.15 = f32[1,128,128]{1,2,0:T(8,128)S(1)} custom-call(f32[1,128,128]{2,1,0:T(8,128)S(1)} %get-tuple-element.37), custom_call_target="InvertDiagBlocksLowerTriangular" | custom-call | tf_op jit(solution)/shard_map/jit(cholesky)/cholesky | solution.py:106
  176.7 0.2 constant_dynamic-update-slice_fusion.1
  176.9 0.2 convolution_subtract_fusion.1
  177.2 8.8 %cholesky.108 = f32[96,96]{1,0:T(8,128)S(1)} custom-call(f32[96,96]{1,0:T(8,128)S(1)} %convolution_subtract_fusion.1), custom_call_target="Cholesky" | custom-call | tf_op jit(solution)/shard_map/jit(cholesky)/cholesky | solution.py:106
  186.0 0.7 compare_reduce_fusion
  186.6 0.6 compare_reduce_fusion.1
  188.6 0.1 fusion.33
  188.7 19.9 %custom-call.16 = f32[2,128,128]{1,2,0:T(8,128)S(1)} custom-call(f32[2,128,128]{2,1,0:T(8,128)S(1)} %pad_maximum_fusion.1), custom_call_target="InvertDiagBlocksLowerTriangular" | custom-call | tf_op jit(solution)/shard_map/jit(_solve_triangular)/triangular_solve | solution.py:107
  208.6 0.3 fusion.31
  208.9 0.4 convolution_subtract_fusion
  209.3 0.4 fusion.38
  209.7 11.1 %fusion.19 = f32[8192]{0:T(1024)S(1)} fusion(f32[8192,224]{1,0:T(8,128)} %bitcast.52, f32[96,224]{0,1:T(8,128)S(1)} %fusion.38, f32[128,224]{0,1:T(8,128)S(1)} %fusion.31), kind=kOutput, calls=%fused_computation.19 | convolution fusion | flops 4936213504 | bytes 7573504 | tf_op jit(solution)/shard_map/dot_general | solution.py:108
  220.8 0.1 div.39
  220.9 0.7 copy.32
  (26 shorter events, 0.4 us)
Async XLA Ops:
  8.9 10.1 %collective-permute-start = (bf16[15,32,224]{2,1,0:T(8,128)(2,1)S(1)}, bf16[15,32,224]{2,1,0:T(8,128)(2,1)S(1)}, u32[]{:S(2)}, u32[]{:S(2)}) collective-permute-start(bf16[15,32,224]{2,1,0:T(8,128)(2,1)S(1)} %get-tuple-element.27), channel_id=1, source_target_pairs={{0,8},{8,16},{16,24},{1,9},{9,17},{17,25},{2,10},{10,18},{18,26},{... | collective-permute-start | bytes 645128 | tf_op jit(solution)/shard_map/ppermute | solution.py:17
  13.8 9.3 %collective-permute-start.1 = (bf16[15,32,224]{2,1,0:T(8,128)(2,1)S(1)}, bf16[15,32,224]{2,1,0:T(8,128)(2,1)S(1)}, u32[]{:S(2)}, u32[]{:S(2)}) collective-permute-start(bf16[15,32,224]{2,1,0:T(8,128)(2,1)S(1)} %get-tuple-element.28), channel_id=1, source_target_pairs={{8,0},{16,8},{24,16},{9,1},{17,9},{25,17},{10,2},{18,10},{26,18},{... | collective-permute-start | bytes 645128 | tf_op jit(solution)/shard_map/ppermute | solution.py:20
  27.8 6.3 %collective-permute-start.2 = (bf16[286,15,224]{2,0,1:T(8,128)(2,1)S(1)}, bf16[286,15,224]{2,0,1:T(8,128)(2,1)}, u32[]{:S(2)}, u32[]{:S(2)}) collective-permute-start(bf16[286,15,224]{2,0,1:T(8,128)(2,1)S(1)} %copy.19), channel_id=1, source_target_pairs={{0,1},{1,2},{2,3},{3,4},{4,5},{5,6},{6,7},{8,9},{9,10},{10,11},{11... | collective-permute-start | bytes 5765768 | tf_op jit(solution)/shard_map/ppermute | solution.py:17
  32.7 6.8 %collective-permute-start.3 = (bf16[286,15,224]{2,0,1:T(8,128)(2,1)}, bf16[286,15,224]{2,0,1:T(8,128)(2,1)}, u32[]{:S(2)}, u32[]{:S(2)}) collective-permute-start(bf16[286,15,224]{2,0,1:T(8,128)(2,1)} %copy.20), channel_id=1, source_target_pairs={{1,0},{2,1},{3,2},{4,3},{5,4},{6,5},{7,6},{9,8},{10,9},{11,10},{12... | collective-permute-start | bytes 5765768 | tf_op jit(solution)/shard_map/ppermute | solution.py:20
  33.9 8.4 %copy-start.1 = (bf16[256,32,224]{2,1,0:T(8,128)(2,1)S(1)}, bf16[256,32,224]{2,1,0:T(8,128)(2,1)}, u32[]{:S(2)}) copy-start(bf16[256,32,224]{2,1,0:T(8,128)(2,1)} %copy.16) | copy-start | bytes 11010052
  42.4 15.9 %copy-start.2 = (bf16[256,32,224]{0,2,1:T(8,128)(2,1)S(1)}, bf16[256,32,224]{0,2,1:T(8,128)(2,1)}, u32[]{:S(2)}) copy-start(bf16[256,32,224]{0,2,1:T(8,128)(2,1)} %param.1) | copy-start | bytes 11010052
  76.4 3.0 %copy-start = (f32[256,32,224]{0,2,1:T(8,128)}, f32[256,32,224]{0,2,1:T(8,128)S(1)}, u32[]{:S(2)}) copy-start(f32[256,32,224]{0,2,1:T(8,128)S(1)} %divide_subtract_fusion) | copy-start | bytes 22020100
  82.6 42.5 %collective-permute-start.4 = (f32[225,112]{1,0:T(8,128)S(1)}, f32[225,112]{1,0:T(8,128)S(1)}, u32[]{:S(2)}, u32[]{:S(2)}) collective-permute-start(f32[225,112]{1,0:T(8,128)S(1)} %pad_maximum_fusion.2), channel_id=1, source_target_pairs={{0,1},{1,0},{2,3},{3,2},{4,5},{5,4},{6,7},{7,6},{8,9},{9,8},{10,11... | collective-permute-start | bytes 302408 | tf_op jit(solution)/shard_map/ppermute | solution.py:37
  125.1 5.6 %collective-permute-start.5 = (f32[225,112]{1,0:T(8,128)S(1)}, f32[225,112]{1,0:T(8,128)S(1)}, u32[]{:S(2)}, u32[]{:S(2)}) collective-permute-start(f32[225,112]{1,0:T(8,128)S(1)} %fusion.46), channel_id=1, source_target_pairs={{0,2},{1,3},{2,0},{3,1},{4,6},{5,7},{6,4},{7,5},{8,10},{9,11},{10,... | collective-permute-start | bytes 302408 | tf_op jit(solution)/shard_map/ppermute | solution.py:37
  130.7 4.9 %collective-permute-start.6 = (f32[225,112]{1,0:T(8,128)S(1)}, f32[225,112]{1,0:T(8,128)S(1)}, u32[]{:S(2)}, u32[]{:S(2)}) collective-permute-start(f32[225,112]{1,0:T(8,128)S(1)} %add.148), channel_id=1, source_target_pairs={{0,4},{1,5},{2,6},{3,7},{4,0},{5,1},{6,2},{7,3},{8,12},{9,13},{10,... | collective-permute-start | bytes 302408 | tf_op jit(solution)/shard_map/ppermute | solution.py:37
  135.6 4.9 %collective-permute-start.7 = (f32[225,112]{1,0:T(8,128)S(1)}, f32[225,112]{1,0:T(8,128)S(1)}, u32[]{:S(2)}, u32[]{:S(2)}) collective-permute-start(f32[225,112]{1,0:T(8,128)S(1)} %add.149), channel_id=1, source_target_pairs={{0,8},{8,0},{16,24},{24,16},{1,9},{9,1},{17,25},{25,17},{2,10},{10... | collective-permute-start | bytes 302408 | tf_op jit(solution)/shard_map/ppermute | solution.py:37
  140.5 12.7 %collective-permute-start.8 = (f32[225,112]{1,0:T(8,128)S(1)}, f32[225,112]{1,0:T(8,128)S(1)}, u32[]{:S(2)}, u32[]{:S(2)}) collective-permute-start(f32[225,112]{1,0:T(8,128)S(1)} %add.150), channel_id=1, source_target_pairs={{0,16},{8,24},{16,0},{24,8},{1,17},{9,25},{17,1},{25,9},{2,18},{10... | collective-permute-start | bytes 302408 | tf_op jit(solution)/shard_map/ppermute | solution.py:37

commit v2 on v1

--- a/solution.py
+++ b/solution.py
@@ -1,6 +1,9 @@
+import functools
+
 import jax
 import jax.numpy as jnp
 from jax import lax
+from jax.experimental import pallas as pl
 from jax.sharding import PartitionSpec as P
 
 HALF = 15
@@ -61,6 +64,43 @@
     return jnp.concatenate([top, bottom], axis=0)
 
 
+def sweep_kernel(n, a_ref, o_ref):
+    size = a_ref.shape[0]
+    o_ref[...] = a_ref[...]
+    rows = lax.broadcasted_iota(jnp.int32, (size, 1), 0)
+    lanes = lax.broadcasted_iota(jnp.int32, (1, size), 1)
+    sub8 = lax.broadcasted_iota(jnp.int32, (8, 1), 0)
+
+    def body(k, carry):
+        base = pl.multiple_of((k // 8) * 8, 8)
+        slab = o_ref[pl.ds(base, 8), :]
+        row = jnp.sum(jnp.where(sub8 == k - base, slab, 0.0), axis=0, keepdims=True)
+        pivot = jnp.sum(jnp.where(lanes == k, row, 0.0), axis=1, keepdims=True)
+        inv = 1.0 / pivot
+        a = o_ref[...]
+        col = jnp.sum(jnp.where(lanes == k, a, 0.0), axis=1, keepdims=True)
+        u = col * inv
+        scaled = row * inv
+        at_row = rows == k
+        at_col = lanes == k
+        edge = jnp.where(at_col, jnp.where(at_row, -inv, u), scaled)
+        o_ref[...] = jnp.where(at_row | at_col, edge, a - u * row)
+        return carry
+
+    lax.fori_loop(0, n, body, 0)
+
+
+def spd_inverse(a):
+    n = a.shape[0]
+    size = -(-n // 128) * 128
+    padded = jnp.eye(size, dtype=jnp.float32).at[:n, :n].set(a)
+    swept = pl.pallas_call(
+        functools.partial(sweep_kernel, n),
+        out_shape=jax.ShapeDtypeStruct((size, size), jnp.float32),
+    )(padded)
+    return -swept[:n, :n]
+
+
 def window_count(first, local, total):
     index = first + jnp.arange(local)
     upper = jnp.minimum(index + HALF, total - 1)
@@ -103,10 +143,9 @@
     covariance = unpack_symmetric(packed) / (total_lines * total_pix)
     identity = jnp.eye(bands, dtype=jnp.float32)
     loaded = covariance + LOAD * (jnp.trace(covariance) / bands) * identity
-    factor = jnp.linalg.cholesky(loaded)
-    inverse = jax.scipy.linalg.solve_triangular(factor, identity, lower=True)
-    whitened = jnp.dot(flat, inverse.T, precision=highest, preferred_element_type=jnp.float32)
-    scores = jnp.sum(whitened * whitened, axis=1) / bands
+    inverse = spd_inverse(loaded)
+    solved = jnp.dot(flat, inverse, precision=highest, preferred_element_type=jnp.float32)
+    scores = jnp.sum(flat * solved, axis=1) / bands
     return scores.reshape(lines_dev, pix_dev)
 
 

time: 222 us -> 218 us (0.982)
  other arithmetic: 55.7 us -> 3.93 us
  Pallas kernels: 0 us -> 37.8 us
  local copies, waits for them, and re-layouts: 34.6 us -> 45.9 us
    another operation x13 -> x0, other arithmetic: 51.7 us -> none  [the longest x7 31.6 us: shards(): factor = jnp.linalg.cholesky(loaded)]
    pallas_call x0 -> x1, Pallas kernels: none -> 37.8 us  [spd_inverse(): pl.pallas_call(functools.partial(sweep_kernel, n), out_shape=jax.ShapeDty...]
    reshape x0 -> x1, local copies, waits for them, and re-layouts: none -> 8.66 us  [shards(): flat = residual.reshape(lines_dev * pix_dev, bands)]
    unnamed x7 -> x9, local copies, waits for them, and re-layouts: 10.8 us -> 11.5 us
  transfers between devices with their start and end apart: 9 -> 9, of which waited for: 7 -> 7; matrix products, arithmetic and copies ran while one was open for 7% -> 11% of each run, Pallas kernels for 0% -> 0%
where the time goes in v2:
time: 218 us; the launch traced here: 217 us
  starting transfers between devices  57.8 us (27%)
  matrix products  47.5 us (22%)
  local copies, waits for them, and re-layouts  45.9 us (21%)
  Pallas kernels  37.8 us (17%)
  waiting for transfers between devices  23.5 us (11%)
  other arithmetic  3.93 us (2%)
    ppermute x5, starting transfers between devices, butterfly_sum(): x = x + lax.ppermute(x, axis, pairs)  47.6 us
    pallas_call x1, Pallas kernels, spd_inverse(): pl.pallas_call(functools.partial(sweep_kernel, n), out_shape=jax.ShapeDty...  37.8 us
    dot_general x1, matrix products, sum_lines(): jnp.einsum('kpb,kl->lpb', values, weights, precision=precision, preferred...  18.1 us
    dot_general x1, matrix products, sum_pixels(): jnp.einsum('lqb,qp->lpb', values, weights, precision=None, preferred_elem...  15.9 us
    ppermute x5, waiting for transfers between devices, butterfly_sum(): x = x + lax.ppermute(x, axis, pairs)  13.1 us
    dot_general x1, matrix products, shards(): jnp.dot(flat, inverse, precision=highest, preferred_element_type=jnp.floa...  12.3 us
    unnamed x9, local copies, waits for them, and re-layouts  11.5 us
    sub x1, local copies, waits for them, and re-layouts, shards(): residual = cube.astype(jnp.float32) - window / count  9.84 us
  transfers between devices with their start and end apart: 9, of which 7 were waited for; matrix products, arithmetic and copies ran while one was open for 11% of the time, Pallas kernels for 0%

profile of v2, /device:TPU:0, one launch (start us, length us, event | category | flops | bytes accessed | tf_op | source)
XLA Modules:
  0.0 217.3 jit_solution(16975077815396370324)
XLA Ops:
  0.0 7.8 %copy.15 = bf16[256,32,224]{2,1,0:T(8,128)(2,1)} copy(bf16[256,32,224]{0,2,1:T(8,128)(2,1)} %param.3) | data formatting | bytes 7340032 | tf_op args[0]
  7.8 1.1 fusion.36
  8.9 4.9 %collective-permute-start = (bf16[15,32,224]{2,1,0:T(8,128)(2,1)S(1)}, bf16[15,32,224]{2,1,0:T(8,128)(2,1)S(1)}, u32[]{:S(2)}, u32[]{:S(2)}) collective-permute-start(bf16[15,32,224]{2,1,0:T(8,128)(2,1)S(1)} %get-tuple-element.19), channel_id=1, source_target_pairs={{0,8},{8,16},{16,24},{1,9},{9,17},{17,25},{2,10},{10,18},{18,26},{... | collective-permute-start | bytes 645128 | tf_op jit(solution)/shard_map/ppermute | solution.py:20
  13.8 1.3 collective-permute-start.1
  15.1 3.9 %collective-permute-done = bf16[15,32,224]{2,1,0:T(8,128)(2,1)S(1)} collective-permute-done((bf16[15,32,224]{2,1,0:T(8,128)(2,1)S(1)}, bf16[15,32,224]{2,1,0:T(8,128)(2,1)S(1)}, u32[]{:S(2)}, u32[]{:S(2)}) %collective-permute-start) | collective-permute-done | bytes 215072 | tf_op jit(solution)/shard_map/ppermute | solution.py:20
  19.0 4.1 %collective-permute-done.1 = bf16[15,32,224]{2,1,0:T(8,128)(2,1)S(1)} collective-permute-done((bf16[15,32,224]{2,1,0:T(8,128)(2,1)S(1)}, bf16[15,32,224]{2,1,0:T(8,128)(2,1)S(1)}, u32[]{:S(2)}, u32[]{:S(2)}) %collective-permute-start.1) | collective-permute-done | bytes 215072 | tf_op jit(solution)/shard_map/ppermute | solution.py:23
  23.2 2.7 %pad_maximum_fusion = bf16[286,32,224]{2,1,0:T(8,128)(2,1)S(1)} fusion(bf16[15,32,224]{2,1,0:T(8,128)(2,1)S(1)} %collective-permute-done.1, bf16[256,32,224]{2,1,0:T(8,128)(2,1)} %copy.15, bf16[15,32,224]{2,1,0:T(8,128)(2,1)S(1)} %collective-permute-done), kind=kLoop, calls=%fused_computation.15 | loop fusion | flops 4100096 | bytes 8200192 | tf_op jit(solution)/shard_map/concatenate | solution.py:24
  25.9 1.0 fusion.35
  27.0 0.8 copy.18
  27.8 2.7 %collective-permute-start.2 = (bf16[286,15,224]{2,0,1:T(8,128)(2,1)S(1)}, bf16[286,15,224]{2,0,1:T(8,128)(2,1)}, u32[]{:S(2)}, u32[]{:S(2)}) collective-permute-start(bf16[286,15,224]{2,0,1:T(8,128)(2,1)S(1)} %copy.18), channel_id=1, source_target_pairs={{0,1},{1,2},{2,3},{3,4},{4,5},{5,6},{6,7},{8,9},{9,10},{10,11},{11... | collective-permute-start | bytes 5765768 | tf_op jit(solution)/shard_map/ppermute | solution.py:20
  30.5 2.2 %copy.19 = bf16[286,15,224]{2,0,1:T(8,128)(2,1)} copy(bf16[286,15,224]{2,1,0:T(8,128)(2,1)S(1)} %get-tuple-element.18) | data formatting | bytes 3843840 | tf_op jit(solution)/shard_map/slice | solution.py:23
  32.7 1.3 collective-permute-start.3
  34.0 0.0 copy-start.1
  34.1 0.1 broadcast_multiply_fusion.1
  34.1 0.0 collective-permute-done.2
  34.1 3.0 %copy.20 = bf16[286,15,224]{2,1,0:T(8,128)(2,1)S(1)} copy(bf16[286,15,224]{2,0,1:T(8,128)(2,1)} %collective-permute-done.2) | data formatting | bytes 3843840 | tf_op jit(solution)/shard_map/ppermute | solution.py:20
  37.2 2.4 %collective-permute-done.3 = bf16[286,15,224]{2,0,1:T(8,128)(2,1)} collective-permute-done((bf16[286,15,224]{2,0,1:T(8,128)(2,1)}, bf16[286,15,224]{2,0,1:T(8,128)(2,1)}, u32[]{:S(2)}, u32[]{:S(2)}) %collective-permute-start.3) | collective-permute-done | bytes 1921952 | tf_op jit(solution)/shard_map/ppermute | solution.py:23
  39.5 2.9 %copy.21 = bf16[286,15,224]{2,1,0:T(8,128)(2,1)S(1)} copy(bf16[286,15,224]{2,0,1:T(8,128)(2,1)} %collective-permute-done.3) | data formatting | bytes 3843840 | tf_op jit(solution)/shard_map/ppermute | solution.py:23
  42.4 0.0 copy-done.1
  42.4 0.0 copy-start.2
  42.4 15.9 %fusion.14 = f32[286,32,224]{2,1,0:T(8,128)} fusion(bf16[286,15,224]{2,1,0:T(8,128)(2,1)S(1)} %copy.21, bf16[15,32,224]{2,1,0:T(8,128)(2,1)S(1)} %collective-permute-done.1, bf16[256,32,224]{2,1,0:T(8,128)(2,1)S(1)} %copy-done.1, bf16[15,32,224]{2,1,0:T(8,128)(2,1)S(1)} %collective-permute-done, bf16[286,15,224]{2,1,0:T(8,128)(2,1)S(1)} %copy.20, ...), kind=kOutput, calls=%fused_computation.18 | convolution fusion | flops 293931584 | bytes 16144256 | tf_op jit(solution)/shard_map/lqb,qp->lpb/dot_general | solution.py:113
  58.3 0.0 copy-done.2
  58.3 18.1 %divide_subtract_fusion = f32[256,32,224]{0,2,1:T(8,128)S(1)} fusion(bf16[256,32,224]{0,2,1:T(8,128)(2,1)S(1)} %copy-done.2, f32[256,32]{0,1:T(8,128)S(1)} %broadcast_multiply_fusion.1, f32[286,32,224]{2,1,0:T(8,128)} %fusion.14, s32[256]{0:T(256)S(1)} %iota_add_fusion), kind=kOutput, calls=%fused_computation.14 | convolution fusion | flops 6303472128 | bytes 19244032 | tf_op jit(solution)/shard_map/kpb,kl->lpb/dot_general | solution.py:120
  76.4 0.0 copy-start
  76.4 3.0 %copy-done = f32[256,32,224]{0,2,1:T(8,128)} copy-done((f32[256,32,224]{0,2,1:T(8,128)}, f32[256,32,224]{0,2,1:T(8,128)S(1)}, u32[]{:S(2)}) %copy-start) | copy-done | bytes 7340056
  79.4 1.1 fusion.20
  80.6 0.1 fusion.37
  80.7 1.9 gather_fusion
  82.6 41.5 %collective-permute-start.4 = (f32[225,112]{1,0:T(8,128)S(1)}, f32[225,112]{1,0:T(8,128)S(1)}, u32[]{:S(2)}, u32[]{:S(2)}) collective-permute-start(f32[225,112]{1,0:T(8,128)S(1)} %pad_maximum_fusion.1), channel_id=1, source_target_pairs={{0,1},{1,0},{2,3},{3,2},{4,5},{5,4},{6,7},{7,6},{8,9},{9,8},{10,11... | collective-permute-start | bytes 302408 | tf_op jit(solution)/shard_map/ppermute | solution.py:40
  124.1 1.0 collective-permute-done.4
  125.1 1.6 collective-permute-start.5
  126.6 4.0 %collective-permute-done.5 = f32[225,112]{1,0:T(8,128)S(1)} collective-permute-done((f32[225,112]{1,0:T(8,128)S(1)}, f32[225,112]{1,0:T(8,128)S(1)}, u32[]{:S(2)}, u32[]{:S(2)}) %collective-permute-start.5) | collective-permute-done | bytes 100832 | tf_op jit(solution)/shard_map/ppermute | solution.py:40
  130.6 0.1 collective-permute-start.6
  130.7 4.8 %collective-permute-done.6 = f32[225,112]{1,0:T(8,128)S(1)} collective-permute-done((f32[225,112]{1,0:T(8,128)S(1)}, f32[225,112]{1,0:T(8,128)S(1)}, u32[]{:S(2)}, u32[]{:S(2)}) %collective-permute-start.6) | collective-permute-done | bytes 100832 | tf_op jit(solution)/shard_map/ppermute | solution.py:40
  135.6 1.6 collective-permute-start.7
  137.2 3.3 %collective-permute-done.7 = f32[225,112]{1,0:T(8,128)S(1)} collective-permute-done((f32[225,112]{1,0:T(8,128)S(1)}, f32[225,112]{1,0:T(8,128)S(1)}, u32[]{:S(2)}, u32[]{:S(2)}) %collective-permute-start.7) | collective-permute-done | bytes 100832 | tf_op jit(solution)/shard_map/ppermute | solution.py:40
  140.5 2.8 %collective-permute-start.8 = (f32[225,112]{1,0:T(8,128)S(1)}, f32[225,112]{1,0:T(8,128)S(1)}, u32[]{:S(2)}, u32[]{:S(2)}) collective-permute-start(f32[225,112]{1,0:T(8,128)S(1)} %add.127), channel_id=1, source_target_pairs={{0,16},{8,24},{16,0},{24,8},{1,17},{9,25},{17,1},{25,9},{2,18},{10... | collective-permute-start | bytes 302408 | tf_op jit(solution)/shard_map/ppermute | solution.py:40
  143.3 9.8 %copy.23 = f32[256,32,224]{2,1,0:T(8,128)} copy(f32[256,32,224]{0,2,1:T(8,128)} %copy-done) | data formatting | bytes 14680064 | tf_op jit(solution)/shard_map/sub | solution.py:138
  153.2 8.7 %copy.29 = f32[8192,224]{0,1:T(8,128)} copy(f32[8192,224]{1,0:T(8,128)} %bitcast.27) | data formatting | bytes 14680064 | tf_op jit(solution)/shard_map/reshape | solution.py:139
  161.8 0.0 collective-permute-done.8
  161.9 0.1 copy.27
  162.0 0.1 copy.28
  162.1 0.7 select_reduce_fusion
  163.5 0.1 select_add_fusion
  163.6 2.0 scatter.4.a_ref
  165.6 0.0 copy-start.3
  165.6 0.7 copy-done.3
  166.4 37.8 %shard_map.17 = f32[256,256]{1,0:T(8,128)} custom-call(f32[256,256]{1,0:T(8,128)} %copy-done.3), custom_call_target="tpu_custom_call" | custom-call | tf_op jit(solution)/shard_map/pallas_call | solution.py:97
  204.1 12.3 %fusion.19 = f32[8192]{0:T(1024)S(1)} fusion(f32[8192,224]{0,1:T(8,128)} %copy.29, f32[8192,224]{1,0:T(8,128)} %bitcast.28, f32[256,256]{1,0:T(8,128)} %shard_map.17), kind=kOutput, calls=%fused_computation.19 | convolution fusion | flops 4936213504 | bytes 15990784 | tf_op jit(solution)/shard_map/dot_general | solution.py:147
  216.5 0.1 div.29
  216.6 0.7 copy.30
  (16 shorter events, 0.2 us)
Async XLA Ops:
  8.9 10.1 %collective-permute-start = (bf16[15,32,224]{2,1,0:T(8,128)(2,1)S(1)}, bf16[15,32,224]{2,1,0:T(8,128)(2,1)S(1)}, u32[]{:S(2)}, u32[]{:S(2)}) collective-permute-start(bf16[15,32,224]{2,1,0:T(8,128)(2,1)S(1)} %get-tuple-element.19), channel_id=1, source_target_pairs={{0,8},{8,16},{16,24},{1,9},{9,17},{17,25},{2,10},{10,18},{18,26},{... | collective-permute-start | bytes 645128 | tf_op jit(solution)/shard_map/ppermute | solution.py:20
  13.8 9.3 %collective-permute-start.1 = (bf16[15,32,224]{2,1,0:T(8,128)(2,1)S(1)}, bf16[15,32,224]{2,1,0:T(8,128)(2,1)S(1)}, u32[]{:S(2)}, u32[]{:S(2)}) collective-permute-start(bf16[15,32,224]{2,1,0:T(8,128)(2,1)S(1)} %get-tuple-element.20), channel_id=1, source_target_pairs={{8,0},{16,8},{24,16},{9,1},{17,9},{25,17},{10,2},{18,10},{26,18},{... | collective-permute-start | bytes 645128 | tf_op jit(solution)/shard_map/ppermute | solution.py:23
  27.8 6.4 %collective-permute-start.2 = (bf16[286,15,224]{2,0,1:T(8,128)(2,1)S(1)}, bf16[286,15,224]{2,0,1:T(8,128)(2,1)}, u32[]{:S(2)}, u32[]{:S(2)}) collective-permute-start(bf16[286,15,224]{2,0,1:T(8,128)(2,1)S(1)} %copy.18), channel_id=1, source_target_pairs={{0,1},{1,2},{2,3},{3,4},{4,5},{5,6},{6,7},{8,9},{9,10},{10,11},{11... | collective-permute-start | bytes 5765768 | tf_op jit(solution)/shard_map/ppermute | solution.py:20
  32.7 6.9 %collective-permute-start.3 = (bf16[286,15,224]{2,0,1:T(8,128)(2,1)}, bf16[286,15,224]{2,0,1:T(8,128)(2,1)}, u32[]{:S(2)}, u32[]{:S(2)}) collective-permute-start(bf16[286,15,224]{2,0,1:T(8,128)(2,1)} %copy.19), channel_id=1, source_target_pairs={{1,0},{2,1},{3,2},{4,3},{5,4},{6,5},{7,6},{9,8},{10,9},{11,10},{12... | collective-permute-start | bytes 5765768 | tf_op jit(solution)/shard_map/ppermute | solution.py:23
  34.0 8.4 %copy-start.1 = (bf16[256,32,224]{2,1,0:T(8,128)(2,1)S(1)}, bf16[256,32,224]{2,1,0:T(8,128)(2,1)}, u32[]{:S(2)}) copy-start(bf16[256,32,224]{2,1,0:T(8,128)(2,1)} %copy.15) | copy-start | bytes 11010052
  42.4 15.9 %copy-start.2 = (bf16[256,32,224]{0,2,1:T(8,128)(2,1)S(1)}, bf16[256,32,224]{0,2,1:T(8,128)(2,1)}, u32[]{:S(2)}) copy-start(bf16[256,32,224]{0,2,1:T(8,128)(2,1)} %param.3) | copy-start | bytes 11010052
  76.4 3.0 %copy-start = (f32[256,32,224]{0,2,1:T(8,128)}, f32[256,32,224]{0,2,1:T(8,128)S(1)}, u32[]{:S(2)}) copy-start(f32[256,32,224]{0,2,1:T(8,128)S(1)} %divide_subtract_fusion) | copy-start | bytes 22020100
  82.6 42.4 %collective-permute-start.4 = (f32[225,112]{1,0:T(8,128)S(1)}, f32[225,112]{1,0:T(8,128)S(1)}, u32[]{:S(2)}, u32[]{:S(2)}) collective-permute-start(f32[225,112]{1,0:T(8,128)S(1)} %pad_maximum_fusion.1), channel_id=1, source_target_pairs={{0,1},{1,0},{2,3},{3,2},{4,5},{5,4},{6,7},{7,6},{8,9},{9,8},{10,11... | collective-permute-start | bytes 302408 | tf_op jit(solution)/shard_map/ppermute | solution.py:40
  125.1 5.6 %collective-permute-start.5 = (f32[225,112]{1,0:T(8,128)S(1)}, f32[225,112]{1,0:T(8,128)S(1)}, u32[]{:S(2)}, u32[]{:S(2)}) collective-permute-start(f32[225,112]{1,0:T(8,128)S(1)} %fusion.34), channel_id=1, source_target_pairs={{0,2},{1,3},{2,0},{3,1},{4,6},{5,7},{6,4},{7,5},{8,10},{9,11},{10,... | collective-permute-start | bytes 302408 | tf_op jit(solution)/shard_map/ppermute | solution.py:40
  130.6 4.9 %collective-permute-start.6 = (f32[225,112]{1,0:T(8,128)S(1)}, f32[225,112]{1,0:T(8,128)S(1)}, u32[]{:S(2)}, u32[]{:S(2)}) collective-permute-start(f32[225,112]{1,0:T(8,128)S(1)} %add.125), channel_id=1, source_target_pairs={{0,4},{1,5},{2,6},{3,7},{4,0},{5,1},{6,2},{7,3},{8,12},{9,13},{10,... | collective-permute-start | bytes 302408 | tf_op jit(solution)/shard_map/ppermute | solution.py:40
  135.6 4.9 %collective-permute-start.7 = (f32[225,112]{1,0:T(8,128)S(1)}, f32[225,112]{1,0:T(8,128)S(1)}, u32[]{:S(2)}, u32[]{:S(2)}) collective-permute-start(f32[225,112]{1,0:T(8,128)S(1)} %add.126), channel_id=1, source_target_pairs={{0,8},{8,0},{16,24},{24,16},{1,9},{9,1},{17,25},{25,17},{2,10},{10... | collective-permute-start | bytes 302408 | tf_op jit(solution)/shard_map/ppermute | solution.py:40
  140.5 21.4 %collective-permute-start.8 = (f32[225,112]{1,0:T(8,128)S(1)}, f32[225,112]{1,0:T(8,128)S(1)}, u32[]{:S(2)}, u32[]{:S(2)}) collective-permute-start(f32[225,112]{1,0:T(8,128)S(1)} %add.127), channel_id=1, source_target_pairs={{0,16},{8,24},{16,0},{24,8},{1,17},{9,25},{17,1},{25,9},{2,18},{10... | collective-permute-start | bytes 302408 | tf_op jit(solution)/shard_map/ppermute | solution.py:40
  165.6 0.7 copy-start.3

commit v3 on v2

--- a/solution.py
+++ b/solution.py
@@ -4,6 +4,7 @@
 import jax.numpy as jnp
 from jax import lax
 from jax.experimental import pallas as pl
+from jax.experimental.layout import Layout, with_layout_constraint
 from jax.sharding import PartitionSpec as P
 
 HALF = 15
@@ -122,6 +123,96 @@
     )
 
 
+def neighbour_pairs(n_track, n_cross, dt, dc):
+    pairs = []
+    for t in range(n_track):
+        for c in range(n_cross):
+            if 0 <= t + dt < n_track and 0 <= c + dc < n_cross:
+                pairs.append(((t + dt) * n_cross + c + dc, t * n_cross + c))
+    return pairs
+
+
+def halos(planes):
+    n_track = lax.axis_size("track")
+    n_cross = lax.axis_size("cross")
+    both = ("track", "cross")
+
+    def fetch(piece, dt, dc):
+        if dt == 0:
+            pairs = [(c + dc, c) for c in range(n_cross) if 0 <= c + dc < n_cross]
+            return lax.ppermute(piece, "cross", pairs)
+        if dc == 0:
+            pairs = [(t + dt, t) for t in range(n_track) if 0 <= t + dt < n_track]
+            return lax.ppermute(piece, "track", pairs)
+        return lax.ppermute(piece, both, neighbour_pairs(n_track, n_cross, dt, dc))
+
+    first, last = slice(0, HALF), slice(-HALF, None)
+    sides = {
+        "left": fetch(planes[last], 0, -1),
+        "right": fetch(planes[first], 0, 1),
+    }
+    tops = {
+        "left": fetch(planes[last, :, last], -1, -1),
+        "middle": fetch(planes[:, :, last], -1, 0),
+        "right": fetch(planes[first, :, last], -1, 1),
+    }
+    bottoms = {
+        "left": fetch(planes[last, :, first], 1, -1),
+        "middle": fetch(planes[:, :, first], 1, 0),
+        "right": fetch(planes[first, :, first], 1, 1),
+    }
+    return sides, tops, bottoms
+
+
+def line_weights(lines):
+    target = jnp.arange(lines)[None, :]
+    middle = jnp.abs(jnp.arange(lines)[:, None] - target) <= HALF
+    side = jnp.arange(HALF)[:, None]
+    top = target <= side
+    bottom = target >= lines - HALF + side
+    return [w.astype(jnp.bfloat16) for w in (top, middle, bottom)]
+
+
+def sum_lines(top, middle, bottom, weights):
+    total = None
+    for values, w in zip((top, middle, bottom), weights):
+        term = jnp.einsum("qbk,kl->qbl", values, w, preferred_element_type=jnp.float32)
+        total = term if total is None else total + term
+    return total
+
+
+def pixel_window_kernel(left_ref, middle_ref, right_ref, out_ref):
+    refs = [(left_ref, q) for q in range(left_ref.shape[0])]
+    refs += [(middle_ref, q) for q in range(middle_ref.shape[0])]
+    refs += [(right_ref, q) for q in range(right_ref.shape[0])]
+
+    def plane(q):
+        ref, i = refs[q]
+        return ref[i]
+
+    span = 2 * HALF + 1
+    running = plane(0)
+    for q in range(1, span):
+        running = running + plane(q)
+    out_ref[0] = running
+    for p in range(1, out_ref.shape[0]):
+        running = running + plane(p + span - 1) - plane(p - 1)
+        out_ref[p] = running
+
+
+def sum_pixels(left, middle, right):
+    width, bands, lines = middle.shape
+    block = 32 if bands % 32 == 0 else bands
+    spec = lambda n: pl.BlockSpec((n, block, lines), lambda i: (0, i, 0))
+    return pl.pallas_call(
+        pixel_window_kernel,
+        grid=(bands // block,),
+        in_specs=[spec(left.shape[0]), spec(width), spec(right.shape[0])],
+        out_specs=spec(width),
+        out_shape=jax.ShapeDtypeStruct((width, bands, lines), jnp.float32),
+    )(left, middle, right)
+
+
 def shards(cube):
     lines_dev, pix_dev, bands = cube.shape
     n_track = lax.axis_size("track")
@@ -129,24 +220,31 @@
     total_lines = lines_dev * n_track
     total_pix = pix_dev * n_cross
     highest = lax.Precision.HIGHEST
-    extended = with_halo(cube, (("track", 0), ("cross", 1)), HALF)
-    across = sum_pixels(extended, pix_dev, jnp.bfloat16)
-    window = sum_lines(across, lines_dev, jnp.float32, highest)
+    planes = jnp.transpose(cube, (1, 2, 0))
+    sides, tops, bottoms = halos(planes)
+    weights = line_weights(lines_dev)
+    middle = sum_lines(tops["middle"], planes, bottoms["middle"], weights)
+    left = sum_lines(tops["left"], sides["left"], bottoms["left"], weights)
+    right = sum_lines(tops["right"], sides["right"], bottoms["right"], weights)
+    window = sum_pixels(left, middle, right)
     line_count = window_count(lax.axis_index("track") * lines_dev, lines_dev, total_lines)
     pixel_count = window_count(lax.axis_index("cross") * pix_dev, pix_dev, total_pix)
-    count = line_count[:, None, None] * pixel_count[None, :, None]
-    residual = cube.astype(jnp.float32) - window / count
-    flat = residual.reshape(lines_dev * pix_dev, bands)
-    flat_bf = flat.astype(jnp.bfloat16)
-    partial_cov = jnp.dot(flat_bf.T, flat_bf, preferred_element_type=jnp.float32)
+    count = pixel_count[:, None, None] * line_count[None, None, :]
+    residual = planes.astype(jnp.float32) - window / count
+    residual_bf = residual.astype(jnp.bfloat16)
+    partial_cov = jnp.einsum(
+        "pjl,pkl->jk", residual_bf, residual_bf, preferred_element_type=jnp.float32
+    )
     packed = butterfly_sum(butterfly_sum(pack_symmetric(partial_cov), "cross"), "track")
     covariance = unpack_symmetric(packed) / (total_lines * total_pix)
     identity = jnp.eye(bands, dtype=jnp.float32)
     loaded = covariance + LOAD * (jnp.trace(covariance) / bands) * identity
     inverse = spd_inverse(loaded)
-    solved = jnp.dot(flat, inverse, precision=highest, preferred_element_type=jnp.float32)
-    scores = jnp.sum(flat * solved, axis=1) / bands
-    return scores.reshape(lines_dev, pix_dev)
+    solved = jnp.einsum(
+        "pbl,bj->pjl", residual, inverse, precision=highest, preferred_element_type=jnp.float32
+    )
+    scores = jnp.sum(residual * solved, axis=1) / bands
+    return scores.T
 
 
 def solution(mesh):

time: 218 us -> 180 us (0.83)
  starting transfers between devices: 57.8 us -> 30.7 us
  local copies, waits for them, and re-layouts: 45.9 us -> 23.7 us
  Pallas kernels: 37.8 us -> 48 us
  waiting for transfers between devices: 23.5 us -> 30.4 us
  matrix products: 47.5 us -> 43.2 us
    ppermute x5, starting transfers between devices: 47.6 us -> 6.83 us  [butterfly_sum(): x = x + lax.ppermute(x, axis, pairs)]
    slice x4 -> x9, local copies, waits for them, and re-layouts: 5.13 us -> 19.1 us  [the longest x2 5.78 us: halos(): planes[:, :, first]]
    ppermute x4 -> x8, starting transfers between devices: 10.2 us -> 23.9 us  [the longest x4 12.6 us: fetch(): return lax.ppermute(piece, both, neighbour_pairs(n_track, n_cross, dt, dc))]
    unnamed x9 -> x12, local copies, waits for them, and re-layouts: 11.5 us -> 0.71 us
    pallas_call x0 -> x1, Pallas kernels: none -> 10.3 us  [sum_pixels(): pl.pallas_call(pixel_window_kernel, grid=(bands // block,), in_specs=[spe...]
    sub x1 -> x0, local copies, waits for them, and re-layouts: 9.84 us -> none  [shards(): residual = cube.astype(jnp.float32) - window / count]
    reshape x1 -> x0, local copies, waits for them, and re-layouts: 8.66 us -> none  [shards(): flat = residual.reshape(lines_dev * pix_dev, bands)]
    ppermute x2 -> x0, local copies, waits for them, and re-layouts: 5.89 us -> none  [the longest x1 3.02 us: with_halo(): lax.ppermute(lax.slice_in_dim(block, block.shape[dim] - width, None, axis...]
  transfers between devices with their start and end apart: 9 -> 13, of which waited for: 7 -> 7; matrix products, arithmetic and copies ran while one was open for 11% -> 19% of each run, Pallas kernels for 0% -> 0%
where the time goes in v3:
time: 180 us; the launch traced here: 179 us
  Pallas kernels  48 us (27%)
  matrix products  43.2 us (24%)
  starting transfers between devices  30.7 us (17%)
  waiting for transfers between devices  30.4 us (17%)
  local copies, waits for them, and re-layouts  23.7 us (13%)
  other arithmetic  2.31 us (1%)
    pallas_call x1, Pallas kernels, spd_inverse(): pl.pallas_call(functools.partial(sweep_kernel, n), out_shape=jax.ShapeDty...  37.7 us
    dot_general x9, matrix products, sum_lines(): jnp.einsum('qbk,kl->qbl', values, w, preferred_element_type=jnp.float32)  20.7 us
    ppermute x5, waiting for transfers between devices, butterfly_sum(): x = x + lax.ppermute(x, axis, pairs)  17.7 us
    dot_general x1, matrix products, shards(): jnp.einsum('pbl,bj->pjl', residual, inverse, precision=highest, preferred...  13.2 us
    ppermute x2, waiting for transfers between devices, fetch(): return lax.ppermute(piece, 'track', pairs)  12.7 us
    ppermute x4, starting transfers between devices, fetch(): return lax.ppermute(piece, both, neighbour_pairs(n_track, n_cross, dt, dc))  12.6 us
    pallas_call x1, Pallas kernels, sum_pixels(): pl.pallas_call(pixel_window_kernel, grid=(bands // block,), in_specs=[spe...  10.3 us
    dot_general x1, matrix products, shards(): jnp.einsum('pjl,pkl->jk', residual_bf, residual_bf, preferred_element_typ...  9.24 us
  transfers between devices with their start and end apart: 13, of which 7 were waited for; matrix products, arithmetic and copies ran while one was open for 19% of the time, Pallas kernels for 0%

profile of v3, /device:TPU:0, one launch (start us, length us, event | category | flops | bytes accessed | tf_op | source)
XLA Modules:
  0.0 179.3 jit_solution(7783759694481312386)
XLA Ops:
  0.0 2.5 %fusion.52 = (bf16[15,224,15]{2,1,0:T(8,128)(2,1)S(1)}, bf16[15,224,15]{2,1,0:T(8,128)(2,1)S(1)}, bf16[15,224,15]{2,1,0:T(8,128)(2,1)S(1)}, bf16[15,224,15]{2,1,0:T(8,128)(2,1)S(1)}) fusion(bf16[32,224,256]{2,1,0:T(8,128)(2,1)} %bitcast.68), kind=kLoop, calls=%fused_computation.64 | loop fusion | bytes 806400 | tf_op jit(solution)/shard_map/slice | solution.py:162
  2.6 1.0 copy.32
  3.6 1.3 collective-permute-start.5
  4.9 1.0 copy.33
  5.9 1.3 collective-permute-start.7
  7.2 3.9 %fusion.53 = (bf16[15,224,256]{2,1,0:T(8,128)(2,1)}, bf16[15,224,256]{2,1,0:T(8,128)(2,1)}) fusion(bf16[32,224,256]{2,1,0:T(8,128)(2,1)} %bitcast.69), kind=kLoop, calls=%fused_computation.65 | loop fusion | bytes 6881280 | tf_op jit(solution)/shard_map/slice | solution.py:152
  11.2 1.3 collective-permute-start.6
  12.4 1.0 copy.26
  13.5 8.7 %collective-permute-start = (bf16[15,224,15]{1,2,0:T(8,128)(2,1)}, bf16[15,224,15]{1,2,0:T(8,128)(2,1)}, u32[]{:S(2)}, u32[]{:S(2)}) collective-permute-start(bf16[15,224,15]{1,2,0:T(8,128)(2,1)} %copy.26), channel_id=1, source_target_pairs={{0,9},{1,10},{2,11},{3,12},{4,13},{5,14},{6,15},{8,17},{9,18},{10,... | collective-permute-start | bytes 302408 | tf_op jit(solution)/shard_map/ppermute | solution.py:147
  22.2 1.0 copy.27
  23.2 1.3 collective-permute-start.2
  24.5 0.5 iota_add_fusion
  25.0 4.1 %fusion.54 = (bf16[32,224,15]{2,1,0:T(8,128)(2,1)S(1)}, bf16[32,224,15]{2,1,0:T(8,128)(2,1)}) fusion(bf16[32,224,256]{2,1,0:T(8,128)(2,1)} %bitcast.70), kind=kLoop, calls=%fused_computation.66 | loop fusion | bytes 860160 | tf_op jit(solution)/shard_map/slice | solution.py:161
  29.2 0.0 copy-done
  29.2 4.1 %fusion.15 = f32[256,32,224]{0,2,1:T(8,128)} fusion(bf16[256,32,224]{0,2,1:T(8,128)(2,1)S(1)} %copy-done), kind=kOutput, calls=%fused_computation.18 | convolution fusion | flops 939720704 | bytes 11010048 | tf_op jit(solution)/shard_map/qbk,kl->qbl/dot_general | solution.py:179
  33.3 2.7 %copy.28 = bf16[32,224,15]{1,0,2:T(8,128)(2,1)} copy(bf16[32,224,15]{2,1,0:T(8,128)(2,1)} %get-tuple-element.24) | data formatting | bytes 430080 | tf_op jit(solution)/shard_map/slice | solution.py:156
  36.0 1.6 copy.30
  37.6 0.1 broadcast_multiply_fusion
  37.7 0.0 collective-permute-done.5
  37.7 4.1 %collective-permute-start.1 = (bf16[15,224,256]{2,1,0:T(8,128)(2,1)}, bf16[15,224,256]{2,1,0:T(8,128)(2,1)S(1)}, u32[]{:S(2)}, u32[]{:S(2)}) collective-permute-start(bf16[15,224,256]{2,1,0:T(8,128)(2,1)} %get-tuple-element.22), channel_id=1, source_target_pairs={{0,1},{1,2},{2,3},{3,4},{4,5},{5,6},{6,7},{8,9},{9,10},{10,11},{11... | collective-permute-start | bytes 5160968 | tf_op jit(solution)/shard_map/ppermute | solution.py:143
  41.8 0.0 slice-start
  41.8 1.7 fusion.27
  43.6 0.0 collective-permute-done
  43.6 4.7 %collective-permute-start.3 = (bf16[32,224,15]{1,0,2:T(8,128)(2,1)}, bf16[32,224,15]{1,0,2:T(8,128)(2,1)S(1)}, u32[]{:S(2)}, u32[]{:S(2)}) collective-permute-start(bf16[32,224,15]{1,0,2:T(8,128)(2,1)} %copy.28), channel_id=1, source_target_pairs={{0,8},{8,16},{16,24},{1,9},{9,17},{17,25},{2,10},{10,18},{18,26},{... | collective-permute-start | bytes 645128 | tf_op jit(solution)/shard_map/ppermute | solution.py:146
  48.3 1.6 fusion.30
  49.8 0.0 slice-start.1
  49.9 0.0 copy-start.3
  49.9 4.1 %collective-permute-done.3 = bf16[32,224,15]{1,0,2:T(8,128)(2,1)S(1)} collective-permute-done((bf16[32,224,15]{1,0,2:T(8,128)(2,1)}, bf16[32,224,15]{1,0,2:T(8,128)(2,1)S(1)}, u32[]{:S(2)}, u32[]{:S(2)}) %collective-permute-start.3) | collective-permute-done | bytes 215072 | tf_op jit(solution)/shard_map/ppermute | solution.py:146
  54.0 0.0 copy-done.2
  54.0 1.3 collective-permute-start.4
  55.3 1.2 fusion.10
  56.5 8.5 %collective-permute-done.4 = bf16[32,224,15]{1,0,2:T(8,128)(2,1)S(1)} collective-permute-done((bf16[32,224,15]{1,0,2:T(8,128)(2,1)S(1)}, bf16[32,224,15]{1,0,2:T(8,128)(2,1)S(1)}, u32[]{:S(2)}, u32[]{:S(2)}) %collective-permute-start.4) | collective-permute-done | bytes 215072 | tf_op jit(solution)/shard_map/ppermute | solution.py:146
  65.0 4.3 %add_bitcast_fusion.middle_ref = f32[32,224,256]{2,1,0:T(8,128)} fusion(f32[256,32,224]{0,2,1:T(8,128)S(1)} %fusion.10, f32[256,32,224]{0,2,1:T(8,128)S(1)} %bitcast.72, bf16[32,224,15]{1,0,2:T(8,128)(2,1)S(1)} %collective-permute-done.4, s32[15]{0:T(128)S(1)} %copy-done.3), kind=kOutput, calls=%fused_computation.4 | convolution fusion | flops 58724096 | bytes 22235196 | tf_op jit(solution)/shard_map/qbk,kl->qbl/dot_general | solution.py:179
  69.3 0.0 collective-permute-done.6
  69.3 0.6 fusion.13
  69.9 0.0 collective-permute-done.7
  70.0 3.3 %add_bitcast_fusion.1.right_ref = f32[15,224,256]{2,1,0:T(8,128)} fusion(f32[256,15,224]{0,2,1:T(8,128)S(1)} %fusion.27, f32[256,15,224]{0,2,1:T(8,128)S(1)} %fusion.13, bf16[15,224,15]{1,2,0:T(8,128)(2,1)} %collective-permute-done.7, s32[15]{0:T(128)S(1)} %copy-done.3), kind=kOutput, calls=%fused_computation.7 | convolution fusion | flops 27528960 | bytes 10422780 | tf_op jit(solution)/shard_map/qbk,kl->qbl/dot_general | solution.py:179
  73.3 0.0 collective-permute-done.1
  73.3 0.6 fusion.17
  73.9 0.0 collective-permute-done.2
  73.9 3.3 %add_bitcast_fusion.2.left_ref = f32[15,224,256]{2,1,0:T(8,128)} fusion(f32[256,15,224]{0,2,1:T(8,128)S(1)} %fusion.30, f32[256,15,224]{0,2,1:T(8,128)S(1)} %fusion.17, bf16[15,224,15]{1,2,0:T(8,128)(2,1)} %collective-permute-done.2, s32[15]{0:T(128)S(1)} %copy-done.3), kind=kOutput, calls=%fused_computation.8 | convolution fusion | flops 27528960 | bytes 10422780 | tf_op jit(solution)/shard_map/qbk,kl->qbl/dot_general | solution.py:179
  77.2 10.3 %shard_map.17 = f32[32,224,256]{2,1,0:T(8,128)} custom-call(f32[15,224,256]{2,1,0:T(8,128)} %add_bitcast_fusion.2.left_ref, f32[32,224,256]{2,1,0:T(8,128)} %add_bitcast_fusion.middle_ref, f32[15,224,256]{2,1,0:T(8,128)} %add_bitcast_fusion.1.right_ref), custom_call_target="tpu_custom_call" | custom-call | tf_op jit(solution)/shard_map/pallas_call | solution.py:207
  87.5 9.2 %fusion.3 = f32[224,224]{1,0:T(8,128)S(1)} fusion(f32[32,224,256]{2,1,0:T(8,128)} %shard_map.17, f32[32,256]{1,0:T(8,128)S(1)} %broadcast_multiply_fusion, bf16[256,32,224]{0,2,1:T(8,128)(2,1)} %param.3), kind=kOutput, calls=%fused_computation.9 | convolution fusion | flops 829423616 | bytes 11243520 | tf_op jit(solution)/shard_map/pjl,pkl->jk/dot_general | solution.py:235
  96.8 0.1 fusion.55
  96.9 1.7 gather_fusion
  98.6 0.2 collective-permute-start.8
  98.8 1.2 collective-permute-done.8
  100.0 2.7 %collective-permute-start.9 = (f32[225,112]{1,0:T(8,128)S(1)}, f32[225,112]{1,0:T(8,128)S(1)}, u32[]{:S(2)}, u32[]{:S(2)}) collective-permute-start(f32[225,112]{1,0:T(8,128)S(1)} %fusion.51), channel_id=1, source_target_pairs={{0,2},{1,3},{2,0},{3,1},{4,6},{5,7},{6,4},{7,5},{8,10},{9,11},{10,... | collective-permute-start | bytes 302408 | tf_op jit(solution)/shard_map/ppermute | solution.py:41
  102.8 3.5 %collective-permute-done.9 = f32[225,112]{1,0:T(8,128)S(1)} collective-permute-done((f32[225,112]{1,0:T(8,128)S(1)}, f32[225,112]{1,0:T(8,128)S(1)}, u32[]{:S(2)}, u32[]{:S(2)}) %collective-permute-start.9) | collective-permute-done | bytes 100832 | tf_op jit(solution)/shard_map/ppermute | solution.py:41
  106.3 0.1 collective-permute-start.10
  106.4 4.8 %collective-permute-done.10 = f32[225,112]{1,0:T(8,128)S(1)} collective-permute-done((f32[225,112]{1,0:T(8,128)S(1)}, f32[225,112]{1,0:T(8,128)S(1)}, u32[]{:S(2)}, u32[]{:S(2)}) %collective-permute-start.10) | collective-permute-done | bytes 100832 | tf_op jit(solution)/shard_map/ppermute | solution.py:41
  111.2 1.8 collective-permute-start.11
  113.0 3.1 %collective-permute-done.11 = f32[225,112]{1,0:T(8,128)S(1)} collective-permute-done((f32[225,112]{1,0:T(8,128)S(1)}, f32[225,112]{1,0:T(8,128)S(1)}, u32[]{:S(2)}, u32[]{:S(2)}) %collective-permute-start.11) | collective-permute-done | bytes 100832 | tf_op jit(solution)/shard_map/ppermute | solution.py:41
  116.2 2.0 %collective-permute-start.12 = (f32[225,112]{1,0:T(8,128)S(1)}, f32[225,112]{1,0:T(8,128)S(1)}, u32[]{:S(2)}, u32[]{:S(2)}) collective-permute-start(f32[225,112]{1,0:T(8,128)S(1)} %add.150), channel_id=1, source_target_pairs={{0,16},{8,24},{16,0},{24,8},{1,17},{9,25},{17,1},{25,9},{2,18},{10... | collective-permute-start | bytes 302408 | tf_op jit(solution)/shard_map/ppermute | solution.py:41
  118.2 5.0 %collective-permute-done.12 = f32[225,112]{1,0:T(8,128)S(1)} collective-permute-done((f32[225,112]{1,0:T(8,128)S(1)}, f32[225,112]{1,0:T(8,128)S(1)}, u32[]{:S(2)}, u32[]{:S(2)}) %collective-permute-start.12) | collective-permute-done | bytes 100832 | tf_op jit(solution)/shard_map/ppermute | solution.py:41
  123.3 0.1 copy.37
  123.4 0.1 copy.38
  123.5 0.7 select_reduce_fusion
  124.9 0.1 select_add_fusion
  125.0 2.0 %scatter.4.a_ref = f32[256,256]{1,0:T(8,128)S(1)} dynamic-update-slice(f32[256,256]{1,0:T(8,128)S(1)} %fusion.19, f32[224,224]{1,0:T(8,128)S(1)} %select_add_fusion, s32[]{:T(128)} %constant.71.clone.1, s32[]{:T(128)} %constant.71.clone.1) | dynamic-update-slice | bytes 401412 | tf_op jit(solution)/shard_map/scatter | solution.py:97
  127.0 0.7 copy-done.1
  127.7 37.7 %shard_map.18 = f32[256,256]{1,0:T(8,128)} custom-call(f32[256,256]{1,0:T(8,128)} %copy-done.1), custom_call_target="tpu_custom_call" | custom-call | tf_op jit(solution)/shard_map/pallas_call | solution.py:98
  165.5 13.2 %fusion = f32[32,256]{1,0:T(8,128)S(1)} fusion(f32[32,224,256]{2,1,0:T(8,128)} %shard_map.17, f32[32,256]{1,0:T(8,128)S(1)} %broadcast_multiply_fusion, f32[256,256]{1,0:T(8,128)} %shard_map.18, bf16[256,32,224]{0,2,1:T(8,128)(2,1)} %param.3), kind=kOutput, calls=%fused_computation.2 | convolution fusion | flops 4947223552 | bytes 22347776 | tf_op jit(solution)/shard_map/pbl,bj->pjl/dot_general | solution.py:243
  178.7 0.6 multiply_bitcast_fusion
  (20 shorter events, 0.2 us)
Async XLA Ops:
  3.6 34.1 %collective-permute-start.5 = (bf16[15,224,15]{1,2,0:T(8,128)(2,1)}, bf16[15,224,15]{1,2,0:T(8,128)(2,1)}, u32[]{:S(2)}, u32[]{:S(2)}) collective-permute-start(bf16[15,224,15]{1,2,0:T(8,128)(2,1)} %copy.32), channel_id=1, source_target_pairs={{1,8},{2,9},{3,10},{4,11},{5,12},{6,13},{7,14},{9,16},{10,17},{11,... | collective-permute-start | bytes 302408 | tf_op jit(solution)/shard_map/ppermute | solution.py:147
  5.9 64.0 %collective-permute-start.7 = (bf16[15,224,15]{1,2,0:T(8,128)(2,1)}, bf16[15,224,15]{1,2,0:T(8,128)(2,1)}, u32[]{:S(2)}, u32[]{:S(2)}) collective-permute-start(bf16[15,224,15]{1,2,0:T(8,128)(2,1)} %copy.33), channel_id=1, source_target_pairs={{9,0},{10,1},{11,2},{12,3},{13,4},{14,5},{15,6},{17,8},{18,9},{19,... | collective-permute-start | bytes 302408 | tf_op jit(solution)/shard_map/ppermute | solution.py:147
  11.2 58.2 %collective-permute-start.6 = (bf16[15,224,256]{2,1,0:T(8,128)(2,1)}, bf16[15,224,256]{2,1,0:T(8,128)(2,1)S(1)}, u32[]{:S(2)}, u32[]{:S(2)}) collective-permute-start(bf16[15,224,256]{2,1,0:T(8,128)(2,1)} %get-tuple-element.21), channel_id=1, source_target_pairs={{1,0},{2,1},{3,2},{4,3},{5,4},{6,5},{7,6},{9,8},{10,9},{11,10},{12... | collective-permute-start | bytes 5160968 | tf_op jit(solution)/shard_map/ppermute | solution.py:143
  13.5 30.1 %collective-permute-start = (bf16[15,224,15]{1,2,0:T(8,128)(2,1)}, bf16[15,224,15]{1,2,0:T(8,128)(2,1)}, u32[]{:S(2)}, u32[]{:S(2)}) collective-permute-start(bf16[15,224,15]{1,2,0:T(8,128)(2,1)} %copy.26), channel_id=1, source_target_pairs={{0,9},{1,10},{2,11},{3,12},{4,13},{5,14},{6,15},{8,17},{9,18},{10,... | collective-permute-start | bytes 302408 | tf_op jit(solution)/shard_map/ppermute | solution.py:147
  23.2 50.7 %collective-permute-start.2 = (bf16[15,224,15]{1,2,0:T(8,128)(2,1)}, bf16[15,224,15]{1,2,0:T(8,128)(2,1)}, u32[]{:S(2)}, u32[]{:S(2)}) collective-permute-start(bf16[15,224,15]{1,2,0:T(8,128)(2,1)} %copy.27), channel_id=1, source_target_pairs={{8,1},{9,2},{10,3},{11,4},{12,5},{13,6},{14,7},{16,9},{17,10},{18,... | collective-permute-start | bytes 302408 | tf_op jit(solution)/shard_map/ppermute | solution.py:147
  25.0 4.1 %copy-start = (bf16[256,32,224]{0,2,1:T(8,128)(2,1)S(1)}, bf16[256,32,224]{0,2,1:T(8,128)(2,1)}, u32[]{:S(2)}) copy-start(bf16[256,32,224]{0,2,1:T(8,128)(2,1)} %param.3) | copy-start | bytes 11010052
  37.6 16.4 %copy-start.2 = (bf16[32,224,15]{1,0,2:T(8,128)(2,1)S(1)}, bf16[32,224,15]{1,0,2:T(8,128)(2,1)}, u32[]{:S(2)}) copy-start(bf16[32,224,15]{1,0,2:T(8,128)(2,1)} %copy.30) | copy-start | bytes 645124
  37.7 35.5 %collective-permute-start.1 = (bf16[15,224,256]{2,1,0:T(8,128)(2,1)}, bf16[15,224,256]{2,1,0:T(8,128)(2,1)S(1)}, u32[]{:S(2)}, u32[]{:S(2)}) collective-permute-start(bf16[15,224,256]{2,1,0:T(8,128)(2,1)} %get-tuple-element.22), channel_id=1, source_target_pairs={{0,1},{1,2},{2,3},{3,4},{4,5},{5,6},{6,7},{8,9},{9,10},{10,11},{11... | collective-permute-start | bytes 5160968 | tf_op jit(solution)/shard_map/ppermute | solution.py:143
  41.8 23.2 %slice-start = ((s8[7340032]{0:T(1024)(128)(4,1)}), s8[4194304]{0:T(1024)(128)(4,1)S(1)}, s32[]{:S(2)}) async-start(s8[7340032]{0:T(1024)(128)(4,1)} %bitcast.71), calls=%async_computation | async-start | bytes 8388608
  43.6 10.4 %collective-permute-start.3 = (bf16[32,224,15]{1,0,2:T(8,128)(2,1)}, bf16[32,224,15]{1,0,2:T(8,128)(2,1)S(1)}, u32[]{:S(2)}, u32[]{:S(2)}) collective-permute-start(bf16[32,224,15]{1,0,2:T(8,128)(2,1)} %copy.28), channel_id=1, source_target_pairs={{0,8},{8,16},{16,24},{1,9},{9,17},{17,25},{2,10},{10,18},{18,26},{... | collective-permute-start | bytes 645128 | tf_op jit(solution)/shard_map/ppermute | solution.py:146
  49.8 15.2 %slice-start.1 = ((s8[7340032]{0:T(1024)(128)(4,1)}), s8[3145728]{0:T(1024)(128)(4,1)S(1)}, s32[]{:S(2)}) async-start(s8[7340032]{0:T(1024)(128)(4,1)} %bitcast.71), calls=%async_computation.1 | async-start | bytes 6291456
  49.9 15.2 %copy-start.3 = (s32[15]{0:T(128)S(1)}, s32[15]{0:T(128)}, u32[]{:S(2)}) copy-start(s32[15]{0:T(128)} %iota_add_fusion) | copy-start | bytes 184
  54.0 11.0 %collective-permute-start.4 = (bf16[32,224,15]{1,0,2:T(8,128)(2,1)S(1)}, bf16[32,224,15]{1,0,2:T(8,128)(2,1)S(1)}, u32[]{:S(2)}, u32[]{:S(2)}) collective-permute-start(bf16[32,224,15]{1,0,2:T(8,128)(2,1)S(1)} %copy-done.2), channel_id=1, source_target_pairs={{8,0},{16,8},{24,16},{9,1},{17,9},{25,17},{10,2},{18,10},{26,18},{... | collective-permute-start | bytes 645128 | tf_op jit(solution)/shard_map/ppermute | solution.py:146
  98.6 1.4 collective-permute-start.8
  100.0 6.3 %collective-permute-start.9 = (f32[225,112]{1,0:T(8,128)S(1)}, f32[225,112]{1,0:T(8,128)S(1)}, u32[]{:S(2)}, u32[]{:S(2)}) collective-permute-start(f32[225,112]{1,0:T(8,128)S(1)} %fusion.51), channel_id=1, source_target_pairs={{0,2},{1,3},{2,0},{3,1},{4,6},{5,7},{6,4},{7,5},{8,10},{9,11},{10,... | collective-permute-start | bytes 302408 | tf_op jit(solution)/shard_map/ppermute | solution.py:41
  106.3 4.9 %collective-permute-start.10 = (f32[225,112]{1,0:T(8,128)S(1)}, f32[225,112]{1,0:T(8,128)S(1)}, u32[]{:S(2)}, u32[]{:S(2)}) collective-permute-start(f32[225,112]{1,0:T(8,128)S(1)} %add.148), channel_id=1, source_target_pairs={{0,4},{1,5},{2,6},{3,7},{4,0},{5,1},{6,2},{7,3},{8,12},{9,13},{10,... | collective-permute-start | bytes 302408 | tf_op jit(solution)/shard_map/ppermute | solution.py:41
  111.2 4.9 %collective-permute-start.11 = (f32[225,112]{1,0:T(8,128)S(1)}, f32[225,112]{1,0:T(8,128)S(1)}, u32[]{:S(2)}, u32[]{:S(2)}) collective-permute-start(f32[225,112]{1,0:T(8,128)S(1)} %add.149), channel_id=1, source_target_pairs={{0,8},{8,0},{16,24},{24,16},{1,9},{9,1},{17,25},{25,17},{2,10},{10... | collective-permute-start | bytes 302408 | tf_op jit(solution)/shard_map/ppermute | solution.py:41
  116.2 7.1 %collective-permute-start.12 = (f32[225,112]{1,0:T(8,128)S(1)}, f32[225,112]{1,0:T(8,128)S(1)}, u32[]{:S(2)}, u32[]{:S(2)}) collective-permute-start(f32[225,112]{1,0:T(8,128)S(1)} %add.150), channel_id=1, source_target_pairs={{0,16},{8,24},{16,0},{24,8},{1,17},{9,25},{17,1},{25,9},{2,18},{10... | collective-permute-start | bytes 302408 | tf_op jit(solution)/shard_map/ppermute | solution.py:41
  127.0 0.7 copy-start.1

commit v4 on v3

--- a/solution.py
+++ b/solution.py
@@ -41,6 +41,18 @@
         x = x + lax.ppermute(x, axis, pairs)
         step *= 2
     return x
+
+
+def ring_sum(x, axis, stride):
+    count = lax.axis_size(axis)
+    groups = count // stride
+    total = x
+    for shift in range(1, groups):
+        pairs = [
+            (i, (i + shift * stride) % count) for i in range(count)
+        ]
+        total = total + lax.ppermute(x, axis, pairs)
+    return total
 
 
 def pack_symmetric(c):
@@ -235,7 +247,9 @@
     partial_cov = jnp.einsum(
         "pjl,pkl->jk", residual_bf, residual_bf, preferred_element_type=jnp.float32
     )
-    packed = butterfly_sum(butterfly_sum(pack_symmetric(partial_cov), "cross"), "track")
+    packed = pack_symmetric(partial_cov)
+    packed = packed + lax.ppermute(packed, "cross", [(i, i ^ 1) for i in range(n_cross)])
+    packed = ring_sum(ring_sum(packed, "cross", 2), "track", 1)
     covariance = unpack_symmetric(packed) / (total_lines * total_pix)
     identity = jnp.eye(bands, dtype=jnp.float32)
     loaded = covariance + LOAD * (jnp.trace(covariance) / bands) * identity

time: 180 us -> 178 us (0.989)
  waiting for transfers between devices: 30.4 us -> 25.6 us
  starting transfers between devices: 30.7 us -> 33.4 us
    ppermute x5 -> x7, waiting for transfers between devices: 17.7 us -> 13.1 us  [the longest x6 11.9 us: ring_sum(): total = total + lax.ppermute(x, axis, pairs)]
    ppermute x5 -> x7, starting transfers between devices: 6.83 us -> 9.33 us  [the longest x6 9.14 us: ring_sum(): total = total + lax.ppermute(x, axis, pairs)]
  transfers between devices with their start and end apart: 13 -> 15, of which waited for: 7 -> 8; matrix products, arithmetic and copies ran while one was open for 19% -> 19% of each run, Pallas kernels for 0% -> 0%
where the time goes in v4:
time: 178 us; the launch traced here: 177 us
  Pallas kernels  48 us (27%)
  matrix products  43.2 us (24%)
  starting transfers between devices  33.4 us (19%)
  waiting for transfers between devices  25.6 us (14%)
  local copies, waits for them, and re-layouts  23.7 us (13%)
  other arithmetic  2.32 us (1%)
    pallas_call x1, Pallas kernels, spd_inverse(): pl.pallas_call(functools.partial(sweep_kernel, n), out_shape=jax.ShapeDty...  37.7 us
    dot_general x9, matrix products, sum_lines(): jnp.einsum('qbk,kl->qbl', values, w, preferred_element_type=jnp.float32)  20.8 us
    dot_general x1, matrix products, shards(): jnp.einsum('pbl,bj->pjl', residual, inverse, precision=highest, preferred...  13.2 us
    ppermute x4, starting transfers between devices, fetch(): return lax.ppermute(piece, both, neighbour_pairs(n_track, n_cross, dt, dc))  12.6 us
    ppermute x2, waiting for transfers between devices, fetch(): return lax.ppermute(piece, 'track', pairs)  12.5 us
    ppermute x6, waiting for transfers between devices, ring_sum(): total = total + lax.ppermute(x, axis, pairs)  11.9 us
    pallas_call x1, Pallas kernels, sum_pixels(): pl.pallas_call(pixel_window_kernel, grid=(bands // block,), in_specs=[spe...  10.3 us
    dot_general x1, matrix products, shards(): jnp.einsum('pjl,pkl->jk', residual_bf, residual_bf, preferred_element_typ...  9.24 us
  transfers between devices with their start and end apart: 15, of which 8 were waited for; matrix products, arithmetic and copies ran while one was open for 19% of the time, Pallas kernels for 0%

profile of v4, /device:TPU:0, one launch (start us, length us, event | category | flops | bytes accessed | tf_op | source)
XLA Modules:
  0.0 177.2 jit_solution(16311131619828745832)
XLA Ops:
  0.0 2.5 %fusion.52 = (bf16[15,224,15]{2,1,0:T(8,128)(2,1)S(1)}, bf16[15,224,15]{2,1,0:T(8,128)(2,1)S(1)}, bf16[15,224,15]{2,1,0:T(8,128)(2,1)S(1)}, bf16[15,224,15]{2,1,0:T(8,128)(2,1)S(1)}) fusion(bf16[32,224,256]{2,1,0:T(8,128)(2,1)} %bitcast.68), kind=kLoop, calls=%fused_computation.66 | loop fusion | bytes 806400 | tf_op jit(solution)/shard_map/slice | solution.py:174
  2.6 1.0 copy.32
  3.6 1.3 collective-permute-start.5
  4.9 1.0 copy.33
  5.9 1.3 collective-permute-start.7
  7.2 3.9 %fusion.53 = (bf16[15,224,256]{2,1,0:T(8,128)(2,1)}, bf16[15,224,256]{2,1,0:T(8,128)(2,1)}) fusion(bf16[32,224,256]{2,1,0:T(8,128)(2,1)} %bitcast.69), kind=kLoop, calls=%fused_computation.67 | loop fusion | bytes 6881280 | tf_op jit(solution)/shard_map/slice | solution.py:164
  11.1 1.3 collective-permute-start.6
  12.4 1.0 copy.26
  13.5 8.7 %collective-permute-start = (bf16[15,224,15]{1,2,0:T(8,128)(2,1)}, bf16[15,224,15]{1,2,0:T(8,128)(2,1)}, u32[]{:S(2)}, u32[]{:S(2)}) collective-permute-start(bf16[15,224,15]{1,2,0:T(8,128)(2,1)} %copy.26), channel_id=1, source_target_pairs={{0,9},{1,10},{2,11},{3,12},{4,13},{5,14},{6,15},{8,17},{9,18},{10,... | collective-permute-start | bytes 302408 | tf_op jit(solution)/shard_map/ppermute | solution.py:159
  22.2 1.0 copy.27
  23.2 1.3 collective-permute-start.2
  24.5 0.5 iota_add_fusion
  25.1 4.1 %fusion.54 = (bf16[32,224,15]{2,1,0:T(8,128)(2,1)S(1)}, bf16[32,224,15]{2,1,0:T(8,128)(2,1)}) fusion(bf16[32,224,256]{2,1,0:T(8,128)(2,1)} %bitcast.70), kind=kLoop, calls=%fused_computation.68 | loop fusion | bytes 860160 | tf_op jit(solution)/shard_map/slice | solution.py:173
  29.2 4.1 %fusion.15 = f32[256,32,224]{0,2,1:T(8,128)} fusion(bf16[256,32,224]{0,2,1:T(8,128)(2,1)S(1)} %copy-done), kind=kOutput, calls=%fused_computation.18 | convolution fusion | flops 939720704 | bytes 11010048 | tf_op jit(solution)/shard_map/qbk,kl->qbl/dot_general | solution.py:191
  33.3 2.7 %copy.28 = bf16[32,224,15]{1,0,2:T(8,128)(2,1)} copy(bf16[32,224,15]{2,1,0:T(8,128)(2,1)} %get-tuple-element.24) | data formatting | bytes 430080 | tf_op jit(solution)/shard_map/slice | solution.py:168
  36.0 1.7 copy.30
  37.7 0.1 broadcast_multiply_fusion
  37.7 0.0 collective-permute-done.5
  37.8 4.1 %collective-permute-start.1 = (bf16[15,224,256]{2,1,0:T(8,128)(2,1)}, bf16[15,224,256]{2,1,0:T(8,128)(2,1)S(1)}, u32[]{:S(2)}, u32[]{:S(2)}) collective-permute-start(bf16[15,224,256]{2,1,0:T(8,128)(2,1)} %get-tuple-element.22), channel_id=1, source_target_pairs={{0,1},{1,2},{2,3},{3,4},{4,5},{5,6},{6,7},{8,9},{9,10},{10,11},{11... | collective-permute-start | bytes 5160968 | tf_op jit(solution)/shard_map/ppermute | solution.py:155
  41.8 0.0 slice-start
  41.8 1.7 fusion.27
  43.6 4.7 %collective-permute-start.3 = (bf16[32,224,15]{1,0,2:T(8,128)(2,1)}, bf16[32,224,15]{1,0,2:T(8,128)(2,1)S(1)}, u32[]{:S(2)}, u32[]{:S(2)}) collective-permute-start(bf16[32,224,15]{1,0,2:T(8,128)(2,1)} %copy.28), channel_id=1, source_target_pairs={{0,8},{8,16},{16,24},{1,9},{9,17},{17,25},{2,10},{10,18},{18,26},{... | collective-permute-start | bytes 645128 | tf_op jit(solution)/shard_map/ppermute | solution.py:158
  48.3 1.6 fusion.30
  49.8 0.0 slice-start.1
  49.8 0.0 copy-start.3
  49.9 4.1 %collective-permute-done.3 = bf16[32,224,15]{1,0,2:T(8,128)(2,1)S(1)} collective-permute-done((bf16[32,224,15]{1,0,2:T(8,128)(2,1)}, bf16[32,224,15]{1,0,2:T(8,128)(2,1)S(1)}, u32[]{:S(2)}, u32[]{:S(2)}) %collective-permute-start.3) | collective-permute-done | bytes 215072 | tf_op jit(solution)/shard_map/ppermute | solution.py:158
  54.0 1.5 collective-permute-start.4
  55.4 1.2 fusion.10
  56.6 8.4 %collective-permute-done.4 = bf16[32,224,15]{1,0,2:T(8,128)(2,1)S(1)} collective-permute-done((bf16[32,224,15]{1,0,2:T(8,128)(2,1)S(1)}, bf16[32,224,15]{1,0,2:T(8,128)(2,1)S(1)}, u32[]{:S(2)}, u32[]{:S(2)}) %collective-permute-start.4) | collective-permute-done | bytes 215072 | tf_op jit(solution)/shard_map/ppermute | solution.py:158
  65.0 4.3 %add_bitcast_fusion.middle_ref = f32[32,224,256]{2,1,0:T(8,128)} fusion(f32[256,32,224]{0,2,1:T(8,128)S(1)} %fusion.10, f32[256,32,224]{0,2,1:T(8,128)S(1)} %bitcast.72, bf16[32,224,15]{1,0,2:T(8,128)(2,1)S(1)} %collective-permute-done.4, s32[15]{0:T(128)S(1)} %copy-done.3), kind=kOutput, calls=%fused_computation.4 | convolution fusion | flops 58724096 | bytes 22235196 | tf_op jit(solution)/shard_map/qbk,kl->qbl/dot_general | solution.py:191
  69.3 0.0 collective-permute-done.6
  69.3 0.6 fusion.13
  69.9 0.0 collective-permute-done.7
  69.9 3.3 %add_bitcast_fusion.1.right_ref = f32[15,224,256]{2,1,0:T(8,128)} fusion(f32[256,15,224]{0,2,1:T(8,128)S(1)} %fusion.27, f32[256,15,224]{0,2,1:T(8,128)S(1)} %fusion.13, bf16[15,224,15]{1,2,0:T(8,128)(2,1)} %collective-permute-done.7, s32[15]{0:T(128)S(1)} %copy-done.3), kind=kOutput, calls=%fused_computation.7 | convolution fusion | flops 27528960 | bytes 10422780 | tf_op jit(solution)/shard_map/qbk,kl->qbl/dot_general | solution.py:191
  73.2 0.6 fusion.17
  73.9 0.0 collective-permute-done.2
  73.9 3.3 %add_bitcast_fusion.2.left_ref = f32[15,224,256]{2,1,0:T(8,128)} fusion(f32[256,15,224]{0,2,1:T(8,128)S(1)} %fusion.30, f32[256,15,224]{0,2,1:T(8,128)S(1)} %fusion.17, bf16[15,224,15]{1,2,0:T(8,128)(2,1)} %collective-permute-done.2, s32[15]{0:T(128)S(1)} %copy-done.3), kind=kOutput, calls=%fused_computation.8 | convolution fusion | flops 27528960 | bytes 10422780 | tf_op jit(solution)/shard_map/qbk,kl->qbl/dot_general | solution.py:191
  77.2 10.3 %shard_map.17 = f32[32,224,256]{2,1,0:T(8,128)} custom-call(f32[15,224,256]{2,1,0:T(8,128)} %add_bitcast_fusion.2.left_ref, f32[32,224,256]{2,1,0:T(8,128)} %add_bitcast_fusion.middle_ref, f32[15,224,256]{2,1,0:T(8,128)} %add_bitcast_fusion.1.right_ref), custom_call_target="tpu_custom_call" | custom-call | tf_op jit(solution)/shard_map/pallas_call | solution.py:219
  87.5 9.2 %fusion.3 = f32[224,224]{1,0:T(8,128)S(1)} fusion(f32[32,224,256]{2,1,0:T(8,128)} %shard_map.17, f32[32,256]{1,0:T(8,128)S(1)} %broadcast_multiply_fusion, bf16[256,32,224]{0,2,1:T(8,128)(2,1)} %param.3), kind=kOutput, calls=%fused_computation.9 | convolution fusion | flops 829423616 | bytes 11243520 | tf_op jit(solution)/shard_map/pjl,pkl->jk/dot_general | solution.py:247
  96.7 0.1 fusion.55
  96.8 1.7 gather_fusion
  98.6 0.2 collective-permute-start.8
  98.7 1.2 collective-permute-done.8
  100.0 0.1 collective-permute-start.10
  100.0 4.1 %collective-permute-start.11 = (f32[225,112]{1,0:T(8,128)S(1)}, f32[225,112]{1,0:T(8,128)S(1)}, u32[]{:S(2)}, u32[]{:S(2)}) collective-permute-start(f32[225,112]{1,0:T(8,128)S(1)} %fusion.51), channel_id=1, source_target_pairs={{0,6},{1,7},{2,0},{3,1},{4,2},{5,3},{6,4},{7,5},{8,14},{9,15},{10,... | collective-permute-start | bytes 302408 | tf_op jit(solution)/shard_map/ppermute | solution.py:54
  104.2 0.0 collective-permute-start.9
  104.2 1.2 collective-permute-done.10
  105.3 2.5 %collective-permute-done.11 = f32[225,112]{1,0:T(8,128)S(1)} collective-permute-done((f32[225,112]{1,0:T(8,128)S(1)}, f32[225,112]{1,0:T(8,128)S(1)}, u32[]{:S(2)}, u32[]{:S(2)}) %collective-permute-start.11) | collective-permute-done | bytes 100832 | tf_op jit(solution)/shard_map/ppermute | solution.py:54
  107.8 2.2 %collective-permute-done.9 = f32[225,112]{1,0:T(8,128)S(1)} collective-permute-done((f32[225,112]{1,0:T(8,128)S(1)}, f32[225,112]{1,0:T(8,128)S(1)}, u32[]{:S(2)}, u32[]{:S(2)}) %collective-permute-start.9) | collective-permute-done | bytes 100832 | tf_op jit(solution)/shard_map/ppermute | solution.py:54
  110.0 1.8 %collective-permute-start.12 = (f32[225,112]{1,0:T(8,128)S(1)}, f32[225,112]{1,0:T(8,128)S(1)}, u32[]{:S(2)}, u32[]{:S(2)}) collective-permute-start(f32[225,112]{1,0:T(8,128)S(1)} %add_add_fusion.1), channel_id=1, source_target_pairs={{0,8},{8,16},{16,24},{24,0},{1,9},{9,17},{17,25},{25,1},{2,10},{10... | collective-permute-start | bytes 302408 | tf_op jit(solution)/shard_map/ppermute | solution.py:54
  111.8 0.3 collective-permute-start.13
  112.1 2.8 %collective-permute-start.14 = (f32[225,112]{1,0:T(8,128)S(1)}, f32[225,112]{1,0:T(8,128)S(1)}, u32[]{:S(2)}, u32[]{:S(2)}) collective-permute-start(f32[225,112]{1,0:T(8,128)S(1)} %add_add_fusion.1), channel_id=1, source_target_pairs={{0,24},{8,0},{16,8},{24,16},{1,25},{9,1},{17,9},{25,17},{2,26},{10... | collective-permute-start | bytes 302408 | tf_op jit(solution)/shard_map/ppermute | solution.py:54
  115.0 3.1 %collective-permute-done.12 = f32[225,112]{1,0:T(8,128)S(1)} collective-permute-done((f32[225,112]{1,0:T(8,128)S(1)}, f32[225,112]{1,0:T(8,128)S(1)}, u32[]{:S(2)}, u32[]{:S(2)}) %collective-permute-start.12) | collective-permute-done | bytes 100832 | tf_op jit(solution)/shard_map/ppermute | solution.py:54
  118.1 3.0 %collective-permute-done.13 = f32[225,112]{1,0:T(8,128)S(1)} collective-permute-done((f32[225,112]{1,0:T(8,128)S(1)}, f32[225,112]{1,0:T(8,128)S(1)}, u32[]{:S(2)}, u32[]{:S(2)}) %collective-permute-start.13) | collective-permute-done | bytes 100832 | tf_op jit(solution)/shard_map/ppermute | solution.py:54
  121.1 0.0 collective-permute-done.14
  121.2 0.1 copy.37
  121.3 0.1 copy.38
  121.4 0.7 select_reduce_fusion
  122.7 0.1 select_add_fusion
  122.9 2.0 %scatter.4.a_ref = f32[256,256]{1,0:T(8,128)S(1)} dynamic-update-slice(f32[256,256]{1,0:T(8,128)S(1)} %fusion.19, f32[224,224]{1,0:T(8,128)S(1)} %select_add_fusion, s32[]{:T(128)} %constant.71.clone.1, s32[]{:T(128)} %constant.71.clone.1) | dynamic-update-slice | bytes 401412 | tf_op jit(solution)/shard_map/scatter | solution.py:109
  124.9 0.7 copy-done.1
  125.6 37.7 %shard_map.18 = f32[256,256]{1,0:T(8,128)} custom-call(f32[256,256]{1,0:T(8,128)} %copy-done.1), custom_call_target="tpu_custom_call" | custom-call | tf_op jit(solution)/shard_map/pallas_call | solution.py:110
  163.4 13.2 %fusion = f32[32,256]{1,0:T(8,128)S(1)} fusion(f32[32,224,256]{2,1,0:T(8,128)} %shard_map.17, f32[32,256]{1,0:T(8,128)S(1)} %broadcast_multiply_fusion, f32[256,256]{1,0:T(8,128)} %shard_map.18, bf16[256,32,224]{0,2,1:T(8,128)(2,1)} %param.3), kind=kOutput, calls=%fused_computation.2 | convolution fusion | flops 4947223552 | bytes 22347776 | tf_op jit(solution)/shard_map/pbl,bj->pjl/dot_general | solution.py:257
  176.5 0.6 multiply_bitcast_fusion
  (22 shorter events, 0.2 us)
Async XLA Ops:
  3.6 34.2 %collective-permute-start.5 = (bf16[15,224,15]{1,2,0:T(8,128)(2,1)}, bf16[15,224,15]{1,2,0:T(8,128)(2,1)}, u32[]{:S(2)}, u32[]{:S(2)}) collective-permute-start(bf16[15,224,15]{1,2,0:T(8,128)(2,1)} %copy.32), channel_id=1, source_target_pairs={{1,8},{2,9},{3,10},{4,11},{5,12},{6,13},{7,14},{9,16},{10,17},{11,... | collective-permute-start | bytes 302408 | tf_op jit(solution)/shard_map/ppermute | solution.py:159
  5.9 64.0 %collective-permute-start.7 = (bf16[15,224,15]{1,2,0:T(8,128)(2,1)}, bf16[15,224,15]{1,2,0:T(8,128)(2,1)}, u32[]{:S(2)}, u32[]{:S(2)}) collective-permute-start(bf16[15,224,15]{1,2,0:T(8,128)(2,1)} %copy.33), channel_id=1, source_target_pairs={{9,0},{10,1},{11,2},{12,3},{13,4},{14,5},{15,6},{17,8},{18,9},{19,... | collective-permute-start | bytes 302408 | tf_op jit(solution)/shard_map/ppermute | solution.py:159
  11.1 58.2 %collective-permute-start.6 = (bf16[15,224,256]{2,1,0:T(8,128)(2,1)}, bf16[15,224,256]{2,1,0:T(8,128)(2,1)S(1)}, u32[]{:S(2)}, u32[]{:S(2)}) collective-permute-start(bf16[15,224,256]{2,1,0:T(8,128)(2,1)} %get-tuple-element.21), channel_id=1, source_target_pairs={{1,0},{2,1},{3,2},{4,3},{5,4},{6,5},{7,6},{9,8},{10,9},{11,10},{12... | collective-permute-start | bytes 5160968 | tf_op jit(solution)/shard_map/ppermute | solution.py:155
  13.5 30.1 %collective-permute-start = (bf16[15,224,15]{1,2,0:T(8,128)(2,1)}, bf16[15,224,15]{1,2,0:T(8,128)(2,1)}, u32[]{:S(2)}, u32[]{:S(2)}) collective-permute-start(bf16[15,224,15]{1,2,0:T(8,128)(2,1)} %copy.26), channel_id=1, source_target_pairs={{0,9},{1,10},{2,11},{3,12},{4,13},{5,14},{6,15},{8,17},{9,18},{10,... | collective-permute-start | bytes 302408 | tf_op jit(solution)/shard_map/ppermute | solution.py:159
  23.2 50.7 %collective-permute-start.2 = (bf16[15,224,15]{1,2,0:T(8,128)(2,1)}, bf16[15,224,15]{1,2,0:T(8,128)(2,1)}, u32[]{:S(2)}, u32[]{:S(2)}) collective-permute-start(bf16[15,224,15]{1,2,0:T(8,128)(2,1)} %copy.27), channel_id=1, source_target_pairs={{8,1},{9,2},{10,3},{11,4},{12,5},{13,6},{14,7},{16,9},{17,10},{18,... | collective-permute-start | bytes 302408 | tf_op jit(solution)/shard_map/ppermute | solution.py:159
  25.0 4.1 %copy-start = (bf16[256,32,224]{0,2,1:T(8,128)(2,1)S(1)}, bf16[256,32,224]{0,2,1:T(8,128)(2,1)}, u32[]{:S(2)}) copy-start(bf16[256,32,224]{0,2,1:T(8,128)(2,1)} %param.3) | copy-start | bytes 11010052
  37.6 16.3 %copy-start.2 = (bf16[32,224,15]{1,0,2:T(8,128)(2,1)S(1)}, bf16[32,224,15]{1,0,2:T(8,128)(2,1)}, u32[]{:S(2)}) copy-start(bf16[32,224,15]{1,0,2:T(8,128)(2,1)} %copy.30) | copy-start | bytes 645124
  37.8 35.5 %collective-permute-start.1 = (bf16[15,224,256]{2,1,0:T(8,128)(2,1)}, bf16[15,224,256]{2,1,0:T(8,128)(2,1)S(1)}, u32[]{:S(2)}, u32[]{:S(2)}) collective-permute-start(bf16[15,224,256]{2,1,0:T(8,128)(2,1)} %get-tuple-element.22), channel_id=1, source_target_pairs={{0,1},{1,2},{2,3},{3,4},{4,5},{5,6},{6,7},{8,9},{9,10},{10,11},{11... | collective-permute-start | bytes 5160968 | tf_op jit(solution)/shard_map/ppermute | solution.py:155
  41.8 23.2 %slice-start = ((s8[7340032]{0:T(1024)(128)(4,1)}), s8[4194304]{0:T(1024)(128)(4,1)S(1)}, s32[]{:S(2)}) async-start(s8[7340032]{0:T(1024)(128)(4,1)} %bitcast.71), calls=%async_computation | async-start | bytes 8388608
  43.6 10.4 %collective-permute-start.3 = (bf16[32,224,15]{1,0,2:T(8,128)(2,1)}, bf16[32,224,15]{1,0,2:T(8,128)(2,1)S(1)}, u32[]{:S(2)}, u32[]{:S(2)}) collective-permute-start(bf16[32,224,15]{1,0,2:T(8,128)(2,1)} %copy.28), channel_id=1, source_target_pairs={{0,8},{8,16},{16,24},{1,9},{9,17},{17,25},{2,10},{10,18},{18,26},{... | collective-permute-start | bytes 645128 | tf_op jit(solution)/shard_map/ppermute | solution.py:158
  49.8 15.2 %slice-start.1 = ((s8[7340032]{0:T(1024)(128)(4,1)}), s8[3145728]{0:T(1024)(128)(4,1)S(1)}, s32[]{:S(2)}) async-start(s8[7340032]{0:T(1024)(128)(4,1)} %bitcast.71), calls=%async_computation.1 | async-start | bytes 6291456
  49.8 15.2 %copy-start.3 = (s32[15]{0:T(128)S(1)}, s32[15]{0:T(128)}, u32[]{:S(2)}) copy-start(s32[15]{0:T(128)} %iota_add_fusion) | copy-start | bytes 184
  54.0 11.0 %collective-permute-start.4 = (bf16[32,224,15]{1,0,2:T(8,128)(2,1)S(1)}, bf16[32,224,15]{1,0,2:T(8,128)(2,1)S(1)}, u32[]{:S(2)}, u32[]{:S(2)}) collective-permute-start(bf16[32,224,15]{1,0,2:T(8,128)(2,1)S(1)} %copy-done.2), channel_id=1, source_target_pairs={{8,0},{16,8},{24,16},{9,1},{17,9},{25,17},{10,2},{18,10},{26,18},{... | collective-permute-start | bytes 645128 | tf_op jit(solution)/shard_map/ppermute | solution.py:158
  98.6 1.4 collective-permute-start.8
  100.0 5.4 %collective-permute-start.10 = (f32[225,112]{1,0:T(8,128)S(1)}, f32[225,112]{1,0:T(8,128)S(1)}, u32[]{:S(2)}, u32[]{:S(2)}) collective-permute-start(f32[225,112]{1,0:T(8,128)S(1)} %fusion.51), channel_id=1, source_target_pairs={{0,4},{1,5},{2,6},{3,7},{4,0},{5,1},{6,2},{7,3},{8,12},{9,13},{10,... | collective-permute-start | bytes 302408 | tf_op jit(solution)/shard_map/ppermute | solution.py:54
  100.0 7.8 %collective-permute-start.11 = (f32[225,112]{1,0:T(8,128)S(1)}, f32[225,112]{1,0:T(8,128)S(1)}, u32[]{:S(2)}, u32[]{:S(2)}) collective-permute-start(f32[225,112]{1,0:T(8,128)S(1)} %fusion.51), channel_id=1, source_target_pairs={{0,6},{1,7},{2,0},{3,1},{4,2},{5,3},{6,4},{7,5},{8,14},{9,15},{10,... | collective-permute-start | bytes 302408 | tf_op jit(solution)/shard_map/ppermute | solution.py:54
  104.2 5.8 %collective-permute-start.9 = (f32[225,112]{1,0:T(8,128)S(1)}, f32[225,112]{1,0:T(8,128)S(1)}, u32[]{:S(2)}, u32[]{:S(2)}) collective-permute-start(f32[225,112]{1,0:T(8,128)S(1)} %fusion.51), channel_id=1, source_target_pairs={{0,2},{1,3},{2,4},{3,5},{4,6},{5,7},{6,0},{7,1},{8,10},{9,11},{10,... | collective-permute-start | bytes 302408 | tf_op jit(solution)/shard_map/ppermute | solution.py:54
  110.0 8.1 %collective-permute-start.12 = (f32[225,112]{1,0:T(8,128)S(1)}, f32[225,112]{1,0:T(8,128)S(1)}, u32[]{:S(2)}, u32[]{:S(2)}) collective-permute-start(f32[225,112]{1,0:T(8,128)S(1)} %add_add_fusion.1), channel_id=1, source_target_pairs={{0,8},{8,16},{16,24},{24,0},{1,9},{9,17},{17,25},{25,1},{2,10},{10... | collective-permute-start | bytes 302408 | tf_op jit(solution)/shard_map/ppermute | solution.py:54
  111.8 9.3 %collective-permute-start.13 = (f32[225,112]{1,0:T(8,128)S(1)}, f32[225,112]{1,0:T(8,128)S(1)}, u32[]{:S(2)}, u32[]{:S(2)}) collective-permute-start(f32[225,112]{1,0:T(8,128)S(1)} %add_add_fusion.1), channel_id=1, source_target_pairs={{0,16},{8,24},{16,0},{24,8},{1,17},{9,25},{17,1},{25,9},{2,18},{10... | collective-permute-start | bytes 302408 | tf_op jit(solution)/shard_map/ppermute | solution.py:54
  112.1 9.0 %collective-permute-start.14 = (f32[225,112]{1,0:T(8,128)S(1)}, f32[225,112]{1,0:T(8,128)S(1)}, u32[]{:S(2)}, u32[]{:S(2)}) collective-permute-start(f32[225,112]{1,0:T(8,128)S(1)} %add_add_fusion.1), channel_id=1, source_target_pairs={{0,24},{8,0},{16,8},{24,16},{1,25},{9,1},{17,9},{25,17},{2,26},{10... | collective-permute-start | bytes 302408 | tf_op jit(solution)/shard_map/ppermute | solution.py:54
  124.9 0.7 copy-start.1

commit v5 on v4

--- a/solution.py
+++ b/solution.py
@@ -159,20 +159,16 @@
         return lax.ppermute(piece, both, neighbour_pairs(n_track, n_cross, dt, dc))
 
     first, last = slice(0, HALF), slice(-HALF, None)
-    sides = {
-        "left": fetch(planes[last], 0, -1),
-        "right": fetch(planes[first], 0, 1),
-    }
-    tops = {
-        "left": fetch(planes[last, :, last], -1, -1),
-        "middle": fetch(planes[:, :, last], -1, 0),
-        "right": fetch(planes[first, :, last], -1, 1),
-    }
-    bottoms = {
-        "left": fetch(planes[last, :, first], 1, -1),
-        "middle": fetch(planes[:, :, first], 1, 0),
-        "right": fetch(planes[first, :, first], 1, 1),
-    }
+    left = fetch(planes[last], 0, -1)
+    right = fetch(planes[first], 0, 1)
+    parts = (left, planes, right)
+    top = fetch(jnp.concatenate([p[:, :, last] for p in parts], axis=0), -1, 0)
+    bottom = fetch(jnp.concatenate([p[:, :, first] for p in parts], axis=0), 1, 0)
+    width = planes.shape[0]
+    cuts = {"left": slice(0, HALF), "middle": slice(HALF, HALF + width), "right": slice(HALF + width, None)}
+    sides = {"left": left, "right": right}
+    tops = {name: top[cut] for name, cut in cuts.items()}
+    bottoms = {name: bottom[cut] for name, cut in cuts.items()}
     return sides, tops, bottoms
 
 

time: 178 us -> 186 us (1.045)
  starting transfers between devices: 33.4 us -> 46 us
  waiting for transfers between devices: 25.6 us -> 17.6 us
  other arithmetic: 2.32 us -> 5.01 us
    ppermute x1, starting transfers between devices: 0.19 us -> 18.4 us  [shards(): lax.ppermute(packed, 'cross', [(i, i ^ 1) for i in range(n_cross)])]
    ppermute x4 -> x0, starting transfers between devices: 12.6 us -> none  [fetch(): return lax.ppermute(piece, both, neighbour_pairs(n_track, n_cross, dt, dc))]
    ppermute x2, waiting for transfers between devices: 12.5 us -> 2.53 us  [fetch(): return lax.ppermute(piece, 'track', pairs)]
    ppermute x6, starting transfers between devices: 9.14 us -> 14.9 us  [ring_sum(): total = total + lax.ppermute(x, axis, pairs)]
    concatenate x0 -> x2, other arithmetic: none -> 3.21 us  [the longest x1 2.03 us: halos(): top = fetch(jnp.concatenate([p[:, :, last] for p in parts], axis=0), -1, 0)]
    ppermute x6, waiting for transfers between devices: 11.9 us -> 14.1 us  [ring_sum(): total = total + lax.ppermute(x, axis, pairs)]
    slice x9 -> x14, local copies, waits for them, and re-layouts: 19.1 us -> 20.7 us  [the longest x6 8.34 us: halos(): p[:, :, first]]
  transfers between devices with their start and end apart: 15 -> 11, of which waited for: 8 -> 6; matrix products, arithmetic and copies ran while one was open for 19% -> 13% of each run, Pallas kernels for 0% -> 0%
where the time goes in v5:
time: 186 us; the launch traced here: 185 us
  Pallas kernels  48 us (26%)
  starting transfers between devices  46 us (25%)
  matrix products  42.2 us (23%)
  local copies, waits for them, and re-layouts  25.3 us (14%)
  waiting for transfers between devices  17.6 us (9%)
  other arithmetic  5.01 us (3%)
    pallas_call x1, Pallas kernels, spd_inverse(): pl.pallas_call(functools.partial(sweep_kernel, n), out_shape=jax.ShapeDty...  37.7 us
    dot_general x9, matrix products, sum_lines(): jnp.einsum('qbk,kl->qbl', values, w, preferred_element_type=jnp.float32)  19.7 us
    ppermute x1, starting transfers between devices, shards(): lax.ppermute(packed, 'cross', [(i, i ^ 1) for i in range(n_cross)])  18.4 us
    ppermute x6, starting transfers between devices, ring_sum(): total = total + lax.ppermute(x, axis, pairs)  14.9 us
    ppermute x6, waiting for transfers between devices, ring_sum(): total = total + lax.ppermute(x, axis, pairs)  14.1 us
    dot_general x1, matrix products, shards(): jnp.einsum('pbl,bj->pjl', residual, inverse, precision=highest, preferred...  13.2 us
    pallas_call x1, Pallas kernels, sum_pixels(): pl.pallas_call(pixel_window_kernel, grid=(bands // block,), in_specs=[spe...  10.2 us
    dot_general x1, matrix products, shards(): jnp.einsum('pjl,pkl->jk', residual_bf, residual_bf, preferred_element_typ...  9.32 us
  transfers between devices with their start and end apart: 11, of which 6 were waited for; matrix products, arithmetic and copies ran while one was open for 13% of the time, Pallas kernels for 0%

profile of v5, /device:TPU:0, one launch (start us, length us, event | category | flops | bytes accessed | tf_op | source)
XLA Modules:
  0.0 185.0 jit_solution(377652316583055304)
XLA Ops:
  0.0 4.1 %fusion.60 = (bf16[15,224,256]{2,1,0:T(8,128)(2,1)}, bf16[15,224,256]{2,1,0:T(8,128)(2,1)}) fusion(bf16[32,224,256]{2,1,0:T(8,128)(2,1)} %bitcast.66), kind=kLoop, calls=%fused_computation.76 | loop fusion | bytes 6881280 | tf_op jit(solution)/shard_map/slice | solution.py:162
  4.1 1.3 collective-permute-start.1
  5.4 4.3 %collective-permute-start = (bf16[15,224,256]{2,1,0:T(8,128)(2,1)}, bf16[15,224,256]{2,1,0:T(8,128)(2,1)}, u32[]{:S(2)}, u32[]{:S(2)}) collective-permute-start(bf16[15,224,256]{2,1,0:T(8,128)(2,1)} %get-tuple-element.19), channel_id=1, source_target_pairs={{0,1},{1,2},{2,3},{3,4},{4,5},{5,6},{6,7},{8,9},{9,10},{10,11},{11... | collective-permute-start | bytes 5160968 | tf_op jit(solution)/shard_map/ppermute | solution.py:155
  9.7 0.0 copy-done
  9.7 2.1 %fusion.59 = (bf16[32,224,15]{2,1,0:T(8,128)(2,1)S(1)}, bf16[32,224,15]{2,1,0:T(8,128)(2,1)}) fusion(bf16[32,224,256]{2,1,0:T(8,128)(2,1)S(1)} %bitcast.67), kind=kLoop, calls=%fused_computation.75 | loop fusion | bytes 860160 | tf_op jit(solution)/shard_map/slice | solution.py:166
  11.8 2.7 %copy.27 = bf16[32,224,15]{1,0,2:T(8,128)(2,1)} copy(bf16[32,224,15]{2,1,0:T(8,128)(2,1)} %get-tuple-element.18) | data formatting | bytes 430080 | tf_op jit(solution)/shard_map/slice | solution.py:165
  14.5 1.7 copy.31
  16.2 0.1 broadcast_multiply_fusion
  16.2 6.1 %fusion.18 = f32[256,32,224]{0,2,1:T(8,128)} fusion(bf16[256,32,224]{0,2,1:T(8,128)(2,1)} %param.3), kind=kOutput, calls=%fused_computation.23 | convolution fusion | flops 939720704 | bytes 11010048 | tf_op jit(solution)/shard_map/qbk,kl->qbl/dot_general | solution.py:187
  22.4 0.0 collective-permute-done.1
  22.4 0.4 fusion.62
  22.8 1.1 copy.28
  23.9 0.0 collective-permute-done
  23.9 2.7 %fusion.61 = (bf16[15,224,15]{2,1,0:T(8,128)(2,1)S(1)}, bf16[15,224,15]{2,1,0:T(8,128)(2,1)}) fusion(bf16[15,224,256]{2,1,0:T(8,128)(2,1)} %collective-permute-done), kind=kLoop, calls=%fused_computation.77 | loop fusion | bytes 403200 | tf_op jit(solution)/shard_map/slice | solution.py:166
  26.5 2.2 %copy.26 = bf16[15,224,15]{1,0,2:T(8,128)(2,1)} copy(bf16[15,224,15]{2,1,0:T(8,128)(2,1)} %get-tuple-element.22) | data formatting | bytes 201600 | tf_op jit(solution)/shard_map/slice | solution.py:165
  28.8 2.0 %pad_maximum_fusion = bf16[62,224,15]{1,0,2:T(8,128)(2,1)} fusion(bf16[15,224,15]{1,0,2:T(8,128)(2,1)} %copy.28, bf16[32,224,15]{1,0,2:T(8,128)(2,1)} %copy.27, bf16[15,224,15]{1,0,2:T(8,128)(2,1)} %copy.26), kind=kLoop, calls=%fused_computation.13 | loop fusion | flops 1249920 | bytes 833280 | tf_op jit(solution)/shard_map/concatenate | solution.py:165
  30.8 5.7 %collective-permute-start.2 = (bf16[62,224,15]{1,0,2:T(8,128)(2,1)}, bf16[62,224,15]{1,0,2:T(8,128)(2,1)}, u32[]{:S(2)}, u32[]{:S(2)}) collective-permute-start(bf16[62,224,15]{1,0,2:T(8,128)(2,1)} %pad_maximum_fusion), channel_id=1, source_target_pairs={{0,8},{8,16},{16,24},{1,9},{9,17},{17,25},{2,10},{10,18},{18,26},{... | collective-permute-start | bytes 1249928 | tf_op jit(solution)/shard_map/ppermute | solution.py:158
  36.5 1.1 copy.32
  37.6 0.4 copy.30
  38.0 1.2 pad_maximum_fusion.1
  39.2 1.5 collective-permute-start.3
  40.7 2.1 %fusion.20 = f32[256,15,224]{0,2,1:T(8,128)S(1)} fusion(bf16[15,224,256]{2,1,0:T(8,128)(2,1)} %collective-permute-done), kind=kOutput, calls=%fused_computation.24 | convolution fusion | flops 440598528 | bytes 5160960 | tf_op jit(solution)/shard_map/qbk,kl->qbl/dot_general | solution.py:187
  42.8 0.6 fusion.16
  43.4 0.0 collective-permute-done.2
  43.4 1.0 fusion.64
  44.5 0.5 fusion.38
  45.0 0.5 fusion.32
  45.4 1.0 slice.117
  46.5 0.0 slice-start
  46.5 0.9 fusion.13
  47.4 2.5 %collective-permute-done.3 = bf16[62,224,15]{1,0,2:T(8,128)(2,1)S(1)} collective-permute-done((bf16[62,224,15]{1,0,2:T(8,128)(2,1)S(1)}, bf16[62,224,15]{1,0,2:T(8,128)(2,1)S(1)}, u32[]{:S(2)}, u32[]{:S(2)}) %collective-permute-start.3) | collective-permute-done | bytes 416672 | tf_op jit(solution)/shard_map/ppermute | solution.py:158
  50.0 0.0 slice-start.1
  50.0 2.4 %fusion.5.left_ref = f32[15,224,256]{2,1,0:T(8,128)} fusion(f32[15,224,256]{2,1,0:T(8,128)S(1)} %fusion.38, f32[256,15,224]{0,2,1:T(8,128)S(1)} %fusion.20, bf16[15,224,15]{1,0,2:T(8,128)(2,1)S(1)} %get-tuple-element.26, s32[15]{0:T(128)S(1)} %iota_add_fusion), kind=kOutput, calls=%fused_computation.11 | convolution fusion | flops 27528960 | bytes 10422780 | tf_op jit(solution)/shard_map/qbk,kl->qbl/dot_general | solution.py:187
  52.4 0.1 slice.118
  52.5 0.0 slice-done.1
  52.5 4.2 %fusion.1.middle_ref = f32[32,224,256]{2,1,0:T(8,128)} fusion(f32[32,224,256]{2,1,0:T(8,128)S(1)} %fusion.13, f32[256,32,224]{0,2,1:T(8,128)S(1)} %bitcast.69, bf16[32,224,15]{1,0,2:T(8,128)(2,1)S(1)} %slice.118, s32[15]{0:T(128)S(1)} %iota_add_fusion), kind=kOutput, calls=%fused_computation.4 | convolution fusion | flops 58724096 | bytes 22235196 | tf_op jit(solution)/shard_map/qbk,kl->qbl/dot_general | solution.py:187
  56.7 2.4 %fusion.4.right_ref = f32[15,224,256]{2,1,0:T(8,128)} fusion(f32[15,224,256]{2,1,0:T(8,128)S(1)} %fusion.32, f32[256,15,224]{0,2,1:T(8,128)S(1)} %fusion.16, bf16[15,224,15]{1,0,2:T(8,128)(2,1)S(1)} %get-tuple-element.25, s32[15]{0:T(128)S(1)} %iota_add_fusion), kind=kOutput, calls=%fused_computation.9 | convolution fusion | flops 27528960 | bytes 10422780 | tf_op jit(solution)/shard_map/qbk,kl->qbl/dot_general | solution.py:187
  59.1 10.2 %shard_map.17 = f32[32,224,256]{2,1,0:T(8,128)} custom-call(f32[15,224,256]{2,1,0:T(8,128)} %fusion.5.left_ref, f32[32,224,256]{2,1,0:T(8,128)} %fusion.1.middle_ref, f32[15,224,256]{2,1,0:T(8,128)} %fusion.4.right_ref), custom_call_target="tpu_custom_call" | custom-call | tf_op jit(solution)/shard_map/pallas_call | solution.py:215
  69.4 9.3 %fusion.6 = f32[224,224]{1,0:T(8,128)S(1)} fusion(f32[32,224,256]{2,1,0:T(8,128)} %shard_map.17, f32[32,256]{1,0:T(8,128)S(1)} %broadcast_multiply_fusion, bf16[256,32,224]{0,2,1:T(8,128)(2,1)} %param.3), kind=kOutput, calls=%fused_computation.12 | convolution fusion | flops 829423616 | bytes 11243520 | tf_op jit(solution)/shard_map/pjl,pkl->jk/dot_general | solution.py:243
  78.7 0.1 fusion.65
  78.8 1.7 gather_fusion
  80.5 18.4 %collective-permute-start.4 = (f32[225,112]{1,0:T(8,128)S(1)}, f32[225,112]{1,0:T(8,128)S(1)}, u32[]{:S(2)}, u32[]{:S(2)}) collective-permute-start(f32[225,112]{1,0:T(8,128)S(1)} %pad_maximum_fusion.2), channel_id=1, source_target_pairs={{0,1},{1,0},{2,3},{3,2},{4,5},{5,4},{6,7},{7,6},{8,9},{9,8},{10,11... | collective-permute-start | bytes 302408 | tf_op jit(solution)/shard_map/ppermute | solution.py:247
  98.9 1.0 collective-permute-done.4
  99.9 6.7 %collective-permute-start.7 = (f32[225,112]{1,0:T(8,128)S(1)}, f32[225,112]{1,0:T(8,128)S(1)}, u32[]{:S(2)}, u32[]{:S(2)}) collective-permute-start(f32[225,112]{1,0:T(8,128)S(1)} %fusion.58), channel_id=1, source_target_pairs={{0,6},{1,7},{2,0},{3,1},{4,2},{5,3},{6,4},{7,5},{8,14},{9,15},{10,... | collective-permute-start | bytes 302408 | tf_op jit(solution)/shard_map/ppermute | solution.py:54
  106.7 2.3 %collective-permute-start.6 = (f32[225,112]{1,0:T(8,128)S(1)}, f32[225,112]{1,0:T(8,128)S(1)}, u32[]{:S(2)}, u32[]{:S(2)}) collective-permute-start(f32[225,112]{1,0:T(8,128)S(1)} %fusion.58), channel_id=1, source_target_pairs={{0,4},{1,5},{2,6},{3,7},{4,0},{5,1},{6,2},{7,3},{8,12},{9,13},{10,... | collective-permute-start | bytes 302408 | tf_op jit(solution)/shard_map/ppermute | solution.py:54
  109.0 1.9 %collective-permute-start.5 = (f32[225,112]{1,0:T(8,128)S(1)}, f32[225,112]{1,0:T(8,128)S(1)}, u32[]{:S(2)}, u32[]{:S(2)}) collective-permute-start(f32[225,112]{1,0:T(8,128)S(1)} %fusion.58), channel_id=1, source_target_pairs={{0,2},{1,3},{2,4},{3,5},{4,6},{5,7},{6,0},{7,1},{8,10},{9,11},{10,... | collective-permute-start | bytes 302408 | tf_op jit(solution)/shard_map/ppermute | solution.py:54
  110.9 0.0 collective-permute-done.7
  110.9 3.4 %collective-permute-done.6 = f32[225,112]{1,0:T(8,128)S(1)} collective-permute-done((f32[225,112]{1,0:T(8,128)S(1)}, f32[225,112]{1,0:T(8,128)S(1)}, u32[]{:S(2)}, u32[]{:S(2)}) %collective-permute-start.6) | collective-permute-done | bytes 100832 | tf_op jit(solution)/shard_map/ppermute | solution.py:54
  114.3 1.8 collective-permute-done.5
  116.2 2.3 %collective-permute-start.10 = (f32[225,112]{1,0:T(8,128)S(1)}, f32[225,112]{1,0:T(8,128)S(1)}, u32[]{:S(2)}, u32[]{:S(2)}) collective-permute-start(f32[225,112]{1,0:T(8,128)S(1)} %add_add_fusion.1), channel_id=1, source_target_pairs={{0,24},{8,0},{16,8},{24,16},{1,25},{9,1},{17,9},{25,17},{2,26},{10... | collective-permute-start | bytes 302408 | tf_op jit(solution)/shard_map/ppermute | solution.py:54
  118.5 0.0 collective-permute-start.9
  118.5 1.6 collective-permute-start.8
  120.1 2.1 %collective-permute-done.10 = f32[225,112]{1,0:T(8,128)S(1)} collective-permute-done((f32[225,112]{1,0:T(8,128)S(1)}, f32[225,112]{1,0:T(8,128)S(1)}, u32[]{:S(2)}, u32[]{:S(2)}) %collective-permute-start.10) | collective-permute-done | bytes 100832 | tf_op jit(solution)/shard_map/ppermute | solution.py:54
  122.2 6.8 %collective-permute-done.9 = f32[225,112]{1,0:T(8,128)S(1)} collective-permute-done((f32[225,112]{1,0:T(8,128)S(1)}, f32[225,112]{1,0:T(8,128)S(1)}, u32[]{:S(2)}, u32[]{:S(2)}) %collective-permute-start.9) | collective-permute-done | bytes 100832 | tf_op jit(solution)/shard_map/ppermute | solution.py:54
  129.0 0.0 collective-permute-done.8
  129.0 0.1 copy.41
  129.1 0.1 copy.42
  129.2 0.7 select_reduce_fusion
  130.6 0.1 select_add_fusion
  130.7 2.0 %scatter.4.a_ref = f32[256,256]{1,0:T(8,128)S(1)} dynamic-update-slice(f32[256,256]{1,0:T(8,128)S(1)} %fusion.22, f32[224,224]{1,0:T(8,128)S(1)} %select_add_fusion, s32[]{:T(128)} %constant.71.clone.1, s32[]{:T(128)} %constant.71.clone.1) | dynamic-update-slice | bytes 401412 | tf_op jit(solution)/shard_map/scatter | solution.py:109
  132.8 0.7 copy-done.1
  133.5 37.7 %shard_map.18 = f32[256,256]{1,0:T(8,128)} custom-call(f32[256,256]{1,0:T(8,128)} %copy-done.1), custom_call_target="tpu_custom_call" | custom-call | tf_op jit(solution)/shard_map/pallas_call | solution.py:110
  171.2 13.2 %fusion = f32[32,256]{1,0:T(8,128)S(1)} fusion(f32[32,224,256]{2,1,0:T(8,128)} %shard_map.17, f32[32,256]{1,0:T(8,128)S(1)} %broadcast_multiply_fusion, f32[256,256]{1,0:T(8,128)} %shard_map.18, bf16[256,32,224]{0,2,1:T(8,128)(2,1)} %param.3), kind=kOutput, calls=%fused_computation.2 | convolution fusion | flops 4947223552 | bytes 22347776 | tf_op jit(solution)/shard_map/pbl,bj->pjl/dot_general | solution.py:253
  184.4 0.6 multiply_bitcast_fusion
  (17 shorter events, 0.2 us)
Async XLA Ops:
  0.0 9.7 %copy-start = (bf16[256,32,224]{0,2,1:T(8,128)(2,1)S(1)}, bf16[256,32,224]{0,2,1:T(8,128)(2,1)}, u32[]{:S(2)}) copy-start(bf16[256,32,224]{0,2,1:T(8,128)(2,1)} %param.3) | copy-start | bytes 11010052
  4.1 18.3 %collective-permute-start.1 = (bf16[15,224,256]{2,1,0:T(8,128)(2,1)}, bf16[15,224,256]{2,1,0:T(8,128)(2,1)S(1)}, u32[]{:S(2)}, u32[]{:S(2)}) collective-permute-start(bf16[15,224,256]{2,1,0:T(8,128)(2,1)} %get-tuple-element.20), channel_id=1, source_target_pairs={{1,0},{2,1},{3,2},{4,3},{5,4},{6,5},{7,6},{9,8},{10,9},{11,10},{12... | collective-permute-start | bytes 5160968 | tf_op jit(solution)/shard_map/ppermute | solution.py:155
  5.4 18.5 %collective-permute-start = (bf16[15,224,256]{2,1,0:T(8,128)(2,1)}, bf16[15,224,256]{2,1,0:T(8,128)(2,1)}, u32[]{:S(2)}, u32[]{:S(2)}) collective-permute-start(bf16[15,224,256]{2,1,0:T(8,128)(2,1)} %get-tuple-element.19), channel_id=1, source_target_pairs={{0,1},{1,2},{2,3},{3,4},{4,5},{5,6},{6,7},{8,9},{9,10},{10,11},{11... | collective-permute-start | bytes 5160968 | tf_op jit(solution)/shard_map/ppermute | solution.py:155
  30.8 12.6 %collective-permute-start.2 = (bf16[62,224,15]{1,0,2:T(8,128)(2,1)}, bf16[62,224,15]{1,0,2:T(8,128)(2,1)}, u32[]{:S(2)}, u32[]{:S(2)}) collective-permute-start(bf16[62,224,15]{1,0,2:T(8,128)(2,1)} %pad_maximum_fusion), channel_id=1, source_target_pairs={{0,8},{8,16},{16,24},{1,9},{9,17},{17,25},{2,10},{10,18},{18,26},{... | collective-permute-start | bytes 1249928 | tf_op jit(solution)/shard_map/ppermute | solution.py:158
  39.2 10.7 %collective-permute-start.3 = (bf16[62,224,15]{1,0,2:T(8,128)(2,1)S(1)}, bf16[62,224,15]{1,0,2:T(8,128)(2,1)S(1)}, u32[]{:S(2)}, u32[]{:S(2)}) collective-permute-start(bf16[62,224,15]{1,0,2:T(8,128)(2,1)S(1)} %pad_maximum_fusion.1), channel_id=1, source_target_pairs={{8,0},{16,8},{24,16},{9,1},{17,9},{25,17},{10,2},{18,10},{26,18},{... | collective-permute-start | bytes 1249928 | tf_op jit(solution)/shard_map/ppermute | solution.py:158
  46.5 6.0 %slice-start = ((s8[7340032]{0:T(1024)(128)(4,1)}), s8[4194304]{0:T(1024)(128)(4,1)S(1)}, s32[]{:S(2)}) async-start(s8[7340032]{0:T(1024)(128)(4,1)} %bitcast.68), calls=%async_computation | async-start | bytes 8388608
  50.0 2.5 %slice-start.1 = ((s8[7340032]{0:T(1024)(128)(4,1)}), s8[3145728]{0:T(1024)(128)(4,1)S(1)}, s32[]{:S(2)}) async-start(s8[7340032]{0:T(1024)(128)(4,1)} %bitcast.68), calls=%async_computation.1 | async-start | bytes 6291456
  80.5 19.4 %collective-permute-start.4 = (f32[225,112]{1,0:T(8,128)S(1)}, f32[225,112]{1,0:T(8,128)S(1)}, u32[]{:S(2)}, u32[]{:S(2)}) collective-permute-start(f32[225,112]{1,0:T(8,128)S(1)} %pad_maximum_fusion.2), channel_id=1, source_target_pairs={{0,1},{1,0},{2,3},{3,2},{4,5},{5,4},{6,7},{7,6},{8,9},{9,8},{10,11... | collective-permute-start | bytes 302408 | tf_op jit(solution)/shard_map/ppermute | solution.py:247
  99.9 11.0 %collective-permute-start.7 = (f32[225,112]{1,0:T(8,128)S(1)}, f32[225,112]{1,0:T(8,128)S(1)}, u32[]{:S(2)}, u32[]{:S(2)}) collective-permute-start(f32[225,112]{1,0:T(8,128)S(1)} %fusion.58), channel_id=1, source_target_pairs={{0,6},{1,7},{2,0},{3,1},{4,2},{5,3},{6,4},{7,5},{8,14},{9,15},{10,... | collective-permute-start | bytes 302408 | tf_op jit(solution)/shard_map/ppermute | solution.py:54
  106.7 7.6 %collective-permute-start.6 = (f32[225,112]{1,0:T(8,128)S(1)}, f32[225,112]{1,0:T(8,128)S(1)}, u32[]{:S(2)}, u32[]{:S(2)}) collective-permute-start(f32[225,112]{1,0:T(8,128)S(1)} %fusion.58), channel_id=1, source_target_pairs={{0,4},{1,5},{2,6},{3,7},{4,0},{5,1},{6,2},{7,3},{8,12},{9,13},{10,... | collective-permute-start | bytes 302408 | tf_op jit(solution)/shard_map/ppermute | solution.py:54
  109.0 7.2 %collective-permute-start.5 = (f32[225,112]{1,0:T(8,128)S(1)}, f32[225,112]{1,0:T(8,128)S(1)}, u32[]{:S(2)}, u32[]{:S(2)}) collective-permute-start(f32[225,112]{1,0:T(8,128)S(1)} %fusion.58), channel_id=1, source_target_pairs={{0,2},{1,3},{2,4},{3,5},{4,6},{5,7},{6,0},{7,1},{8,10},{9,11},{10,... | collective-permute-start | bytes 302408 | tf_op jit(solution)/shard_map/ppermute | solution.py:54
  116.2 6.0 %collective-permute-start.10 = (f32[225,112]{1,0:T(8,128)S(1)}, f32[225,112]{1,0:T(8,128)S(1)}, u32[]{:S(2)}, u32[]{:S(2)}) collective-permute-start(f32[225,112]{1,0:T(8,128)S(1)} %add_add_fusion.1), channel_id=1, source_target_pairs={{0,24},{8,0},{16,8},{24,16},{1,25},{9,1},{17,9},{25,17},{2,26},{10... | collective-permute-start | bytes 302408 | tf_op jit(solution)/shard_map/ppermute | solution.py:54
  118.5 10.5 %collective-permute-start.9 = (f32[225,112]{1,0:T(8,128)S(1)}, f32[225,112]{1,0:T(8,128)S(1)}, u32[]{:S(2)}, u32[]{:S(2)}) collective-permute-start(f32[225,112]{1,0:T(8,128)S(1)} %add_add_fusion.1), channel_id=1, source_target_pairs={{0,16},{8,24},{16,0},{24,8},{1,17},{9,25},{17,1},{25,9},{2,18},{10... | collective-permute-start | bytes 302408 | tf_op jit(solution)/shard_map/ppermute | solution.py:54
  118.5 10.4 %collective-permute-start.8 = (f32[225,112]{1,0:T(8,128)S(1)}, f32[225,112]{1,0:T(8,128)S(1)}, u32[]{:S(2)}, u32[]{:S(2)}) collective-permute-start(f32[225,112]{1,0:T(8,128)S(1)} %add_add_fusion.1), channel_id=1, source_target_pairs={{0,8},{8,16},{16,24},{24,0},{1,9},{9,17},{17,25},{25,1},{2,10},{10... | collective-permute-start | bytes 302408 | tf_op jit(solution)/shard_map/ppermute | solution.py:54
  132.8 0.7 copy-start.1

commit v6 on v4

--- a/solution.py
+++ b/solution.py
@@ -163,15 +163,17 @@
         "left": fetch(planes[last], 0, -1),
         "right": fetch(planes[first], 0, 1),
     }
+    top = fetch(planes[:, :, last], -1, 0)
+    bottom = fetch(planes[:, :, first], 1, 0)
     tops = {
-        "left": fetch(planes[last, :, last], -1, -1),
-        "middle": fetch(planes[:, :, last], -1, 0),
-        "right": fetch(planes[first, :, last], -1, 1),
+        "left": fetch(top[last], 0, -1),
+        "middle": top,
+        "right": fetch(top[first], 0, 1),
     }
     bottoms = {
-        "left": fetch(planes[last, :, first], 1, -1),
-        "middle": fetch(planes[:, :, first], 1, 0),
-        "right": fetch(planes[first, :, first], 1, 1),
+        "left": fetch(bottom[last], 0, -1),
+        "middle": bottom,
+        "right": fetch(bottom[first], 0, 1),
     }
     return sides, tops, bottoms
 

time: 178 us -> 170 us (0.955)
  waiting for transfers between devices: 25.6 us -> 15 us
  starting transfers between devices: 33.4 us -> 40.5 us
  local copies, waits for them, and re-layouts: 23.7 us -> 19.1 us
    ppermute x4 -> x0, starting transfers between devices: 12.6 us -> none  [fetch(): return lax.ppermute(piece, both, neighbour_pairs(n_track, n_cross, dt, dc))]
    ppermute x2, waiting for transfers between devices: 12.5 us -> 0.01 us  [fetch(): return lax.ppermute(piece, 'track', pairs)]
    ppermute x1, starting transfers between devices: 0.19 us -> 12.6 us  [shards(): lax.ppermute(packed, 'cross', [(i, i ^ 1) for i in range(n_cross)])]
    ppermute x2 -> x6, starting transfers between devices: 5.35 us -> 14 us  [fetch(): return lax.ppermute(piece, 'cross', pairs)]
    slice x8 -> x9, local copies, waits for them, and re-layouts: 15.2 us -> 10.5 us  [the longest x2 5.62 us: halos(): bottom = fetch(planes[:, :, first], 1, 0)]
    ppermute x6, starting transfers between devices: 9.14 us -> 7 us  [ring_sum(): total = total + lax.ppermute(x, axis, pairs)]
    ppermute x6, waiting for transfers between devices: 11.9 us -> 14 us  [ring_sum(): total = total + lax.ppermute(x, axis, pairs)]
  transfers between devices with their start and end apart: 15 -> 15, of which waited for: 8 -> 5; matrix products, arithmetic and copies ran while one was open for 19% -> 16% of each run, Pallas kernels for 0% -> 0%
where the time goes in v6:
time: 170 us; the launch traced here: 169 us
  Pallas kernels  48 us (28%)
  matrix products  43.9 us (26%)
  starting transfers between devices  40.5 us (24%)
  local copies, waits for them, and re-layouts  19.1 us (11%)
  waiting for transfers between devices  15 us (9%)
  other arithmetic  1.79 us (1%)
    pallas_call x1, Pallas kernels, spd_inverse(): pl.pallas_call(functools.partial(sweep_kernel, n), out_shape=jax.ShapeDty...  37.7 us
    dot_general x9, matrix products, sum_lines(): jnp.einsum('qbk,kl->qbl', values, w, preferred_element_type=jnp.float32)  21.5 us
    ppermute x6, starting transfers between devices, fetch(): return lax.ppermute(piece, 'cross', pairs)  14 us
    ppermute x6, waiting for transfers between devices, ring_sum(): total = total + lax.ppermute(x, axis, pairs)  14 us
    dot_general x1, matrix products, shards(): jnp.einsum('pbl,bj->pjl', residual, inverse, precision=highest, preferred...  13.1 us
    ppermute x1, starting transfers between devices, shards(): lax.ppermute(packed, 'cross', [(i, i ^ 1) for i in range(n_cross)])  12.6 us
    pallas_call x1, Pallas kernels, sum_pixels(): pl.pallas_call(pixel_window_kernel, grid=(bands // block,), in_specs=[spe...  10.2 us
    dot_general x1, matrix products, shards(): jnp.einsum('pjl,pkl->jk', residual_bf, residual_bf, preferred_element_typ...  9.24 us
  transfers between devices with their start and end apart: 15, of which 5 were waited for; matrix products, arithmetic and copies ran while one was open for 16% of the time, Pallas kernels for 0%

profile of v6, /device:TPU:0, one launch (start us, length us, event | category | flops | bytes accessed | tf_op | source)
XLA Modules:
  0.0 169.1 jit_solution(227042548229463048)
XLA Ops:
  0.0 3.9 %fusion.53 = (bf16[32,224,15]{2,1,0:T(8,128)(2,1)S(1)}, bf16[32,224,15]{2,1,0:T(8,128)(2,1)}) fusion(bf16[32,224,256]{2,1,0:T(8,128)(2,1)} %bitcast.68), kind=kLoop, calls=%fused_computation.67 | loop fusion | bytes 860160 | tf_op jit(solution)/shard_map/slice | solution.py:167
  3.9 2.7 %copy.26 = bf16[32,224,15]{1,0,2:T(8,128)(2,1)} copy(bf16[32,224,15]{2,1,0:T(8,128)(2,1)} %get-tuple-element.20) | data formatting | bytes 430080 | tf_op jit(solution)/shard_map/slice | solution.py:166
  6.6 5.6 %collective-permute-start = (bf16[32,224,15]{1,0,2:T(8,128)(2,1)}, bf16[32,224,15]{1,0,2:T(8,128)(2,1)}, u32[]{:S(2)}, u32[]{:S(2)}) collective-permute-start(bf16[32,224,15]{1,0,2:T(8,128)(2,1)} %copy.26), channel_id=1, source_target_pairs={{0,8},{8,16},{16,24},{1,9},{9,17},{17,25},{2,10},{10,18},{18,26},{... | collective-permute-start | bytes 645128 | tf_op jit(solution)/shard_map/ppermute | solution.py:158
  12.3 4.0 %fusion.52 = (bf16[15,224,256]{2,1,0:T(8,128)(2,1)}, bf16[15,224,256]{2,1,0:T(8,128)(2,1)}) fusion(bf16[32,224,256]{2,1,0:T(8,128)(2,1)} %bitcast.69), kind=kLoop, calls=%fused_computation.66 | loop fusion | bytes 6881280 | tf_op jit(solution)/shard_map/slice | solution.py:164
  16.3 1.6 collective-permute-start.2
  17.9 1.7 copy.28
  19.5 1.3 collective-permute-start.3
  20.8 1.3 collective-permute-start.6
  22.1 6.1 %fusion.15 = f32[256,32,224]{0,2,1:T(8,128)} fusion(bf16[256,32,224]{0,2,1:T(8,128)(2,1)} %param.3), kind=kOutput, calls=%fused_computation.18 | convolution fusion | flops 939720704 | bytes 11010048 | tf_op jit(solution)/shard_map/qbk,kl->qbl/dot_general | solution.py:193
  28.3 0.1 broadcast_multiply_fusion
  28.4 0.0 collective-permute-done
  28.4 1.0 fusion.55
  29.4 4.5 %collective-permute-start.1 = (bf16[15,224,15]{1,2,0:T(8,128)(2,1)S(1)}, bf16[15,224,15]{1,2,0:T(8,128)(2,1)S(1)}, u32[]{:S(2)}, u32[]{:S(2)}) collective-permute-start(bf16[15,224,15]{1,2,0:T(8,128)(2,1)S(1)} %copy.27), channel_id=1, source_target_pairs={{0,1},{1,2},{2,3},{3,4},{4,5},{5,6},{6,7},{8,9},{9,10},{10,11},{11... | collective-permute-start | bytes 302408 | tf_op jit(solution)/shard_map/ppermute | solution.py:155
  33.9 0.0 collective-permute-done.3
  33.9 1.0 fusion.54
  35.0 3.6 %collective-permute-start.4 = (bf16[15,224,15]{1,2,0:T(8,128)(2,1)S(1)}, bf16[15,224,15]{1,2,0:T(8,128)(2,1)S(1)}, u32[]{:S(2)}, u32[]{:S(2)}) collective-permute-start(bf16[15,224,15]{1,2,0:T(8,128)(2,1)S(1)} %copy.29), channel_id=1, source_target_pairs={{0,1},{1,2},{2,3},{3,4},{4,5},{5,6},{6,7},{8,9},{9,10},{10,11},{11... | collective-permute-start | bytes 302408 | tf_op jit(solution)/shard_map/ppermute | solution.py:155
  38.7 0.0 copy-start
  38.7 1.6 collective-permute-start.5
  40.3 2.6 %fusion.10 = f32[256,32,224]{0,2,1:T(8,128)S(1)} fusion(bf16[32,224,15]{1,0,2:T(8,128)(2,1)} %collective-permute-done), kind=kOutput, calls=%fused_computation.12 | convolution fusion | flops 55054080 | bytes 7555072 | tf_op jit(solution)/shard_map/qbk,kl->qbl/dot_general | solution.py:193
  42.9 0.0 copy-done
  42.9 5.3 %add_bitcast_fusion.middle_ref = f32[32,224,256]{2,1,0:T(8,128)} fusion(f32[256,32,224]{0,2,1:T(8,128)S(1)} %fusion.10, f32[256,32,224]{0,2,1:T(8,128)S(1)} %copy-done, bf16[32,224,15]{1,0,2:T(8,128)(2,1)} %collective-permute-done.3, s32[15]{0:T(128)S(1)} %iota_add_fusion), kind=kOutput, calls=%fused_computation.4 | convolution fusion | flops 58724096 | bytes 22235196 | tf_op jit(solution)/shard_map/qbk,kl->qbl/dot_general | solution.py:193
  48.3 0.0 collective-permute-done.1
  48.3 1.5 collective-permute-start.7
  49.8 0.7 fusion.30
  50.4 0.0 collective-permute-done.5
  50.4 0.7 fusion.27
  51.1 0.0 collective-permute-done.2
  51.1 0.6 fusion.17
  51.8 0.0 collective-permute-done.4
  51.8 2.4 %add_bitcast_fusion.2.left_ref = f32[15,224,256]{2,1,0:T(8,128)} fusion(f32[256,15,224]{0,2,1:T(8,128)S(1)} %fusion.30, f32[256,15,224]{0,2,1:T(8,128)S(1)} %fusion.17, bf16[15,224,15]{1,2,0:T(8,128)(2,1)S(1)} %collective-permute-done.4, s32[15]{0:T(128)S(1)} %iota_add_fusion), kind=kOutput, calls=%fused_computation.8 | convolution fusion | flops 27528960 | bytes 10422780 | tf_op jit(solution)/shard_map/qbk,kl->qbl/dot_general | solution.py:193
  54.2 0.0 collective-permute-done.6
  54.2 0.6 fusion.13
  54.8 0.0 collective-permute-done.7
  54.8 2.4 %add_bitcast_fusion.1.right_ref = f32[15,224,256]{2,1,0:T(8,128)} fusion(f32[256,15,224]{0,2,1:T(8,128)S(1)} %fusion.27, f32[256,15,224]{0,2,1:T(8,128)S(1)} %fusion.13, bf16[15,224,15]{1,2,0:T(8,128)(2,1)S(1)} %collective-permute-done.7, s32[15]{0:T(128)S(1)} %iota_add_fusion), kind=kOutput, calls=%fused_computation.7 | convolution fusion | flops 27528960 | bytes 10422780 | tf_op jit(solution)/shard_map/qbk,kl->qbl/dot_general | solution.py:193
  57.3 10.2 %shard_map.17 = f32[32,224,256]{2,1,0:T(8,128)} custom-call(f32[15,224,256]{2,1,0:T(8,128)} %add_bitcast_fusion.2.left_ref, f32[32,224,256]{2,1,0:T(8,128)} %add_bitcast_fusion.middle_ref, f32[15,224,256]{2,1,0:T(8,128)} %add_bitcast_fusion.1.right_ref), custom_call_target="tpu_custom_call" | custom-call | tf_op jit(solution)/shard_map/pallas_call | solution.py:221
  67.5 9.2 %fusion.3 = f32[224,224]{1,0:T(8,128)S(1)} fusion(f32[32,224,256]{2,1,0:T(8,128)} %shard_map.17, f32[32,256]{1,0:T(8,128)S(1)} %broadcast_multiply_fusion, bf16[256,32,224]{0,2,1:T(8,128)(2,1)} %param.3), kind=kOutput, calls=%fused_computation.9 | convolution fusion | flops 829423616 | bytes 11243520 | tf_op jit(solution)/shard_map/pjl,pkl->jk/dot_general | solution.py:249
  76.7 0.1 fusion.56
  76.8 1.7 gather_fusion
  78.5 12.6 %collective-permute-start.8 = (f32[225,112]{1,0:T(8,128)S(1)}, f32[225,112]{1,0:T(8,128)S(1)}, u32[]{:S(2)}, u32[]{:S(2)}) collective-permute-start(f32[225,112]{1,0:T(8,128)S(1)} %pad_maximum_fusion), channel_id=1, source_target_pairs={{0,1},{1,0},{2,3},{3,2},{4,5},{5,4},{6,7},{7,6},{8,9},{9,8},{10,11... | collective-permute-start | bytes 302408 | tf_op jit(solution)/shard_map/ppermute | solution.py:253
  91.1 1.0 collective-permute-done.8
  92.1 0.1 collective-permute-start.11
  92.2 3.0 %collective-permute-start.10 = (f32[225,112]{1,0:T(8,128)S(1)}, f32[225,112]{1,0:T(8,128)S(1)}, u32[]{:S(2)}, u32[]{:S(2)}) collective-permute-start(f32[225,112]{1,0:T(8,128)S(1)} %fusion.51), channel_id=1, source_target_pairs={{0,4},{1,5},{2,6},{3,7},{4,0},{5,1},{6,2},{7,3},{8,12},{9,13},{10,... | collective-permute-start | bytes 302408 | tf_op jit(solution)/shard_map/ppermute | solution.py:54
  95.1 0.0 collective-permute-start.9
  95.1 2.9 %collective-permute-done.11 = f32[225,112]{1,0:T(8,128)S(1)} collective-permute-done((f32[225,112]{1,0:T(8,128)S(1)}, f32[225,112]{1,0:T(8,128)S(1)}, u32[]{:S(2)}, u32[]{:S(2)}) %collective-permute-start.11) | collective-permute-done | bytes 100832 | tf_op jit(solution)/shard_map/ppermute | solution.py:54
  98.0 3.1 %collective-permute-done.10 = f32[225,112]{1,0:T(8,128)S(1)} collective-permute-done((f32[225,112]{1,0:T(8,128)S(1)}, f32[225,112]{1,0:T(8,128)S(1)}, u32[]{:S(2)}, u32[]{:S(2)}) %collective-permute-start.10) | collective-permute-done | bytes 100832 | tf_op jit(solution)/shard_map/ppermute | solution.py:54
  101.1 0.0 collective-permute-done.9
  101.2 0.8 collective-permute-start.14
  102.0 1.6 collective-permute-start.13
  103.6 1.6 collective-permute-start.12
  105.2 1.4 collective-permute-done.14
  106.6 6.5 %collective-permute-done.13 = f32[225,112]{1,0:T(8,128)S(1)} collective-permute-done((f32[225,112]{1,0:T(8,128)S(1)}, f32[225,112]{1,0:T(8,128)S(1)}, u32[]{:S(2)}, u32[]{:S(2)}) %collective-permute-start.13) | collective-permute-done | bytes 100832 | tf_op jit(solution)/shard_map/ppermute | solution.py:54
  113.2 0.0 collective-permute-done.12
  113.2 0.1 copy.37
  113.3 0.1 copy.38
  113.4 0.7 select_reduce_fusion
  114.8 0.1 select_add_fusion
  114.9 2.0 %scatter.4.a_ref = f32[256,256]{1,0:T(8,128)S(1)} dynamic-update-slice(f32[256,256]{1,0:T(8,128)S(1)} %fusion.19, f32[224,224]{1,0:T(8,128)S(1)} %select_add_fusion, s32[]{:T(128)} %constant.71.clone.1, s32[]{:T(128)} %constant.71.clone.1) | dynamic-update-slice | bytes 401412 | tf_op jit(solution)/shard_map/scatter | solution.py:109
  117.0 0.0 copy-start.1
  117.0 0.7 copy-done.1
  117.7 37.7 %shard_map.18 = f32[256,256]{1,0:T(8,128)} custom-call(f32[256,256]{1,0:T(8,128)} %copy-done.1), custom_call_target="tpu_custom_call" | custom-call | tf_op jit(solution)/shard_map/pallas_call | solution.py:110
  155.4 13.1 %fusion = f32[32,256]{1,0:T(8,128)S(1)} fusion(f32[32,224,256]{2,1,0:T(8,128)} %shard_map.17, f32[32,256]{1,0:T(8,128)S(1)} %broadcast_multiply_fusion, f32[256,256]{1,0:T(8,128)} %shard_map.18, bf16[256,32,224]{0,2,1:T(8,128)(2,1)} %param.3), kind=kOutput, calls=%fused_computation.2 | convolution fusion | flops 4947223552 | bytes 22347776 | tf_op jit(solution)/shard_map/pbl,bj->pjl/dot_general | solution.py:259
  168.5 0.6 multiply_bitcast_fusion
  (16 shorter events, 0.3 us)
Async XLA Ops:
  6.6 21.7 %collective-permute-start = (bf16[32,224,15]{1,0,2:T(8,128)(2,1)}, bf16[32,224,15]{1,0,2:T(8,128)(2,1)}, u32[]{:S(2)}, u32[]{:S(2)}) collective-permute-start(bf16[32,224,15]{1,0,2:T(8,128)(2,1)} %copy.26), channel_id=1, source_target_pairs={{0,8},{8,16},{16,24},{1,9},{9,17},{17,25},{2,10},{10,18},{18,26},{... | collective-permute-start | bytes 645128 | tf_op jit(solution)/shard_map/ppermute | solution.py:158
  16.3 34.8 %collective-permute-start.2 = (bf16[15,224,256]{2,1,0:T(8,128)(2,1)}, bf16[15,224,256]{2,1,0:T(8,128)(2,1)S(1)}, u32[]{:S(2)}, u32[]{:S(2)}) collective-permute-start(bf16[15,224,256]{2,1,0:T(8,128)(2,1)} %get-tuple-element.18), channel_id=1, source_target_pairs={{0,1},{1,2},{2,3},{3,4},{4,5},{5,6},{6,7},{8,9},{9,10},{10,11},{11... | collective-permute-start | bytes 5160968 | tf_op jit(solution)/shard_map/ppermute | solution.py:155
  19.5 14.4 %collective-permute-start.3 = (bf16[32,224,15]{1,0,2:T(8,128)(2,1)}, bf16[32,224,15]{1,0,2:T(8,128)(2,1)}, u32[]{:S(2)}, u32[]{:S(2)}) collective-permute-start(bf16[32,224,15]{1,0,2:T(8,128)(2,1)} %copy.28), channel_id=1, source_target_pairs={{8,0},{16,8},{24,16},{9,1},{17,9},{25,17},{10,2},{18,10},{26,18},{... | collective-permute-start | bytes 645128 | tf_op jit(solution)/shard_map/ppermute | solution.py:158
  20.8 33.4 %collective-permute-start.6 = (bf16[15,224,256]{2,1,0:T(8,128)(2,1)}, bf16[15,224,256]{2,1,0:T(8,128)(2,1)S(1)}, u32[]{:S(2)}, u32[]{:S(2)}) collective-permute-start(bf16[15,224,256]{2,1,0:T(8,128)(2,1)} %get-tuple-element.17), channel_id=1, source_target_pairs={{1,0},{2,1},{3,2},{4,3},{5,4},{6,5},{7,6},{9,8},{10,9},{11,10},{12... | collective-permute-start | bytes 5160968 | tf_op jit(solution)/shard_map/ppermute | solution.py:155
  29.4 18.8 %collective-permute-start.1 = (bf16[15,224,15]{1,2,0:T(8,128)(2,1)S(1)}, bf16[15,224,15]{1,2,0:T(8,128)(2,1)S(1)}, u32[]{:S(2)}, u32[]{:S(2)}) collective-permute-start(bf16[15,224,15]{1,2,0:T(8,128)(2,1)S(1)} %copy.27), channel_id=1, source_target_pairs={{0,1},{1,2},{2,3},{3,4},{4,5},{5,6},{6,7},{8,9},{9,10},{10,11},{11... | collective-permute-start | bytes 302408 | tf_op jit(solution)/shard_map/ppermute | solution.py:155
  35.0 16.8 %collective-permute-start.4 = (bf16[15,224,15]{1,2,0:T(8,128)(2,1)S(1)}, bf16[15,224,15]{1,2,0:T(8,128)(2,1)S(1)}, u32[]{:S(2)}, u32[]{:S(2)}) collective-permute-start(bf16[15,224,15]{1,2,0:T(8,128)(2,1)S(1)} %copy.29), channel_id=1, source_target_pairs={{0,1},{1,2},{2,3},{3,4},{4,5},{5,6},{6,7},{8,9},{9,10},{10,11},{11... | collective-permute-start | bytes 302408 | tf_op jit(solution)/shard_map/ppermute | solution.py:155
  38.7 4.2 %copy-start = (f32[256,32,224]{0,2,1:T(8,128)S(1)}, f32[256,32,224]{0,2,1:T(8,128)}, u32[]{:S(2)}) copy-start(f32[256,32,224]{0,2,1:T(8,128)} %fusion.15) | copy-start | bytes 22020100
  38.7 11.7 %collective-permute-start.5 = (bf16[15,224,15]{1,2,0:T(8,128)(2,1)S(1)}, bf16[15,224,15]{1,2,0:T(8,128)(2,1)S(1)}, u32[]{:S(2)}, u32[]{:S(2)}) collective-permute-start(bf16[15,224,15]{1,2,0:T(8,128)(2,1)S(1)} %copy.32), channel_id=1, source_target_pairs={{1,0},{2,1},{3,2},{4,3},{5,4},{6,5},{7,6},{9,8},{10,9},{11,10},{12... | collective-permute-start | bytes 302408 | tf_op jit(solution)/shard_map/ppermute | solution.py:155
  48.3 6.6 %collective-permute-start.7 = (bf16[15,224,15]{1,2,0:T(8,128)(2,1)S(1)}, bf16[15,224,15]{1,2,0:T(8,128)(2,1)S(1)}, u32[]{:S(2)}, u32[]{:S(2)}) collective-permute-start(bf16[15,224,15]{1,2,0:T(8,128)(2,1)S(1)} %copy.33), channel_id=1, source_target_pairs={{1,0},{2,1},{3,2},{4,3},{5,4},{6,5},{7,6},{9,8},{10,9},{11,10},{12... | collective-permute-start | bytes 302408 | tf_op jit(solution)/shard_map/ppermute | solution.py:155
  78.5 13.6 %collective-permute-start.8 = (f32[225,112]{1,0:T(8,128)S(1)}, f32[225,112]{1,0:T(8,128)S(1)}, u32[]{:S(2)}, u32[]{:S(2)}) collective-permute-start(f32[225,112]{1,0:T(8,128)S(1)} %pad_maximum_fusion), channel_id=1, source_target_pairs={{0,1},{1,0},{2,3},{3,2},{4,5},{5,4},{6,7},{7,6},{8,9},{9,8},{10,11... | collective-permute-start | bytes 302408 | tf_op jit(solution)/shard_map/ppermute | solution.py:253
  92.1 5.9 %collective-permute-start.11 = (f32[225,112]{1,0:T(8,128)S(1)}, f32[225,112]{1,0:T(8,128)S(1)}, u32[]{:S(2)}, u32[]{:S(2)}) collective-permute-start(f32[225,112]{1,0:T(8,128)S(1)} %fusion.51), channel_id=1, source_target_pairs={{0,6},{1,7},{2,0},{3,1},{4,2},{5,3},{6,4},{7,5},{8,14},{9,15},{10,... | collective-permute-start | bytes 302408 | tf_op jit(solution)/shard_map/ppermute | solution.py:54
  92.2 9.0 %collective-permute-start.10 = (f32[225,112]{1,0:T(8,128)S(1)}, f32[225,112]{1,0:T(8,128)S(1)}, u32[]{:S(2)}, u32[]{:S(2)}) collective-permute-start(f32[225,112]{1,0:T(8,128)S(1)} %fusion.51), channel_id=1, source_target_pairs={{0,4},{1,5},{2,6},{3,7},{4,0},{5,1},{6,2},{7,3},{8,12},{9,13},{10,... | collective-permute-start | bytes 302408 | tf_op jit(solution)/shard_map/ppermute | solution.py:54
  95.1 6.0 %collective-permute-start.9 = (f32[225,112]{1,0:T(8,128)S(1)}, f32[225,112]{1,0:T(8,128)S(1)}, u32[]{:S(2)}, u32[]{:S(2)}) collective-permute-start(f32[225,112]{1,0:T(8,128)S(1)} %fusion.51), channel_id=1, source_target_pairs={{0,2},{1,3},{2,4},{3,5},{4,6},{5,7},{6,0},{7,1},{8,10},{9,11},{10,... | collective-permute-start | bytes 302408 | tf_op jit(solution)/shard_map/ppermute | solution.py:54
  101.2 5.4 %collective-permute-start.14 = (f32[225,112]{1,0:T(8,128)S(1)}, f32[225,112]{1,0:T(8,128)S(1)}, u32[]{:S(2)}, u32[]{:S(2)}) collective-permute-start(f32[225,112]{1,0:T(8,128)S(1)} %add_add_fusion.1), channel_id=1, source_target_pairs={{0,24},{8,0},{16,8},{24,16},{1,25},{9,1},{17,9},{25,17},{2,26},{10... | collective-permute-start | bytes 302408 | tf_op jit(solution)/shard_map/ppermute | solution.py:54
  102.0 11.2 %collective-permute-start.13 = (f32[225,112]{1,0:T(8,128)S(1)}, f32[225,112]{1,0:T(8,128)S(1)}, u32[]{:S(2)}, u32[]{:S(2)}) collective-permute-start(f32[225,112]{1,0:T(8,128)S(1)} %add_add_fusion.1), channel_id=1, source_target_pairs={{0,16},{8,24},{16,0},{24,8},{1,17},{9,25},{17,1},{25,9},{2,18},{10... | collective-permute-start | bytes 302408 | tf_op jit(solution)/shard_map/ppermute | solution.py:54
  103.6 9.6 %collective-permute-start.12 = (f32[225,112]{1,0:T(8,128)S(1)}, f32[225,112]{1,0:T(8,128)S(1)}, u32[]{:S(2)}, u32[]{:S(2)}) collective-permute-start(f32[225,112]{1,0:T(8,128)S(1)} %add_add_fusion.1), channel_id=1, source_target_pairs={{0,8},{8,16},{16,24},{24,0},{1,9},{9,17},{17,25},{25,1},{2,10},{10... | collective-permute-start | bytes 302408 | tf_op jit(solution)/shard_map/ppermute | solution.py:54
  117.0 0.7 copy-start.1

commit v7 on v6

--- a/solution.py
+++ b/solution.py
@@ -195,7 +195,7 @@
     return total
 
 
-def pixel_window_kernel(left_ref, middle_ref, right_ref, out_ref):
+def residual_kernel(left_ref, middle_ref, right_ref, x_ref, count_ref, out_ref, out_bf_ref):
     refs = [(left_ref, q) for q in range(left_ref.shape[0])]
     refs += [(middle_ref, q) for q in range(middle_ref.shape[0])]
     refs += [(right_ref, q) for q in range(right_ref.shape[0])]
@@ -203,28 +203,37 @@
     def plane(q):
         ref, i = refs[q]
         return ref[i]
+
+    def emit(p, running):
+        value = x_ref[p].astype(jnp.float32) - running / count_ref[p]
+        out_ref[p] = value
+        out_bf_ref[p] = value.astype(jnp.bfloat16)
 
     span = 2 * HALF + 1
     running = plane(0)
     for q in range(1, span):
         running = running + plane(q)
-    out_ref[0] = running
+    emit(0, running)
     for p in range(1, out_ref.shape[0]):
         running = running + plane(p + span - 1) - plane(p - 1)
-        out_ref[p] = running
-
-
-def sum_pixels(left, middle, right):
+        emit(p, running)
+
+
+def residuals(left, middle, right, planes, count):
     width, bands, lines = middle.shape
     block = 32 if bands % 32 == 0 else bands
     spec = lambda n: pl.BlockSpec((n, block, lines), lambda i: (0, i, 0))
+    count_spec = pl.BlockSpec((width, 1, lines), lambda i: (0, 0, 0))
     return pl.pallas_call(
-        pixel_window_kernel,
+        residual_kernel,
         grid=(bands // block,),
-        in_specs=[spec(left.shape[0]), spec(width), spec(right.shape[0])],
-        out_specs=spec(width),
-        out_shape=jax.ShapeDtypeStruct((width, bands, lines), jnp.float32),
-    )(left, middle, right)
+        in_specs=[spec(left.shape[0]), spec(width), spec(right.shape[0]), spec(width), count_spec],
+        out_specs=[spec(width), spec(width)],
+        out_shape=[
+            jax.ShapeDtypeStruct((width, bands, lines), jnp.float32),
+            jax.ShapeDtypeStruct((width, bands, lines), jnp.bfloat16),
+        ],
+    )(left, middle, right, planes, count)
 
 
 def shards(cube):
@@ -240,12 +249,10 @@
     middle = sum_lines(tops["middle"], planes, bottoms["middle"], weights)
     left = sum_lines(tops["left"], sides["left"], bottoms["left"], weights)
     right = sum_lines(tops["right"], sides["right"], bottoms["right"], weights)
-    window = sum_pixels(left, middle, right)
     line_count = window_count(lax.axis_index("track") * lines_dev, lines_dev, total_lines)
     pixel_count = window_count(lax.axis_index("cross") * pix_dev, pix_dev, total_pix)
     count = pixel_count[:, None, None] * line_count[None, None, :]
-    residual = planes.astype(jnp.float32) - window / count
-    residual_bf = residual.astype(jnp.bfloat16)
+    residual, residual_bf = residuals(left, middle, right, planes, count)
     partial_cov = jnp.einsum(
         "pjl,pkl->jk", residual_bf, residual_bf, preferred_element_type=jnp.float32
     )

time: 170 us -> 168 us (0.988)
  matrix products: 43.9 us -> 33.3 us
  starting transfers between devices: 40.5 us -> 47.8 us
  Pallas kernels: 48 us -> 50.3 us
    ppermute x6, starting transfers between devices: 14 us -> 28.5 us  [fetch(): return lax.ppermute(piece, 'cross', pairs)]
    ppermute x1, starting transfers between devices: 12.6 us -> 0.07 us  [shards(): lax.ppermute(packed, 'cross', [(i, i ^ 1) for i in range(n_cross)])]
    ppermute x6, starting transfers between devices: 7 us -> 12.1 us  [ring_sum(): total = total + lax.ppermute(x, axis, pairs)]
    dot_general x1, matrix products: 9.24 us -> 4.29 us  [shards(): jnp.einsum('pjl,pkl->jk', residual_bf, residual_bf, preferred_element_typ...]
    dot_general x1, matrix products: 13.1 us -> 10.2 us  [shards(): jnp.einsum('pbl,bj->pjl', residual, inverse, precision=highest, preferred...]
    dot_general x9, matrix products: 21.5 us -> 18.8 us  [sum_lines(): jnp.einsum('qbk,kl->qbl', values, w, preferred_element_type=jnp.float32)]
    pallas_call x1, Pallas kernels: 10.2 us -> 12.6 us  [residuals(): pl.pallas_call(residual_kernel, grid=(bands // block,), in_specs=[spec(le...]
    ppermute x6, waiting for transfers between devices: 14 us -> 12.1 us  [ring_sum(): total = total + lax.ppermute(x, axis, pairs)]
  transfers between devices with their start and end apart: 15 -> 15, of which waited for: 5 -> 7; matrix products, arithmetic and copies ran while one was open for 16% -> 15% of each run, Pallas kernels for 0% -> 0%
where the time goes in v7:
time: 168 us; the launch traced here: 167 us
  Pallas kernels  50.3 us (30%)
  starting transfers between devices  47.8 us (28%)
  matrix products  33.3 us (20%)
  local copies, waits for them, and re-layouts  19 us (11%)
  waiting for transfers between devices  13.5 us (8%)
  other arithmetic  2.45 us (1%)
    pallas_call x1, Pallas kernels, spd_inverse(): pl.pallas_call(functools.partial(sweep_kernel, n), out_shape=jax.ShapeDty...  37.7 us
    ppermute x6, starting transfers between devices, fetch(): return lax.ppermute(piece, 'cross', pairs)  28.5 us
    dot_general x9, matrix products, sum_lines(): jnp.einsum('qbk,kl->qbl', values, w, preferred_element_type=jnp.float32)  18.8 us
    pallas_call x1, Pallas kernels, residuals(): pl.pallas_call(residual_kernel, grid=(bands // block,), in_specs=[spec(le...  12.6 us
    ppermute x6, waiting for transfers between devices, ring_sum(): total = total + lax.ppermute(x, axis, pairs)  12.1 us
    ppermute x6, starting transfers between devices, ring_sum(): total = total + lax.ppermute(x, axis, pairs)  12.1 us
    dot_general x1, matrix products, shards(): jnp.einsum('pbl,bj->pjl', residual, inverse, precision=highest, preferred...  10.2 us
    ppermute x2, starting transfers between devices, fetch(): return lax.ppermute(piece, 'track', pairs)  7.15 us
  transfers between devices with their start and end apart: 15, of which 7 were waited for; matrix products, arithmetic and copies ran while one was open for 15% of the time, Pallas kernels for 0%

profile of v7, /device:TPU:0, one launch (start us, length us, event | category | flops | bytes accessed | tf_op | source)
XLA Modules:
  0.0 167.3 jit_solution(17438559235309189711)
XLA Ops:
  0.0 3.9 %fusion.46 = (bf16[32,224,15]{2,1,0:T(8,128)(2,1)S(1)}, bf16[32,224,15]{2,1,0:T(8,128)(2,1)}) fusion(bf16[32,224,256]{2,1,0:T(8,128)(2,1)} %bitcast.63), kind=kLoop, calls=%fused_computation.62 | loop fusion | bytes 860160 | tf_op jit(solution)/shard_map/slice | solution.py:167
  3.9 2.7 %copy.26 = bf16[32,224,15]{1,0,2:T(8,128)(2,1)} copy(bf16[32,224,15]{2,1,0:T(8,128)(2,1)} %get-tuple-element.24) | data formatting | bytes 430080 | tf_op jit(solution)/shard_map/slice | solution.py:166
  6.6 5.6 %collective-permute-start = (bf16[32,224,15]{1,0,2:T(8,128)(2,1)}, bf16[32,224,15]{1,0,2:T(8,128)(2,1)}, u32[]{:S(2)}, u32[]{:S(2)}) collective-permute-start(bf16[32,224,15]{1,0,2:T(8,128)(2,1)} %copy.26), channel_id=1, source_target_pairs={{0,8},{8,16},{16,24},{1,9},{9,17},{17,25},{2,10},{10,18},{18,26},{... | collective-permute-start | bytes 645128 | tf_op jit(solution)/shard_map/ppermute | solution.py:158
  12.2 1.7 copy.28
  13.9 0.0 copy-start
  13.9 1.5 collective-permute-start.3
  15.4 4.0 %fusion.45 = (bf16[15,224,256]{2,1,0:T(8,128)(2,1)}, bf16[15,224,256]{2,1,0:T(8,128)(2,1)}) fusion(bf16[32,224,256]{2,1,0:T(8,128)(2,1)} %bitcast.64), kind=kLoop, calls=%fused_computation.61 | loop fusion | bytes 6881280 | tf_op jit(solution)/shard_map/slice | solution.py:164
  19.4 1.3 collective-permute-start.6
  20.7 3.1 %collective-permute-start.2 = (bf16[15,224,256]{2,1,0:T(8,128)(2,1)}, bf16[15,224,256]{2,1,0:T(8,128)(2,1)S(1)}, u32[]{:S(2)}, u32[]{:S(2)}) collective-permute-start(bf16[15,224,256]{2,1,0:T(8,128)(2,1)} %get-tuple-element.22), channel_id=1, source_target_pairs={{0,1},{1,2},{2,3},{3,4},{4,5},{5,6},{6,7},{8,9},{9,10},{10,11},{11... | collective-permute-start | bytes 5160968 | tf_op jit(solution)/shard_map/ppermute | solution.py:155
  23.9 0.0 copy-done
  23.9 4.1 %fusion.10 = f32[256,32,224]{0,2,1:T(8,128)} fusion(bf16[256,32,224]{0,2,1:T(8,128)(2,1)S(1)} %copy-done), kind=kOutput, calls=%fused_computation.15 | convolution fusion | flops 939720704 | bytes 11010048 | tf_op jit(solution)/shard_map/qbk,kl->qbl/dot_general | solution.py:193
  28.0 0.7 broadcast_multiply_fusion.count_ref
  28.7 0.0 collective-permute-done
  28.7 1.0 fusion.48
  29.8 1.3 collective-permute-start.5
  31.1 0.0 collective-permute-done.3
  31.1 1.0 fusion.47
  32.1 1.3 collective-permute-start.7
  33.5 0.0 copy-start.1
  33.5 4.4 %collective-permute-start.1 = (bf16[15,224,15]{1,2,0:T(8,128)(2,1)S(1)}, bf16[15,224,15]{1,2,0:T(8,128)(2,1)S(1)}, u32[]{:S(2)}, u32[]{:S(2)}) collective-permute-start(bf16[15,224,15]{1,2,0:T(8,128)(2,1)S(1)} %copy.27), channel_id=1, source_target_pairs={{0,1},{1,2},{2,3},{3,4},{4,5},{5,6},{6,7},{8,9},{9,10},{10,11},{11... | collective-permute-start | bytes 302408 | tf_op jit(solution)/shard_map/ppermute | solution.py:155
  38.0 2.1 %fusion.5 = f32[256,32,224]{0,2,1:T(8,128)S(1)} fusion(bf16[32,224,15]{1,0,2:T(8,128)(2,1)} %collective-permute-done), kind=kOutput, calls=%fused_computation.9 | convolution fusion | flops 55054080 | bytes 7555072 | tf_op jit(solution)/shard_map/qbk,kl->qbl/dot_general | solution.py:193
  40.1 0.0 copy-done.1
  40.1 5.1 %add_bitcast_fusion.middle_ref = f32[32,224,256]{2,1,0:T(8,128)} fusion(f32[256,32,224]{0,2,1:T(8,128)S(1)} %fusion.5, f32[256,32,224]{0,2,1:T(8,128)S(1)} %copy-done.1, bf16[32,224,15]{1,0,2:T(8,128)(2,1)} %collective-permute-done.3, s32[15]{0:T(128)S(1)} %iota_add_fusion), kind=kOutput, calls=%fused_computation.3 | convolution fusion | flops 58724096 | bytes 22235196 | tf_op jit(solution)/shard_map/qbk,kl->qbl/dot_general | solution.py:193
  45.3 0.0 collective-permute-done.5
  45.3 17.0 %collective-permute-start.4 = (bf16[15,224,15]{1,2,0:T(8,128)(2,1)S(1)}, bf16[15,224,15]{1,2,0:T(8,128)(2,1)S(1)}, u32[]{:S(2)}, u32[]{:S(2)}) collective-permute-start(bf16[15,224,15]{1,2,0:T(8,128)(2,1)S(1)} %copy.29), channel_id=1, source_target_pairs={{0,1},{1,2},{2,3},{3,4},{4,5},{5,6},{6,7},{8,9},{9,10},{10,11},{11... | collective-permute-start | bytes 302408 | tf_op jit(solution)/shard_map/ppermute | solution.py:155
  62.3 0.7 fusion.22
  63.0 0.0 collective-permute-done.1
  63.0 0.7 fusion.25
  63.7 0.0 collective-permute-done.6
  63.7 0.6 fusion.8
  64.3 0.0 collective-permute-done.7
  64.3 2.4 %add_bitcast_fusion.1.right_ref = f32[15,224,256]{2,1,0:T(8,128)} fusion(f32[256,15,224]{0,2,1:T(8,128)S(1)} %fusion.22, f32[256,15,224]{0,2,1:T(8,128)S(1)} %fusion.8, bf16[15,224,15]{1,2,0:T(8,128)(2,1)S(1)} %collective-permute-done.7, s32[15]{0:T(128)S(1)} %iota_add_fusion), kind=kOutput, calls=%fused_computation.4 | convolution fusion | flops 27528960 | bytes 10422780 | tf_op jit(solution)/shard_map/qbk,kl->qbl/dot_general | solution.py:193
  66.8 0.0 collective-permute-done.2
  66.8 0.6 fusion.12
  67.4 0.0 collective-permute-done.4
  67.4 2.5 %add_bitcast_fusion.2.left_ref = f32[15,224,256]{2,1,0:T(8,128)} fusion(f32[256,15,224]{0,2,1:T(8,128)S(1)} %fusion.25, f32[256,15,224]{0,2,1:T(8,128)S(1)} %fusion.12, bf16[15,224,15]{1,2,0:T(8,128)(2,1)S(1)} %collective-permute-done.4, s32[15]{0:T(128)S(1)} %iota_add_fusion), kind=kOutput, calls=%fused_computation.5 | convolution fusion | flops 27528960 | bytes 10422780 | tf_op jit(solution)/shard_map/qbk,kl->qbl/dot_general | solution.py:193
  69.9 12.6 %shard_map.17 = (f32[32,224,256]{2,1,0:T(8,128)}, bf16[32,224,256]{2,1,0:T(8,128)(2,1)}) custom-call(f32[15,224,256]{2,1,0:T(8,128)} %add_bitcast_fusion.2.left_ref, f32[32,224,256]{2,1,0:T(8,128)} %add_bitcast_fusion.middle_ref, f32[15,224,256]{2,1,0:T(8,128)} %add_bitcast_fusion.1.right_ref, bf16[32,224,256]{2,1,0:T(8,128)(2,1)} %bitcast.65, ...), custom_call_target="tpu_custom_call" | custom-call | tf_op jit(solution)/shard_map/pallas_call | solution.py:227
  82.4 4.3 %convolution_bitcast_fusion = f32[224,224]{1,0:T(8,128)S(1)} fusion(bf16[32,224,256]{2,1,0:T(8,128)(2,1)} %get-tuple-element.20), kind=kOutput, calls=%fused_computation.6 | convolution fusion | flops 822083584 | bytes 3870720 | tf_op jit(solution)/shard_map/pjl,pkl->jk/dot_general | solution.py:256
  86.7 0.1 fusion.49
  86.8 1.7 %gather_fusion = f32[112]{0:T(128)S(1)} fusion(f32[112,112]{1,0:T(8,128)S(1)} %get-tuple-element.31, s32[112]{0:T(128)S(1)} %or_bitcast_fusion), kind=kCustom, calls=%fused_computation | custom fusion | bytes 1792 | tf_op jit(solution)/shard_map/jit(diagonal)/cond/branch_0_fun/gather | solution.py:64
  88.5 0.1 collective-permute-start.8
  88.6 1.3 collective-permute-done.8
  89.9 3.9 %collective-permute-start.10 = (f32[225,112]{1,0:T(8,128)S(1)}, f32[225,112]{1,0:T(8,128)S(1)}, u32[]{:S(2)}, u32[]{:S(2)}) collective-permute-start(f32[225,112]{1,0:T(8,128)S(1)} %fusion.44), channel_id=1, source_target_pairs={{0,4},{1,5},{2,6},{3,7},{4,0},{5,1},{6,2},{7,3},{8,12},{9,13},{10,... | collective-permute-start | bytes 302408 | tf_op jit(solution)/shard_map/ppermute | solution.py:54
  93.9 0.8 collective-permute-start.11
  94.7 1.2 collective-permute-start.9
  95.9 1.5 collective-permute-done.10
  97.4 2.3 %collective-permute-done.11 = f32[225,112]{1,0:T(8,128)S(1)} collective-permute-done((f32[225,112]{1,0:T(8,128)S(1)}, f32[225,112]{1,0:T(8,128)S(1)}, u32[]{:S(2)}, u32[]{:S(2)}) %collective-permute-start.11) | collective-permute-done | bytes 100832 | tf_op jit(solution)/shard_map/ppermute | solution.py:54
  99.7 1.5 collective-permute-done.9
  101.2 2.9 %collective-permute-start.12 = (f32[225,112]{1,0:T(8,128)S(1)}, f32[225,112]{1,0:T(8,128)S(1)}, u32[]{:S(2)}, u32[]{:S(2)}) collective-permute-start(f32[225,112]{1,0:T(8,128)S(1)} %add_add_fusion.1), channel_id=1, source_target_pairs={{0,8},{8,16},{16,24},{24,0},{1,9},{9,17},{17,25},{25,1},{2,10},{10... | collective-permute-start | bytes 302408 | tf_op jit(solution)/shard_map/ppermute | solution.py:54
  104.1 2.6 %collective-permute-start.13 = (f32[225,112]{1,0:T(8,128)S(1)}, f32[225,112]{1,0:T(8,128)S(1)}, u32[]{:S(2)}, u32[]{:S(2)}) collective-permute-start(f32[225,112]{1,0:T(8,128)S(1)} %add_add_fusion.1), channel_id=1, source_target_pairs={{0,16},{8,24},{16,0},{24,8},{1,17},{9,25},{17,1},{25,9},{2,18},{10... | collective-permute-start | bytes 302408 | tf_op jit(solution)/shard_map/ppermute | solution.py:54
  106.7 0.6 collective-permute-start.14
  107.4 3.0 %collective-permute-done.12 = f32[225,112]{1,0:T(8,128)S(1)} collective-permute-done((f32[225,112]{1,0:T(8,128)S(1)}, f32[225,112]{1,0:T(8,128)S(1)}, u32[]{:S(2)}, u32[]{:S(2)}) %collective-permute-start.12) | collective-permute-done | bytes 100832 | tf_op jit(solution)/shard_map/ppermute | solution.py:54
  110.4 3.6 %collective-permute-done.13 = f32[225,112]{1,0:T(8,128)S(1)} collective-permute-done((f32[225,112]{1,0:T(8,128)S(1)}, f32[225,112]{1,0:T(8,128)S(1)}, u32[]{:S(2)}, u32[]{:S(2)}) %collective-permute-start.13) | collective-permute-done | bytes 100832 | tf_op jit(solution)/shard_map/ppermute | solution.py:54
  114.1 0.2 collective-permute-done.14
  114.3 0.1 copy.37
  114.4 0.1 copy.38
  114.5 0.7 select_reduce_fusion
  115.9 0.1 select_add_fusion
  116.0 2.0 %scatter.4.a_ref = f32[256,256]{1,0:T(8,128)S(1)} dynamic-update-slice(f32[256,256]{1,0:T(8,128)S(1)} %fusion.14, f32[224,224]{1,0:T(8,128)S(1)} %select_add_fusion, s32[]{:T(128)} %constant.71.clone.1, s32[]{:T(128)} %constant.71.clone.1) | dynamic-update-slice | bytes 401412 | tf_op jit(solution)/shard_map/scatter | solution.py:109
  118.1 0.0 copy-start.2
  118.1 0.7 copy-done.2
  118.7 37.7 %shard_map.18 = f32[256,256]{1,0:T(8,128)} custom-call(f32[256,256]{1,0:T(8,128)} %copy-done.2), custom_call_target="tpu_custom_call" | custom-call | tf_op jit(solution)/shard_map/pallas_call | solution.py:110
  156.5 10.2 %fusion = f32[32,256]{1,0:T(8,128)S(1)} fusion(f32[32,224,256]{2,1,0:T(8,128)} %get-tuple-element.19, f32[256,256]{1,0:T(8,128)} %shard_map.18), kind=kOutput, calls=%fused_computation.2 | convolution fusion | flops 4936213504 | bytes 14942208 | tf_op jit(solution)/shard_map/pbl,bj->pjl/dot_general | solution.py:266
  166.7 0.6 multiply_bitcast_fusion
  (16 shorter events, 0.4 us)
Async XLA Ops:
  6.6 22.1 %collective-permute-start = (bf16[32,224,15]{1,0,2:T(8,128)(2,1)}, bf16[32,224,15]{1,0,2:T(8,128)(2,1)}, u32[]{:S(2)}, u32[]{:S(2)}) collective-permute-start(bf16[32,224,15]{1,0,2:T(8,128)(2,1)} %copy.26), channel_id=1, source_target_pairs={{0,8},{8,16},{16,24},{1,9},{9,17},{17,25},{2,10},{10,18},{18,26},{... | collective-permute-start | bytes 645128 | tf_op jit(solution)/shard_map/ppermute | solution.py:158
  13.9 10.0 %copy-start = (bf16[256,32,224]{0,2,1:T(8,128)(2,1)S(1)}, bf16[256,32,224]{0,2,1:T(8,128)(2,1)}, u32[]{:S(2)}) copy-start(bf16[256,32,224]{0,2,1:T(8,128)(2,1)} %param.3) | copy-start | bytes 11010052
  13.9 17.2 %collective-permute-start.3 = (bf16[32,224,15]{1,0,2:T(8,128)(2,1)}, bf16[32,224,15]{1,0,2:T(8,128)(2,1)}, u32[]{:S(2)}, u32[]{:S(2)}) collective-permute-start(bf16[32,224,15]{1,0,2:T(8,128)(2,1)} %copy.28), channel_id=1, source_target_pairs={{8,0},{16,8},{24,16},{9,1},{17,9},{25,17},{10,2},{18,10},{26,18},{... | collective-permute-start | bytes 645128 | tf_op jit(solution)/shard_map/ppermute | solution.py:158
  19.4 44.2 %collective-permute-start.6 = (bf16[15,224,256]{2,1,0:T(8,128)(2,1)}, bf16[15,224,256]{2,1,0:T(8,128)(2,1)S(1)}, u32[]{:S(2)}, u32[]{:S(2)}) collective-permute-start(bf16[15,224,256]{2,1,0:T(8,128)(2,1)} %get-tuple-element.21), channel_id=1, source_target_pairs={{1,0},{2,1},{3,2},{4,3},{5,4},{6,5},{7,6},{9,8},{10,9},{11,10},{12... | collective-permute-start | bytes 5160968 | tf_op jit(solution)/shard_map/ppermute | solution.py:155
  20.7 46.0 %collective-permute-start.2 = (bf16[15,224,256]{2,1,0:T(8,128)(2,1)}, bf16[15,224,256]{2,1,0:T(8,128)(2,1)S(1)}, u32[]{:S(2)}, u32[]{:S(2)}) collective-permute-start(bf16[15,224,256]{2,1,0:T(8,128)(2,1)} %get-tuple-element.22), channel_id=1, source_target_pairs={{0,1},{1,2},{2,3},{3,4},{4,5},{5,6},{6,7},{8,9},{9,10},{10,11},{11... | collective-permute-start | bytes 5160968 | tf_op jit(solution)/shard_map/ppermute | solution.py:155
  29.8 15.5 %collective-permute-start.5 = (bf16[15,224,15]{1,2,0:T(8,128)(2,1)S(1)}, bf16[15,224,15]{1,2,0:T(8,128)(2,1)S(1)}, u32[]{:S(2)}, u32[]{:S(2)}) collective-permute-start(bf16[15,224,15]{1,2,0:T(8,128)(2,1)S(1)} %copy.32), channel_id=1, source_target_pairs={{1,0},{2,1},{3,2},{4,3},{5,4},{6,5},{7,6},{9,8},{10,9},{11,10},{12... | collective-permute-start | bytes 302408 | tf_op jit(solution)/shard_map/ppermute | solution.py:155
  32.1 32.2 %collective-permute-start.7 = (bf16[15,224,15]{1,2,0:T(8,128)(2,1)S(1)}, bf16[15,224,15]{1,2,0:T(8,128)(2,1)S(1)}, u32[]{:S(2)}, u32[]{:S(2)}) collective-permute-start(bf16[15,224,15]{1,2,0:T(8,128)(2,1)S(1)} %copy.33), channel_id=1, source_target_pairs={{1,0},{2,1},{3,2},{4,3},{5,4},{6,5},{7,6},{9,8},{10,9},{11,10},{12... | collective-permute-start | bytes 302408 | tf_op jit(solution)/shard_map/ppermute | solution.py:155
  33.5 6.6 %copy-start.1 = (f32[256,32,224]{0,2,1:T(8,128)S(1)}, f32[256,32,224]{0,2,1:T(8,128)}, u32[]{:S(2)}) copy-start(f32[256,32,224]{0,2,1:T(8,128)} %fusion.10) | copy-start | bytes 22020100
  33.5 29.5 %collective-permute-start.1 = (bf16[15,224,15]{1,2,0:T(8,128)(2,1)S(1)}, bf16[15,224,15]{1,2,0:T(8,128)(2,1)S(1)}, u32[]{:S(2)}, u32[]{:S(2)}) collective-permute-start(bf16[15,224,15]{1,2,0:T(8,128)(2,1)S(1)} %copy.27), channel_id=1, source_target_pairs={{0,1},{1,2},{2,3},{3,4},{4,5},{5,6},{6,7},{8,9},{9,10},{10,11},{11... | collective-permute-start | bytes 302408 | tf_op jit(solution)/shard_map/ppermute | solution.py:155
  45.3 22.1 %collective-permute-start.4 = (bf16[15,224,15]{1,2,0:T(8,128)(2,1)S(1)}, bf16[15,224,15]{1,2,0:T(8,128)(2,1)S(1)}, u32[]{:S(2)}, u32[]{:S(2)}) collective-permute-start(bf16[15,224,15]{1,2,0:T(8,128)(2,1)S(1)} %copy.29), channel_id=1, source_target_pairs={{0,1},{1,2},{2,3},{3,4},{4,5},{5,6},{6,7},{8,9},{9,10},{10,11},{11... | collective-permute-start | bytes 302408 | tf_op jit(solution)/shard_map/ppermute | solution.py:155
  88.5 1.4 collective-permute-start.8
  89.9 7.5 %collective-permute-start.10 = (f32[225,112]{1,0:T(8,128)S(1)}, f32[225,112]{1,0:T(8,128)S(1)}, u32[]{:S(2)}, u32[]{:S(2)}) collective-permute-start(f32[225,112]{1,0:T(8,128)S(1)} %fusion.44), channel_id=1, source_target_pairs={{0,4},{1,5},{2,6},{3,7},{4,0},{5,1},{6,2},{7,3},{8,12},{9,13},{10,... | collective-permute-start | bytes 302408 | tf_op jit(solution)/shard_map/ppermute | solution.py:54
  93.9 5.8 %collective-permute-start.11 = (f32[225,112]{1,0:T(8,128)S(1)}, f32[225,112]{1,0:T(8,128)S(1)}, u32[]{:S(2)}, u32[]{:S(2)}) collective-permute-start(f32[225,112]{1,0:T(8,128)S(1)} %fusion.44), channel_id=1, source_target_pairs={{0,6},{1,7},{2,0},{3,1},{4,2},{5,3},{6,4},{7,5},{8,14},{9,15},{10,... | collective-permute-start | bytes 302408 | tf_op jit(solution)/shard_map/ppermute | solution.py:54
  94.7 6.5 %collective-permute-start.9 = (f32[225,112]{1,0:T(8,128)S(1)}, f32[225,112]{1,0:T(8,128)S(1)}, u32[]{:S(2)}, u32[]{:S(2)}) collective-permute-start(f32[225,112]{1,0:T(8,128)S(1)} %fusion.44), channel_id=1, source_target_pairs={{0,2},{1,3},{2,4},{3,5},{4,6},{5,7},{6,0},{7,1},{8,10},{9,11},{10,... | collective-permute-start | bytes 302408 | tf_op jit(solution)/shard_map/ppermute | solution.py:54
  101.2 9.2 %collective-permute-start.12 = (f32[225,112]{1,0:T(8,128)S(1)}, f32[225,112]{1,0:T(8,128)S(1)}, u32[]{:S(2)}, u32[]{:S(2)}) collective-permute-start(f32[225,112]{1,0:T(8,128)S(1)} %add_add_fusion.1), channel_id=1, source_target_pairs={{0,8},{8,16},{16,24},{24,0},{1,9},{9,17},{17,25},{25,1},{2,10},{10... | collective-permute-start | bytes 302408 | tf_op jit(solution)/shard_map/ppermute | solution.py:54
  104.1 10.0 %collective-permute-start.13 = (f32[225,112]{1,0:T(8,128)S(1)}, f32[225,112]{1,0:T(8,128)S(1)}, u32[]{:S(2)}, u32[]{:S(2)}) collective-permute-start(f32[225,112]{1,0:T(8,128)S(1)} %add_add_fusion.1), channel_id=1, source_target_pairs={{0,16},{8,24},{16,0},{24,8},{1,17},{9,25},{17,1},{25,9},{2,18},{10... | collective-permute-start | bytes 302408 | tf_op jit(solution)/shard_map/ppermute | solution.py:54
  106.7 7.5 %collective-permute-start.14 = (f32[225,112]{1,0:T(8,128)S(1)}, f32[225,112]{1,0:T(8,128)S(1)}, u32[]{:S(2)}, u32[]{:S(2)}) collective-permute-start(f32[225,112]{1,0:T(8,128)S(1)} %add_add_fusion.1), channel_id=1, source_target_pairs={{0,24},{8,0},{16,8},{24,16},{1,25},{9,1},{17,9},{25,17},{2,26},{10... | collective-permute-start | bytes 302408 | tf_op jit(solution)/shard_map/ppermute | solution.py:54
  118.1 0.7 copy-start.2

commit v8 on v7

--- a/solution.py
+++ b/solution.py
@@ -163,27 +163,28 @@
         "left": fetch(planes[last], 0, -1),
         "right": fetch(planes[first], 0, 1),
     }
-    top = fetch(planes[:, :, last], -1, 0)
-    bottom = fetch(planes[:, :, first], 1, 0)
+    tile = min(128, planes.shape[2])
+    top = fetch(planes[:, :, -tile:], -1, 0)
+    bottom = fetch(planes[:, :, :tile], 1, 0)
     tops = {
-        "left": fetch(top[last], 0, -1),
+        "left": fetch(top[last][:, :, last], 0, -1),
         "middle": top,
-        "right": fetch(top[first], 0, 1),
+        "right": fetch(top[first][:, :, last], 0, 1),
     }
     bottoms = {
-        "left": fetch(bottom[last], 0, -1),
+        "left": fetch(bottom[last][:, :, first], 0, -1),
         "middle": bottom,
-        "right": fetch(bottom[first], 0, 1),
+        "right": fetch(bottom[first][:, :, first], 0, 1),
     }
     return sides, tops, bottoms
 
 
-def line_weights(lines):
+def line_weights(lines, rows):
     target = jnp.arange(lines)[None, :]
     middle = jnp.abs(jnp.arange(lines)[:, None] - target) <= HALF
-    side = jnp.arange(HALF)[:, None]
-    top = target <= side
-    bottom = target >= lines - HALF + side
+    side = jnp.arange(rows)[:, None]
+    top = side >= target + rows - HALF
+    bottom = side <= target + HALF - lines
     return [w.astype(jnp.bfloat16) for w in (top, middle, bottom)]
 
 
@@ -245,10 +246,11 @@
     highest = lax.Precision.HIGHEST
     planes = jnp.transpose(cube, (1, 2, 0))
     sides, tops, bottoms = halos(planes)
-    weights = line_weights(lines_dev)
-    middle = sum_lines(tops["middle"], planes, bottoms["middle"], weights)
-    left = sum_lines(tops["left"], sides["left"], bottoms["left"], weights)
-    right = sum_lines(tops["right"], sides["right"], bottoms["right"], weights)
+    wide = line_weights(lines_dev, tops["middle"].shape[2])
+    narrow = line_weights(lines_dev, HALF)
+    middle = sum_lines(tops["middle"], planes, bottoms["middle"], wide)
+    left = sum_lines(tops["left"], sides["left"], bottoms["left"], narrow)
+    right = sum_lines(tops["right"], sides["right"], bottoms["right"], narrow)
     line_count = window_count(lax.axis_index("track") * lines_dev, lines_dev, total_lines)
     pixel_count = window_count(lax.axis_index("cross") * pix_dev, pix_dev, total_pix)
     count = pixel_count[:, None, None] * line_count[None, None, :]

time: 168 us -> 192 us (1.14)
  waiting for transfers between devices: 13.5 us -> 36.7 us
  starting transfers between devices: 47.8 us -> 31.9 us
  matrix products: 33.3 us -> 43 us
  local copies, waits for them, and re-layouts: 19 us -> 25.6 us
    ppermute x2, waiting for transfers between devices: 0.01 us -> 23.9 us  [fetch(): return lax.ppermute(piece, 'track', pairs)]
    ppermute x6, starting transfers between devices: 28.5 us -> 15.4 us  [fetch(): return lax.ppermute(piece, 'cross', pairs)]
    dot_general x9, matrix products: 18.8 us -> 28.5 us  [sum_lines(): jnp.einsum('qbk,kl->qbl', values, w, preferred_element_type=jnp.float32)]
    slice x9 -> x7, local copies, waits for them, and re-layouts: 10.4 us -> 14.3 us  [the longest x2 5.06 us: halos(): bottom[first][:, :, first]]
    unnamed x6 -> x14, local copies, waits for them, and re-layouts: 0.69 us -> 3.29 us
    ppermute x6, starting transfers between devices: 12.1 us -> 10.1 us  [ring_sum(): total = total + lax.ppermute(x, axis, pairs)]
  transfers between devices with their start and end apart: 15 -> 15, of which waited for: 7 -> 8; matrix products, arithmetic and copies ran while one was open for 15% -> 22% of each run, Pallas kernels for 0% -> 0%
where the time goes in v8:
time: 192 us; the launch traced here: 191 us
  Pallas kernels  50.4 us (26%)
  matrix products  43 us (22%)
  waiting for transfers between devices  36.7 us (19%)
  starting transfers between devices  31.9 us (17%)
  local copies, waits for them, and re-layouts  25.6 us (13%)
  other arithmetic  2.47 us (1%)
    pallas_call x1, Pallas kernels, spd_inverse(): pl.pallas_call(functools.partial(sweep_kernel, n), out_shape=jax.ShapeDty...  37.7 us
    dot_general x9, matrix products, sum_lines(): jnp.einsum('qbk,kl->qbl', values, w, preferred_element_type=jnp.float32)  28.5 us
    ppermute x2, waiting for transfers between devices, fetch(): return lax.ppermute(piece, 'track', pairs)  23.9 us
    ppermute x6, starting transfers between devices, fetch(): return lax.ppermute(piece, 'cross', pairs)  15.4 us
    pallas_call x1, Pallas kernels, residuals(): pl.pallas_call(residual_kernel, grid=(bands // block,), in_specs=[spec(le...  12.6 us
    ppermute x6, waiting for transfers between devices, ring_sum(): total = total + lax.ppermute(x, axis, pairs)  11.5 us
    dot_general x1, matrix products, shards(): jnp.einsum('pbl,bj->pjl', residual, inverse, precision=highest, preferred...  10.2 us
    ppermute x6, starting transfers between devices, ring_sum(): total = total + lax.ppermute(x, axis, pairs)  10.1 us
  transfers between devices with their start and end apart: 15, of which 8 were waited for; matrix products, arithmetic and copies ran while one was open for 22% of the time, Pallas kernels for 0%

profile of v8, /device:TPU:0, one launch (start us, length us, event | category | flops | bytes accessed | tf_op | source)
XLA Modules:
  0.0 191.1 jit_solution(9855144765150010530)
XLA Ops:
  0.0 4.1 %fusion.46 = (bf16[15,224,256]{2,1,0:T(8,128)(2,1)}, bf16[15,224,256]{2,1,0:T(8,128)(2,1)}) fusion(bf16[32,224,256]{2,1,0:T(8,128)(2,1)} %bitcast.71), kind=kLoop, calls=%fused_computation.65 | loop fusion | bytes 6881280 | tf_op jit(solution)/shard_map/slice | solution.py:164
  4.2 1.3 collective-permute-start.6
  5.4 4.3 %collective-permute-start.2 = (bf16[15,224,256]{2,1,0:T(8,128)(2,1)}, bf16[15,224,256]{2,1,0:T(8,128)(2,1)}, u32[]{:S(2)}, u32[]{:S(2)}) collective-permute-start(bf16[15,224,256]{2,1,0:T(8,128)(2,1)} %get-tuple-element.22), channel_id=1, source_target_pairs={{0,1},{1,2},{2,3},{3,4},{4,5},{5,6},{6,7},{8,9},{9,10},{10,11},{11... | collective-permute-start | bytes 5160968 | tf_op jit(solution)/shard_map/ppermute | solution.py:155
  9.7 2.4 %fusion.47 = (bf16[32,224,128]{2,1,0:T(8,128)(2,1)}, bf16[32,224,128]{2,1,0:T(8,128)(2,1)}) fusion(bf16[32,224,256]{2,1,0:T(8,128)(2,1)S(1)} %bitcast.73), kind=kLoop, calls=%fused_computation.66 | loop fusion | bytes 7340032 | tf_op jit(solution)/shard_map/slice | solution.py:168
  12.1 5.0 %collective-permute-start = (bf16[32,224,128]{2,1,0:T(8,128)(2,1)}, bf16[32,224,128]{2,1,0:T(8,128)(2,1)S(1)}, u32[]{:S(2)}, u32[]{:S(2)}) collective-permute-start(bf16[32,224,128]{2,1,0:T(8,128)(2,1)} %get-tuple-element.24), channel_id=1, source_target_pairs={{0,8},{8,16},{16,24},{1,9},{9,17},{17,25},{2,10},{10,18},{18,26},{... | collective-permute-start | bytes 5505032 | tf_op jit(solution)/shard_map/ppermute | solution.py:158
  17.2 1.3 collective-permute-start.3
  18.5 0.7 broadcast_multiply_fusion.count_ref
  19.3 6.1 %fusion.4 = f32[256,32,224]{0,2,1:T(8,128)} fusion(bf16[256,32,224]{0,2,1:T(8,128)(2,1)} %param.3), kind=kOutput, calls=%fused_computation.11 | convolution fusion | flops 939720704 | bytes 11010048 | tf_op jit(solution)/shard_map/qbk,kl->qbl/dot_general | solution.py:194
  25.4 0.0 collective-permute-done.6
  25.4 3.9 %fusion.2 = f32[256,15,224]{0,2,1:T(8,128)} fusion(bf16[15,224,256]{2,1,0:T(8,128)(2,1)} %collective-permute-done.6), kind=kOutput, calls=%fused_computation.10 | convolution fusion | flops 440598528 | bytes 5160960 | tf_op jit(solution)/shard_map/qbk,kl->qbl/dot_general | solution.py:194
  29.3 0.0 collective-permute-done.2
  29.3 3.9 %fusion.6 = f32[256,15,224]{0,2,1:T(8,128)} fusion(bf16[15,224,256]{2,1,0:T(8,128)(2,1)} %collective-permute-done.2), kind=kOutput, calls=%fused_computation.12 | convolution fusion | flops 440598528 | bytes 5160960 | tf_op jit(solution)/shard_map/qbk,kl->qbl/dot_general | solution.py:194
  33.2 23.5 %collective-permute-done = bf16[32,224,128]{2,1,0:T(8,128)(2,1)S(1)} collective-permute-done((bf16[32,224,128]{2,1,0:T(8,128)(2,1)}, bf16[32,224,128]{2,1,0:T(8,128)(2,1)S(1)}, u32[]{:S(2)}, u32[]{:S(2)}) %collective-permute-start) | collective-permute-done | bytes 1835040 | tf_op jit(solution)/shard_map/ppermute | solution.py:158
  56.7 1.5 fusion.49
  58.2 1.0 copy.24
  59.2 1.3 collective-permute-start.5
  60.5 0.4 collective-permute-done.3
  60.9 2.9 %fusion.48 = (bf16[15,224,15]{2,1,0:T(8,128)(2,1)}, bf16[15,224,15]{2,1,0:T(8,128)(2,1)}) fusion(bf16[32,224,128]{2,1,0:T(8,128)(2,1)} %collective-permute-done.3), kind=kLoop, calls=%fused_computation.67 | loop fusion | bytes 403200 | tf_op jit(solution)/shard_map/slice | solution.py:177
  63.8 2.2 %copy.25 = bf16[15,224,15]{1,2,0:T(8,128)(2,1)} copy(bf16[15,224,15]{2,1,0:T(8,128)(2,1)} %get-tuple-element.25) | data formatting | bytes 201600 | tf_op jit(solution)/shard_map/slice | solution.py:177
  66.0 1.3 collective-permute-start.7
  67.3 2.2 %copy.22 = bf16[15,224,15]{1,2,0:T(8,128)(2,1)} copy(bf16[15,224,15]{2,1,0:T(8,128)(2,1)} %get-tuple-element.28) | data formatting | bytes 201600 | tf_op jit(solution)/shard_map/slice | solution.py:170
  69.4 3.2 %collective-permute-start.1 = (bf16[15,224,15]{1,2,0:T(8,128)(2,1)}, bf16[15,224,15]{1,2,0:T(8,128)(2,1)S(1)}, u32[]{:S(2)}, u32[]{:S(2)}) collective-permute-start(bf16[15,224,15]{1,2,0:T(8,128)(2,1)} %copy.22), channel_id=1, source_target_pairs={{0,1},{1,2},{2,3},{3,4},{4,5},{5,6},{6,7},{8,9},{9,10},{10,11},{11... | collective-permute-start | bytes 302408 | tf_op jit(solution)/shard_map/ppermute | solution.py:155
  72.7 2.2 %copy.23 = bf16[15,224,15]{1,2,0:T(8,128)(2,1)} copy(bf16[15,224,15]{2,1,0:T(8,128)(2,1)} %get-tuple-element.26) | data formatting | bytes 201600 | tf_op jit(solution)/shard_map/slice | solution.py:175
  74.9 4.1 %collective-permute-start.4 = (bf16[15,224,15]{1,2,0:T(8,128)(2,1)}, bf16[15,224,15]{1,2,0:T(8,128)(2,1)S(1)}, u32[]{:S(2)}, u32[]{:S(2)}) collective-permute-start(bf16[15,224,15]{1,2,0:T(8,128)(2,1)} %copy.23), channel_id=1, source_target_pairs={{0,1},{1,2},{2,3},{3,4},{4,5},{5,6},{6,7},{8,9},{9,10},{10,11},{11... | collective-permute-start | bytes 302408 | tf_op jit(solution)/shard_map/ppermute | solution.py:155
  78.9 2.6 %fusion.15 = f32[256,32,224]{0,2,1:T(8,128)S(1)} fusion(bf16[32,224,128]{2,1,0:T(8,128)(2,1)} %copy-done.3, s32[256]{0:T(256)S(1)} %iota_add_fusion), kind=kOutput, calls=%fused_computation.26 | convolution fusion | flops 469794816 | bytes 9176064 | tf_op jit(solution)/shard_map/qbk,kl->qbl/dot_general | solution.py:194
  81.5 0.0 slice-done
  81.6 5.7 %add_bitcast_fusion.middle_ref = f32[32,224,256]{2,1,0:T(8,128)} fusion(f32[256,32,224]{0,2,1:T(8,128)S(1)} %fusion.15, f32[256,32,224]{0,2,1:T(8,128)S(1)} %bitcast.75, bf16[32,224,128]{2,1,0:T(8,128)(2,1)} %collective-permute-done.3, s32[256]{0:T(256)S(1)} %iota_add_fusion.1), kind=kOutput, calls=%fused_computation.3 | convolution fusion | flops 473464832 | bytes 23856128 | tf_op jit(solution)/shard_map/qbk,kl->qbl/dot_general | solution.py:194
  87.3 0.0 collective-permute-done.5
  87.3 0.7 fusion.26
  88.0 0.0 collective-permute-done.7
  88.0 1.3 copy-done.2
  89.3 2.4 %add_bitcast_fusion.1.right_ref = f32[15,224,256]{2,1,0:T(8,128)} fusion(f32[256,15,224]{0,2,1:T(8,128)S(1)} %fusion.26, f32[256,15,224]{0,2,1:T(8,128)S(1)} %copy-done.2, bf16[15,224,15]{1,2,0:T(8,128)(2,1)S(1)} %collective-permute-done.7, s32[256]{0:T(256)S(1)} %iota_add_fusion.1), kind=kOutput, calls=%fused_computation.4 | convolution fusion | flops 27528960 | bytes 10423744 | tf_op jit(solution)/shard_map/qbk,kl->qbl/dot_general | solution.py:194
  91.7 0.0 collective-permute-done.1
  91.7 0.7 fusion.28
  92.4 0.0 collective-permute-done.4
  92.4 1.3 copy-done.1
  93.7 2.5 %add_bitcast_fusion.2.left_ref = f32[15,224,256]{2,1,0:T(8,128)} fusion(f32[256,15,224]{0,2,1:T(8,128)S(1)} %fusion.28, f32[256,15,224]{0,2,1:T(8,128)S(1)} %copy-done.1, bf16[15,224,15]{1,2,0:T(8,128)(2,1)S(1)} %collective-permute-done.4, s32[256]{0:T(256)S(1)} %iota_add_fusion.1), kind=kOutput, calls=%fused_computation.5 | convolution fusion | flops 27528960 | bytes 10423744 | tf_op jit(solution)/shard_map/qbk,kl->qbl/dot_general | solution.py:194
  96.2 12.6 %shard_map.17 = (f32[32,224,256]{2,1,0:T(8,128)}, bf16[32,224,256]{2,1,0:T(8,128)(2,1)}) custom-call(f32[15,224,256]{2,1,0:T(8,128)} %add_bitcast_fusion.2.left_ref, f32[32,224,256]{2,1,0:T(8,128)} %add_bitcast_fusion.middle_ref, f32[15,224,256]{2,1,0:T(8,128)} %add_bitcast_fusion.1.right_ref, bf16[32,224,256]{2,1,0:T(8,128)(2,1)} %bitcast.72, ...), custom_call_target="tpu_custom_call" | custom-call | tf_op jit(solution)/shard_map/pallas_call | solution.py:228
  108.8 4.3 %convolution_bitcast_fusion = f32[224,224]{1,0:T(8,128)S(1)} fusion(bf16[32,224,256]{2,1,0:T(8,128)(2,1)} %get-tuple-element.20), kind=kOutput, calls=%fused_computation.6 | convolution fusion | flops 822083584 | bytes 3870720 | tf_op jit(solution)/shard_map/pjl,pkl->jk/dot_general | solution.py:258
  113.1 0.1 fusion.50
  113.2 1.7 gather_fusion
  114.9 0.1 collective-permute-start.8
  115.0 1.3 collective-permute-done.8
  116.3 1.6 collective-permute-start.10
  117.9 2.0 %collective-permute-start.11 = (f32[225,112]{1,0:T(8,128)S(1)}, f32[225,112]{1,0:T(8,128)S(1)}, u32[]{:S(2)}, u32[]{:S(2)}) collective-permute-start(f32[225,112]{1,0:T(8,128)S(1)} %fusion.45), channel_id=1, source_target_pairs={{0,6},{1,7},{2,0},{3,1},{4,2},{5,3},{6,4},{7,5},{8,14},{9,15},{10,... | collective-permute-start | bytes 302408 | tf_op jit(solution)/shard_map/ppermute | solution.py:54
  119.9 0.1 collective-permute-start.9
  119.9 1.7 collective-permute-done.10
  121.7 2.2 %collective-permute-done.11 = f32[225,112]{1,0:T(8,128)S(1)} collective-permute-done((f32[225,112]{1,0:T(8,128)S(1)}, f32[225,112]{1,0:T(8,128)S(1)}, u32[]{:S(2)}, u32[]{:S(2)}) %collective-permute-start.11) | collective-permute-done | bytes 100832 | tf_op jit(solution)/shard_map/ppermute | solution.py:54
  123.9 2.0 %collective-permute-done.9 = f32[225,112]{1,0:T(8,128)S(1)} collective-permute-done((f32[225,112]{1,0:T(8,128)S(1)}, f32[225,112]{1,0:T(8,128)S(1)}, u32[]{:S(2)}, u32[]{:S(2)}) %collective-permute-start.9) | collective-permute-done | bytes 100832 | tf_op jit(solution)/shard_map/ppermute | solution.py:54
  125.9 2.5 %collective-permute-start.12 = (f32[225,112]{1,0:T(8,128)S(1)}, f32[225,112]{1,0:T(8,128)S(1)}, u32[]{:S(2)}, u32[]{:S(2)}) collective-permute-start(f32[225,112]{1,0:T(8,128)S(1)} %add_add_fusion.1), channel_id=1, source_target_pairs={{0,8},{8,16},{16,24},{24,0},{1,9},{9,17},{17,25},{25,1},{2,10},{10... | collective-permute-start | bytes 302408 | tf_op jit(solution)/shard_map/ppermute | solution.py:54
  128.4 2.2 %collective-permute-start.13 = (f32[225,112]{1,0:T(8,128)S(1)}, f32[225,112]{1,0:T(8,128)S(1)}, u32[]{:S(2)}, u32[]{:S(2)}) collective-permute-start(f32[225,112]{1,0:T(8,128)S(1)} %add_add_fusion.1), channel_id=1, source_target_pairs={{0,16},{8,24},{16,0},{24,8},{1,17},{9,25},{17,1},{25,9},{2,18},{10... | collective-permute-start | bytes 302408 | tf_op jit(solution)/shard_map/ppermute | solution.py:54
  130.6 1.8 collective-permute-start.14
  132.4 1.6 collective-permute-done.12
  134.0 4.0 %collective-permute-done.13 = f32[225,112]{1,0:T(8,128)S(1)} collective-permute-done((f32[225,112]{1,0:T(8,128)S(1)}, f32[225,112]{1,0:T(8,128)S(1)}, u32[]{:S(2)}, u32[]{:S(2)}) %collective-permute-start.13) | collective-permute-done | bytes 100832 | tf_op jit(solution)/shard_map/ppermute | solution.py:54
  138.0 0.0 collective-permute-done.14
  138.0 0.1 copy.29
  138.2 0.1 copy.30
  138.2 0.7 select_reduce_fusion
  139.6 0.1 select_add_fusion
  139.7 2.0 %scatter.4.a_ref = f32[256,256]{1,0:T(8,128)S(1)} dynamic-update-slice(f32[256,256]{1,0:T(8,128)S(1)} %fusion.8, f32[224,224]{1,0:T(8,128)S(1)} %select_add_fusion, s32[]{:T(128)} %constant.80.clone.1, s32[]{:T(128)} %constant.80.clone.1) | dynamic-update-slice | bytes 401412 | tf_op jit(solution)/shard_map/scatter | solution.py:109
  141.8 0.7 copy-done.4
  142.5 37.7 %shard_map.18 = f32[256,256]{1,0:T(8,128)} custom-call(f32[256,256]{1,0:T(8,128)} %copy-done.4), custom_call_target="tpu_custom_call" | custom-call | tf_op jit(solution)/shard_map/pallas_call | solution.py:110
  180.2 10.2 %fusion = f32[32,256]{1,0:T(8,128)S(1)} fusion(f32[32,224,256]{2,1,0:T(8,128)} %get-tuple-element.19, f32[256,256]{1,0:T(8,128)} %shard_map.18), kind=kOutput, calls=%fused_computation.2 | convolution fusion | flops 4936213504 | bytes 14942208 | tf_op jit(solution)/shard_map/pbl,bj->pjl/dot_general | solution.py:268
  190.5 0.6 multiply_bitcast_fusion
  (24 shorter events, 0.2 us)
Async XLA Ops:
  0.0 9.7 %copy-start = (bf16[256,32,224]{0,2,1:T(8,128)(2,1)S(1)}, bf16[256,32,224]{0,2,1:T(8,128)(2,1)}, u32[]{:S(2)}) copy-start(bf16[256,32,224]{0,2,1:T(8,128)(2,1)} %param.3) | copy-start | bytes 11010052
  4.2 21.2 %collective-permute-start.6 = (bf16[15,224,256]{2,1,0:T(8,128)(2,1)}, bf16[15,224,256]{2,1,0:T(8,128)(2,1)}, u32[]{:S(2)}, u32[]{:S(2)}) collective-permute-start(bf16[15,224,256]{2,1,0:T(8,128)(2,1)} %get-tuple-element.21), channel_id=1, source_target_pairs={{1,0},{2,1},{3,2},{4,3},{5,4},{6,5},{7,6},{9,8},{10,9},{11,10},{12... | collective-permute-start | bytes 5160968 | tf_op jit(solution)/shard_map/ppermute | solution.py:155
  5.4 23.8 %collective-permute-start.2 = (bf16[15,224,256]{2,1,0:T(8,128)(2,1)}, bf16[15,224,256]{2,1,0:T(8,128)(2,1)}, u32[]{:S(2)}, u32[]{:S(2)}) collective-permute-start(bf16[15,224,256]{2,1,0:T(8,128)(2,1)} %get-tuple-element.22), channel_id=1, source_target_pairs={{0,1},{1,2},{2,3},{3,4},{4,5},{5,6},{6,7},{8,9},{9,10},{10,11},{11... | collective-permute-start | bytes 5160968 | tf_op jit(solution)/shard_map/ppermute | solution.py:155
  12.1 44.6 %collective-permute-start = (bf16[32,224,128]{2,1,0:T(8,128)(2,1)}, bf16[32,224,128]{2,1,0:T(8,128)(2,1)S(1)}, u32[]{:S(2)}, u32[]{:S(2)}) collective-permute-start(bf16[32,224,128]{2,1,0:T(8,128)(2,1)} %get-tuple-element.24), channel_id=1, source_target_pairs={{0,8},{8,16},{16,24},{1,9},{9,17},{17,25},{2,10},{10,18},{18,26},{... | collective-permute-start | bytes 5505032 | tf_op jit(solution)/shard_map/ppermute | solution.py:158
  17.2 43.8 %collective-permute-start.3 = (bf16[32,224,128]{2,1,0:T(8,128)(2,1)}, bf16[32,224,128]{2,1,0:T(8,128)(2,1)}, u32[]{:S(2)}, u32[]{:S(2)}) collective-permute-start(bf16[32,224,128]{2,1,0:T(8,128)(2,1)} %get-tuple-element.23), channel_id=1, source_target_pairs={{8,0},{16,8},{24,16},{9,1},{17,9},{25,17},{10,2},{18,10},{26,18},{... | collective-permute-start | bytes 5505032 | tf_op jit(solution)/shard_map/ppermute | solution.py:158
  56.7 3.8 %copy-start.3 = (bf16[32,224,128]{2,1,0:T(8,128)(2,1)}, bf16[32,224,128]{2,1,0:T(8,128)(2,1)S(1)}, u32[]{:S(2)}) copy-start(bf16[32,224,128]{2,1,0:T(8,128)(2,1)S(1)} %collective-permute-done) | copy-start | bytes 5505028
  59.2 28.1 %collective-permute-start.5 = (bf16[15,224,15]{1,2,0:T(8,128)(2,1)}, bf16[15,224,15]{1,2,0:T(8,128)(2,1)S(1)}, u32[]{:S(2)}, u32[]{:S(2)}) collective-permute-start(bf16[15,224,15]{1,2,0:T(8,128)(2,1)} %copy.24), channel_id=1, source_target_pairs={{1,0},{2,1},{3,2},{4,3},{5,4},{6,5},{7,6},{9,8},{10,9},{11,10},{12... | collective-permute-start | bytes 302408 | tf_op jit(solution)/shard_map/ppermute | solution.py:155
  60.9 20.6 %slice-start = ((s8[7340032]{0:T(1024)(128)(4,1)}), s8[3145728]{0:T(1024)(128)(4,1)S(1)}, s32[]{:S(2)}) async-start(s8[7340032]{0:T(1024)(128)(4,1)} %bitcast.74), calls=%async_computation | async-start | bytes 6291456
  66.0 22.0 %collective-permute-start.7 = (bf16[15,224,15]{1,2,0:T(8,128)(2,1)}, bf16[15,224,15]{1,2,0:T(8,128)(2,1)S(1)}, u32[]{:S(2)}, u32[]{:S(2)}) collective-permute-start(bf16[15,224,15]{1,2,0:T(8,128)(2,1)} %copy.25), channel_id=1, source_target_pairs={{1,0},{2,1},{3,2},{4,3},{5,4},{6,5},{7,6},{9,8},{10,9},{11,10},{12... | collective-permute-start | bytes 302408 | tf_op jit(solution)/shard_map/ppermute | solution.py:155
  69.4 22.3 %collective-permute-start.1 = (bf16[15,224,15]{1,2,0:T(8,128)(2,1)}, bf16[15,224,15]{1,2,0:T(8,128)(2,1)S(1)}, u32[]{:S(2)}, u32[]{:S(2)}) collective-permute-start(bf16[15,224,15]{1,2,0:T(8,128)(2,1)} %copy.22), channel_id=1, source_target_pairs={{0,1},{1,2},{2,3},{3,4},{4,5},{5,6},{6,7},{8,9},{9,10},{10,11},{11... | collective-permute-start | bytes 302408 | tf_op jit(solution)/shard_map/ppermute | solution.py:155
  74.9 6.7 %slice-start.1 = ((s8[7340032]{0:T(1024)(128)(4,1)}), s8[4194304]{0:T(1024)(128)(4,1)S(1)}, s32[]{:S(2)}) async-start(s8[7340032]{0:T(1024)(128)(4,1)} %bitcast.74), calls=%async_computation.1 | async-start | bytes 8388608
  74.9 17.5 %collective-permute-start.4 = (bf16[15,224,15]{1,2,0:T(8,128)(2,1)}, bf16[15,224,15]{1,2,0:T(8,128)(2,1)S(1)}, u32[]{:S(2)}, u32[]{:S(2)}) collective-permute-start(bf16[15,224,15]{1,2,0:T(8,128)(2,1)} %copy.23), channel_id=1, source_target_pairs={{0,1},{1,2},{2,3},{3,4},{4,5},{5,6},{6,7},{8,9},{9,10},{10,11},{11... | collective-permute-start | bytes 302408 | tf_op jit(solution)/shard_map/ppermute | solution.py:155
  87.3 2.0 %copy-start.2 = (f32[256,15,224]{0,2,1:T(8,128)S(1)}, f32[256,15,224]{0,2,1:T(8,128)}, u32[]{:S(2)}) copy-start(f32[256,15,224]{0,2,1:T(8,128)} %fusion.2) | copy-start | bytes 10321924
  91.7 2.0 %copy-start.1 = (f32[256,15,224]{0,2,1:T(8,128)S(1)}, f32[256,15,224]{0,2,1:T(8,128)}, u32[]{:S(2)}) copy-start(f32[256,15,224]{0,2,1:T(8,128)} %fusion.6) | copy-start | bytes 10321924
  114.9 1.4 collective-permute-start.8
  116.3 5.4 %collective-permute-start.10 = (f32[225,112]{1,0:T(8,128)S(1)}, f32[225,112]{1,0:T(8,128)S(1)}, u32[]{:S(2)}, u32[]{:S(2)}) collective-permute-start(f32[225,112]{1,0:T(8,128)S(1)} %fusion.45), channel_id=1, source_target_pairs={{0,4},{1,5},{2,6},{3,7},{4,0},{5,1},{6,2},{7,3},{8,12},{9,13},{10,... | collective-permute-start | bytes 302408 | tf_op jit(solution)/shard_map/ppermute | solution.py:54
  117.9 6.0 %collective-permute-start.11 = (f32[225,112]{1,0:T(8,128)S(1)}, f32[225,112]{1,0:T(8,128)S(1)}, u32[]{:S(2)}, u32[]{:S(2)}) collective-permute-start(f32[225,112]{1,0:T(8,128)S(1)} %fusion.45), channel_id=1, source_target_pairs={{0,6},{1,7},{2,0},{3,1},{4,2},{5,3},{6,4},{7,5},{8,14},{9,15},{10,... | collective-permute-start | bytes 302408 | tf_op jit(solution)/shard_map/ppermute | solution.py:54
  119.9 6.0 %collective-permute-start.9 = (f32[225,112]{1,0:T(8,128)S(1)}, f32[225,112]{1,0:T(8,128)S(1)}, u32[]{:S(2)}, u32[]{:S(2)}) collective-permute-start(f32[225,112]{1,0:T(8,128)S(1)} %fusion.45), channel_id=1, source_target_pairs={{0,2},{1,3},{2,4},{3,5},{4,6},{5,7},{6,0},{7,1},{8,10},{9,11},{10,... | collective-permute-start | bytes 302408 | tf_op jit(solution)/shard_map/ppermute | solution.py:54
  125.9 8.1 %collective-permute-start.12 = (f32[225,112]{1,0:T(8,128)S(1)}, f32[225,112]{1,0:T(8,128)S(1)}, u32[]{:S(2)}, u32[]{:S(2)}) collective-permute-start(f32[225,112]{1,0:T(8,128)S(1)} %add_add_fusion.1), channel_id=1, source_target_pairs={{0,8},{8,16},{16,24},{24,0},{1,9},{9,17},{17,25},{25,1},{2,10},{10... | collective-permute-start | bytes 302408 | tf_op jit(solution)/shard_map/ppermute | solution.py:54
  128.4 9.5 %collective-permute-start.13 = (f32[225,112]{1,0:T(8,128)S(1)}, f32[225,112]{1,0:T(8,128)S(1)}, u32[]{:S(2)}, u32[]{:S(2)}) collective-permute-start(f32[225,112]{1,0:T(8,128)S(1)} %add_add_fusion.1), channel_id=1, source_target_pairs={{0,16},{8,24},{16,0},{24,8},{1,17},{9,25},{17,1},{25,9},{2,18},{10... | collective-permute-start | bytes 302408 | tf_op jit(solution)/shard_map/ppermute | solution.py:54
  130.6 7.3 %collective-permute-start.14 = (f32[225,112]{1,0:T(8,128)S(1)}, f32[225,112]{1,0:T(8,128)S(1)}, u32[]{:S(2)}, u32[]{:S(2)}) collective-permute-start(f32[225,112]{1,0:T(8,128)S(1)} %add_add_fusion.1), channel_id=1, source_target_pairs={{0,24},{8,0},{16,8},{24,16},{1,25},{9,1},{17,9},{25,17},{2,26},{10... | collective-permute-start | bytes 302408 | tf_op jit(solution)/shard_map/ppermute | solution.py:54
  141.8 0.7 copy-start.4

commit v9 on v7

--- a/solution.py
+++ b/solution.py
@@ -84,27 +84,43 @@
     lanes = lax.broadcasted_iota(jnp.int32, (1, size), 1)
     sub8 = lax.broadcasted_iota(jnp.int32, (8, 1), 0)
 
-    def body(k, carry):
+    def pick(v, j):
+        return jnp.sum(jnp.where(lanes == j, v, 0.0), axis=1, keepdims=True)
+
+    def body(m, carry):
+        k = 2 * m
         base = pl.multiple_of((k // 8) * 8, 8)
         slab = o_ref[pl.ds(base, 8), :]
-        row = jnp.sum(jnp.where(sub8 == k - base, slab, 0.0), axis=0, keepdims=True)
-        pivot = jnp.sum(jnp.where(lanes == k, row, 0.0), axis=1, keepdims=True)
-        inv = 1.0 / pivot
+        r0 = jnp.sum(jnp.where(sub8 == k - base, slab, 0.0), axis=0, keepdims=True)
+        r1 = jnp.sum(jnp.where(sub8 == k + 1 - base, slab, 0.0), axis=0, keepdims=True)
+        a00, a01, a11 = pick(r0, k), pick(r0, k + 1), pick(r1, k + 1)
+        det = a00 * a11 - a01 * a01
+        p00, p01, p11 = a11 / det, -a01 / det, a00 / det
         a = o_ref[...]
-        col = jnp.sum(jnp.where(lanes == k, a, 0.0), axis=1, keepdims=True)
-        u = col * inv
-        scaled = row * inv
-        at_row = rows == k
-        at_col = lanes == k
-        edge = jnp.where(at_col, jnp.where(at_row, -inv, u), scaled)
-        o_ref[...] = jnp.where(at_row | at_col, edge, a - u * row)
+        c0 = jnp.sum(jnp.where(lanes == k, a, 0.0), axis=1, keepdims=True)
+        c1 = jnp.sum(jnp.where(lanes == k + 1, a, 0.0), axis=1, keepdims=True)
+        u0 = c0 * p00 + c1 * p01
+        u1 = c0 * p01 + c1 * p11
+        s0 = r0 * p00 + r1 * p01
+        s1 = r0 * p01 + r1 * p11
+        main = a - u0 * r0 - u1 * r1
+        row0, row1 = rows == k, rows == k + 1
+        col0, col1 = lanes == k, lanes == k + 1
+        in_rows = row0 | row1
+        in_cols = col0 | col1
+        corner = jnp.where(row0, jnp.where(col0, -p00, -p01), jnp.where(col0, -p01, -p11))
+        side_cols = jnp.where(col0, u0, u1)
+        side_rows = jnp.where(row0, s0, s1)
+        edge = jnp.where(in_rows, jnp.where(in_cols, corner, side_rows), side_cols)
+        o_ref[...] = jnp.where(in_rows | in_cols, edge, main)
         return carry
 
-    lax.fori_loop(0, n, body, 0)
+    lax.fori_loop(0, n // 2, body, 0)
 
 
 def spd_inverse(a):
     n = a.shape[0]
+    assert n % 2 == 0
     size = -(-n // 128) * 128
     padded = jnp.eye(size, dtype=jnp.float32).at[:n, :n].set(a)
     swept = pl.pallas_call(

time: 168 us -> 159 us (0.946)
  Pallas kernels: 50.3 us -> 41 us
    pallas_call x1, Pallas kernels: 37.7 us -> 28.4 us  [spd_inverse(): pl.pallas_call(functools.partial(sweep_kernel, n), out_shape=jax.ShapeDty...]
  transfers between devices with their start and end apart: 15 -> 15, of which waited for: 7 -> 7; matrix products, arithmetic and copies ran while one was open for 15% -> 16% of each run, Pallas kernels for 0% -> 0%
where the time goes in v9:
time: 159 us; the launch traced here: 158 us
  starting transfers between devices  47.8 us (30%)
  Pallas kernels  41 us (26%)
  matrix products  33.3 us (21%)
  local copies, waits for them, and re-layouts  19 us (12%)
  waiting for transfers between devices  13.5 us (8%)
  other arithmetic  2.45 us (2%)
    ppermute x6, starting transfers between devices, fetch(): return lax.ppermute(piece, 'cross', pairs)  28.5 us
    pallas_call x1, Pallas kernels, spd_inverse(): pl.pallas_call(functools.partial(sweep_kernel, n), out_shape=jax.ShapeDty...  28.4 us
    dot_general x9, matrix products, sum_lines(): jnp.einsum('qbk,kl->qbl', values, w, preferred_element_type=jnp.float32)  18.8 us
    pallas_call x1, Pallas kernels, residuals(): pl.pallas_call(residual_kernel, grid=(bands // block,), in_specs=[spec(le...  12.6 us
    ppermute x6, waiting for transfers between devices, ring_sum(): total = total + lax.ppermute(x, axis, pairs)  12.1 us
    ppermute x6, starting transfers between devices, ring_sum(): total = total + lax.ppermute(x, axis, pairs)  12.1 us
    dot_general x1, matrix products, shards(): jnp.einsum('pbl,bj->pjl', residual, inverse, precision=highest, preferred...  10.2 us
    ppermute x2, starting transfers between devices, fetch(): return lax.ppermute(piece, 'track', pairs)  7.15 us
  transfers between devices with their start and end apart: 15, of which 7 were waited for; matrix products, arithmetic and copies ran while one was open for 16% of the time, Pallas kernels for 0%

profile of v9, /device:TPU:0, one launch (start us, length us, event | category | flops | bytes accessed | tf_op | source)
XLA Modules:
  0.0 158.0 jit_solution(17315287440211170003)
XLA Ops:
  0.0 3.9 %fusion.46 = (bf16[32,224,15]{2,1,0:T(8,128)(2,1)S(1)}, bf16[32,224,15]{2,1,0:T(8,128)(2,1)}) fusion(bf16[32,224,256]{2,1,0:T(8,128)(2,1)} %bitcast.63), kind=kLoop, calls=%fused_computation.62 | loop fusion | bytes 860160 | tf_op jit(solution)/shard_map/slice | solution.py:183
  3.9 2.7 %copy.26 = bf16[32,224,15]{1,0,2:T(8,128)(2,1)} copy(bf16[32,224,15]{2,1,0:T(8,128)(2,1)} %get-tuple-element.24) | data formatting | bytes 430080 | tf_op jit(solution)/shard_map/slice | solution.py:182
  6.6 5.6 %collective-permute-start = (bf16[32,224,15]{1,0,2:T(8,128)(2,1)}, bf16[32,224,15]{1,0,2:T(8,128)(2,1)}, u32[]{:S(2)}, u32[]{:S(2)}) collective-permute-start(bf16[32,224,15]{1,0,2:T(8,128)(2,1)} %copy.26), channel_id=1, source_target_pairs={{0,8},{8,16},{16,24},{1,9},{9,17},{17,25},{2,10},{10,18},{18,26},{... | collective-permute-start | bytes 645128 | tf_op jit(solution)/shard_map/ppermute | solution.py:174
  12.2 1.7 %copy.28 = bf16[32,224,15]{1,0,2:T(8,128)(2,1)} copy(bf16[32,224,15]{2,1,0:T(8,128)(2,1)S(1)} %get-tuple-element.23) | data formatting | bytes 430080 | tf_op jit(solution)/shard_map/slice | solution.py:183
  13.9 0.0 copy-start
  13.9 1.5 collective-permute-start.3
  15.4 4.0 %fusion.45 = (bf16[15,224,256]{2,1,0:T(8,128)(2,1)}, bf16[15,224,256]{2,1,0:T(8,128)(2,1)}) fusion(bf16[32,224,256]{2,1,0:T(8,128)(2,1)} %bitcast.64), kind=kLoop, calls=%fused_computation.61 | loop fusion | bytes 6881280 | tf_op jit(solution)/shard_map/slice | solution.py:180
  19.4 1.3 collective-permute-start.6
  20.7 3.1 %collective-permute-start.2 = (bf16[15,224,256]{2,1,0:T(8,128)(2,1)}, bf16[15,224,256]{2,1,0:T(8,128)(2,1)S(1)}, u32[]{:S(2)}, u32[]{:S(2)}) collective-permute-start(bf16[15,224,256]{2,1,0:T(8,128)(2,1)} %get-tuple-element.22), channel_id=1, source_target_pairs={{0,1},{1,2},{2,3},{3,4},{4,5},{5,6},{6,7},{8,9},{9,10},{10,11},{11... | collective-permute-start | bytes 5160968 | tf_op jit(solution)/shard_map/ppermute | solution.py:171
  23.9 0.0 copy-done
  23.9 4.1 %fusion.10 = f32[256,32,224]{0,2,1:T(8,128)} fusion(bf16[256,32,224]{0,2,1:T(8,128)(2,1)S(1)} %copy-done), kind=kOutput, calls=%fused_computation.15 | convolution fusion | flops 939720704 | bytes 11010048 | tf_op jit(solution)/shard_map/qbk,kl->qbl/dot_general | solution.py:209
  28.0 0.7 broadcast_multiply_fusion.count_ref
  28.7 0.0 collective-permute-done
  28.7 1.0 fusion.48
  29.8 1.3 collective-permute-start.5
  31.1 0.0 collective-permute-done.3
  31.1 1.0 fusion.47
  32.1 1.3 collective-permute-start.7
  33.5 0.0 copy-start.1
  33.5 4.4 %collective-permute-start.1 = (bf16[15,224,15]{1,2,0:T(8,128)(2,1)S(1)}, bf16[15,224,15]{1,2,0:T(8,128)(2,1)S(1)}, u32[]{:S(2)}, u32[]{:S(2)}) collective-permute-start(bf16[15,224,15]{1,2,0:T(8,128)(2,1)S(1)} %copy.27), channel_id=1, source_target_pairs={{0,1},{1,2},{2,3},{3,4},{4,5},{5,6},{6,7},{8,9},{9,10},{10,11},{11... | collective-permute-start | bytes 302408 | tf_op jit(solution)/shard_map/ppermute | solution.py:171
  38.0 2.1 %fusion.5 = f32[256,32,224]{0,2,1:T(8,128)S(1)} fusion(bf16[32,224,15]{1,0,2:T(8,128)(2,1)} %collective-permute-done), kind=kOutput, calls=%fused_computation.9 | convolution fusion | flops 55054080 | bytes 7555072 | tf_op jit(solution)/shard_map/qbk,kl->qbl/dot_general | solution.py:209
  40.1 0.0 copy-done.1
  40.1 5.1 %add_bitcast_fusion.middle_ref = f32[32,224,256]{2,1,0:T(8,128)} fusion(f32[256,32,224]{0,2,1:T(8,128)S(1)} %fusion.5, f32[256,32,224]{0,2,1:T(8,128)S(1)} %copy-done.1, bf16[32,224,15]{1,0,2:T(8,128)(2,1)} %collective-permute-done.3, s32[15]{0:T(128)S(1)} %iota_add_fusion), kind=kOutput, calls=%fused_computation.3 | convolution fusion | flops 58724096 | bytes 22235196 | tf_op jit(solution)/shard_map/qbk,kl->qbl/dot_general | solution.py:209
  45.3 0.0 collective-permute-done.5
  45.3 17.0 %collective-permute-start.4 = (bf16[15,224,15]{1,2,0:T(8,128)(2,1)S(1)}, bf16[15,224,15]{1,2,0:T(8,128)(2,1)S(1)}, u32[]{:S(2)}, u32[]{:S(2)}) collective-permute-start(bf16[15,224,15]{1,2,0:T(8,128)(2,1)S(1)} %copy.29), channel_id=1, source_target_pairs={{0,1},{1,2},{2,3},{3,4},{4,5},{5,6},{6,7},{8,9},{9,10},{10,11},{11... | collective-permute-start | bytes 302408 | tf_op jit(solution)/shard_map/ppermute | solution.py:171
  62.3 0.7 fusion.22
  63.0 0.0 collective-permute-done.1
  63.0 0.7 fusion.25
  63.7 0.0 collective-permute-done.6
  63.7 0.6 fusion.8
  64.3 0.0 collective-permute-done.7
  64.3 2.4 %add_bitcast_fusion.1.right_ref = f32[15,224,256]{2,1,0:T(8,128)} fusion(f32[256,15,224]{0,2,1:T(8,128)S(1)} %fusion.22, f32[256,15,224]{0,2,1:T(8,128)S(1)} %fusion.8, bf16[15,224,15]{1,2,0:T(8,128)(2,1)S(1)} %collective-permute-done.7, s32[15]{0:T(128)S(1)} %iota_add_fusion), kind=kOutput, calls=%fused_computation.4 | convolution fusion | flops 27528960 | bytes 10422780 | tf_op jit(solution)/shard_map/qbk,kl->qbl/dot_general | solution.py:209
  66.8 0.0 collective-permute-done.2
  66.8 0.6 fusion.12
  67.4 0.0 collective-permute-done.4
  67.4 2.5 %add_bitcast_fusion.2.left_ref = f32[15,224,256]{2,1,0:T(8,128)} fusion(f32[256,15,224]{0,2,1:T(8,128)S(1)} %fusion.25, f32[256,15,224]{0,2,1:T(8,128)S(1)} %fusion.12, bf16[15,224,15]{1,2,0:T(8,128)(2,1)S(1)} %collective-permute-done.4, s32[15]{0:T(128)S(1)} %iota_add_fusion), kind=kOutput, calls=%fused_computation.5 | convolution fusion | flops 27528960 | bytes 10422780 | tf_op jit(solution)/shard_map/qbk,kl->qbl/dot_general | solution.py:209
  69.9 12.6 %shard_map.17 = (f32[32,224,256]{2,1,0:T(8,128)}, bf16[32,224,256]{2,1,0:T(8,128)(2,1)}) custom-call(f32[15,224,256]{2,1,0:T(8,128)} %add_bitcast_fusion.2.left_ref, f32[32,224,256]{2,1,0:T(8,128)} %add_bitcast_fusion.middle_ref, f32[15,224,256]{2,1,0:T(8,128)} %add_bitcast_fusion.1.right_ref, bf16[32,224,256]{2,1,0:T(8,128)(2,1)} %bitcast.65, ...), custom_call_target="tpu_custom_call" | custom-call | tf_op jit(solution)/shard_map/pallas_call | solution.py:243
  82.4 4.3 %convolution_bitcast_fusion = f32[224,224]{1,0:T(8,128)S(1)} fusion(bf16[32,224,256]{2,1,0:T(8,128)(2,1)} %get-tuple-element.20), kind=kOutput, calls=%fused_computation.6 | convolution fusion | flops 822083584 | bytes 3870720 | tf_op jit(solution)/shard_map/pjl,pkl->jk/dot_general | solution.py:272
  86.7 0.1 fusion.49
  86.8 1.7 %gather_fusion = f32[112]{0:T(128)S(1)} fusion(f32[112,112]{1,0:T(8,128)S(1)} %get-tuple-element.31, s32[112]{0:T(128)S(1)} %or_bitcast_fusion), kind=kCustom, calls=%fused_computation | custom fusion | bytes 1792 | tf_op jit(solution)/shard_map/jit(diagonal)/cond/branch_0_fun/gather | solution.py:64
  88.5 0.1 collective-permute-start.8
  88.6 1.3 collective-permute-done.8
  89.9 3.9 %collective-permute-start.10 = (f32[225,112]{1,0:T(8,128)S(1)}, f32[225,112]{1,0:T(8,128)S(1)}, u32[]{:S(2)}, u32[]{:S(2)}) collective-permute-start(f32[225,112]{1,0:T(8,128)S(1)} %fusion.44), channel_id=1, source_target_pairs={{0,4},{1,5},{2,6},{3,7},{4,0},{5,1},{6,2},{7,3},{8,12},{9,13},{10,... | collective-permute-start | bytes 302408 | tf_op jit(solution)/shard_map/ppermute | solution.py:54
  93.9 0.8 collective-permute-start.11
  94.7 1.2 collective-permute-start.9
  95.9 1.5 collective-permute-done.10
  97.4 2.3 %collective-permute-done.11 = f32[225,112]{1,0:T(8,128)S(1)} collective-permute-done((f32[225,112]{1,0:T(8,128)S(1)}, f32[225,112]{1,0:T(8,128)S(1)}, u32[]{:S(2)}, u32[]{:S(2)}) %collective-permute-start.11) | collective-permute-done | bytes 100832 | tf_op jit(solution)/shard_map/ppermute | solution.py:54
  99.7 1.5 collective-permute-done.9
  101.2 2.9 %collective-permute-start.12 = (f32[225,112]{1,0:T(8,128)S(1)}, f32[225,112]{1,0:T(8,128)S(1)}, u32[]{:S(2)}, u32[]{:S(2)}) collective-permute-start(f32[225,112]{1,0:T(8,128)S(1)} %add_add_fusion.1), channel_id=1, source_target_pairs={{0,8},{8,16},{16,24},{24,0},{1,9},{9,17},{17,25},{25,1},{2,10},{10... | collective-permute-start | bytes 302408 | tf_op jit(solution)/shard_map/ppermute | solution.py:54
  104.1 2.6 %collective-permute-start.13 = (f32[225,112]{1,0:T(8,128)S(1)}, f32[225,112]{1,0:T(8,128)S(1)}, u32[]{:S(2)}, u32[]{:S(2)}) collective-permute-start(f32[225,112]{1,0:T(8,128)S(1)} %add_add_fusion.1), channel_id=1, source_target_pairs={{0,16},{8,24},{16,0},{24,8},{1,17},{9,25},{17,1},{25,9},{2,18},{10... | collective-permute-start | bytes 302408 | tf_op jit(solution)/shard_map/ppermute | solution.py:54
  106.7 0.6 collective-permute-start.14
  107.4 3.0 %collective-permute-done.12 = f32[225,112]{1,0:T(8,128)S(1)} collective-permute-done((f32[225,112]{1,0:T(8,128)S(1)}, f32[225,112]{1,0:T(8,128)S(1)}, u32[]{:S(2)}, u32[]{:S(2)}) %collective-permute-start.12) | collective-permute-done | bytes 100832 | tf_op jit(solution)/shard_map/ppermute | solution.py:54
  110.4 3.6 %collective-permute-done.13 = f32[225,112]{1,0:T(8,128)S(1)} collective-permute-done((f32[225,112]{1,0:T(8,128)S(1)}, f32[225,112]{1,0:T(8,128)S(1)}, u32[]{:S(2)}, u32[]{:S(2)}) %collective-permute-start.13) | collective-permute-done | bytes 100832 | tf_op jit(solution)/shard_map/ppermute | solution.py:54
  114.1 0.2 collective-permute-done.14
  114.3 0.1 copy.37
  114.4 0.1 copy.38
  114.5 0.7 select_reduce_fusion
  115.9 0.1 select_add_fusion
  116.0 2.0 %scatter.4.a_ref = f32[256,256]{1,0:T(8,128)S(1)} dynamic-update-slice(f32[256,256]{1,0:T(8,128)S(1)} %fusion.14, f32[224,224]{1,0:T(8,128)S(1)} %select_add_fusion, s32[]{:T(128)} %constant.71.clone.1, s32[]{:T(128)} %constant.71.clone.1) | dynamic-update-slice | bytes 401412 | tf_op jit(solution)/shard_map/scatter | solution.py:125
  118.1 0.0 copy-start.2
  118.1 0.7 copy-done.2
  118.7 28.4 %shard_map.18 = f32[256,256]{1,0:T(8,128)} custom-call(f32[256,256]{1,0:T(8,128)} %copy-done.2), custom_call_target="tpu_custom_call" | custom-call | tf_op jit(solution)/shard_map/pallas_call | solution.py:126
  147.2 10.2 %fusion = f32[32,256]{1,0:T(8,128)S(1)} fusion(f32[32,224,256]{2,1,0:T(8,128)} %get-tuple-element.19, f32[256,256]{1,0:T(8,128)} %shard_map.18), kind=kOutput, calls=%fused_computation.2 | convolution fusion | flops 4936213504 | bytes 14942208 | tf_op jit(solution)/shard_map/pbl,bj->pjl/dot_general | solution.py:282
  157.4 0.6 multiply_bitcast_fusion
  (16 shorter events, 0.4 us)
Async XLA Ops:
  6.6 22.1 %collective-permute-start = (bf16[32,224,15]{1,0,2:T(8,128)(2,1)}, bf16[32,224,15]{1,0,2:T(8,128)(2,1)}, u32[]{:S(2)}, u32[]{:S(2)}) collective-permute-start(bf16[32,224,15]{1,0,2:T(8,128)(2,1)} %copy.26), channel_id=1, source_target_pairs={{0,8},{8,16},{16,24},{1,9},{9,17},{17,25},{2,10},{10,18},{18,26},{... | collective-permute-start | bytes 645128 | tf_op jit(solution)/shard_map/ppermute | solution.py:174
  13.9 10.0 %copy-start = (bf16[256,32,224]{0,2,1:T(8,128)(2,1)S(1)}, bf16[256,32,224]{0,2,1:T(8,128)(2,1)}, u32[]{:S(2)}) copy-start(bf16[256,32,224]{0,2,1:T(8,128)(2,1)} %param.3) | copy-start | bytes 11010052
  13.9 17.2 %collective-permute-start.3 = (bf16[32,224,15]{1,0,2:T(8,128)(2,1)}, bf16[32,224,15]{1,0,2:T(8,128)(2,1)}, u32[]{:S(2)}, u32[]{:S(2)}) collective-permute-start(bf16[32,224,15]{1,0,2:T(8,128)(2,1)} %copy.28), channel_id=1, source_target_pairs={{8,0},{16,8},{24,16},{9,1},{17,9},{25,17},{10,2},{18,10},{26,18},{... | collective-permute-start | bytes 645128 | tf_op jit(solution)/shard_map/ppermute | solution.py:174
  19.4 44.2 %collective-permute-start.6 = (bf16[15,224,256]{2,1,0:T(8,128)(2,1)}, bf16[15,224,256]{2,1,0:T(8,128)(2,1)S(1)}, u32[]{:S(2)}, u32[]{:S(2)}) collective-permute-start(bf16[15,224,256]{2,1,0:T(8,128)(2,1)} %get-tuple-element.21), channel_id=1, source_target_pairs={{1,0},{2,1},{3,2},{4,3},{5,4},{6,5},{7,6},{9,8},{10,9},{11,10},{12... | collective-permute-start | bytes 5160968 | tf_op jit(solution)/shard_map/ppermute | solution.py:171
  20.7 46.0 %collective-permute-start.2 = (bf16[15,224,256]{2,1,0:T(8,128)(2,1)}, bf16[15,224,256]{2,1,0:T(8,128)(2,1)S(1)}, u32[]{:S(2)}, u32[]{:S(2)}) collective-permute-start(bf16[15,224,256]{2,1,0:T(8,128)(2,1)} %get-tuple-element.22), channel_id=1, source_target_pairs={{0,1},{1,2},{2,3},{3,4},{4,5},{5,6},{6,7},{8,9},{9,10},{10,11},{11... | collective-permute-start | bytes 5160968 | tf_op jit(solution)/shard_map/ppermute | solution.py:171
  29.8 15.5 %collective-permute-start.5 = (bf16[15,224,15]{1,2,0:T(8,128)(2,1)S(1)}, bf16[15,224,15]{1,2,0:T(8,128)(2,1)S(1)}, u32[]{:S(2)}, u32[]{:S(2)}) collective-permute-start(bf16[15,224,15]{1,2,0:T(8,128)(2,1)S(1)} %copy.32), channel_id=1, source_target_pairs={{1,0},{2,1},{3,2},{4,3},{5,4},{6,5},{7,6},{9,8},{10,9},{11,10},{12... | collective-permute-start | bytes 302408 | tf_op jit(solution)/shard_map/ppermute | solution.py:171
  32.1 32.2 %collective-permute-start.7 = (bf16[15,224,15]{1,2,0:T(8,128)(2,1)S(1)}, bf16[15,224,15]{1,2,0:T(8,128)(2,1)S(1)}, u32[]{:S(2)}, u32[]{:S(2)}) collective-permute-start(bf16[15,224,15]{1,2,0:T(8,128)(2,1)S(1)} %copy.33), channel_id=1, source_target_pairs={{1,0},{2,1},{3,2},{4,3},{5,4},{6,5},{7,6},{9,8},{10,9},{11,10},{12... | collective-permute-start | bytes 302408 | tf_op jit(solution)/shard_map/ppermute | solution.py:171
  33.5 6.6 %copy-start.1 = (f32[256,32,224]{0,2,1:T(8,128)S(1)}, f32[256,32,224]{0,2,1:T(8,128)}, u32[]{:S(2)}) copy-start(f32[256,32,224]{0,2,1:T(8,128)} %fusion.10) | copy-start | bytes 22020100
  33.5 29.5 %collective-permute-start.1 = (bf16[15,224,15]{1,2,0:T(8,128)(2,1)S(1)}, bf16[15,224,15]{1,2,0:T(8,128)(2,1)S(1)}, u32[]{:S(2)}, u32[]{:S(2)}) collective-permute-start(bf16[15,224,15]{1,2,0:T(8,128)(2,1)S(1)} %copy.27), channel_id=1, source_target_pairs={{0,1},{1,2},{2,3},{3,4},{4,5},{5,6},{6,7},{8,9},{9,10},{10,11},{11... | collective-permute-start | bytes 302408 | tf_op jit(solution)/shard_map/ppermute | solution.py:171
  45.3 22.1 %collective-permute-start.4 = (bf16[15,224,15]{1,2,0:T(8,128)(2,1)S(1)}, bf16[15,224,15]{1,2,0:T(8,128)(2,1)S(1)}, u32[]{:S(2)}, u32[]{:S(2)}) collective-permute-start(bf16[15,224,15]{1,2,0:T(8,128)(2,1)S(1)} %copy.29), channel_id=1, source_target_pairs={{0,1},{1,2},{2,3},{3,4},{4,5},{5,6},{6,7},{8,9},{9,10},{10,11},{11... | collective-permute-start | bytes 302408 | tf_op jit(solution)/shard_map/ppermute | solution.py:171
  88.5 1.4 collective-permute-start.8
  89.9 7.5 %collective-permute-start.10 = (f32[225,112]{1,0:T(8,128)S(1)}, f32[225,112]{1,0:T(8,128)S(1)}, u32[]{:S(2)}, u32[]{:S(2)}) collective-permute-start(f32[225,112]{1,0:T(8,128)S(1)} %fusion.44), channel_id=1, source_target_pairs={{0,4},{1,5},{2,6},{3,7},{4,0},{5,1},{6,2},{7,3},{8,12},{9,13},{10,... | collective-permute-start | bytes 302408 | tf_op jit(solution)/shard_map/ppermute | solution.py:54
  93.9 5.8 %collective-permute-start.11 = (f32[225,112]{1,0:T(8,128)S(1)}, f32[225,112]{1,0:T(8,128)S(1)}, u32[]{:S(2)}, u32[]{:S(2)}) collective-permute-start(f32[225,112]{1,0:T(8,128)S(1)} %fusion.44), channel_id=1, source_target_pairs={{0,6},{1,7},{2,0},{3,1},{4,2},{5,3},{6,4},{7,5},{8,14},{9,15},{10,... | collective-permute-start | bytes 302408 | tf_op jit(solution)/shard_map/ppermute | solution.py:54
  94.7 6.5 %collective-permute-start.9 = (f32[225,112]{1,0:T(8,128)S(1)}, f32[225,112]{1,0:T(8,128)S(1)}, u32[]{:S(2)}, u32[]{:S(2)}) collective-permute-start(f32[225,112]{1,0:T(8,128)S(1)} %fusion.44), channel_id=1, source_target_pairs={{0,2},{1,3},{2,4},{3,5},{4,6},{5,7},{6,0},{7,1},{8,10},{9,11},{10,... | collective-permute-start | bytes 302408 | tf_op jit(solution)/shard_map/ppermute | solution.py:54
  101.2 9.2 %collective-permute-start.12 = (f32[225,112]{1,0:T(8,128)S(1)}, f32[225,112]{1,0:T(8,128)S(1)}, u32[]{:S(2)}, u32[]{:S(2)}) collective-permute-start(f32[225,112]{1,0:T(8,128)S(1)} %add_add_fusion.1), channel_id=1, source_target_pairs={{0,8},{8,16},{16,24},{24,0},{1,9},{9,17},{17,25},{25,1},{2,10},{10... | collective-permute-start | bytes 302408 | tf_op jit(solution)/shard_map/ppermute | solution.py:54
  104.1 10.0 %collective-permute-start.13 = (f32[225,112]{1,0:T(8,128)S(1)}, f32[225,112]{1,0:T(8,128)S(1)}, u32[]{:S(2)}, u32[]{:S(2)}) collective-permute-start(f32[225,112]{1,0:T(8,128)S(1)} %add_add_fusion.1), channel_id=1, source_target_pairs={{0,16},{8,24},{16,0},{24,8},{1,17},{9,25},{17,1},{25,9},{2,18},{10... | collective-permute-start | bytes 302408 | tf_op jit(solution)/shard_map/ppermute | solution.py:54
  106.7 7.5 %collective-permute-start.14 = (f32[225,112]{1,0:T(8,128)S(1)}, f32[225,112]{1,0:T(8,128)S(1)}, u32[]{:S(2)}, u32[]{:S(2)}) collective-permute-start(f32[225,112]{1,0:T(8,128)S(1)} %add_add_fusion.1), channel_id=1, source_target_pairs={{0,24},{8,0},{16,8},{24,16},{1,25},{9,1},{17,9},{25,17},{2,26},{10... | collective-permute-start | bytes 302408 | tf_op jit(solution)/shard_map/ppermute | solution.py:54
  118.1 0.7 copy-start.2

commit v10 on v9

--- a/solution.py
+++ b/solution.py
@@ -78,10 +78,11 @@
 
 
 def sweep_kernel(n, a_ref, o_ref):
-    size = a_ref.shape[0]
-    o_ref[...] = a_ref[...]
+    size = o_ref.shape[0]
     rows = lax.broadcasted_iota(jnp.int32, (size, 1), 0)
     lanes = lax.broadcasted_iota(jnp.int32, (1, size), 1)
+    o_ref[...] = jnp.where(rows == lanes, 1.0, 0.0).astype(jnp.float32)
+    o_ref[:n, :n] = a_ref[...]
     sub8 = lax.broadcasted_iota(jnp.int32, (8, 1), 0)
 
     def pick(v, j):
@@ -122,11 +123,10 @@
     n = a.shape[0]
     assert n % 2 == 0
     size = -(-n // 128) * 128
-    padded = jnp.eye(size, dtype=jnp.float32).at[:n, :n].set(a)
     swept = pl.pallas_call(
         functools.partial(sweep_kernel, n),
         out_shape=jax.ShapeDtypeStruct((size, size), jnp.float32),
-    )(padded)
+    )(a)
     return -swept[:n, :n]
 
 

time: 159 us -> 157 us (0.987)
  local copies, waits for them, and re-layouts: 19 us -> 16.3 us
    scatter x1 -> x0, local copies, waits for them, and re-layouts: 2.04 us -> none  [spd_inverse(): padded = jnp.eye(size, dtype=jnp.float32).at[:n, :n].set(a)]
where the time goes in v10:
time: 157 us; the launch traced here: 156 us
  starting transfers between devices  47.8 us (30%)
  Pallas kernels  41 us (26%)
  matrix products  33.3 us (21%)
  local copies, waits for them, and re-layouts  16.3 us (10%)
  waiting for transfers between devices  13.5 us (9%)
  other arithmetic  3.12 us (2%)
    ppermute x6, starting transfers between devices, fetch(): return lax.ppermute(piece, 'cross', pairs)  28.5 us
    pallas_call x1, Pallas kernels, spd_inverse(): pl.pallas_call(functools.partial(sweep_kernel, n), out_shape=jax.ShapeDty...  28.4 us
    dot_general x9, matrix products, sum_lines(): jnp.einsum('qbk,kl->qbl', values, w, preferred_element_type=jnp.float32)  18.8 us
    pallas_call x1, Pallas kernels, residuals(): pl.pallas_call(residual_kernel, grid=(bands // block,), in_specs=[spec(le...  12.6 us
    ppermute x6, waiting for transfers between devices, ring_sum(): total = total + lax.ppermute(x, axis, pairs)  12.1 us
    ppermute x6, starting transfers between devices, ring_sum(): total = total + lax.ppermute(x, axis, pairs)  12.1 us
    dot_general x1, matrix products, shards(): jnp.einsum('pbl,bj->pjl', residual, inverse, precision=highest, preferred...  10.2 us
    ppermute x2, starting transfers between devices, fetch(): return lax.ppermute(piece, 'track', pairs)  7.16 us
  transfers between devices with their start and end apart: 15, of which 7 were waited for; matrix products, arithmetic and copies ran while one was open for 16% of the time, Pallas kernels for 0%

profile of v10, /device:TPU:0, one launch (start us, length us, event | category | flops | bytes accessed | tf_op | source)
XLA Modules:
  0.0 156.0 jit_solution(9035057134284424318)
XLA Ops:
  0.0 3.9 %fusion.45 = (bf16[32,224,15]{2,1,0:T(8,128)(2,1)S(1)}, bf16[32,224,15]{2,1,0:T(8,128)(2,1)}) fusion(bf16[32,224,256]{2,1,0:T(8,128)(2,1)} %bitcast.63), kind=kLoop, calls=%fused_computation.60 | loop fusion | bytes 860160 | tf_op jit(solution)/shard_map/slice | solution.py:183
  3.9 2.7 %copy.26 = bf16[32,224,15]{1,0,2:T(8,128)(2,1)} copy(bf16[32,224,15]{2,1,0:T(8,128)(2,1)} %get-tuple-element.12) | data formatting | bytes 430080 | tf_op jit(solution)/shard_map/slice | solution.py:182
  6.6 5.6 %collective-permute-start = (bf16[32,224,15]{1,0,2:T(8,128)(2,1)}, bf16[32,224,15]{1,0,2:T(8,128)(2,1)}, u32[]{:S(2)}, u32[]{:S(2)}) collective-permute-start(bf16[32,224,15]{1,0,2:T(8,128)(2,1)} %copy.26), channel_id=1, source_target_pairs={{0,8},{8,16},{16,24},{1,9},{9,17},{17,25},{2,10},{10,18},{18,26},{... | collective-permute-start | bytes 645128 | tf_op jit(solution)/shard_map/ppermute | solution.py:174
  12.2 1.7 %copy.28 = bf16[32,224,15]{1,0,2:T(8,128)(2,1)} copy(bf16[32,224,15]{2,1,0:T(8,128)(2,1)S(1)} %get-tuple-element.11) | data formatting | bytes 430080 | tf_op jit(solution)/shard_map/slice | solution.py:183
  13.9 0.0 copy-start
  13.9 1.5 collective-permute-start.3
  15.5 4.0 %fusion.44 = (bf16[15,224,256]{2,1,0:T(8,128)(2,1)}, bf16[15,224,256]{2,1,0:T(8,128)(2,1)}) fusion(bf16[32,224,256]{2,1,0:T(8,128)(2,1)} %bitcast.64), kind=kLoop, calls=%fused_computation.59 | loop fusion | bytes 6881280 | tf_op jit(solution)/shard_map/slice | solution.py:180
  19.5 1.3 collective-permute-start.6
  20.7 3.1 %collective-permute-start.2 = (bf16[15,224,256]{2,1,0:T(8,128)(2,1)}, bf16[15,224,256]{2,1,0:T(8,128)(2,1)S(1)}, u32[]{:S(2)}, u32[]{:S(2)}) collective-permute-start(bf16[15,224,256]{2,1,0:T(8,128)(2,1)} %get-tuple-element.10), channel_id=1, source_target_pairs={{0,1},{1,2},{2,3},{3,4},{4,5},{5,6},{6,7},{8,9},{9,10},{10,11},{11... | collective-permute-start | bytes 5160968 | tf_op jit(solution)/shard_map/ppermute | solution.py:171
  23.9 0.0 copy-done
  23.9 4.1 %fusion.10 = f32[256,32,224]{0,2,1:T(8,128)} fusion(bf16[256,32,224]{0,2,1:T(8,128)(2,1)S(1)} %copy-done), kind=kOutput, calls=%fused_computation.14 | convolution fusion | flops 939720704 | bytes 11010048 | tf_op jit(solution)/shard_map/qbk,kl->qbl/dot_general | solution.py:209
  28.0 0.7 broadcast_multiply_fusion.count_ref
  28.7 0.0 collective-permute-done
  28.7 1.0 fusion.47
  29.8 1.3 collective-permute-start.5
  31.1 0.0 collective-permute-done.3
  31.1 1.0 fusion.46
  32.2 1.3 collective-permute-start.7
  33.5 0.0 copy-start.1
  33.5 4.4 %collective-permute-start.1 = (bf16[15,224,15]{1,2,0:T(8,128)(2,1)S(1)}, bf16[15,224,15]{1,2,0:T(8,128)(2,1)S(1)}, u32[]{:S(2)}, u32[]{:S(2)}) collective-permute-start(bf16[15,224,15]{1,2,0:T(8,128)(2,1)S(1)} %copy.27), channel_id=1, source_target_pairs={{0,1},{1,2},{2,3},{3,4},{4,5},{5,6},{6,7},{8,9},{9,10},{10,11},{11... | collective-permute-start | bytes 302408 | tf_op jit(solution)/shard_map/ppermute | solution.py:171
  38.0 2.1 %fusion.5 = f32[256,32,224]{0,2,1:T(8,128)S(1)} fusion(bf16[32,224,15]{1,0,2:T(8,128)(2,1)} %collective-permute-done), kind=kOutput, calls=%fused_computation.9 | convolution fusion | flops 55054080 | bytes 7555072 | tf_op jit(solution)/shard_map/qbk,kl->qbl/dot_general | solution.py:209
  40.1 0.0 copy-done.1
  40.1 5.1 %add_bitcast_fusion.middle_ref = f32[32,224,256]{2,1,0:T(8,128)} fusion(f32[256,32,224]{0,2,1:T(8,128)S(1)} %fusion.5, f32[256,32,224]{0,2,1:T(8,128)S(1)} %copy-done.1, bf16[32,224,15]{1,0,2:T(8,128)(2,1)} %collective-permute-done.3, s32[15]{0:T(128)S(1)} %iota_add_fusion), kind=kOutput, calls=%fused_computation.3 | convolution fusion | flops 58724096 | bytes 22235196 | tf_op jit(solution)/shard_map/qbk,kl->qbl/dot_general | solution.py:209
  45.3 0.0 collective-permute-done.5
  45.3 17.0 %collective-permute-start.4 = (bf16[15,224,15]{1,2,0:T(8,128)(2,1)S(1)}, bf16[15,224,15]{1,2,0:T(8,128)(2,1)S(1)}, u32[]{:S(2)}, u32[]{:S(2)}) collective-permute-start(bf16[15,224,15]{1,2,0:T(8,128)(2,1)S(1)} %copy.29), channel_id=1, source_target_pairs={{0,1},{1,2},{2,3},{3,4},{4,5},{5,6},{6,7},{8,9},{9,10},{10,11},{11... | collective-permute-start | bytes 302408 | tf_op jit(solution)/shard_map/ppermute | solution.py:171
  62.3 0.7 fusion.21
  63.0 0.0 collective-permute-done.1
  63.0 0.7 fusion.24
  63.7 0.0 collective-permute-done.6
  63.7 0.6 fusion.8
  64.3 0.0 collective-permute-done.7
  64.3 2.4 %add_bitcast_fusion.1.right_ref = f32[15,224,256]{2,1,0:T(8,128)} fusion(f32[256,15,224]{0,2,1:T(8,128)S(1)} %fusion.21, f32[256,15,224]{0,2,1:T(8,128)S(1)} %fusion.8, bf16[15,224,15]{1,2,0:T(8,128)(2,1)S(1)} %collective-permute-done.7, s32[15]{0:T(128)S(1)} %iota_add_fusion), kind=kOutput, calls=%fused_computation.4 | convolution fusion | flops 27528960 | bytes 10422780 | tf_op jit(solution)/shard_map/qbk,kl->qbl/dot_general | solution.py:209
  66.8 0.0 collective-permute-done.2
  66.8 0.6 fusion.12
  67.4 0.0 collective-permute-done.4
  67.4 2.5 %add_bitcast_fusion.2.left_ref = f32[15,224,256]{2,1,0:T(8,128)} fusion(f32[256,15,224]{0,2,1:T(8,128)S(1)} %fusion.24, f32[256,15,224]{0,2,1:T(8,128)S(1)} %fusion.12, bf16[15,224,15]{1,2,0:T(8,128)(2,1)S(1)} %collective-permute-done.4, s32[15]{0:T(128)S(1)} %iota_add_fusion), kind=kOutput, calls=%fused_computation.5 | convolution fusion | flops 27528960 | bytes 10422780 | tf_op jit(solution)/shard_map/qbk,kl->qbl/dot_general | solution.py:209
  69.9 12.6 %shard_map.17 = (f32[32,224,256]{2,1,0:T(8,128)}, bf16[32,224,256]{2,1,0:T(8,128)(2,1)}) custom-call(f32[15,224,256]{2,1,0:T(8,128)} %add_bitcast_fusion.2.left_ref, f32[32,224,256]{2,1,0:T(8,128)} %add_bitcast_fusion.middle_ref, f32[15,224,256]{2,1,0:T(8,128)} %add_bitcast_fusion.1.right_ref, bf16[32,224,256]{2,1,0:T(8,128)(2,1)} %bitcast.65, ...), custom_call_target="tpu_custom_call" | custom-call | tf_op jit(solution)/shard_map/pallas_call | solution.py:243
  82.5 4.3 %convolution_bitcast_fusion = f32[224,224]{1,0:T(8,128)S(1)} fusion(bf16[32,224,256]{2,1,0:T(8,128)(2,1)} %get-tuple-element.8), kind=kOutput, calls=%fused_computation.6 | convolution fusion | flops 822083584 | bytes 3870720 | tf_op jit(solution)/shard_map/pjl,pkl->jk/dot_general | solution.py:272
  86.8 0.1 fusion.48
  86.9 1.7 %gather_fusion = f32[112]{0:T(128)S(1)} fusion(f32[112,112]{1,0:T(8,128)S(1)} %get-tuple-element.19, s32[112]{0:T(128)S(1)} %or_bitcast_fusion), kind=kCustom, calls=%fused_computation | custom fusion | bytes 1792 | tf_op jit(solution)/shard_map/jit(diagonal)/cond/branch_0_fun/gather | solution.py:64
  88.6 0.1 collective-permute-start.8
  88.7 1.3 collective-permute-done.8
  90.0 3.9 %collective-permute-start.10 = (f32[225,112]{1,0:T(8,128)S(1)}, f32[225,112]{1,0:T(8,128)S(1)}, u32[]{:S(2)}, u32[]{:S(2)}) collective-permute-start(f32[225,112]{1,0:T(8,128)S(1)} %fusion.43), channel_id=1, source_target_pairs={{0,4},{1,5},{2,6},{3,7},{4,0},{5,1},{6,2},{7,3},{8,12},{9,13},{10,... | collective-permute-start | bytes 302408 | tf_op jit(solution)/shard_map/ppermute | solution.py:54
  93.9 0.8 collective-permute-start.11
  94.8 1.2 collective-permute-start.9
  95.9 1.5 collective-permute-done.10
  97.5 2.2 %collective-permute-done.11 = f32[225,112]{1,0:T(8,128)S(1)} collective-permute-done((f32[225,112]{1,0:T(8,128)S(1)}, f32[225,112]{1,0:T(8,128)S(1)}, u32[]{:S(2)}, u32[]{:S(2)}) %collective-permute-start.11) | collective-permute-done | bytes 100832 | tf_op jit(solution)/shard_map/ppermute | solution.py:54
  99.7 1.5 collective-permute-done.9
  101.3 2.9 %collective-permute-start.12 = (f32[225,112]{1,0:T(8,128)S(1)}, f32[225,112]{1,0:T(8,128)S(1)}, u32[]{:S(2)}, u32[]{:S(2)}) collective-permute-start(f32[225,112]{1,0:T(8,128)S(1)} %add_add_fusion.1), channel_id=1, source_target_pairs={{0,8},{8,16},{16,24},{24,0},{1,9},{9,17},{17,25},{25,1},{2,10},{10... | collective-permute-start | bytes 302408 | tf_op jit(solution)/shard_map/ppermute | solution.py:54
  104.2 2.6 %collective-permute-start.13 = (f32[225,112]{1,0:T(8,128)S(1)}, f32[225,112]{1,0:T(8,128)S(1)}, u32[]{:S(2)}, u32[]{:S(2)}) collective-permute-start(f32[225,112]{1,0:T(8,128)S(1)} %add_add_fusion.1), channel_id=1, source_target_pairs={{0,16},{8,24},{16,0},{24,8},{1,17},{9,25},{17,1},{25,9},{2,18},{10... | collective-permute-start | bytes 302408 | tf_op jit(solution)/shard_map/ppermute | solution.py:54
  106.8 0.7 collective-permute-start.14
  107.5 3.0 %collective-permute-done.12 = f32[225,112]{1,0:T(8,128)S(1)} collective-permute-done((f32[225,112]{1,0:T(8,128)S(1)}, f32[225,112]{1,0:T(8,128)S(1)}, u32[]{:S(2)}, u32[]{:S(2)}) %collective-permute-start.12) | collective-permute-done | bytes 100832 | tf_op jit(solution)/shard_map/ppermute | solution.py:54
  110.5 3.6 %collective-permute-done.13 = f32[225,112]{1,0:T(8,128)S(1)} collective-permute-done((f32[225,112]{1,0:T(8,128)S(1)}, f32[225,112]{1,0:T(8,128)S(1)}, u32[]{:S(2)}, u32[]{:S(2)}) %collective-permute-start.13) | collective-permute-done | bytes 100832 | tf_op jit(solution)/shard_map/ppermute | solution.py:54
  114.1 0.2 collective-permute-done.14
  114.3 0.1 copy.37
  114.5 0.1 copy.38
  114.6 0.7 select_reduce_fusion
  115.9 0.8 select_add_fusion.a_ref
  116.7 28.4 %shard_map.18 = f32[256,256]{1,0:T(8,128)} custom-call(f32[224,224]{1,0:T(8,128)} %select_add_fusion.a_ref), custom_call_target="tpu_custom_call" | custom-call | tf_op jit(solution)/shard_map/pallas_call | solution.py:126
  145.2 10.2 %fusion = f32[32,256]{1,0:T(8,128)S(1)} fusion(f32[32,224,256]{2,1,0:T(8,128)} %get-tuple-element.7, f32[256,256]{1,0:T(8,128)} %shard_map.18), kind=kOutput, calls=%fused_computation.2 | convolution fusion | flops 4936213504 | bytes 14942208 | tf_op jit(solution)/shard_map/pbl,bj->pjl/dot_general | solution.py:282
  155.4 0.6 multiply_bitcast_fusion
  (15 shorter events, 0.3 us)
Async XLA Ops:
  6.6 22.1 %collective-permute-start = (bf16[32,224,15]{1,0,2:T(8,128)(2,1)}, bf16[32,224,15]{1,0,2:T(8,128)(2,1)}, u32[]{:S(2)}, u32[]{:S(2)}) collective-permute-start(bf16[32,224,15]{1,0,2:T(8,128)(2,1)} %copy.26), channel_id=1, source_target_pairs={{0,8},{8,16},{16,24},{1,9},{9,17},{17,25},{2,10},{10,18},{18,26},{... | collective-permute-start | bytes 645128 | tf_op jit(solution)/shard_map/ppermute | solution.py:174
  13.9 10.0 %copy-start = (bf16[256,32,224]{0,2,1:T(8,128)(2,1)S(1)}, bf16[256,32,224]{0,2,1:T(8,128)(2,1)}, u32[]{:S(2)}) copy-start(bf16[256,32,224]{0,2,1:T(8,128)(2,1)} %param.1) | copy-start | bytes 11010052
  13.9 17.2 %collective-permute-start.3 = (bf16[32,224,15]{1,0,2:T(8,128)(2,1)}, bf16[32,224,15]{1,0,2:T(8,128)(2,1)}, u32[]{:S(2)}, u32[]{:S(2)}) collective-permute-start(bf16[32,224,15]{1,0,2:T(8,128)(2,1)} %copy.28), channel_id=1, source_target_pairs={{8,0},{16,8},{24,16},{9,1},{17,9},{25,17},{10,2},{18,10},{26,18},{... | collective-permute-start | bytes 645128 | tf_op jit(solution)/shard_map/ppermute | solution.py:174
  19.5 44.2 %collective-permute-start.6 = (bf16[15,224,256]{2,1,0:T(8,128)(2,1)}, bf16[15,224,256]{2,1,0:T(8,128)(2,1)S(1)}, u32[]{:S(2)}, u32[]{:S(2)}) collective-permute-start(bf16[15,224,256]{2,1,0:T(8,128)(2,1)} %get-tuple-element.9), channel_id=1, source_target_pairs={{1,0},{2,1},{3,2},{4,3},{5,4},{6,5},{7,6},{9,8},{10,9},{11,10},{12... | collective-permute-start | bytes 5160968 | tf_op jit(solution)/shard_map/ppermute | solution.py:171
  20.7 46.0 %collective-permute-start.2 = (bf16[15,224,256]{2,1,0:T(8,128)(2,1)}, bf16[15,224,256]{2,1,0:T(8,128)(2,1)S(1)}, u32[]{:S(2)}, u32[]{:S(2)}) collective-permute-start(bf16[15,224,256]{2,1,0:T(8,128)(2,1)} %get-tuple-element.10), channel_id=1, source_target_pairs={{0,1},{1,2},{2,3},{3,4},{4,5},{5,6},{6,7},{8,9},{9,10},{10,11},{11... | collective-permute-start | bytes 5160968 | tf_op jit(solution)/shard_map/ppermute | solution.py:171
  29.8 15.5 %collective-permute-start.5 = (bf16[15,224,15]{1,2,0:T(8,128)(2,1)S(1)}, bf16[15,224,15]{1,2,0:T(8,128)(2,1)S(1)}, u32[]{:S(2)}, u32[]{:S(2)}) collective-permute-start(bf16[15,224,15]{1,2,0:T(8,128)(2,1)S(1)} %copy.32), channel_id=1, source_target_pairs={{1,0},{2,1},{3,2},{4,3},{5,4},{6,5},{7,6},{9,8},{10,9},{11,10},{12... | collective-permute-start | bytes 302408 | tf_op jit(solution)/shard_map/ppermute | solution.py:171
  32.2 32.2 %collective-permute-start.7 = (bf16[15,224,15]{1,2,0:T(8,128)(2,1)S(1)}, bf16[15,224,15]{1,2,0:T(8,128)(2,1)S(1)}, u32[]{:S(2)}, u32[]{:S(2)}) collective-permute-start(bf16[15,224,15]{1,2,0:T(8,128)(2,1)S(1)} %copy.33), channel_id=1, source_target_pairs={{1,0},{2,1},{3,2},{4,3},{5,4},{6,5},{7,6},{9,8},{10,9},{11,10},{12... | collective-permute-start | bytes 302408 | tf_op jit(solution)/shard_map/ppermute | solution.py:171
  33.5 6.6 %copy-start.1 = (f32[256,32,224]{0,2,1:T(8,128)S(1)}, f32[256,32,224]{0,2,1:T(8,128)}, u32[]{:S(2)}) copy-start(f32[256,32,224]{0,2,1:T(8,128)} %fusion.10) | copy-start | bytes 22020100
  33.5 29.5 %collective-permute-start.1 = (bf16[15,224,15]{1,2,0:T(8,128)(2,1)S(1)}, bf16[15,224,15]{1,2,0:T(8,128)(2,1)S(1)}, u32[]{:S(2)}, u32[]{:S(2)}) collective-permute-start(bf16[15,224,15]{1,2,0:T(8,128)(2,1)S(1)} %copy.27), channel_id=1, source_target_pairs={{0,1},{1,2},{2,3},{3,4},{4,5},{5,6},{6,7},{8,9},{9,10},{10,11},{11... | collective-permute-start | bytes 302408 | tf_op jit(solution)/shard_map/ppermute | solution.py:171
  45.3 22.1 %collective-permute-start.4 = (bf16[15,224,15]{1,2,0:T(8,128)(2,1)S(1)}, bf16[15,224,15]{1,2,0:T(8,128)(2,1)S(1)}, u32[]{:S(2)}, u32[]{:S(2)}) collective-permute-start(bf16[15,224,15]{1,2,0:T(8,128)(2,1)S(1)} %copy.29), channel_id=1, source_target_pairs={{0,1},{1,2},{2,3},{3,4},{4,5},{5,6},{6,7},{8,9},{9,10},{10,11},{11... | collective-permute-start | bytes 302408 | tf_op jit(solution)/shard_map/ppermute | solution.py:171
  88.6 1.4 collective-permute-start.8
  90.0 7.5 %collective-permute-start.10 = (f32[225,112]{1,0:T(8,128)S(1)}, f32[225,112]{1,0:T(8,128)S(1)}, u32[]{:S(2)}, u32[]{:S(2)}) collective-permute-start(f32[225,112]{1,0:T(8,128)S(1)} %fusion.43), channel_id=1, source_target_pairs={{0,4},{1,5},{2,6},{3,7},{4,0},{5,1},{6,2},{7,3},{8,12},{9,13},{10,... | collective-permute-start | bytes 302408 | tf_op jit(solution)/shard_map/ppermute | solution.py:54
  93.9 5.8 %collective-permute-start.11 = (f32[225,112]{1,0:T(8,128)S(1)}, f32[225,112]{1,0:T(8,128)S(1)}, u32[]{:S(2)}, u32[]{:S(2)}) collective-permute-start(f32[225,112]{1,0:T(8,128)S(1)} %fusion.43), channel_id=1, source_target_pairs={{0,6},{1,7},{2,0},{3,1},{4,2},{5,3},{6,4},{7,5},{8,14},{9,15},{10,... | collective-permute-start | bytes 302408 | tf_op jit(solution)/shard_map/ppermute | solution.py:54
  94.8 6.5 %collective-permute-start.9 = (f32[225,112]{1,0:T(8,128)S(1)}, f32[225,112]{1,0:T(8,128)S(1)}, u32[]{:S(2)}, u32[]{:S(2)}) collective-permute-start(f32[225,112]{1,0:T(8,128)S(1)} %fusion.43), channel_id=1, source_target_pairs={{0,2},{1,3},{2,4},{3,5},{4,6},{5,7},{6,0},{7,1},{8,10},{9,11},{10,... | collective-permute-start | bytes 302408 | tf_op jit(solution)/shard_map/ppermute | solution.py:54
  101.3 9.2 %collective-permute-start.12 = (f32[225,112]{1,0:T(8,128)S(1)}, f32[225,112]{1,0:T(8,128)S(1)}, u32[]{:S(2)}, u32[]{:S(2)}) collective-permute-start(f32[225,112]{1,0:T(8,128)S(1)} %add_add_fusion.1), channel_id=1, source_target_pairs={{0,8},{8,16},{16,24},{24,0},{1,9},{9,17},{17,25},{25,1},{2,10},{10... | collective-permute-start | bytes 302408 | tf_op jit(solution)/shard_map/ppermute | solution.py:54
  104.2 9.9 %collective-permute-start.13 = (f32[225,112]{1,0:T(8,128)S(1)}, f32[225,112]{1,0:T(8,128)S(1)}, u32[]{:S(2)}, u32[]{:S(2)}) collective-permute-start(f32[225,112]{1,0:T(8,128)S(1)} %add_add_fusion.1), channel_id=1, source_target_pairs={{0,16},{8,24},{16,0},{24,8},{1,17},{9,25},{17,1},{25,9},{2,18},{10... | collective-permute-start | bytes 302408 | tf_op jit(solution)/shard_map/ppermute | solution.py:54
  106.8 7.5 %collective-permute-start.14 = (f32[225,112]{1,0:T(8,128)S(1)}, f32[225,112]{1,0:T(8,128)S(1)}, u32[]{:S(2)}, u32[]{:S(2)}) collective-permute-start(f32[225,112]{1,0:T(8,128)S(1)} %add_add_fusion.1), channel_id=1, source_target_pairs={{0,24},{8,0},{16,8},{24,16},{1,25},{9,1},{17,9},{25,17},{2,26},{10... | collective-permute-start | bytes 302408 | tf_op jit(solution)/shard_map/ppermute | solution.py:54

commit v11 on v10

--- a/solution.py
+++ b/solution.py
@@ -181,16 +181,10 @@
     }
     top = fetch(planes[:, :, last], -1, 0)
     bottom = fetch(planes[:, :, first], 1, 0)
-    tops = {
-        "left": fetch(top[last], 0, -1),
-        "middle": top,
-        "right": fetch(top[first], 0, 1),
-    }
-    bottoms = {
-        "left": fetch(bottom[last], 0, -1),
-        "middle": bottom,
-        "right": fetch(bottom[first], 0, 1),
-    }
+    from_left = fetch(jnp.stack([top[last], bottom[last]]), 0, -1)
+    from_right = fetch(jnp.stack([top[first], bottom[first]]), 0, 1)
+    tops = {"left": from_left[0], "middle": top, "right": from_right[0]}
+    bottoms = {"left": from_left[1], "middle": bottom, "right": from_right[1]}
     return sides, tops, bottoms
 
 

time: 157 us -> 158 us (level)
    ppermute x6 -> x4, starting transfers between devices: 28.5 us -> 9.71 us  [fetch(): return lax.ppermute(piece, 'cross', pairs)]
    ppermute x1, starting transfers between devices: 0.1 us -> 17.3 us  [shards(): lax.ppermute(packed, 'cross', [(i, i ^ 1) for i in range(n_cross)])]
    slice x2 -> x1, local copies, waits for them, and re-layouts: 5.6 us -> 1.67 us  [halos(): bottom = fetch(planes[:, :, first], 1, 0)]
    slice x1 -> x2, local copies, waits for them, and re-layouts: 2.68 us -> 6.62 us  [halos(): top = fetch(planes[:, :, last], -1, 0)]
    another operation x0 -> x6, local copies, waits for them, and re-layouts: none -> 2.73 us  [the longest x4 2.36 us: halos(): from_right = fetch(jnp.stack([top[first], bottom[first]]), 0, 1)]
    ppermute x6, starting transfers between devices: 12.1 us -> 14 us  [ring_sum(): total = total + lax.ppermute(x, axis, pairs)]
  transfers between devices with their start and end apart: 15 -> 13, of which waited for: 7 -> 7; matrix products, arithmetic and copies ran while one was open for 16% -> 17% of each run, Pallas kernels for 0% -> 0%
where the time goes in v11:
time: 158 us; the launch traced here: 157 us
  starting transfers between devices  48.3 us (31%)
  Pallas kernels  41 us (26%)
  matrix products  33.2 us (21%)
  local copies, waits for them, and re-layouts  17.5 us (11%)
  waiting for transfers between devices  12.2 us (8%)
  other arithmetic  4.27 us (3%)
    pallas_call x1, Pallas kernels, spd_inverse(): pl.pallas_call(functools.partial(sweep_kernel, n), out_shape=jax.ShapeDty...  28.4 us
    dot_general x9, matrix products, sum_lines(): jnp.einsum('qbk,kl->qbl', values, w, preferred_element_type=jnp.float32)  18.7 us
    ppermute x1, starting transfers between devices, shards(): lax.ppermute(packed, 'cross', [(i, i ^ 1) for i in range(n_cross)])  17.3 us
    ppermute x6, starting transfers between devices, ring_sum(): total = total + lax.ppermute(x, axis, pairs)  14 us
    pallas_call x1, Pallas kernels, residuals(): pl.pallas_call(residual_kernel, grid=(bands // block,), in_specs=[spec(le...  12.6 us
    ppermute x6, waiting for transfers between devices, ring_sum(): total = total + lax.ppermute(x, axis, pairs)  11.3 us
    dot_general x1, matrix products, shards(): jnp.einsum('pbl,bj->pjl', residual, inverse, precision=highest, preferred...  10.2 us
    ppermute x4, starting transfers between devices, fetch(): return lax.ppermute(piece, 'cross', pairs)  9.71 us
  transfers between devices with their start and end apart: 13, of which 7 were waited for; matrix products, arithmetic and copies ran while one was open for 17% of the time, Pallas kernels for 0%

profile of v11, /device:TPU:0, one launch (start us, length us, event | category | flops | bytes accessed | tf_op | source)
XLA Modules:
  0.0 157.5 jit_solution(14312055948131186656)
XLA Ops:
  0.0 3.9 %fusion.43 = (bf16[32,224,15]{2,1,0:T(8,128)(2,1)}, bf16[32,224,15]{2,1,0:T(8,128)(2,1)S(1)}) fusion(bf16[32,224,256]{2,1,0:T(8,128)(2,1)} %bitcast.83), kind=kLoop, calls=%fused_computation.72 | loop fusion | bytes 860160 | tf_op jit(solution)/shard_map/slice | solution.py:182
  3.9 2.7 %copy.26 = bf16[32,224,15]{1,0,2:T(8,128)(2,1)} copy(bf16[32,224,15]{2,1,0:T(8,128)(2,1)} %get-tuple-element.11) | data formatting | bytes 430080 | tf_op jit(solution)/shard_map/slice | solution.py:182
  6.6 5.6 %collective-permute-start = (bf16[32,224,15]{1,0,2:T(8,128)(2,1)}, bf16[32,224,15]{1,0,2:T(8,128)(2,1)}, u32[]{:S(2)}, u32[]{:S(2)}) collective-permute-start(bf16[32,224,15]{1,0,2:T(8,128)(2,1)} %copy.26), channel_id=1, source_target_pairs={{0,8},{8,16},{16,24},{1,9},{9,17},{17,25},{2,10},{10,18},{18,26},{... | collective-permute-start | bytes 645128 | tf_op jit(solution)/shard_map/ppermute | solution.py:174
  12.2 1.7 %copy.27 = bf16[32,224,15]{1,0,2:T(8,128)(2,1)} copy(bf16[32,224,15]{2,1,0:T(8,128)(2,1)S(1)} %get-tuple-element.12) | data formatting | bytes 430080 | tf_op jit(solution)/shard_map/slice | solution.py:183
  13.9 1.5 collective-permute-start.1
  15.5 4.0 %fusion.42 = (bf16[15,224,256]{2,1,0:T(8,128)(2,1)}, bf16[15,224,256]{2,1,0:T(8,128)(2,1)}) fusion(bf16[32,224,256]{2,1,0:T(8,128)(2,1)} %bitcast.84), kind=kLoop, calls=%fused_computation.71 | loop fusion | bytes 6881280 | tf_op jit(solution)/shard_map/slice | solution.py:180
  19.5 1.3 collective-permute-start.5
  20.7 3.1 %collective-permute-start.3 = (bf16[15,224,256]{2,1,0:T(8,128)(2,1)}, bf16[15,224,256]{2,1,0:T(8,128)(2,1)S(1)}, u32[]{:S(2)}, u32[]{:S(2)}) collective-permute-start(bf16[15,224,256]{2,1,0:T(8,128)(2,1)} %get-tuple-element.10), channel_id=1, source_target_pairs={{0,1},{1,2},{2,3},{3,4},{4,5},{5,6},{6,7},{8,9},{9,10},{10,11},{11... | collective-permute-start | bytes 5160968 | tf_op jit(solution)/shard_map/ppermute | solution.py:171
  23.9 0.0 copy-done
  23.9 4.1 %fusion.12 = f32[256,32,224]{0,2,1:T(8,128)} fusion(bf16[256,32,224]{0,2,1:T(8,128)(2,1)S(1)} %copy-done), kind=kOutput, calls=%fused_computation.16 | convolution fusion | flops 939720704 | bytes 11010048 | tf_op jit(solution)/shard_map/qbk,kl->qbl/dot_general | solution.py:203
  28.0 0.7 broadcast_multiply_fusion.count_ref
  28.7 0.0 collective-permute-done
  28.7 1.0 slice_bitcast_fusion.1
  29.7 0.2 copy.34
  29.9 0.0 collective-permute-done.1
  29.9 1.0 slice_bitcast_fusion
  31.0 0.2 copy.35
  31.1 0.6 pad_maximum_fusion.1
  31.7 1.3 collective-permute-start.4
  33.0 0.2 copy.28
  33.2 0.2 copy.29
  33.4 0.6 pad_maximum_fusion
  34.0 0.0 copy-start.1
  34.0 4.0 %collective-permute-start.2 = (bf16[2,15,224,15]{2,0,3,1:T(2,128)(2,1)S(1)}, bf16[2,15,224,15]{2,0,3,1:T(2,128)(2,1)S(1)}, u32[]{:S(2)}, u32[]{:S(2)}) collective-permute-start(bf16[2,15,224,15]{2,0,3,1:T(2,128)(2,1)S(1)} %pad_maximum_fusion), channel_id=1, source_target_pairs={{0,1},{1,2},{2,3},{3,4},{4,5},{5,6},{6,7},{8,9},{9,10},{10,11},{11... | collective-permute-start | bytes 604808 | tf_op jit(solution)/shard_map/ppermute | solution.py:171
  38.0 2.1 %fusion.7 = f32[256,32,224]{0,2,1:T(8,128)S(1)} fusion(bf16[32,224,15]{1,0,2:T(8,128)(2,1)} %collective-permute-done), kind=kOutput, calls=%fused_computation.11 | convolution fusion | flops 55054080 | bytes 7555072 | tf_op jit(solution)/shard_map/qbk,kl->qbl/dot_general | solution.py:203
  40.1 0.0 copy-done.1
  40.1 5.3 %add_bitcast_fusion.middle_ref = f32[32,224,256]{2,1,0:T(8,128)} fusion(f32[256,32,224]{0,2,1:T(8,128)S(1)} %fusion.7, f32[256,32,224]{0,2,1:T(8,128)S(1)} %copy-done.1, bf16[32,224,15]{1,0,2:T(8,128)(2,1)} %collective-permute-done.1, s32[15]{0:T(128)S(1)} %iota_add_fusion), kind=kOutput, calls=%fused_computation.3 | convolution fusion | flops 58724096 | bytes 22235196 | tf_op jit(solution)/shard_map/qbk,kl->qbl/dot_general | solution.py:203
  45.5 0.0 collective-permute-done.4
  45.5 0.3 fusion.44
  45.8 0.0 collective-permute-done.2
  45.8 0.3 fusion.45
  46.1 0.5 fusion.22
  46.7 0.5 fusion.24
  47.2 0.0 collective-permute-done.5
  47.2 0.6 fusion.10
  47.8 2.4 %fusion.1.right_ref = f32[15,224,256]{2,1,0:T(8,128)} fusion(f32[15,224,256]{2,1,0:T(8,128)S(1)} %fusion.22, f32[256,15,224]{0,2,1:T(8,128)S(1)} %fusion.10, bf16[1,15,224,15]{2,0,3,1:T(2,128)(2,1)S(1)} %get-tuple-element.17, s32[15]{0:T(128)S(1)} %iota_add_fusion), kind=kOutput, calls=%fused_computation.5 | convolution fusion | flops 27528960 | bytes 10422780 | tf_op jit(solution)/shard_map/qbk,kl->qbl/dot_general | solution.py:203
  50.2 0.0 collective-permute-done.3
  50.2 0.6 fusion.14
  50.9 2.5 %fusion.2.left_ref = f32[15,224,256]{2,1,0:T(8,128)} fusion(f32[15,224,256]{2,1,0:T(8,128)S(1)} %fusion.24, f32[256,15,224]{0,2,1:T(8,128)S(1)} %fusion.14, bf16[1,15,224,15]{2,0,3,1:T(2,128)(2,1)S(1)} %get-tuple-element.19, s32[15]{0:T(128)S(1)} %iota_add_fusion), kind=kOutput, calls=%fused_computation.7 | convolution fusion | flops 27528960 | bytes 10422780 | tf_op jit(solution)/shard_map/qbk,kl->qbl/dot_general | solution.py:203
  53.3 12.6 %shard_map.17 = (f32[32,224,256]{2,1,0:T(8,128)}, bf16[32,224,256]{2,1,0:T(8,128)(2,1)}) custom-call(f32[15,224,256]{2,1,0:T(8,128)} %fusion.2.left_ref, f32[32,224,256]{2,1,0:T(8,128)} %add_bitcast_fusion.middle_ref, f32[15,224,256]{2,1,0:T(8,128)} %fusion.1.right_ref, bf16[32,224,256]{2,1,0:T(8,128)(2,1)} %bitcast.85, ...), custom_call_target="tpu_custom_call" | custom-call | tf_op jit(solution)/shard_map/pallas_call | solution.py:237
  65.9 4.3 %convolution_bitcast_fusion = f32[224,224]{1,0:T(8,128)S(1)} fusion(bf16[32,224,256]{2,1,0:T(8,128)(2,1)} %get-tuple-element.8), kind=kOutput, calls=%fused_computation.8 | convolution fusion | flops 822083584 | bytes 3870720 | tf_op jit(solution)/shard_map/pjl,pkl->jk/dot_general | solution.py:266
  70.2 0.1 fusion.46
  70.3 1.7 %gather_fusion = f32[112]{0:T(128)S(1)} fusion(f32[112,112]{1,0:T(8,128)S(1)} %get-tuple-element.23, s32[112]{0:T(128)S(1)} %or_bitcast_fusion), kind=kCustom, calls=%fused_computation | custom fusion | bytes 1792 | tf_op jit(solution)/shard_map/jit(diagonal)/cond/branch_0_fun/gather | solution.py:64
  72.0 17.3 %collective-permute-start.6 = (f32[225,112]{1,0:T(8,128)S(1)}, f32[225,112]{1,0:T(8,128)S(1)}, u32[]{:S(2)}, u32[]{:S(2)}) collective-permute-start(f32[225,112]{1,0:T(8,128)S(1)} %pad_maximum_fusion.2), channel_id=1, source_target_pairs={{0,1},{1,0},{2,3},{3,2},{4,5},{5,4},{6,7},{7,6},{8,9},{9,8},{10,11... | collective-permute-start | bytes 302408 | tf_op jit(solution)/shard_map/ppermute | solution.py:270
  89.4 1.0 collective-permute-done.6
  90.4 3.3 %collective-permute-start.7 = (f32[225,112]{1,0:T(8,128)S(1)}, f32[225,112]{1,0:T(8,128)S(1)}, u32[]{:S(2)}, u32[]{:S(2)}) collective-permute-start(f32[225,112]{1,0:T(8,128)S(1)} %fusion.41), channel_id=1, source_target_pairs={{0,2},{1,3},{2,4},{3,5},{4,6},{5,7},{6,0},{7,1},{8,10},{9,11},{10,... | collective-permute-start | bytes 302408 | tf_op jit(solution)/shard_map/ppermute | solution.py:54
  93.6 3.1 %collective-permute-start.8 = (f32[225,112]{1,0:T(8,128)S(1)}, f32[225,112]{1,0:T(8,128)S(1)}, u32[]{:S(2)}, u32[]{:S(2)}) collective-permute-start(f32[225,112]{1,0:T(8,128)S(1)} %fusion.41), channel_id=1, source_target_pairs={{0,4},{1,5},{2,6},{3,7},{4,0},{5,1},{6,2},{7,3},{8,12},{9,13},{10,... | collective-permute-start | bytes 302408 | tf_op jit(solution)/shard_map/ppermute | solution.py:54
  96.7 1.7 %collective-permute-start.9 = (f32[225,112]{1,0:T(8,128)S(1)}, f32[225,112]{1,0:T(8,128)S(1)}, u32[]{:S(2)}, u32[]{:S(2)}) collective-permute-start(f32[225,112]{1,0:T(8,128)S(1)} %fusion.41), channel_id=1, source_target_pairs={{0,6},{1,7},{2,0},{3,1},{4,2},{5,3},{6,4},{7,5},{8,14},{9,15},{10,... | collective-permute-start | bytes 302408 | tf_op jit(solution)/shard_map/ppermute | solution.py:54
  98.5 1.7 %collective-permute-done.7 = f32[225,112]{1,0:T(8,128)S(1)} collective-permute-done((f32[225,112]{1,0:T(8,128)S(1)}, f32[225,112]{1,0:T(8,128)S(1)}, u32[]{:S(2)}, u32[]{:S(2)}) %collective-permute-start.7) | collective-permute-done | bytes 100832 | tf_op jit(solution)/shard_map/ppermute | solution.py:54
  100.2 2.0 %collective-permute-done.8 = f32[225,112]{1,0:T(8,128)S(1)} collective-permute-done((f32[225,112]{1,0:T(8,128)S(1)}, f32[225,112]{1,0:T(8,128)S(1)}, u32[]{:S(2)}, u32[]{:S(2)}) %collective-permute-start.8) | collective-permute-done | bytes 100832 | tf_op jit(solution)/shard_map/ppermute | solution.py:54
  102.2 0.6 collective-permute-done.9
  102.9 2.7 %collective-permute-start.10 = (f32[225,112]{1,0:T(8,128)S(1)}, f32[225,112]{1,0:T(8,128)S(1)}, u32[]{:S(2)}, u32[]{:S(2)}) collective-permute-start(f32[225,112]{1,0:T(8,128)S(1)} %add_add_fusion.1), channel_id=1, source_target_pairs={{0,8},{8,16},{16,24},{24,0},{1,9},{9,17},{17,25},{25,1},{2,10},{10... | collective-permute-start | bytes 302408 | tf_op jit(solution)/shard_map/ppermute | solution.py:54
  105.6 2.6 %collective-permute-start.11 = (f32[225,112]{1,0:T(8,128)S(1)}, f32[225,112]{1,0:T(8,128)S(1)}, u32[]{:S(2)}, u32[]{:S(2)}) collective-permute-start(f32[225,112]{1,0:T(8,128)S(1)} %add_add_fusion.1), channel_id=1, source_target_pairs={{0,16},{8,24},{16,0},{24,8},{1,17},{9,25},{17,1},{25,9},{2,18},{10... | collective-permute-start | bytes 302408 | tf_op jit(solution)/shard_map/ppermute | solution.py:54
  108.2 0.6 collective-permute-start.12
  108.9 3.1 %collective-permute-done.10 = f32[225,112]{1,0:T(8,128)S(1)} collective-permute-done((f32[225,112]{1,0:T(8,128)S(1)}, f32[225,112]{1,0:T(8,128)S(1)}, u32[]{:S(2)}, u32[]{:S(2)}) %collective-permute-start.10) | collective-permute-done | bytes 100832 | tf_op jit(solution)/shard_map/ppermute | solution.py:54
  111.9 3.6 %collective-permute-done.11 = f32[225,112]{1,0:T(8,128)S(1)} collective-permute-done((f32[225,112]{1,0:T(8,128)S(1)}, f32[225,112]{1,0:T(8,128)S(1)}, u32[]{:S(2)}, u32[]{:S(2)}) %collective-permute-start.11) | collective-permute-done | bytes 100832 | tf_op jit(solution)/shard_map/ppermute | solution.py:54
  115.6 0.2 collective-permute-done.12
  115.8 0.1 copy.41
  115.9 0.1 copy.42
  116.0 0.7 select_reduce_fusion
  117.4 0.8 select_add_fusion.a_ref
  118.2 28.4 %shard_map.18 = f32[256,256]{1,0:T(8,128)} custom-call(f32[224,224]{1,0:T(8,128)} %select_add_fusion.a_ref), custom_call_target="tpu_custom_call" | custom-call | tf_op jit(solution)/shard_map/pallas_call | solution.py:126
  146.6 10.2 %fusion = f32[32,256]{1,0:T(8,128)S(1)} fusion(f32[32,224,256]{2,1,0:T(8,128)} %get-tuple-element.7, f32[256,256]{1,0:T(8,128)} %shard_map.18), kind=kOutput, calls=%fused_computation.2 | convolution fusion | flops 4936213504 | bytes 14942208 | tf_op jit(solution)/shard_map/pbl,bj->pjl/dot_general | solution.py:276
  156.8 0.6 multiply_bitcast_fusion
  (12 shorter events, 0.2 us)
Async XLA Ops:
  6.6 22.1 %collective-permute-start = (bf16[32,224,15]{1,0,2:T(8,128)(2,1)}, bf16[32,224,15]{1,0,2:T(8,128)(2,1)}, u32[]{:S(2)}, u32[]{:S(2)}) collective-permute-start(bf16[32,224,15]{1,0,2:T(8,128)(2,1)} %copy.26), channel_id=1, source_target_pairs={{0,8},{8,16},{16,24},{1,9},{9,17},{17,25},{2,10},{10,18},{18,26},{... | collective-permute-start | bytes 645128 | tf_op jit(solution)/shard_map/ppermute | solution.py:174
  13.9 10.0 %copy-start = (bf16[256,32,224]{0,2,1:T(8,128)(2,1)S(1)}, bf16[256,32,224]{0,2,1:T(8,128)(2,1)}, u32[]{:S(2)}) copy-start(bf16[256,32,224]{0,2,1:T(8,128)(2,1)} %param.1) | copy-start | bytes 11010052
  13.9 16.0 %collective-permute-start.1 = (bf16[32,224,15]{1,0,2:T(8,128)(2,1)}, bf16[32,224,15]{1,0,2:T(8,128)(2,1)}, u32[]{:S(2)}, u32[]{:S(2)}) collective-permute-start(bf16[32,224,15]{1,0,2:T(8,128)(2,1)} %copy.27), channel_id=1, source_target_pairs={{8,0},{16,8},{24,16},{9,1},{17,9},{25,17},{10,2},{18,10},{26,18},{... | collective-permute-start | bytes 645128 | tf_op jit(solution)/shard_map/ppermute | solution.py:174
  19.5 27.7 %collective-permute-start.5 = (bf16[15,224,256]{2,1,0:T(8,128)(2,1)}, bf16[15,224,256]{2,1,0:T(8,128)(2,1)S(1)}, u32[]{:S(2)}, u32[]{:S(2)}) collective-permute-start(bf16[15,224,256]{2,1,0:T(8,128)(2,1)} %get-tuple-element.9), channel_id=1, source_target_pairs={{1,0},{2,1},{3,2},{4,3},{5,4},{6,5},{7,6},{9,8},{10,9},{11,10},{12... | collective-permute-start | bytes 5160968 | tf_op jit(solution)/shard_map/ppermute | solution.py:171
  20.7 29.5 %collective-permute-start.3 = (bf16[15,224,256]{2,1,0:T(8,128)(2,1)}, bf16[15,224,256]{2,1,0:T(8,128)(2,1)S(1)}, u32[]{:S(2)}, u32[]{:S(2)}) collective-permute-start(bf16[15,224,256]{2,1,0:T(8,128)(2,1)} %get-tuple-element.10), channel_id=1, source_target_pairs={{0,1},{1,2},{2,3},{3,4},{4,5},{5,6},{6,7},{8,9},{9,10},{10,11},{11... | collective-permute-start | bytes 5160968 | tf_op jit(solution)/shard_map/ppermute | solution.py:171
  31.7 13.7 %collective-permute-start.4 = (bf16[2,15,224,15]{2,0,3,1:T(2,128)(2,1)S(1)}, bf16[2,15,224,15]{2,0,3,1:T(2,128)(2,1)S(1)}, u32[]{:S(2)}, u32[]{:S(2)}) collective-permute-start(bf16[2,15,224,15]{2,0,3,1:T(2,128)(2,1)S(1)} %pad_maximum_fusion.1), channel_id=1, source_target_pairs={{1,0},{2,1},{3,2},{4,3},{5,4},{6,5},{7,6},{9,8},{10,9},{11,10},{12... | collective-permute-start | bytes 604808 | tf_op jit(solution)/shard_map/ppermute | solution.py:171
  34.0 6.2 %copy-start.1 = (f32[256,32,224]{0,2,1:T(8,128)S(1)}, f32[256,32,224]{0,2,1:T(8,128)}, u32[]{:S(2)}) copy-start(f32[256,32,224]{0,2,1:T(8,128)} %fusion.12) | copy-start | bytes 22020100
  34.0 11.8 %collective-permute-start.2 = (bf16[2,15,224,15]{2,0,3,1:T(2,128)(2,1)S(1)}, bf16[2,15,224,15]{2,0,3,1:T(2,128)(2,1)S(1)}, u32[]{:S(2)}, u32[]{:S(2)}) collective-permute-start(bf16[2,15,224,15]{2,0,3,1:T(2,128)(2,1)S(1)} %pad_maximum_fusion), channel_id=1, source_target_pairs={{0,1},{1,2},{2,3},{3,4},{4,5},{5,6},{6,7},{8,9},{9,10},{10,11},{11... | collective-permute-start | bytes 604808 | tf_op jit(solution)/shard_map/ppermute | solution.py:171
  72.0 18.3 %collective-permute-start.6 = (f32[225,112]{1,0:T(8,128)S(1)}, f32[225,112]{1,0:T(8,128)S(1)}, u32[]{:S(2)}, u32[]{:S(2)}) collective-permute-start(f32[225,112]{1,0:T(8,128)S(1)} %pad_maximum_fusion.2), channel_id=1, source_target_pairs={{0,1},{1,0},{2,3},{3,2},{4,5},{5,4},{6,7},{7,6},{8,9},{9,8},{10,11... | collective-permute-start | bytes 302408 | tf_op jit(solution)/shard_map/ppermute | solution.py:270
  90.4 9.8 %collective-permute-start.7 = (f32[225,112]{1,0:T(8,128)S(1)}, f32[225,112]{1,0:T(8,128)S(1)}, u32[]{:S(2)}, u32[]{:S(2)}) collective-permute-start(f32[225,112]{1,0:T(8,128)S(1)} %fusion.41), channel_id=1, source_target_pairs={{0,2},{1,3},{2,4},{3,5},{4,6},{5,7},{6,0},{7,1},{8,10},{9,11},{10,... | collective-permute-start | bytes 302408 | tf_op jit(solution)/shard_map/ppermute | solution.py:54
  93.6 8.6 %collective-permute-start.8 = (f32[225,112]{1,0:T(8,128)S(1)}, f32[225,112]{1,0:T(8,128)S(1)}, u32[]{:S(2)}, u32[]{:S(2)}) collective-permute-start(f32[225,112]{1,0:T(8,128)S(1)} %fusion.41), channel_id=1, source_target_pairs={{0,4},{1,5},{2,6},{3,7},{4,0},{5,1},{6,2},{7,3},{8,12},{9,13},{10,... | collective-permute-start | bytes 302408 | tf_op jit(solution)/shard_map/ppermute | solution.py:54
  96.7 6.1 %collective-permute-start.9 = (f32[225,112]{1,0:T(8,128)S(1)}, f32[225,112]{1,0:T(8,128)S(1)}, u32[]{:S(2)}, u32[]{:S(2)}) collective-permute-start(f32[225,112]{1,0:T(8,128)S(1)} %fusion.41), channel_id=1, source_target_pairs={{0,6},{1,7},{2,0},{3,1},{4,2},{5,3},{6,4},{7,5},{8,14},{9,15},{10,... | collective-permute-start | bytes 302408 | tf_op jit(solution)/shard_map/ppermute | solution.py:54
  102.9 9.0 %collective-permute-start.10 = (f32[225,112]{1,0:T(8,128)S(1)}, f32[225,112]{1,0:T(8,128)S(1)}, u32[]{:S(2)}, u32[]{:S(2)}) collective-permute-start(f32[225,112]{1,0:T(8,128)S(1)} %add_add_fusion.1), channel_id=1, source_target_pairs={{0,8},{8,16},{16,24},{24,0},{1,9},{9,17},{17,25},{25,1},{2,10},{10... | collective-permute-start | bytes 302408 | tf_op jit(solution)/shard_map/ppermute | solution.py:54
  105.6 10.0 %collective-permute-start.11 = (f32[225,112]{1,0:T(8,128)S(1)}, f32[225,112]{1,0:T(8,128)S(1)}, u32[]{:S(2)}, u32[]{:S(2)}) collective-permute-start(f32[225,112]{1,0:T(8,128)S(1)} %add_add_fusion.1), channel_id=1, source_target_pairs={{0,16},{8,24},{16,0},{24,8},{1,17},{9,25},{17,1},{25,9},{2,18},{10... | collective-permute-start | bytes 302408 | tf_op jit(solution)/shard_map/ppermute | solution.py:54
  108.2 7.5 %collective-permute-start.12 = (f32[225,112]{1,0:T(8,128)S(1)}, f32[225,112]{1,0:T(8,128)S(1)}, u32[]{:S(2)}, u32[]{:S(2)}) collective-permute-start(f32[225,112]{1,0:T(8,128)S(1)} %add_add_fusion.1), channel_id=1, source_target_pairs={{0,24},{8,0},{16,8},{24,16},{1,25},{9,1},{17,9},{25,17},{2,26},{10... | collective-permute-start | bytes 302408 | tf_op jit(solution)/shard_map/ppermute | solution.py:54

commit v12 on v10

--- a/solution.py
+++ b/solution.py
@@ -237,7 +237,7 @@
 
 def residuals(left, middle, right, planes, count):
     width, bands, lines = middle.shape
-    block = 32 if bands % 32 == 0 else bands
+    block = next((b for b in (56, 32, 16, 8) if bands % b == 0), bands)
     spec = lambda n: pl.BlockSpec((n, block, lines), lambda i: (0, i, 0))
     count_spec = pl.BlockSpec((width, 1, lines), lambda i: (0, 0, 0))
     return pl.pallas_call(

time: 157 us -> 154 us (0.981)
  Pallas kernels: 41 us -> 38.7 us
    pallas_call x1, Pallas kernels: 12.6 us -> 10.3 us  [residuals(): pl.pallas_call(residual_kernel, grid=(bands // block,), in_specs=[spec(le...]
where the time goes in v12:
time: 154 us; the launch traced here: 153 us
  starting transfers between devices  47.6 us (31%)
  Pallas kernels  38.7 us (25%)
  matrix products  33.3 us (22%)
  local copies, waits for them, and re-layouts  16.3 us (11%)
  waiting for transfers between devices  13.5 us (9%)
  other arithmetic  3.12 us (2%)
    ppermute x6, starting transfers between devices, fetch(): return lax.ppermute(piece, 'cross', pairs)  28.5 us
    pallas_call x1, Pallas kernels, spd_inverse(): pl.pallas_call(functools.partial(sweep_kernel, n), out_shape=jax.ShapeDty...  28.4 us
    dot_general x9, matrix products, sum_lines(): jnp.einsum('qbk,kl->qbl', values, w, preferred_element_type=jnp.float32)  18.8 us
    ppermute x6, waiting for transfers between devices, ring_sum(): total = total + lax.ppermute(x, axis, pairs)  12.1 us
    ppermute x6, starting transfers between devices, ring_sum(): total = total + lax.ppermute(x, axis, pairs)  11.9 us
    pallas_call x1, Pallas kernels, residuals(): pl.pallas_call(residual_kernel, grid=(bands // block,), in_specs=[spec(le...  10.3 us
    dot_general x1, matrix products, shards(): jnp.einsum('pbl,bj->pjl', residual, inverse, precision=highest, preferred...  10.2 us
    ppermute x2, starting transfers between devices, fetch(): return lax.ppermute(piece, 'track', pairs)  7.16 us
  transfers between devices with their start and end apart: 15, of which 7 were waited for; matrix products, arithmetic and copies ran while one was open for 16% of the time, Pallas kernels for 0%

profile of v12, /device:TPU:0, one launch (start us, length us, event | category | flops | bytes accessed | tf_op | source)
XLA Modules:
  0.0 153.5 jit_solution(16507189832481575606)
XLA Ops:
  0.0 3.9 %fusion.45 = (bf16[32,224,15]{2,1,0:T(8,128)(2,1)S(1)}, bf16[32,224,15]{2,1,0:T(8,128)(2,1)}) fusion(bf16[32,224,256]{2,1,0:T(8,128)(2,1)} %bitcast.63), kind=kLoop, calls=%fused_computation.60 | loop fusion | bytes 860160 | tf_op jit(solution)/shard_map/slice | solution.py:183
  3.9 2.7 %copy.26 = bf16[32,224,15]{1,0,2:T(8,128)(2,1)} copy(bf16[32,224,15]{2,1,0:T(8,128)(2,1)} %get-tuple-element.12) | data formatting | bytes 430080 | tf_op jit(solution)/shard_map/slice | solution.py:182
  6.6 5.6 %collective-permute-start = (bf16[32,224,15]{1,0,2:T(8,128)(2,1)}, bf16[32,224,15]{1,0,2:T(8,128)(2,1)}, u32[]{:S(2)}, u32[]{:S(2)}) collective-permute-start(bf16[32,224,15]{1,0,2:T(8,128)(2,1)} %copy.26), channel_id=1, source_target_pairs={{0,8},{8,16},{16,24},{1,9},{9,17},{17,25},{2,10},{10,18},{18,26},{... | collective-permute-start | bytes 645128 | tf_op jit(solution)/shard_map/ppermute | solution.py:174
  12.2 1.7 %copy.28 = bf16[32,224,15]{1,0,2:T(8,128)(2,1)} copy(bf16[32,224,15]{2,1,0:T(8,128)(2,1)S(1)} %get-tuple-element.11) | data formatting | bytes 430080 | tf_op jit(solution)/shard_map/slice | solution.py:183
  13.9 0.0 copy-start
  13.9 1.5 %collective-permute-start.3 = (bf16[32,224,15]{1,0,2:T(8,128)(2,1)}, bf16[32,224,15]{1,0,2:T(8,128)(2,1)}, u32[]{:S(2)}, u32[]{:S(2)}) collective-permute-start(bf16[32,224,15]{1,0,2:T(8,128)(2,1)} %copy.28), channel_id=1, source_target_pairs={{8,0},{16,8},{24,16},{9,1},{17,9},{25,17},{10,2},{18,10},{26,18},{... | collective-permute-start | bytes 645128 | tf_op jit(solution)/shard_map/ppermute | solution.py:174
  15.5 4.0 %fusion.44 = (bf16[15,224,256]{2,1,0:T(8,128)(2,1)}, bf16[15,224,256]{2,1,0:T(8,128)(2,1)}) fusion(bf16[32,224,256]{2,1,0:T(8,128)(2,1)} %bitcast.64), kind=kLoop, calls=%fused_computation.59 | loop fusion | bytes 6881280 | tf_op jit(solution)/shard_map/slice | solution.py:180
  19.5 1.3 collective-permute-start.6
  20.7 3.1 %collective-permute-start.2 = (bf16[15,224,256]{2,1,0:T(8,128)(2,1)}, bf16[15,224,256]{2,1,0:T(8,128)(2,1)S(1)}, u32[]{:S(2)}, u32[]{:S(2)}) collective-permute-start(bf16[15,224,256]{2,1,0:T(8,128)(2,1)} %get-tuple-element.10), channel_id=1, source_target_pairs={{0,1},{1,2},{2,3},{3,4},{4,5},{5,6},{6,7},{8,9},{9,10},{10,11},{11... | collective-permute-start | bytes 5160968 | tf_op jit(solution)/shard_map/ppermute | solution.py:171
  23.9 0.0 copy-done
  23.9 4.1 %fusion.10 = f32[256,32,224]{0,2,1:T(8,128)} fusion(bf16[256,32,224]{0,2,1:T(8,128)(2,1)S(1)} %copy-done), kind=kOutput, calls=%fused_computation.14 | convolution fusion | flops 939720704 | bytes 11010048 | tf_op jit(solution)/shard_map/qbk,kl->qbl/dot_general | solution.py:209
  28.0 0.7 broadcast_multiply_fusion.count_ref
  28.7 0.0 collective-permute-done
  28.7 1.0 fusion.47
  29.8 1.3 collective-permute-start.5
  31.1 0.0 collective-permute-done.3
  31.1 1.0 fusion.46
  32.2 1.3 collective-permute-start.7
  33.5 0.0 copy-start.1
  33.5 4.4 %collective-permute-start.1 = (bf16[15,224,15]{1,2,0:T(8,128)(2,1)S(1)}, bf16[15,224,15]{1,2,0:T(8,128)(2,1)S(1)}, u32[]{:S(2)}, u32[]{:S(2)}) collective-permute-start(bf16[15,224,15]{1,2,0:T(8,128)(2,1)S(1)} %copy.27), channel_id=1, source_target_pairs={{0,1},{1,2},{2,3},{3,4},{4,5},{5,6},{6,7},{8,9},{9,10},{10,11},{11... | collective-permute-start | bytes 302408 | tf_op jit(solution)/shard_map/ppermute | solution.py:171
  38.0 2.1 %fusion.5 = f32[256,32,224]{0,2,1:T(8,128)S(1)} fusion(bf16[32,224,15]{1,0,2:T(8,128)(2,1)} %collective-permute-done), kind=kOutput, calls=%fused_computation.9 | convolution fusion | flops 55054080 | bytes 7555072 | tf_op jit(solution)/shard_map/qbk,kl->qbl/dot_general | solution.py:209
  40.1 0.0 copy-done.1
  40.1 5.1 %add_bitcast_fusion.middle_ref = f32[32,224,256]{2,1,0:T(8,128)} fusion(f32[256,32,224]{0,2,1:T(8,128)S(1)} %fusion.5, f32[256,32,224]{0,2,1:T(8,128)S(1)} %copy-done.1, bf16[32,224,15]{1,0,2:T(8,128)(2,1)} %collective-permute-done.3, s32[15]{0:T(128)S(1)} %iota_add_fusion), kind=kOutput, calls=%fused_computation.3 | convolution fusion | flops 58724096 | bytes 22235196 | tf_op jit(solution)/shard_map/qbk,kl->qbl/dot_general | solution.py:209
  45.3 0.0 collective-permute-done.5
  45.3 17.0 %collective-permute-start.4 = (bf16[15,224,15]{1,2,0:T(8,128)(2,1)S(1)}, bf16[15,224,15]{1,2,0:T(8,128)(2,1)S(1)}, u32[]{:S(2)}, u32[]{:S(2)}) collective-permute-start(bf16[15,224,15]{1,2,0:T(8,128)(2,1)S(1)} %copy.29), channel_id=1, source_target_pairs={{0,1},{1,2},{2,3},{3,4},{4,5},{5,6},{6,7},{8,9},{9,10},{10,11},{11... | collective-permute-start | bytes 302408 | tf_op jit(solution)/shard_map/ppermute | solution.py:171
  62.3 0.7 fusion.21
  63.0 0.0 collective-permute-done.1
  63.0 0.7 fusion.24
  63.7 0.0 collective-permute-done.6
  63.7 0.6 fusion.8
  64.3 0.0 collective-permute-done.7
  64.3 2.4 %add_bitcast_fusion.1.right_ref = f32[15,224,256]{2,1,0:T(8,128)} fusion(f32[256,15,224]{0,2,1:T(8,128)S(1)} %fusion.21, f32[256,15,224]{0,2,1:T(8,128)S(1)} %fusion.8, bf16[15,224,15]{1,2,0:T(8,128)(2,1)S(1)} %collective-permute-done.7, s32[15]{0:T(128)S(1)} %iota_add_fusion), kind=kOutput, calls=%fused_computation.4 | convolution fusion | flops 27528960 | bytes 10422780 | tf_op jit(solution)/shard_map/qbk,kl->qbl/dot_general | solution.py:209
  66.8 0.0 collective-permute-done.2
  66.8 0.6 fusion.12
  67.4 0.0 collective-permute-done.4
  67.4 2.5 %add_bitcast_fusion.2.left_ref = f32[15,224,256]{2,1,0:T(8,128)} fusion(f32[256,15,224]{0,2,1:T(8,128)S(1)} %fusion.24, f32[256,15,224]{0,2,1:T(8,128)S(1)} %fusion.12, bf16[15,224,15]{1,2,0:T(8,128)(2,1)S(1)} %collective-permute-done.4, s32[15]{0:T(128)S(1)} %iota_add_fusion), kind=kOutput, calls=%fused_computation.5 | convolution fusion | flops 27528960 | bytes 10422780 | tf_op jit(solution)/shard_map/qbk,kl->qbl/dot_general | solution.py:209
  69.9 10.3 %shard_map.17 = (f32[32,224,256]{2,1,0:T(8,128)}, bf16[32,224,256]{2,1,0:T(8,128)(2,1)}) custom-call(f32[15,224,256]{2,1,0:T(8,128)} %add_bitcast_fusion.2.left_ref, f32[32,224,256]{2,1,0:T(8,128)} %add_bitcast_fusion.middle_ref, f32[15,224,256]{2,1,0:T(8,128)} %add_bitcast_fusion.1.right_ref, bf16[32,224,256]{2,1,0:T(8,128)(2,1)} %bitcast.65, ...), custom_call_target="tpu_custom_call" | custom-call | tf_op jit(solution)/shard_map/pallas_call | solution.py:243
  80.1 4.3 %convolution_bitcast_fusion = f32[224,224]{1,0:T(8,128)S(1)} fusion(bf16[32,224,256]{2,1,0:T(8,128)(2,1)} %get-tuple-element.8), kind=kOutput, calls=%fused_computation.6 | convolution fusion | flops 822083584 | bytes 3870720 | tf_op jit(solution)/shard_map/pjl,pkl->jk/dot_general | solution.py:272
  84.4 0.1 fusion.48
  84.5 1.7 %gather_fusion = f32[112]{0:T(128)S(1)} fusion(f32[112,112]{1,0:T(8,128)S(1)} %get-tuple-element.19, s32[112]{0:T(128)S(1)} %or_bitcast_fusion), kind=kCustom, calls=%fused_computation | custom fusion | bytes 1792 | tf_op jit(solution)/shard_map/jit(diagonal)/cond/branch_0_fun/gather | solution.py:64
  86.2 0.1 collective-permute-start.8
  86.3 1.3 collective-permute-done.8
  87.7 3.9 %collective-permute-start.10 = (f32[225,112]{1,0:T(8,128)S(1)}, f32[225,112]{1,0:T(8,128)S(1)}, u32[]{:S(2)}, u32[]{:S(2)}) collective-permute-start(f32[225,112]{1,0:T(8,128)S(1)} %fusion.43), channel_id=1, source_target_pairs={{0,4},{1,5},{2,6},{3,7},{4,0},{5,1},{6,2},{7,3},{8,12},{9,13},{10,... | collective-permute-start | bytes 302408 | tf_op jit(solution)/shard_map/ppermute | solution.py:54
  91.6 0.8 collective-permute-start.11
  92.4 1.2 collective-permute-start.9
  93.6 1.5 collective-permute-done.10
  95.1 2.2 %collective-permute-done.11 = f32[225,112]{1,0:T(8,128)S(1)} collective-permute-done((f32[225,112]{1,0:T(8,128)S(1)}, f32[225,112]{1,0:T(8,128)S(1)}, u32[]{:S(2)}, u32[]{:S(2)}) %collective-permute-start.11) | collective-permute-done | bytes 100832 | tf_op jit(solution)/shard_map/ppermute | solution.py:54
  97.4 1.5 %collective-permute-done.9 = f32[225,112]{1,0:T(8,128)S(1)} collective-permute-done((f32[225,112]{1,0:T(8,128)S(1)}, f32[225,112]{1,0:T(8,128)S(1)}, u32[]{:S(2)}, u32[]{:S(2)}) %collective-permute-start.9) | collective-permute-done | bytes 100832 | tf_op jit(solution)/shard_map/ppermute | solution.py:54
  98.9 2.7 %collective-permute-start.12 = (f32[225,112]{1,0:T(8,128)S(1)}, f32[225,112]{1,0:T(8,128)S(1)}, u32[]{:S(2)}, u32[]{:S(2)}) collective-permute-start(f32[225,112]{1,0:T(8,128)S(1)} %add_add_fusion.1), channel_id=1, source_target_pairs={{0,8},{8,16},{16,24},{24,0},{1,9},{9,17},{17,25},{25,1},{2,10},{10... | collective-permute-start | bytes 302408 | tf_op jit(solution)/shard_map/ppermute | solution.py:54
  101.6 2.6 %collective-permute-start.13 = (f32[225,112]{1,0:T(8,128)S(1)}, f32[225,112]{1,0:T(8,128)S(1)}, u32[]{:S(2)}, u32[]{:S(2)}) collective-permute-start(f32[225,112]{1,0:T(8,128)S(1)} %add_add_fusion.1), channel_id=1, source_target_pairs={{0,16},{8,24},{16,0},{24,8},{1,17},{9,25},{17,1},{25,9},{2,18},{10... | collective-permute-start | bytes 302408 | tf_op jit(solution)/shard_map/ppermute | solution.py:54
  104.2 0.7 collective-permute-start.14
  104.9 3.0 %collective-permute-done.12 = f32[225,112]{1,0:T(8,128)S(1)} collective-permute-done((f32[225,112]{1,0:T(8,128)S(1)}, f32[225,112]{1,0:T(8,128)S(1)}, u32[]{:S(2)}, u32[]{:S(2)}) %collective-permute-start.12) | collective-permute-done | bytes 100832 | tf_op jit(solution)/shard_map/ppermute | solution.py:54
  108.0 3.6 %collective-permute-done.13 = f32[225,112]{1,0:T(8,128)S(1)} collective-permute-done((f32[225,112]{1,0:T(8,128)S(1)}, f32[225,112]{1,0:T(8,128)S(1)}, u32[]{:S(2)}, u32[]{:S(2)}) %collective-permute-start.13) | collective-permute-done | bytes 100832 | tf_op jit(solution)/shard_map/ppermute | solution.py:54
  111.6 0.2 collective-permute-done.14
  111.8 0.1 copy.37
  111.9 0.1 copy.38
  112.0 0.7 select_reduce_fusion
  113.4 0.8 select_add_fusion.a_ref
  114.2 28.4 %shard_map.18 = f32[256,256]{1,0:T(8,128)} custom-call(f32[224,224]{1,0:T(8,128)} %select_add_fusion.a_ref), custom_call_target="tpu_custom_call" | custom-call | tf_op jit(solution)/shard_map/pallas_call | solution.py:126
  142.6 10.2 %fusion = f32[32,256]{1,0:T(8,128)S(1)} fusion(f32[32,224,256]{2,1,0:T(8,128)} %get-tuple-element.7, f32[256,256]{1,0:T(8,128)} %shard_map.18), kind=kOutput, calls=%fused_computation.2 | convolution fusion | flops 4936213504 | bytes 14942208 | tf_op jit(solution)/shard_map/pbl,bj->pjl/dot_general | solution.py:282
  152.9 0.6 multiply_bitcast_fusion
  (15 shorter events, 0.3 us)
Async XLA Ops:
  6.6 22.1 %collective-permute-start = (bf16[32,224,15]{1,0,2:T(8,128)(2,1)}, bf16[32,224,15]{1,0,2:T(8,128)(2,1)}, u32[]{:S(2)}, u32[]{:S(2)}) collective-permute-start(bf16[32,224,15]{1,0,2:T(8,128)(2,1)} %copy.26), channel_id=1, source_target_pairs={{0,8},{8,16},{16,24},{1,9},{9,17},{17,25},{2,10},{10,18},{18,26},{... | collective-permute-start | bytes 645128 | tf_op jit(solution)/shard_map/ppermute | solution.py:174
  13.9 10.0 %copy-start = (bf16[256,32,224]{0,2,1:T(8,128)(2,1)S(1)}, bf16[256,32,224]{0,2,1:T(8,128)(2,1)}, u32[]{:S(2)}) copy-start(bf16[256,32,224]{0,2,1:T(8,128)(2,1)} %param.1) | copy-start | bytes 11010052
  13.9 17.2 %collective-permute-start.3 = (bf16[32,224,15]{1,0,2:T(8,128)(2,1)}, bf16[32,224,15]{1,0,2:T(8,128)(2,1)}, u32[]{:S(2)}, u32[]{:S(2)}) collective-permute-start(bf16[32,224,15]{1,0,2:T(8,128)(2,1)} %copy.28), channel_id=1, source_target_pairs={{8,0},{16,8},{24,16},{9,1},{17,9},{25,17},{10,2},{18,10},{26,18},{... | collective-permute-start | bytes 645128 | tf_op jit(solution)/shard_map/ppermute | solution.py:174
  19.5 44.2 %collective-permute-start.6 = (bf16[15,224,256]{2,1,0:T(8,128)(2,1)}, bf16[15,224,256]{2,1,0:T(8,128)(2,1)S(1)}, u32[]{:S(2)}, u32[]{:S(2)}) collective-permute-start(bf16[15,224,256]{2,1,0:T(8,128)(2,1)} %get-tuple-element.9), channel_id=1, source_target_pairs={{1,0},{2,1},{3,2},{4,3},{5,4},{6,5},{7,6},{9,8},{10,9},{11,10},{12... | collective-permute-start | bytes 5160968 | tf_op jit(solution)/shard_map/ppermute | solution.py:171
  20.7 46.0 %collective-permute-start.2 = (bf16[15,224,256]{2,1,0:T(8,128)(2,1)}, bf16[15,224,256]{2,1,0:T(8,128)(2,1)S(1)}, u32[]{:S(2)}, u32[]{:S(2)}) collective-permute-start(bf16[15,224,256]{2,1,0:T(8,128)(2,1)} %get-tuple-element.10), channel_id=1, source_target_pairs={{0,1},{1,2},{2,3},{3,4},{4,5},{5,6},{6,7},{8,9},{9,10},{10,11},{11... | collective-permute-start | bytes 5160968 | tf_op jit(solution)/shard_map/ppermute | solution.py:171
  29.8 15.5 %collective-permute-start.5 = (bf16[15,224,15]{1,2,0:T(8,128)(2,1)S(1)}, bf16[15,224,15]{1,2,0:T(8,128)(2,1)S(1)}, u32[]{:S(2)}, u32[]{:S(2)}) collective-permute-start(bf16[15,224,15]{1,2,0:T(8,128)(2,1)S(1)} %copy.32), channel_id=1, source_target_pairs={{1,0},{2,1},{3,2},{4,3},{5,4},{6,5},{7,6},{9,8},{10,9},{11,10},{12... | collective-permute-start | bytes 302408 | tf_op jit(solution)/shard_map/ppermute | solution.py:171
  32.2 32.2 %collective-permute-start.7 = (bf16[15,224,15]{1,2,0:T(8,128)(2,1)S(1)}, bf16[15,224,15]{1,2,0:T(8,128)(2,1)S(1)}, u32[]{:S(2)}, u32[]{:S(2)}) collective-permute-start(bf16[15,224,15]{1,2,0:T(8,128)(2,1)S(1)} %copy.33), channel_id=1, source_target_pairs={{1,0},{2,1},{3,2},{4,3},{5,4},{6,5},{7,6},{9,8},{10,9},{11,10},{12... | collective-permute-start | bytes 302408 | tf_op jit(solution)/shard_map/ppermute | solution.py:171
  33.5 6.6 %copy-start.1 = (f32[256,32,224]{0,2,1:T(8,128)S(1)}, f32[256,32,224]{0,2,1:T(8,128)}, u32[]{:S(2)}) copy-start(f32[256,32,224]{0,2,1:T(8,128)} %fusion.10) | copy-start | bytes 22020100
  33.5 29.5 %collective-permute-start.1 = (bf16[15,224,15]{1,2,0:T(8,128)(2,1)S(1)}, bf16[15,224,15]{1,2,0:T(8,128)(2,1)S(1)}, u32[]{:S(2)}, u32[]{:S(2)}) collective-permute-start(bf16[15,224,15]{1,2,0:T(8,128)(2,1)S(1)} %copy.27), channel_id=1, source_target_pairs={{0,1},{1,2},{2,3},{3,4},{4,5},{5,6},{6,7},{8,9},{9,10},{10,11},{11... | collective-permute-start | bytes 302408 | tf_op jit(solution)/shard_map/ppermute | solution.py:171
  45.3 22.1 %collective-permute-start.4 = (bf16[15,224,15]{1,2,0:T(8,128)(2,1)S(1)}, bf16[15,224,15]{1,2,0:T(8,128)(2,1)S(1)}, u32[]{:S(2)}, u32[]{:S(2)}) collective-permute-start(bf16[15,224,15]{1,2,0:T(8,128)(2,1)S(1)} %copy.29), channel_id=1, source_target_pairs={{0,1},{1,2},{2,3},{3,4},{4,5},{5,6},{6,7},{8,9},{9,10},{10,11},{11... | collective-permute-start | bytes 302408 | tf_op jit(solution)/shard_map/ppermute | solution.py:171
  86.2 1.4 collective-permute-start.8
  87.7 7.5 %collective-permute-start.10 = (f32[225,112]{1,0:T(8,128)S(1)}, f32[225,112]{1,0:T(8,128)S(1)}, u32[]{:S(2)}, u32[]{:S(2)}) collective-permute-start(f32[225,112]{1,0:T(8,128)S(1)} %fusion.43), channel_id=1, source_target_pairs={{0,4},{1,5},{2,6},{3,7},{4,0},{5,1},{6,2},{7,3},{8,12},{9,13},{10,... | collective-permute-start | bytes 302408 | tf_op jit(solution)/shard_map/ppermute | solution.py:54
  91.6 5.8 %collective-permute-start.11 = (f32[225,112]{1,0:T(8,128)S(1)}, f32[225,112]{1,0:T(8,128)S(1)}, u32[]{:S(2)}, u32[]{:S(2)}) collective-permute-start(f32[225,112]{1,0:T(8,128)S(1)} %fusion.43), channel_id=1, source_target_pairs={{0,6},{1,7},{2,0},{3,1},{4,2},{5,3},{6,4},{7,5},{8,14},{9,15},{10,... | collective-permute-start | bytes 302408 | tf_op jit(solution)/shard_map/ppermute | solution.py:54
  92.4 6.5 %collective-permute-start.9 = (f32[225,112]{1,0:T(8,128)S(1)}, f32[225,112]{1,0:T(8,128)S(1)}, u32[]{:S(2)}, u32[]{:S(2)}) collective-permute-start(f32[225,112]{1,0:T(8,128)S(1)} %fusion.43), channel_id=1, source_target_pairs={{0,2},{1,3},{2,4},{3,5},{4,6},{5,7},{6,0},{7,1},{8,10},{9,11},{10,... | collective-permute-start | bytes 302408 | tf_op jit(solution)/shard_map/ppermute | solution.py:54
  98.9 9.0 %collective-permute-start.12 = (f32[225,112]{1,0:T(8,128)S(1)}, f32[225,112]{1,0:T(8,128)S(1)}, u32[]{:S(2)}, u32[]{:S(2)}) collective-permute-start(f32[225,112]{1,0:T(8,128)S(1)} %add_add_fusion.1), channel_id=1, source_target_pairs={{0,8},{8,16},{16,24},{24,0},{1,9},{9,17},{17,25},{25,1},{2,10},{10... | collective-permute-start | bytes 302408 | tf_op jit(solution)/shard_map/ppermute | solution.py:54
  101.6 9.9 %collective-permute-start.13 = (f32[225,112]{1,0:T(8,128)S(1)}, f32[225,112]{1,0:T(8,128)S(1)}, u32[]{:S(2)}, u32[]{:S(2)}) collective-permute-start(f32[225,112]{1,0:T(8,128)S(1)} %add_add_fusion.1), channel_id=1, source_target_pairs={{0,16},{8,24},{16,0},{24,8},{1,17},{9,25},{17,1},{25,9},{2,18},{10... | collective-permute-start | bytes 302408 | tf_op jit(solution)/shard_map/ppermute | solution.py:54
  104.2 7.5 %collective-permute-start.14 = (f32[225,112]{1,0:T(8,128)S(1)}, f32[225,112]{1,0:T(8,128)S(1)}, u32[]{:S(2)}, u32[]{:S(2)}) collective-permute-start(f32[225,112]{1,0:T(8,128)S(1)} %add_add_fusion.1), channel_id=1, source_target_pairs={{0,24},{8,0},{16,8},{24,16},{1,25},{9,1},{17,9},{25,17},{2,26},{10... | collective-permute-start | bytes 302408 | tf_op jit(solution)/shard_map/ppermute | solution.py:54

commit v13 on v12

--- a/solution.py
+++ b/solution.py
@@ -175,9 +175,10 @@
         return lax.ppermute(piece, both, neighbour_pairs(n_track, n_cross, dt, dc))
 
     first, last = slice(0, HALF), slice(-HALF, None)
+    to_right, to_left, planes = lax.optimization_barrier((planes[last], planes[first], planes))
     sides = {
-        "left": fetch(planes[last], 0, -1),
-        "right": fetch(planes[first], 0, 1),
+        "left": fetch(to_right, 0, -1),
+        "right": fetch(to_left, 0, 1),
     }
     top = fetch(planes[:, :, last], -1, 0)
     bottom = fetch(planes[:, :, first], 1, 0)

time: 154 us -> 152 us (0.987)
  starting transfers between devices: 47.6 us -> 45.7 us
  local copies, waits for them, and re-layouts: 16.3 us -> 14.6 us
    slice x2, local copies, waits for them, and re-layouts: 5.6 us -> 3.76 us  [halos(): bottom = fetch(planes[:, :, first], 1, 0)]
    ppermute x6, starting transfers between devices: 28.5 us -> 26.7 us  [fetch(): return lax.ppermute(piece, 'cross', pairs)]
  transfers between devices with their start and end apart: 15 -> 15, of which waited for: 7 -> 7; matrix products, arithmetic and copies ran while one was open for 16% -> 15% of each run, Pallas kernels for 0% -> 0%
where the time goes in v13:
time: 152 us; the launch traced here: 151 us
  starting transfers between devices  45.7 us (30%)
  Pallas kernels  38.7 us (25%)
  matrix products  34.7 us (23%)
  local copies, waits for them, and re-layouts  14.6 us (10%)
  waiting for transfers between devices  13.5 us (9%)
  other arithmetic  3.13 us (2%)
    pallas_call x1, Pallas kernels, spd_inverse(): pl.pallas_call(functools.partial(sweep_kernel, n), out_shape=jax.ShapeDty...  28.4 us
    ppermute x6, starting transfers between devices, fetch(): return lax.ppermute(piece, 'cross', pairs)  26.7 us
    dot_general x9, matrix products, sum_lines(): jnp.einsum('qbk,kl->qbl', values, w, preferred_element_type=jnp.float32)  20.2 us
    ppermute x6, waiting for transfers between devices, ring_sum(): total = total + lax.ppermute(x, axis, pairs)  12.1 us
    ppermute x6, starting transfers between devices, ring_sum(): total = total + lax.ppermute(x, axis, pairs)  12.1 us
    pallas_call x1, Pallas kernels, residuals(): pl.pallas_call(residual_kernel, grid=(bands // block,), in_specs=[spec(le...  10.3 us
    dot_general x1, matrix products, shards(): jnp.einsum('pbl,bj->pjl', residual, inverse, precision=highest, preferred...  10.2 us
    ppermute x2, starting transfers between devices, fetch(): return lax.ppermute(piece, 'track', pairs)  6.89 us
  transfers between devices with their start and end apart: 15, of which 7 were waited for; matrix products, arithmetic and copies ran while one was open for 15% of the time, Pallas kernels for 0%

profile of v13, /device:TPU:0, one launch (start us, length us, event | category | flops | bytes accessed | tf_op | source)
XLA Modules:
  0.0 151.3 jit_solution(15300730636432474431)
XLA Ops:
  0.0 0.0 copy-start
  0.0 4.2 %fusion.46 = (bf16[15,224,256]{2,1,0:T(8,128)(2,1)}, bf16[15,224,256]{2,1,0:T(8,128)(2,1)}) fusion(bf16[32,224,256]{2,1,0:T(8,128)(2,1)} %bitcast.61), kind=kLoop, calls=%fused_computation.61 | loop fusion | bytes 6881280 | tf_op jit(solution)/shard_map/slice | solution.py:178
  4.2 0.0 copy-done
  4.2 2.1 %fusion.45 = (bf16[32,224,15]{2,1,0:T(8,128)(2,1)S(1)}, bf16[32,224,15]{2,1,0:T(8,128)(2,1)}) fusion(bf16[32,224,256]{2,1,0:T(8,128)(2,1)S(1)} %bitcast.63), kind=kLoop, calls=%fused_computation.60 | loop fusion | bytes 860160 | tf_op jit(solution)/shard_map/slice | solution.py:184
  6.3 2.7 %copy.26 = bf16[32,224,15]{1,0,2:T(8,128)(2,1)} copy(bf16[32,224,15]{2,1,0:T(8,128)(2,1)} %get-tuple-element.16) | data formatting | bytes 430080 | tf_op jit(solution)/shard_map/slice | solution.py:183
  8.9 5.6 %collective-permute-start = (bf16[32,224,15]{1,0,2:T(8,128)(2,1)}, bf16[32,224,15]{1,0,2:T(8,128)(2,1)}, u32[]{:S(2)}, u32[]{:S(2)}) collective-permute-start(bf16[32,224,15]{1,0,2:T(8,128)(2,1)} %copy.26), channel_id=1, source_target_pairs={{0,8},{8,16},{16,24},{1,9},{9,17},{17,25},{2,10},{10,18},{18,26},{... | collective-permute-start | bytes 645128 | tf_op jit(solution)/shard_map/ppermute | solution.py:174
  14.6 1.7 %copy.28 = bf16[32,224,15]{1,0,2:T(8,128)(2,1)} copy(bf16[32,224,15]{2,1,0:T(8,128)(2,1)S(1)} %get-tuple-element.15) | data formatting | bytes 430080 | tf_op jit(solution)/shard_map/slice | solution.py:184
  16.2 1.3 collective-permute-start.3
  17.5 1.3 collective-permute-start.6
  18.8 3.1 %collective-permute-start.2 = (bf16[15,224,256]{2,1,0:T(8,128)(2,1)}, bf16[15,224,256]{2,1,0:T(8,128)(2,1)S(1)}, u32[]{:S(2)}, u32[]{:S(2)}) collective-permute-start(bf16[15,224,256]{2,1,0:T(8,128)(2,1)} %get-tuple-element.11), channel_id=1, source_target_pairs={{0,1},{1,2},{2,3},{3,4},{4,5},{5,6},{6,7},{8,9},{9,10},{10,11},{11... | collective-permute-start | bytes 5160968 | tf_op jit(solution)/shard_map/ppermute | solution.py:171
  22.0 6.1 %fusion.11 = f32[256,32,224]{0,2,1:T(8,128)} fusion(bf16[256,32,224]{0,2,1:T(8,128)(2,1)} %param.1), kind=kOutput, calls=%fused_computation.15 | convolution fusion | flops 939720704 | bytes 11010048 | tf_op jit(solution)/shard_map/qbk,kl->qbl/dot_general | solution.py:210
  28.1 0.7 broadcast_multiply_fusion.count_ref
  28.8 0.0 collective-permute-done
  28.8 1.0 fusion.48
  29.9 1.3 collective-permute-start.5
  31.2 0.0 collective-permute-done.3
  31.2 1.0 fusion.47
  32.3 1.3 collective-permute-start.7
  33.6 0.0 copy-start.1
  33.6 4.4 %collective-permute-start.1 = (bf16[15,224,15]{1,2,0:T(8,128)(2,1)S(1)}, bf16[15,224,15]{1,2,0:T(8,128)(2,1)S(1)}, u32[]{:S(2)}, u32[]{:S(2)}) collective-permute-start(bf16[15,224,15]{1,2,0:T(8,128)(2,1)S(1)} %copy.27), channel_id=1, source_target_pairs={{0,1},{1,2},{2,3},{3,4},{4,5},{5,6},{6,7},{8,9},{9,10},{10,11},{11... | collective-permute-start | bytes 302408 | tf_op jit(solution)/shard_map/ppermute | solution.py:171
  38.1 1.9 %fusion.6 = f32[32,224,256]{2,1,0:T(8,128)S(1)} fusion(bf16[32,224,15]{1,0,2:T(8,128)(2,1)} %collective-permute-done), kind=kOutput, calls=%fused_computation.10 | convolution fusion | flops 55054080 | bytes 7555072 | tf_op jit(solution)/shard_map/qbk,kl->qbl/dot_general | solution.py:210
  39.9 0.0 copy-done.1
  39.9 5.2 %fusion.1.middle_ref = f32[32,224,256]{2,1,0:T(8,128)} fusion(f32[32,224,256]{2,1,0:T(8,128)S(1)} %fusion.6, f32[256,32,224]{0,2,1:T(8,128)S(1)} %copy-done.1, bf16[32,224,15]{1,0,2:T(8,128)(2,1)} %collective-permute-done.3, s32[15]{0:T(128)S(1)} %iota_add_fusion), kind=kOutput, calls=%fused_computation.4 | convolution fusion | flops 58724096 | bytes 22235196 | tf_op jit(solution)/shard_map/qbk,kl->qbl/dot_general | solution.py:210
  45.1 0.0 collective-permute-done.5
  45.2 15.2 %collective-permute-start.4 = (bf16[15,224,15]{1,2,0:T(8,128)(2,1)S(1)}, bf16[15,224,15]{1,2,0:T(8,128)(2,1)S(1)}, u32[]{:S(2)}, u32[]{:S(2)}) collective-permute-start(bf16[15,224,15]{1,2,0:T(8,128)(2,1)S(1)} %copy.29), channel_id=1, source_target_pairs={{0,1},{1,2},{2,3},{3,4},{4,5},{5,6},{6,7},{8,9},{9,10},{10,11},{11... | collective-permute-start | bytes 302408 | tf_op jit(solution)/shard_map/ppermute | solution.py:171
  60.4 0.5 fusion.22
  60.9 0.0 collective-permute-done.1
  60.9 0.5 fusion.25
  61.4 0.0 collective-permute-done.6
  61.4 0.6 fusion.9
  62.0 0.0 collective-permute-done.7
  62.0 2.4 %add_add_fusion.right_ref = f32[15,224,256]{2,1,0:T(8,128)} fusion(f32[15,224,256]{2,1,0:T(8,128)S(1)} %fusion.22, f32[15,224,256]{2,1,0:T(8,128)S(1)} %fusion.9, bf16[15,224,15]{1,2,0:T(8,128)(2,1)S(1)} %collective-permute-done.7, s32[15]{0:T(128)S(1)} %iota_add_fusion), kind=kOutput, calls=%fused_computation.5 | convolution fusion | flops 27528960 | bytes 10422780 | tf_op jit(solution)/shard_map/qbk,kl->qbl/dot_general | solution.py:210
  64.4 0.0 collective-permute-done.2
  64.4 0.6 fusion.13
  65.1 0.0 collective-permute-done.4
  65.1 2.4 %add_add_fusion.1.left_ref = f32[15,224,256]{2,1,0:T(8,128)} fusion(f32[15,224,256]{2,1,0:T(8,128)S(1)} %fusion.25, f32[15,224,256]{2,1,0:T(8,128)S(1)} %fusion.13, bf16[15,224,15]{1,2,0:T(8,128)(2,1)S(1)} %collective-permute-done.4, s32[15]{0:T(128)S(1)} %iota_add_fusion), kind=kOutput, calls=%fused_computation.6 | convolution fusion | flops 27528960 | bytes 10422780 | tf_op jit(solution)/shard_map/qbk,kl->qbl/dot_general | solution.py:210
  67.5 10.3 %shard_map.17 = (f32[32,224,256]{2,1,0:T(8,128)}, bf16[32,224,256]{2,1,0:T(8,128)(2,1)}) custom-call(f32[15,224,256]{2,1,0:T(8,128)} %add_add_fusion.1.left_ref, f32[32,224,256]{2,1,0:T(8,128)} %fusion.1.middle_ref, f32[15,224,256]{2,1,0:T(8,128)} %add_add_fusion.right_ref, bf16[32,224,256]{2,1,0:T(8,128)(2,1)} %bitcast.62, ...), custom_call_target="tpu_custom_call" | custom-call | tf_op jit(solution)/shard_map/pallas_call | solution.py:244
  77.8 4.3 %convolution_bitcast_fusion = f32[224,224]{1,0:T(8,128)S(1)} fusion(bf16[32,224,256]{2,1,0:T(8,128)(2,1)} %get-tuple-element.14), kind=kOutput, calls=%fused_computation.7 | convolution fusion | flops 822083584 | bytes 3870720 | tf_op jit(solution)/shard_map/pjl,pkl->jk/dot_general | solution.py:273
  82.1 0.1 fusion.49
  82.2 1.7 %gather_fusion = f32[112]{0:T(128)S(1)} fusion(f32[112,112]{1,0:T(8,128)S(1)} %get-tuple-element.25, s32[112]{0:T(128)S(1)} %or_bitcast_fusion), kind=kCustom, calls=%fused_computation | custom fusion | bytes 1792 | tf_op jit(solution)/shard_map/jit(diagonal)/cond/branch_0_fun/gather | solution.py:64
  83.9 0.1 collective-permute-start.8
  84.0 1.3 collective-permute-done.8
  85.3 4.1 %collective-permute-start.10 = (f32[225,112]{1,0:T(8,128)S(1)}, f32[225,112]{1,0:T(8,128)S(1)}, u32[]{:S(2)}, u32[]{:S(2)}) collective-permute-start(f32[225,112]{1,0:T(8,128)S(1)} %fusion.44), channel_id=1, source_target_pairs={{0,4},{1,5},{2,6},{3,7},{4,0},{5,1},{6,2},{7,3},{8,12},{9,13},{10,... | collective-permute-start | bytes 302408 | tf_op jit(solution)/shard_map/ppermute | solution.py:54
  89.4 0.7 collective-permute-start.11
  90.1 1.3 collective-permute-start.9
  91.4 1.5 %collective-permute-done.10 = f32[225,112]{1,0:T(8,128)S(1)} collective-permute-done((f32[225,112]{1,0:T(8,128)S(1)}, f32[225,112]{1,0:T(8,128)S(1)}, u32[]{:S(2)}, u32[]{:S(2)}) %collective-permute-start.10) | collective-permute-done | bytes 100832 | tf_op jit(solution)/shard_map/ppermute | solution.py:54
  92.9 2.2 %collective-permute-done.11 = f32[225,112]{1,0:T(8,128)S(1)} collective-permute-done((f32[225,112]{1,0:T(8,128)S(1)}, f32[225,112]{1,0:T(8,128)S(1)}, u32[]{:S(2)}, u32[]{:S(2)}) %collective-permute-start.11) | collective-permute-done | bytes 100832 | tf_op jit(solution)/shard_map/ppermute | solution.py:54
  95.2 1.5 %collective-permute-done.9 = f32[225,112]{1,0:T(8,128)S(1)} collective-permute-done((f32[225,112]{1,0:T(8,128)S(1)}, f32[225,112]{1,0:T(8,128)S(1)}, u32[]{:S(2)}, u32[]{:S(2)}) %collective-permute-start.9) | collective-permute-done | bytes 100832 | tf_op jit(solution)/shard_map/ppermute | solution.py:54
  96.8 2.7 %collective-permute-start.12 = (f32[225,112]{1,0:T(8,128)S(1)}, f32[225,112]{1,0:T(8,128)S(1)}, u32[]{:S(2)}, u32[]{:S(2)}) collective-permute-start(f32[225,112]{1,0:T(8,128)S(1)} %add_add_fusion.3), channel_id=1, source_target_pairs={{0,8},{8,16},{16,24},{24,0},{1,9},{9,17},{17,25},{25,1},{2,10},{10... | collective-permute-start | bytes 302408 | tf_op jit(solution)/shard_map/ppermute | solution.py:54
  99.5 2.6 %collective-permute-start.13 = (f32[225,112]{1,0:T(8,128)S(1)}, f32[225,112]{1,0:T(8,128)S(1)}, u32[]{:S(2)}, u32[]{:S(2)}) collective-permute-start(f32[225,112]{1,0:T(8,128)S(1)} %add_add_fusion.3), channel_id=1, source_target_pairs={{0,16},{8,24},{16,0},{24,8},{1,17},{9,25},{17,1},{25,9},{2,18},{10... | collective-permute-start | bytes 302408 | tf_op jit(solution)/shard_map/ppermute | solution.py:54
  102.1 0.7 collective-permute-start.14
  102.7 3.0 %collective-permute-done.12 = f32[225,112]{1,0:T(8,128)S(1)} collective-permute-done((f32[225,112]{1,0:T(8,128)S(1)}, f32[225,112]{1,0:T(8,128)S(1)}, u32[]{:S(2)}, u32[]{:S(2)}) %collective-permute-start.12) | collective-permute-done | bytes 100832 | tf_op jit(solution)/shard_map/ppermute | solution.py:54
  105.8 3.6 %collective-permute-done.13 = f32[225,112]{1,0:T(8,128)S(1)} collective-permute-done((f32[225,112]{1,0:T(8,128)S(1)}, f32[225,112]{1,0:T(8,128)S(1)}, u32[]{:S(2)}, u32[]{:S(2)}) %collective-permute-start.13) | collective-permute-done | bytes 100832 | tf_op jit(solution)/shard_map/ppermute | solution.py:54
  109.4 0.2 collective-permute-done.14
  109.6 0.1 copy.37
  109.8 0.1 copy.38
  109.8 0.7 select_reduce_fusion
  111.2 0.8 select_add_fusion.a_ref
  112.0 28.4 %shard_map.18 = f32[256,256]{1,0:T(8,128)} custom-call(f32[224,224]{1,0:T(8,128)} %select_add_fusion.a_ref), custom_call_target="tpu_custom_call" | custom-call | tf_op jit(solution)/shard_map/pallas_call | solution.py:126
  140.5 10.2 %fusion = f32[32,256]{1,0:T(8,128)S(1)} fusion(f32[32,224,256]{2,1,0:T(8,128)} %get-tuple-element.13, f32[256,256]{1,0:T(8,128)} %shard_map.18), kind=kOutput, calls=%fused_computation.2 | convolution fusion | flops 4936213504 | bytes 14942208 | tf_op jit(solution)/shard_map/pbl,bj->pjl/dot_general | solution.py:283
  150.7 0.6 multiply_bitcast_fusion
  (15 shorter events, 0.4 us)
Async XLA Ops:
  0.0 4.2 %copy-start = (bf16[256,32,224]{0,2,1:T(8,128)(2,1)S(1)}, bf16[256,32,224]{0,2,1:T(8,128)(2,1)}, u32[]{:S(2)}) copy-start(bf16[256,32,224]{0,2,1:T(8,128)(2,1)} %param.1) | copy-start | bytes 11010052
  8.9 19.9 %collective-permute-start = (bf16[32,224,15]{1,0,2:T(8,128)(2,1)}, bf16[32,224,15]{1,0,2:T(8,128)(2,1)}, u32[]{:S(2)}, u32[]{:S(2)}) collective-permute-start(bf16[32,224,15]{1,0,2:T(8,128)(2,1)} %copy.26), channel_id=1, source_target_pairs={{0,8},{8,16},{16,24},{1,9},{9,17},{17,25},{2,10},{10,18},{18,26},{... | collective-permute-start | bytes 645128 | tf_op jit(solution)/shard_map/ppermute | solution.py:174
  16.2 15.0 %collective-permute-start.3 = (bf16[32,224,15]{1,0,2:T(8,128)(2,1)}, bf16[32,224,15]{1,0,2:T(8,128)(2,1)}, u32[]{:S(2)}, u32[]{:S(2)}) collective-permute-start(bf16[32,224,15]{1,0,2:T(8,128)(2,1)} %copy.28), channel_id=1, source_target_pairs={{8,0},{16,8},{24,16},{9,1},{17,9},{25,17},{10,2},{18,10},{26,18},{... | collective-permute-start | bytes 645128 | tf_op jit(solution)/shard_map/ppermute | solution.py:174
  17.5 43.9 %collective-permute-start.6 = (bf16[15,224,256]{2,1,0:T(8,128)(2,1)}, bf16[15,224,256]{2,1,0:T(8,128)(2,1)S(1)}, u32[]{:S(2)}, u32[]{:S(2)}) collective-permute-start(bf16[15,224,256]{2,1,0:T(8,128)(2,1)} %get-tuple-element.12), channel_id=1, source_target_pairs={{1,0},{2,1},{3,2},{4,3},{5,4},{6,5},{7,6},{9,8},{10,9},{11,10},{12... | collective-permute-start | bytes 5160968 | tf_op jit(solution)/shard_map/ppermute | solution.py:171
  18.8 45.6 %collective-permute-start.2 = (bf16[15,224,256]{2,1,0:T(8,128)(2,1)}, bf16[15,224,256]{2,1,0:T(8,128)(2,1)S(1)}, u32[]{:S(2)}, u32[]{:S(2)}) collective-permute-start(bf16[15,224,256]{2,1,0:T(8,128)(2,1)} %get-tuple-element.11), channel_id=1, source_target_pairs={{0,1},{1,2},{2,3},{3,4},{4,5},{5,6},{6,7},{8,9},{9,10},{10,11},{11... | collective-permute-start | bytes 5160968 | tf_op jit(solution)/shard_map/ppermute | solution.py:171
  29.9 15.3 %collective-permute-start.5 = (bf16[15,224,15]{1,2,0:T(8,128)(2,1)S(1)}, bf16[15,224,15]{1,2,0:T(8,128)(2,1)S(1)}, u32[]{:S(2)}, u32[]{:S(2)}) collective-permute-start(bf16[15,224,15]{1,2,0:T(8,128)(2,1)S(1)} %copy.32), channel_id=1, source_target_pairs={{1,0},{2,1},{3,2},{4,3},{5,4},{6,5},{7,6},{9,8},{10,9},{11,10},{12... | collective-permute-start | bytes 302408 | tf_op jit(solution)/shard_map/ppermute | solution.py:171
  32.3 29.8 %collective-permute-start.7 = (bf16[15,224,15]{1,2,0:T(8,128)(2,1)S(1)}, bf16[15,224,15]{1,2,0:T(8,128)(2,1)S(1)}, u32[]{:S(2)}, u32[]{:S(2)}) collective-permute-start(bf16[15,224,15]{1,2,0:T(8,128)(2,1)S(1)} %copy.33), channel_id=1, source_target_pairs={{1,0},{2,1},{3,2},{4,3},{5,4},{6,5},{7,6},{9,8},{10,9},{11,10},{12... | collective-permute-start | bytes 302408 | tf_op jit(solution)/shard_map/ppermute | solution.py:171
  33.6 6.3 %copy-start.1 = (f32[256,32,224]{0,2,1:T(8,128)S(1)}, f32[256,32,224]{0,2,1:T(8,128)}, u32[]{:S(2)}) copy-start(f32[256,32,224]{0,2,1:T(8,128)} %fusion.11) | copy-start | bytes 22020100
  33.6 27.3 %collective-permute-start.1 = (bf16[15,224,15]{1,2,0:T(8,128)(2,1)S(1)}, bf16[15,224,15]{1,2,0:T(8,128)(2,1)S(1)}, u32[]{:S(2)}, u32[]{:S(2)}) collective-permute-start(bf16[15,224,15]{1,2,0:T(8,128)(2,1)S(1)} %copy.27), channel_id=1, source_target_pairs={{0,1},{1,2},{2,3},{3,4},{4,5},{5,6},{6,7},{8,9},{9,10},{10,11},{11... | collective-permute-start | bytes 302408 | tf_op jit(solution)/shard_map/ppermute | solution.py:171
  45.2 19.9 %collective-permute-start.4 = (bf16[15,224,15]{1,2,0:T(8,128)(2,1)S(1)}, bf16[15,224,15]{1,2,0:T(8,128)(2,1)S(1)}, u32[]{:S(2)}, u32[]{:S(2)}) collective-permute-start(bf16[15,224,15]{1,2,0:T(8,128)(2,1)S(1)} %copy.29), channel_id=1, source_target_pairs={{0,1},{1,2},{2,3},{3,4},{4,5},{5,6},{6,7},{8,9},{9,10},{10,11},{11... | collective-permute-start | bytes 302408 | tf_op jit(solution)/shard_map/ppermute | solution.py:171
  83.9 1.4 collective-permute-start.8
  85.3 7.6 %collective-permute-start.10 = (f32[225,112]{1,0:T(8,128)S(1)}, f32[225,112]{1,0:T(8,128)S(1)}, u32[]{:S(2)}, u32[]{:S(2)}) collective-permute-start(f32[225,112]{1,0:T(8,128)S(1)} %fusion.44), channel_id=1, source_target_pairs={{0,4},{1,5},{2,6},{3,7},{4,0},{5,1},{6,2},{7,3},{8,12},{9,13},{10,... | collective-permute-start | bytes 302408 | tf_op jit(solution)/shard_map/ppermute | solution.py:54
  89.4 5.8 %collective-permute-start.11 = (f32[225,112]{1,0:T(8,128)S(1)}, f32[225,112]{1,0:T(8,128)S(1)}, u32[]{:S(2)}, u32[]{:S(2)}) collective-permute-start(f32[225,112]{1,0:T(8,128)S(1)} %fusion.44), channel_id=1, source_target_pairs={{0,6},{1,7},{2,0},{3,1},{4,2},{5,3},{6,4},{7,5},{8,14},{9,15},{10,... | collective-permute-start | bytes 302408 | tf_op jit(solution)/shard_map/ppermute | solution.py:54
  90.1 6.7 %collective-permute-start.9 = (f32[225,112]{1,0:T(8,128)S(1)}, f32[225,112]{1,0:T(8,128)S(1)}, u32[]{:S(2)}, u32[]{:S(2)}) collective-permute-start(f32[225,112]{1,0:T(8,128)S(1)} %fusion.44), channel_id=1, source_target_pairs={{0,2},{1,3},{2,4},{3,5},{4,6},{5,7},{6,0},{7,1},{8,10},{9,11},{10,... | collective-permute-start | bytes 302408 | tf_op jit(solution)/shard_map/ppermute | solution.py:54
  96.8 9.0 %collective-permute-start.12 = (f32[225,112]{1,0:T(8,128)S(1)}, f32[225,112]{1,0:T(8,128)S(1)}, u32[]{:S(2)}, u32[]{:S(2)}) collective-permute-start(f32[225,112]{1,0:T(8,128)S(1)} %add_add_fusion.3), channel_id=1, source_target_pairs={{0,8},{8,16},{16,24},{24,0},{1,9},{9,17},{17,25},{25,1},{2,10},{10... | collective-permute-start | bytes 302408 | tf_op jit(solution)/shard_map/ppermute | solution.py:54
  99.5 9.9 %collective-permute-start.13 = (f32[225,112]{1,0:T(8,128)S(1)}, f32[225,112]{1,0:T(8,128)S(1)}, u32[]{:S(2)}, u32[]{:S(2)}) collective-permute-start(f32[225,112]{1,0:T(8,128)S(1)} %add_add_fusion.3), channel_id=1, source_target_pairs={{0,16},{8,24},{16,0},{24,8},{1,17},{9,25},{17,1},{25,9},{2,18},{10... | collective-permute-start | bytes 302408 | tf_op jit(solution)/shard_map/ppermute | solution.py:54
  102.1 7.5 %collective-permute-start.14 = (f32[225,112]{1,0:T(8,128)S(1)}, f32[225,112]{1,0:T(8,128)S(1)}, u32[]{:S(2)}, u32[]{:S(2)}) collective-permute-start(f32[225,112]{1,0:T(8,128)S(1)} %add_add_fusion.3), channel_id=1, source_target_pairs={{0,24},{8,0},{16,8},{24,16},{1,25},{9,1},{17,9},{25,17},{2,26},{10... | collective-permute-start | bytes 302408 | tf_op jit(solution)/shard_map/ppermute | solution.py:54

commit v14 on v13

--- a/solution.py
+++ b/solution.py
@@ -61,7 +61,8 @@
     col = jnp.arange(h)[None, :]
     c11, c12, c22 = c[:h, :h], c[:h, h:], c[h:, h:]
     mixed = jnp.where(col >= row, c11, c22)
-    return jnp.concatenate([c12, mixed, jnp.diagonal(c22)[None, :]], axis=0)
+    diagonal = jnp.sum(jnp.where(col == row, c22, 0.0), axis=0, keepdims=True)
+    return jnp.concatenate([c12, mixed, diagonal], axis=0)
 
 
 def unpack_symmetric(p):

time: 152 us -> 145 us (0.954)
  starting transfers between devices: 45.7 us -> 33.5 us
  waiting for transfers between devices: 13.5 us -> 21.5 us
  local copies, waits for them, and re-layouts: 14.6 us -> 12 us
    ppermute x6, starting transfers between devices: 26.7 us -> 15.1 us  [fetch(): return lax.ppermute(piece, 'cross', pairs)]
    ppermute x6, waiting for transfers between devices: 0.02 us -> 5.7 us  [fetch(): return lax.ppermute(piece, 'cross', pairs)]
    ppermute x6, starting transfers between devices: 12.1 us -> 8.57 us  [ring_sum(): total = total + lax.ppermute(x, axis, pairs)]
    ppermute x1, starting transfers between devices: 0.07 us -> 3.54 us  [shards(): lax.ppermute(packed, 'cross', [(i, i ^ 1) for i in range(n_cross)])]
    ppermute x6, waiting for transfers between devices: 12.1 us -> 14.9 us  [ring_sum(): total = total + lax.ppermute(x, axis, pairs)]
    gather x1 -> x0, local copies, waits for them, and re-layouts: 1.68 us -> none  [pack_symmetric(): return jnp.concatenate([c12, mixed, jnp.diagonal(c22)[None, :]], axis=0)]
  transfers between devices with their start and end apart: 15 -> 15, of which waited for: 7 -> 6; matrix products, arithmetic and copies ran while one was open for 15% -> 18% of each run, Pallas kernels for 0% -> 0%
where the time goes in v14:
time: 145 us
  Pallas kernels  38.7 us (27%)
  matrix products  35.1 us (24%)
  starting transfers between devices  33.5 us (23%)
  waiting for transfers between devices  21.5 us (15%)
  local copies, waits for them, and re-layouts  12 us (8%)
  other arithmetic  3.11 us (2%)
    pallas_call x1, Pallas kernels, spd_inverse(): pl.pallas_call(functools.partial(sweep_kernel, n), out_shape=jax.ShapeDty...  28.4 us
    dot_general x9, matrix products, sum_lines(): jnp.einsum('qbk,kl->qbl', values, w, preferred_element_type=jnp.float32)  20.6 us
    ppermute x6, starting transfers between devices, fetch(): return lax.ppermute(piece, 'cross', pairs)  15.1 us
    ppermute x6, waiting for transfers between devices, ring_sum(): total = total + lax.ppermute(x, axis, pairs)  14.9 us
    pallas_call x1, Pallas kernels, residuals(): pl.pallas_call(residual_kernel, grid=(bands // block,), in_specs=[spec(le...  10.2 us
    dot_general x1, matrix products, shards(): jnp.einsum('pbl,bj->pjl', residual, inverse, precision=highest, preferred...  10.2 us
    ppermute x6, starting transfers between devices, ring_sum(): total = total + lax.ppermute(x, axis, pairs)  8.57 us
    ppermute x2, starting transfers between devices, fetch(): return lax.ppermute(piece, 'track', pairs)  6.3 us
  transfers between devices with their start and end apart: 15, of which 6 were waited for; matrix products, arithmetic and copies ran while one was open for 18% of the time, Pallas kernels for 0%

profile of v14, /device:TPU:0, one launch (start us, length us, event | category | flops | bytes accessed | tf_op | source)
XLA Modules:
  0.0 144.9 jit_solution(13019887472642192937)
XLA Ops:
  0.0 0.0 copy-start
  0.0 4.2 %fusion.46 = (bf16[15,224,256]{2,1,0:T(8,128)(2,1)}, bf16[15,224,256]{2,1,0:T(8,128)(2,1)}) fusion(bf16[32,224,256]{2,1,0:T(8,128)(2,1)} %bitcast.59), kind=kLoop, calls=%fused_computation.60 | loop fusion | bytes 6881280 | tf_op jit(solution)/shard_map/slice | solution.py:179
  4.2 2.5 %collective-permute-start.2 = (bf16[15,224,256]{2,1,0:T(8,128)(2,1)}, bf16[15,224,256]{2,1,0:T(8,128)(2,1)S(1)}, u32[]{:S(2)}, u32[]{:S(2)}) collective-permute-start(bf16[15,224,256]{2,1,0:T(8,128)(2,1)} %get-tuple-element.11), channel_id=1, source_target_pairs={{0,1},{1,2},{2,3},{3,4},{4,5},{5,6},{6,7},{8,9},{9,10},{10,11},{11... | collective-permute-start | bytes 5160968 | tf_op jit(solution)/shard_map/ppermute | solution.py:172
  6.6 1.3 collective-permute-start.6
  7.9 0.0 copy-done
  7.9 2.1 %fusion.45 = (bf16[32,224,15]{2,1,0:T(8,128)(2,1)S(1)}, bf16[32,224,15]{2,1,0:T(8,128)(2,1)}) fusion(bf16[32,224,256]{2,1,0:T(8,128)(2,1)S(1)} %bitcast.61), kind=kLoop, calls=%fused_computation.59 | loop fusion | bytes 860160 | tf_op jit(solution)/shard_map/slice | solution.py:185
  10.1 2.7 %copy.14 = bf16[32,224,15]{1,0,2:T(8,128)(2,1)} copy(bf16[32,224,15]{2,1,0:T(8,128)(2,1)} %get-tuple-element.16) | data formatting | bytes 430080 | tf_op jit(solution)/shard_map/slice | solution.py:184
  12.8 5.0 %collective-permute-start = (bf16[32,224,15]{1,0,2:T(8,128)(2,1)}, bf16[32,224,15]{1,0,2:T(8,128)(2,1)}, u32[]{:S(2)}, u32[]{:S(2)}) collective-permute-start(bf16[32,224,15]{1,0,2:T(8,128)(2,1)} %copy.14), channel_id=1, source_target_pairs={{0,8},{8,16},{16,24},{1,9},{9,17},{17,25},{2,10},{10,18},{18,26},{... | collective-permute-start | bytes 645128 | tf_op jit(solution)/shard_map/ppermute | solution.py:175
  17.8 1.7 %copy.16 = bf16[32,224,15]{1,0,2:T(8,128)(2,1)} copy(bf16[32,224,15]{2,1,0:T(8,128)(2,1)S(1)} %get-tuple-element.15) | data formatting | bytes 430080 | tf_op jit(solution)/shard_map/slice | solution.py:185
  19.4 1.3 collective-permute-start.3
  20.8 6.1 %fusion.11 = f32[256,32,224]{0,2,1:T(8,128)} fusion(bf16[256,32,224]{0,2,1:T(8,128)(2,1)} %param.1), kind=kOutput, calls=%fused_computation.14 | convolution fusion | flops 939720704 | bytes 11010048 | tf_op jit(solution)/shard_map/qbk,kl->qbl/dot_general | solution.py:211
  26.9 0.7 broadcast_multiply_fusion.count_ref
  27.6 0.0 collective-permute-done
  27.6 1.0 fusion.48
  28.7 3.9 %collective-permute-start.1 = (bf16[15,224,15]{1,2,0:T(8,128)(2,1)S(1)}, bf16[15,224,15]{1,2,0:T(8,128)(2,1)S(1)}, u32[]{:S(2)}, u32[]{:S(2)}) collective-permute-start(bf16[15,224,15]{1,2,0:T(8,128)(2,1)S(1)} %copy.15), channel_id=1, source_target_pairs={{0,1},{1,2},{2,3},{3,4},{4,5},{5,6},{6,7},{8,9},{9,10},{10,11},{11... | collective-permute-start | bytes 302408 | tf_op jit(solution)/shard_map/ppermute | solution.py:172
  32.6 1.3 collective-permute-start.5
  33.9 0.0 collective-permute-done.3
  34.0 0.0 copy-start.1
  34.0 4.8 %collective-permute-start.4 = (bf16[15,224,15]{1,2,0:T(8,128)(2,1)S(1)}, bf16[15,224,15]{1,2,0:T(8,128)(2,1)S(1)}, u32[]{:S(2)}, u32[]{:S(2)}) collective-permute-start(bf16[15,224,15]{1,2,0:T(8,128)(2,1)S(1)} %copy.17), channel_id=1, source_target_pairs={{0,1},{1,2},{2,3},{3,4},{4,5},{5,6},{6,7},{8,9},{9,10},{10,11},{11... | collective-permute-start | bytes 302408 | tf_op jit(solution)/shard_map/ppermute | solution.py:172
  38.9 1.9 %fusion.6 = f32[32,224,256]{2,1,0:T(8,128)S(1)} fusion(bf16[32,224,15]{1,0,2:T(8,128)(2,1)} %collective-permute-done), kind=kOutput, calls=%fused_computation.9 | convolution fusion | flops 55054080 | bytes 7555072 | tf_op jit(solution)/shard_map/qbk,kl->qbl/dot_general | solution.py:211
  40.8 0.0 copy-done.1
  40.8 4.1 %fusion.1.middle_ref = f32[32,224,256]{2,1,0:T(8,128)} fusion(f32[32,224,256]{2,1,0:T(8,128)S(1)} %fusion.6, f32[256,32,224]{0,2,1:T(8,128)S(1)} %copy-done.1, bf16[32,224,15]{1,0,2:T(8,128)(2,1)S(1)} %collective-permute-done.3, s32[15]{0:T(128)S(1)} %iota_add_fusion), kind=kOutput, calls=%fused_computation.3 | convolution fusion | flops 58724096 | bytes 22235196 | tf_op jit(solution)/shard_map/qbk,kl->qbl/dot_general | solution.py:211
  44.9 0.0 collective-permute-done.5
  44.9 1.3 collective-permute-start.7
  46.2 0.5 fusion.22
  46.7 0.0 collective-permute-done.1
  46.7 0.5 fusion.25
  47.2 0.0 collective-permute-done.6
  47.2 2.1 %fusion.9 = f32[15,224,256]{2,1,0:T(8,128)S(1)} fusion(bf16[15,224,256]{2,1,0:T(8,128)(2,1)} %collective-permute-done.6), kind=kOutput, calls=%fused_computation.13 | convolution fusion | flops 440598528 | bytes 5160960 | tf_op jit(solution)/shard_map/qbk,kl->qbl/dot_general | solution.py:211
  49.3 5.7 %collective-permute-done.7 = bf16[15,224,15]{1,2,0:T(8,128)(2,1)S(1)} collective-permute-done((bf16[15,224,15]{1,2,0:T(8,128)(2,1)S(1)}, bf16[15,224,15]{1,2,0:T(8,128)(2,1)S(1)}, u32[]{:S(2)}, u32[]{:S(2)}) %collective-permute-start.7) | collective-permute-done | bytes 100832 | tf_op jit(solution)/shard_map/ppermute | solution.py:172
  55.0 2.4 %add_add_fusion.right_ref = f32[15,224,256]{2,1,0:T(8,128)} fusion(f32[15,224,256]{2,1,0:T(8,128)S(1)} %fusion.22, f32[15,224,256]{2,1,0:T(8,128)S(1)} %fusion.9, bf16[15,224,15]{1,2,0:T(8,128)(2,1)S(1)} %collective-permute-done.7, s32[15]{0:T(128)S(1)} %iota_add_fusion), kind=kOutput, calls=%fused_computation.4 | convolution fusion | flops 27528960 | bytes 10422780 | tf_op jit(solution)/shard_map/qbk,kl->qbl/dot_general | solution.py:211
  57.4 0.0 collective-permute-done.2
  57.4 0.6 fusion.13
  58.1 0.0 collective-permute-done.4
  58.1 2.4 %add_add_fusion.1.left_ref = f32[15,224,256]{2,1,0:T(8,128)} fusion(f32[15,224,256]{2,1,0:T(8,128)S(1)} %fusion.25, f32[15,224,256]{2,1,0:T(8,128)S(1)} %fusion.13, bf16[15,224,15]{1,2,0:T(8,128)(2,1)S(1)} %collective-permute-done.4, s32[15]{0:T(128)S(1)} %iota_add_fusion), kind=kOutput, calls=%fused_computation.5 | convolution fusion | flops 27528960 | bytes 10422780 | tf_op jit(solution)/shard_map/qbk,kl->qbl/dot_general | solution.py:211
  60.5 10.2 %shard_map.17 = (f32[32,224,256]{2,1,0:T(8,128)}, bf16[32,224,256]{2,1,0:T(8,128)(2,1)}) custom-call(f32[15,224,256]{2,1,0:T(8,128)} %add_add_fusion.1.left_ref, f32[32,224,256]{2,1,0:T(8,128)} %fusion.1.middle_ref, f32[15,224,256]{2,1,0:T(8,128)} %add_add_fusion.right_ref, bf16[32,224,256]{2,1,0:T(8,128)(2,1)} %bitcast.60, ...), custom_call_target="tpu_custom_call" | custom-call | tf_op jit(solution)/shard_map/pallas_call | solution.py:245
  70.7 4.3 %convolution_bitcast_fusion = f32[224,224]{1,0:T(8,128)S(1)} fusion(bf16[32,224,256]{2,1,0:T(8,128)(2,1)} %get-tuple-element.14), kind=kOutput, calls=%fused_computation.6 | convolution fusion | flops 822083584 | bytes 3870720 | tf_op jit(solution)/shard_map/pjl,pkl->jk/dot_general | solution.py:274
  75.0 0.1 fusion.49
  75.2 3.5 %collective-permute-start.8 = (f32[225,112]{1,0:T(8,128)S(1)}, f32[225,112]{1,0:T(8,128)S(1)}, u32[]{:S(2)}, u32[]{:S(2)}) collective-permute-start(f32[225,112]{1,0:T(8,128)S(1)} %pad_maximum_fusion), channel_id=1, source_target_pairs={{0,1},{1,0},{2,3},{3,2},{4,5},{5,4},{6,7},{7,6},{8,9},{9,8},{10,11... | collective-permute-start | bytes 302408 | tf_op jit(solution)/shard_map/ppermute | solution.py:278
  78.7 1.0 collective-permute-done.8
  79.7 0.1 collective-permute-start.11
  79.7 3.9 %collective-permute-start.10 = (f32[225,112]{1,0:T(8,128)S(1)}, f32[225,112]{1,0:T(8,128)S(1)}, u32[]{:S(2)}, u32[]{:S(2)}) collective-permute-start(f32[225,112]{1,0:T(8,128)S(1)} %fusion.44), channel_id=1, source_target_pairs={{0,4},{1,5},{2,6},{3,7},{4,0},{5,1},{6,2},{7,3},{8,12},{9,13},{10,... | collective-permute-start | bytes 302408 | tf_op jit(solution)/shard_map/ppermute | solution.py:54
  83.6 0.0 collective-permute-start.9
  83.6 2.4 %collective-permute-done.11 = f32[225,112]{1,0:T(8,128)S(1)} collective-permute-done((f32[225,112]{1,0:T(8,128)S(1)}, f32[225,112]{1,0:T(8,128)S(1)}, u32[]{:S(2)}, u32[]{:S(2)}) %collective-permute-start.11) | collective-permute-done | bytes 100832 | tf_op jit(solution)/shard_map/ppermute | solution.py:54
  86.0 3.6 %collective-permute-done.10 = f32[225,112]{1,0:T(8,128)S(1)} collective-permute-done((f32[225,112]{1,0:T(8,128)S(1)}, f32[225,112]{1,0:T(8,128)S(1)}, u32[]{:S(2)}, u32[]{:S(2)}) %collective-permute-start.10) | collective-permute-done | bytes 100832 | tf_op jit(solution)/shard_map/ppermute | solution.py:54
  89.6 0.0 collective-permute-done.9
  89.6 3.6 %collective-permute-start.14 = (f32[225,112]{1,0:T(8,128)S(1)}, f32[225,112]{1,0:T(8,128)S(1)}, u32[]{:S(2)}, u32[]{:S(2)}) collective-permute-start(f32[225,112]{1,0:T(8,128)S(1)} %add_add_fusion.3), channel_id=1, source_target_pairs={{0,24},{8,0},{16,8},{24,16},{1,25},{9,1},{17,9},{25,17},{2,26},{10... | collective-permute-start | bytes 302408 | tf_op jit(solution)/shard_map/ppermute | solution.py:54
  93.3 0.0 collective-permute-start.13
  93.3 1.0 collective-permute-start.12
  94.3 2.7 %collective-permute-done.14 = f32[225,112]{1,0:T(8,128)S(1)} collective-permute-done((f32[225,112]{1,0:T(8,128)S(1)}, f32[225,112]{1,0:T(8,128)S(1)}, u32[]{:S(2)}, u32[]{:S(2)}) %collective-permute-start.14) | collective-permute-done | bytes 100832 | tf_op jit(solution)/shard_map/ppermute | solution.py:54
  97.0 6.2 %collective-permute-done.13 = f32[225,112]{1,0:T(8,128)S(1)} collective-permute-done((f32[225,112]{1,0:T(8,128)S(1)}, f32[225,112]{1,0:T(8,128)S(1)}, u32[]{:S(2)}, u32[]{:S(2)}) %collective-permute-start.13) | collective-permute-done | bytes 100832 | tf_op jit(solution)/shard_map/ppermute | solution.py:54
  103.2 0.0 collective-permute-done.12
  103.2 0.1 copy.25
  103.4 0.1 copy.26
  103.5 0.7 select_reduce_fusion
  104.8 0.8 select_add_fusion.a_ref
  105.6 28.4 %shard_map.18 = f32[256,256]{1,0:T(8,128)} custom-call(f32[224,224]{1,0:T(8,128)} %select_add_fusion.a_ref), custom_call_target="tpu_custom_call" | custom-call | tf_op jit(solution)/shard_map/pallas_call | solution.py:127
  134.1 10.2 %fusion = f32[32,256]{1,0:T(8,128)S(1)} fusion(f32[32,224,256]{2,1,0:T(8,128)} %get-tuple-element.13, f32[256,256]{1,0:T(8,128)} %shard_map.18), kind=kOutput, calls=%fused_computation.1 | convolution fusion | flops 4936213504 | bytes 14942208 | tf_op jit(solution)/shard_map/pbl,bj->pjl/dot_general | solution.py:284
  144.3 0.6 multiply_bitcast_fusion
  (15 shorter events, 0.4 us)
Async XLA Ops:
  0.0 7.9 %copy-start = (bf16[256,32,224]{0,2,1:T(8,128)(2,1)S(1)}, bf16[256,32,224]{0,2,1:T(8,128)(2,1)}, u32[]{:S(2)}) copy-start(bf16[256,32,224]{0,2,1:T(8,128)(2,1)} %param.1) | copy-start | bytes 11010052
  4.2 53.3 %collective-permute-start.2 = (bf16[15,224,256]{2,1,0:T(8,128)(2,1)}, bf16[15,224,256]{2,1,0:T(8,128)(2,1)S(1)}, u32[]{:S(2)}, u32[]{:S(2)}) collective-permute-start(bf16[15,224,256]{2,1,0:T(8,128)(2,1)} %get-tuple-element.11), channel_id=1, source_target_pairs={{0,1},{1,2},{2,3},{3,4},{4,5},{5,6},{6,7},{8,9},{9,10},{10,11},{11... | collective-permute-start | bytes 5160968 | tf_op jit(solution)/shard_map/ppermute | solution.py:172
  6.6 40.6 %collective-permute-start.6 = (bf16[15,224,256]{2,1,0:T(8,128)(2,1)}, bf16[15,224,256]{2,1,0:T(8,128)(2,1)}, u32[]{:S(2)}, u32[]{:S(2)}) collective-permute-start(bf16[15,224,256]{2,1,0:T(8,128)(2,1)} %get-tuple-element.12), channel_id=1, source_target_pairs={{1,0},{2,1},{3,2},{4,3},{5,4},{6,5},{7,6},{9,8},{10,9},{11,10},{12... | collective-permute-start | bytes 5160968 | tf_op jit(solution)/shard_map/ppermute | solution.py:172
  12.8 14.8 %collective-permute-start = (bf16[32,224,15]{1,0,2:T(8,128)(2,1)}, bf16[32,224,15]{1,0,2:T(8,128)(2,1)}, u32[]{:S(2)}, u32[]{:S(2)}) collective-permute-start(bf16[32,224,15]{1,0,2:T(8,128)(2,1)} %copy.14), channel_id=1, source_target_pairs={{0,8},{8,16},{16,24},{1,9},{9,17},{17,25},{2,10},{10,18},{18,26},{... | collective-permute-start | bytes 645128 | tf_op jit(solution)/shard_map/ppermute | solution.py:175
  19.4 14.5 %collective-permute-start.3 = (bf16[32,224,15]{1,0,2:T(8,128)(2,1)}, bf16[32,224,15]{1,0,2:T(8,128)(2,1)S(1)}, u32[]{:S(2)}, u32[]{:S(2)}) collective-permute-start(bf16[32,224,15]{1,0,2:T(8,128)(2,1)} %copy.16), channel_id=1, source_target_pairs={{8,0},{16,8},{24,16},{9,1},{17,9},{25,17},{10,2},{18,10},{26,18},{... | collective-permute-start | bytes 645128 | tf_op jit(solution)/shard_map/ppermute | solution.py:175
  28.7 18.0 %collective-permute-start.1 = (bf16[15,224,15]{1,2,0:T(8,128)(2,1)S(1)}, bf16[15,224,15]{1,2,0:T(8,128)(2,1)S(1)}, u32[]{:S(2)}, u32[]{:S(2)}) collective-permute-start(bf16[15,224,15]{1,2,0:T(8,128)(2,1)S(1)} %copy.15), channel_id=1, source_target_pairs={{0,1},{1,2},{2,3},{3,4},{4,5},{5,6},{6,7},{8,9},{9,10},{10,11},{11... | collective-permute-start | bytes 302408 | tf_op jit(solution)/shard_map/ppermute | solution.py:172
  32.6 12.3 %collective-permute-start.5 = (bf16[15,224,15]{1,2,0:T(8,128)(2,1)S(1)}, bf16[15,224,15]{1,2,0:T(8,128)(2,1)S(1)}, u32[]{:S(2)}, u32[]{:S(2)}) collective-permute-start(bf16[15,224,15]{1,2,0:T(8,128)(2,1)S(1)} %copy.20), channel_id=1, source_target_pairs={{1,0},{2,1},{3,2},{4,3},{5,4},{6,5},{7,6},{9,8},{10,9},{11,10},{12... | collective-permute-start | bytes 302408 | tf_op jit(solution)/shard_map/ppermute | solution.py:172
  34.0 6.7 %copy-start.1 = (f32[256,32,224]{0,2,1:T(8,128)S(1)}, f32[256,32,224]{0,2,1:T(8,128)}, u32[]{:S(2)}) copy-start(f32[256,32,224]{0,2,1:T(8,128)} %fusion.11) | copy-start | bytes 22020100
  34.0 24.0 %collective-permute-start.4 = (bf16[15,224,15]{1,2,0:T(8,128)(2,1)S(1)}, bf16[15,224,15]{1,2,0:T(8,128)(2,1)S(1)}, u32[]{:S(2)}, u32[]{:S(2)}) collective-permute-start(bf16[15,224,15]{1,2,0:T(8,128)(2,1)S(1)} %copy.17), channel_id=1, source_target_pairs={{0,1},{1,2},{2,3},{3,4},{4,5},{5,6},{6,7},{8,9},{9,10},{10,11},{11... | collective-permute-start | bytes 302408 | tf_op jit(solution)/shard_map/ppermute | solution.py:172
  44.9 10.1 %collective-permute-start.7 = (bf16[15,224,15]{1,2,0:T(8,128)(2,1)S(1)}, bf16[15,224,15]{1,2,0:T(8,128)(2,1)S(1)}, u32[]{:S(2)}, u32[]{:S(2)}) collective-permute-start(bf16[15,224,15]{1,2,0:T(8,128)(2,1)S(1)} %copy.21), channel_id=1, source_target_pairs={{1,0},{2,1},{3,2},{4,3},{5,4},{6,5},{7,6},{9,8},{10,9},{11,10},{12... | collective-permute-start | bytes 302408 | tf_op jit(solution)/shard_map/ppermute | solution.py:172
  75.2 4.5 %collective-permute-start.8 = (f32[225,112]{1,0:T(8,128)S(1)}, f32[225,112]{1,0:T(8,128)S(1)}, u32[]{:S(2)}, u32[]{:S(2)}) collective-permute-start(f32[225,112]{1,0:T(8,128)S(1)} %pad_maximum_fusion), channel_id=1, source_target_pairs={{0,1},{1,0},{2,3},{3,2},{4,5},{5,4},{6,7},{7,6},{8,9},{9,8},{10,11... | collective-permute-start | bytes 302408 | tf_op jit(solution)/shard_map/ppermute | solution.py:278
  79.7 6.3 %collective-permute-start.11 = (f32[225,112]{1,0:T(8,128)S(1)}, f32[225,112]{1,0:T(8,128)S(1)}, u32[]{:S(2)}, u32[]{:S(2)}) collective-permute-start(f32[225,112]{1,0:T(8,128)S(1)} %fusion.44), channel_id=1, source_target_pairs={{0,6},{1,7},{2,0},{3,1},{4,2},{5,3},{6,4},{7,5},{8,14},{9,15},{10,... | collective-permute-start | bytes 302408 | tf_op jit(solution)/shard_map/ppermute | solution.py:54
  79.7 9.9 %collective-permute-start.10 = (f32[225,112]{1,0:T(8,128)S(1)}, f32[225,112]{1,0:T(8,128)S(1)}, u32[]{:S(2)}, u32[]{:S(2)}) collective-permute-start(f32[225,112]{1,0:T(8,128)S(1)} %fusion.44), channel_id=1, source_target_pairs={{0,4},{1,5},{2,6},{3,7},{4,0},{5,1},{6,2},{7,3},{8,12},{9,13},{10,... | collective-permute-start | bytes 302408 | tf_op jit(solution)/shard_map/ppermute | solution.py:54
  83.6 6.0 %collective-permute-start.9 = (f32[225,112]{1,0:T(8,128)S(1)}, f32[225,112]{1,0:T(8,128)S(1)}, u32[]{:S(2)}, u32[]{:S(2)}) collective-permute-start(f32[225,112]{1,0:T(8,128)S(1)} %fusion.44), channel_id=1, source_target_pairs={{0,2},{1,3},{2,4},{3,5},{4,6},{5,7},{6,0},{7,1},{8,10},{9,11},{10,... | collective-permute-start | bytes 302408 | tf_op jit(solution)/shard_map/ppermute | solution.py:54
  89.6 7.3 %collective-permute-start.14 = (f32[225,112]{1,0:T(8,128)S(1)}, f32[225,112]{1,0:T(8,128)S(1)}, u32[]{:S(2)}, u32[]{:S(2)}) collective-permute-start(f32[225,112]{1,0:T(8,128)S(1)} %add_add_fusion.3), channel_id=1, source_target_pairs={{0,24},{8,0},{16,8},{24,16},{1,25},{9,1},{17,9},{25,17},{2,26},{10... | collective-permute-start | bytes 302408 | tf_op jit(solution)/shard_map/ppermute | solution.py:54
  93.3 9.9 %collective-permute-start.13 = (f32[225,112]{1,0:T(8,128)S(1)}, f32[225,112]{1,0:T(8,128)S(1)}, u32[]{:S(2)}, u32[]{:S(2)}) collective-permute-start(f32[225,112]{1,0:T(8,128)S(1)} %add_add_fusion.3), channel_id=1, source_target_pairs={{0,16},{8,24},{16,0},{24,8},{1,17},{9,25},{17,1},{25,9},{2,18},{10... | collective-permute-start | bytes 302408 | tf_op jit(solution)/shard_map/ppermute | solution.py:54
  93.3 9.9 %collective-permute-start.12 = (f32[225,112]{1,0:T(8,128)S(1)}, f32[225,112]{1,0:T(8,128)S(1)}, u32[]{:S(2)}, u32[]{:S(2)}) collective-permute-start(f32[225,112]{1,0:T(8,128)S(1)} %add_add_fusion.3), channel_id=1, source_target_pairs={{0,8},{8,16},{16,24},{24,0},{1,9},{9,17},{17,25},{25,1},{2,10},{10... | collective-permute-start | bytes 302408 | tf_op jit(solution)/shard_map/ppermute | solution.py:54

commit v15 on v14

--- a/solution.py
+++ b/solution.py
@@ -78,12 +78,17 @@
     return jnp.concatenate([top, bottom], axis=0)
 
 
-def sweep_kernel(n, a_ref, o_ref):
+def sweep_kernel(n, load, a_ref, o_ref):
     size = o_ref.shape[0]
     rows = lax.broadcasted_iota(jnp.int32, (size, 1), 0)
     lanes = lax.broadcasted_iota(jnp.int32, (1, size), 1)
     o_ref[...] = jnp.where(rows == lanes, 1.0, 0.0).astype(jnp.float32)
     o_ref[:n, :n] = a_ref[...]
+    if load:
+        on_diagonal = (rows == lanes) & (rows < n)
+        full = o_ref[...]
+        trace = jnp.sum(jnp.where(on_diagonal, full, 0.0), axis=(0, 1), keepdims=True)
+        o_ref[...] = jnp.where(on_diagonal, full + load * (trace / n), full)
     sub8 = lax.broadcasted_iota(jnp.int32, (8, 1), 0)
 
     def pick(v, j):
@@ -120,12 +125,12 @@
     lax.fori_loop(0, n // 2, body, 0)
 
 
-def spd_inverse(a):
+def spd_inverse(a, load=0.0):
     n = a.shape[0]
     assert n % 2 == 0
     size = -(-n // 128) * 128
     swept = pl.pallas_call(
-        functools.partial(sweep_kernel, n),
+        functools.partial(sweep_kernel, n, load),
         out_shape=jax.ShapeDtypeStruct((size, size), jnp.float32),
     )(a)
     return -swept[:n, :n]
@@ -278,9 +283,7 @@
     packed = packed + lax.ppermute(packed, "cross", [(i, i ^ 1) for i in range(n_cross)])
     packed = ring_sum(ring_sum(packed, "cross", 2), "track", 1)
     covariance = unpack_symmetric(packed) / (total_lines * total_pix)
-    identity = jnp.eye(bands, dtype=jnp.float32)
-    loaded = covariance + LOAD * (jnp.trace(covariance) / bands) * identity
-    inverse = spd_inverse(loaded)
+    inverse = spd_inverse(covariance, LOAD)
     solved = jnp.einsum(
         "pbl,bj->pjl", residual, inverse, precision=highest, preferred_element_type=jnp.float32
     )

time: 145 us -> 144 us (level)
  transfers between devices with their start and end apart: 15 -> 15, of which waited for: 6 -> 6; matrix products, arithmetic and copies ran while one was open for 18% -> 19% of each run, Pallas kernels for 0% -> 0%
where the time goes in v15:
time: 144 us
  Pallas kernels  38.8 us (27%)
  matrix products  35.2 us (24%)
  starting transfers between devices  33.5 us (23%)
  waiting for transfers between devices  21.6 us (15%)
  local copies, waits for them, and re-layouts  12 us (8%)
  other arithmetic  2.4 us (2%)
    pallas_call x1, Pallas kernels, spd_inverse(): pl.pallas_call(functools.partial(sweep_kernel, n, load), out_shape=jax.Sh...  28.6 us
    dot_general x9, matrix products, sum_lines(): jnp.einsum('qbk,kl->qbl', values, w, preferred_element_type=jnp.float32)  20.7 us
    ppermute x6, starting transfers between devices, fetch(): return lax.ppermute(piece, 'cross', pairs)  15.1 us
    ppermute x6, waiting for transfers between devices, ring_sum(): total = total + lax.ppermute(x, axis, pairs)  14.9 us
    pallas_call x1, Pallas kernels, residuals(): pl.pallas_call(residual_kernel, grid=(bands // block,), in_specs=[spec(le...  10.3 us
    dot_general x1, matrix products, shards(): jnp.einsum('pbl,bj->pjl', residual, inverse, precision=highest, preferred...  10.2 us
    ppermute x6, starting transfers between devices, ring_sum(): total = total + lax.ppermute(x, axis, pairs)  8.58 us
    ppermute x2, starting transfers between devices, fetch(): return lax.ppermute(piece, 'track', pairs)  6.29 us
  transfers between devices with their start and end apart: 15, of which 6 were waited for; matrix products, arithmetic and copies ran while one was open for 19% of the time, Pallas kernels for 0%

profile of v15, /device:TPU:0, one launch (start us, length us, event | category | flops | bytes accessed | tf_op | source)
XLA Modules:
  0.0 143.7 jit_solution(1272111936511177761)
XLA Ops:
  0.0 0.0 copy-start
  0.0 4.2 %fusion.46 = (bf16[15,224,256]{2,1,0:T(8,128)(2,1)}, bf16[15,224,256]{2,1,0:T(8,128)(2,1)}) fusion(bf16[32,224,256]{2,1,0:T(8,128)(2,1)} %bitcast.59), kind=kLoop, calls=%fused_computation.57 | loop fusion | bytes 6881280 | tf_op jit(solution)/shard_map/slice | solution.py:184
  4.2 2.5 %collective-permute-start.2 = (bf16[15,224,256]{2,1,0:T(8,128)(2,1)}, bf16[15,224,256]{2,1,0:T(8,128)(2,1)S(1)}, u32[]{:S(2)}, u32[]{:S(2)}) collective-permute-start(bf16[15,224,256]{2,1,0:T(8,128)(2,1)} %get-tuple-element.11), channel_id=1, source_target_pairs={{0,1},{1,2},{2,3},{3,4},{4,5},{5,6},{6,7},{8,9},{9,10},{10,11},{11... | collective-permute-start | bytes 5160968 | tf_op jit(solution)/shard_map/ppermute | solution.py:177
  6.6 1.3 collective-permute-start.6
  7.9 0.0 copy-done
  7.9 2.1 %fusion.45 = (bf16[32,224,15]{2,1,0:T(8,128)(2,1)S(1)}, bf16[32,224,15]{2,1,0:T(8,128)(2,1)}) fusion(bf16[32,224,256]{2,1,0:T(8,128)(2,1)S(1)} %bitcast.61), kind=kLoop, calls=%fused_computation.56 | loop fusion | bytes 860160 | tf_op jit(solution)/shard_map/slice | solution.py:190
  10.0 2.7 %copy.14 = bf16[32,224,15]{1,0,2:T(8,128)(2,1)} copy(bf16[32,224,15]{2,1,0:T(8,128)(2,1)} %get-tuple-element.16) | data formatting | bytes 430080 | tf_op jit(solution)/shard_map/slice | solution.py:189
  12.7 5.0 %collective-permute-start = (bf16[32,224,15]{1,0,2:T(8,128)(2,1)}, bf16[32,224,15]{1,0,2:T(8,128)(2,1)}, u32[]{:S(2)}, u32[]{:S(2)}) collective-permute-start(bf16[32,224,15]{1,0,2:T(8,128)(2,1)} %copy.14), channel_id=1, source_target_pairs={{0,8},{8,16},{16,24},{1,9},{9,17},{17,25},{2,10},{10,18},{18,26},{... | collective-permute-start | bytes 645128 | tf_op jit(solution)/shard_map/ppermute | solution.py:180
  17.7 1.7 %copy.16 = bf16[32,224,15]{1,0,2:T(8,128)(2,1)} copy(bf16[32,224,15]{2,1,0:T(8,128)(2,1)S(1)} %get-tuple-element.15) | data formatting | bytes 430080 | tf_op jit(solution)/shard_map/slice | solution.py:190
  19.4 1.3 collective-permute-start.3
  20.7 6.1 %fusion.11 = f32[256,32,224]{0,2,1:T(8,128)} fusion(bf16[256,32,224]{0,2,1:T(8,128)(2,1)} %param.1), kind=kOutput, calls=%fused_computation.14 | convolution fusion | flops 939720704 | bytes 11010048 | tf_op jit(solution)/shard_map/qbk,kl->qbl/dot_general | solution.py:216
  26.9 0.7 broadcast_multiply_fusion.count_ref
  27.6 0.0 collective-permute-done
  27.6 1.0 fusion.48
  28.7 3.9 %collective-permute-start.1 = (bf16[15,224,15]{1,2,0:T(8,128)(2,1)S(1)}, bf16[15,224,15]{1,2,0:T(8,128)(2,1)S(1)}, u32[]{:S(2)}, u32[]{:S(2)}) collective-permute-start(bf16[15,224,15]{1,2,0:T(8,128)(2,1)S(1)} %copy.15), channel_id=1, source_target_pairs={{0,1},{1,2},{2,3},{3,4},{4,5},{5,6},{6,7},{8,9},{9,10},{10,11},{11... | collective-permute-start | bytes 302408 | tf_op jit(solution)/shard_map/ppermute | solution.py:177
  32.6 1.3 collective-permute-start.5
  33.9 0.0 collective-permute-done.3
  34.0 0.0 copy-start.1
  34.0 4.8 %collective-permute-start.4 = (bf16[15,224,15]{1,2,0:T(8,128)(2,1)S(1)}, bf16[15,224,15]{1,2,0:T(8,128)(2,1)S(1)}, u32[]{:S(2)}, u32[]{:S(2)}) collective-permute-start(bf16[15,224,15]{1,2,0:T(8,128)(2,1)S(1)} %copy.17), channel_id=1, source_target_pairs={{0,1},{1,2},{2,3},{3,4},{4,5},{5,6},{6,7},{8,9},{9,10},{10,11},{11... | collective-permute-start | bytes 302408 | tf_op jit(solution)/shard_map/ppermute | solution.py:177
  38.8 1.9 %fusion.6 = f32[32,224,256]{2,1,0:T(8,128)S(1)} fusion(bf16[32,224,15]{1,0,2:T(8,128)(2,1)} %collective-permute-done), kind=kOutput, calls=%fused_computation.9 | convolution fusion | flops 55054080 | bytes 7555072 | tf_op jit(solution)/shard_map/qbk,kl->qbl/dot_general | solution.py:216
  40.7 0.0 copy-done.1
  40.7 4.1 %fusion.1.middle_ref = f32[32,224,256]{2,1,0:T(8,128)} fusion(f32[32,224,256]{2,1,0:T(8,128)S(1)} %fusion.6, f32[256,32,224]{0,2,1:T(8,128)S(1)} %copy-done.1, bf16[32,224,15]{1,0,2:T(8,128)(2,1)S(1)} %collective-permute-done.3, s32[15]{0:T(128)S(1)} %iota_add_fusion), kind=kOutput, calls=%fused_computation.3 | convolution fusion | flops 58724096 | bytes 22235196 | tf_op jit(solution)/shard_map/qbk,kl->qbl/dot_general | solution.py:216
  44.9 0.0 collective-permute-done.5
  44.9 1.3 collective-permute-start.7
  46.2 0.5 fusion.22
  46.7 0.0 collective-permute-done.1
  46.7 0.5 fusion.25
  47.2 0.0 collective-permute-done.6
  47.2 2.1 %fusion.9 = f32[15,224,256]{2,1,0:T(8,128)S(1)} fusion(bf16[15,224,256]{2,1,0:T(8,128)(2,1)} %collective-permute-done.6), kind=kOutput, calls=%fused_computation.13 | convolution fusion | flops 440598528 | bytes 5160960 | tf_op jit(solution)/shard_map/qbk,kl->qbl/dot_general | solution.py:216
  49.3 5.7 %collective-permute-done.7 = bf16[15,224,15]{1,2,0:T(8,128)(2,1)S(1)} collective-permute-done((bf16[15,224,15]{1,2,0:T(8,128)(2,1)S(1)}, bf16[15,224,15]{1,2,0:T(8,128)(2,1)S(1)}, u32[]{:S(2)}, u32[]{:S(2)}) %collective-permute-start.7) | collective-permute-done | bytes 100832 | tf_op jit(solution)/shard_map/ppermute | solution.py:177
  55.0 2.4 %add_add_fusion.right_ref = f32[15,224,256]{2,1,0:T(8,128)} fusion(f32[15,224,256]{2,1,0:T(8,128)S(1)} %fusion.22, f32[15,224,256]{2,1,0:T(8,128)S(1)} %fusion.9, bf16[15,224,15]{1,2,0:T(8,128)(2,1)S(1)} %collective-permute-done.7, s32[15]{0:T(128)S(1)} %iota_add_fusion), kind=kOutput, calls=%fused_computation.4 | convolution fusion | flops 27528960 | bytes 10422780 | tf_op jit(solution)/shard_map/qbk,kl->qbl/dot_general | solution.py:216
  57.4 0.0 collective-permute-done.2
  57.4 0.6 fusion.13
  58.0 0.0 collective-permute-done.4
  58.1 2.4 %add_add_fusion.1.left_ref = f32[15,224,256]{2,1,0:T(8,128)} fusion(f32[15,224,256]{2,1,0:T(8,128)S(1)} %fusion.25, f32[15,224,256]{2,1,0:T(8,128)S(1)} %fusion.13, bf16[15,224,15]{1,2,0:T(8,128)(2,1)S(1)} %collective-permute-done.4, s32[15]{0:T(128)S(1)} %iota_add_fusion), kind=kOutput, calls=%fused_computation.5 | convolution fusion | flops 27528960 | bytes 10422780 | tf_op jit(solution)/shard_map/qbk,kl->qbl/dot_general | solution.py:216
  60.5 10.3 %shard_map.17 = (f32[32,224,256]{2,1,0:T(8,128)}, bf16[32,224,256]{2,1,0:T(8,128)(2,1)}) custom-call(f32[15,224,256]{2,1,0:T(8,128)} %add_add_fusion.1.left_ref, f32[32,224,256]{2,1,0:T(8,128)} %fusion.1.middle_ref, f32[15,224,256]{2,1,0:T(8,128)} %add_add_fusion.right_ref, bf16[32,224,256]{2,1,0:T(8,128)(2,1)} %bitcast.60, ...), custom_call_target="tpu_custom_call" | custom-call | tf_op jit(solution)/shard_map/pallas_call | solution.py:250
  70.8 4.3 %convolution_bitcast_fusion = f32[224,224]{1,0:T(8,128)S(1)} fusion(bf16[32,224,256]{2,1,0:T(8,128)(2,1)} %get-tuple-element.14), kind=kOutput, calls=%fused_computation.6 | convolution fusion | flops 822083584 | bytes 3870720 | tf_op jit(solution)/shard_map/pjl,pkl->jk/dot_general | solution.py:279
  75.0 0.1 fusion.49
  75.2 3.5 %collective-permute-start.8 = (f32[225,112]{1,0:T(8,128)S(1)}, f32[225,112]{1,0:T(8,128)S(1)}, u32[]{:S(2)}, u32[]{:S(2)}) collective-permute-start(f32[225,112]{1,0:T(8,128)S(1)} %pad_maximum_fusion), channel_id=1, source_target_pairs={{0,1},{1,0},{2,3},{3,2},{4,5},{5,4},{6,7},{7,6},{8,9},{9,8},{10,11... | collective-permute-start | bytes 302408 | tf_op jit(solution)/shard_map/ppermute | solution.py:283
  78.7 1.0 collective-permute-done.8
  79.7 0.1 collective-permute-start.11
  79.8 3.9 %collective-permute-start.10 = (f32[225,112]{1,0:T(8,128)S(1)}, f32[225,112]{1,0:T(8,128)S(1)}, u32[]{:S(2)}, u32[]{:S(2)}) collective-permute-start(f32[225,112]{1,0:T(8,128)S(1)} %fusion.44), channel_id=1, source_target_pairs={{0,4},{1,5},{2,6},{3,7},{4,0},{5,1},{6,2},{7,3},{8,12},{9,13},{10,... | collective-permute-start | bytes 302408 | tf_op jit(solution)/shard_map/ppermute | solution.py:54
  83.6 0.0 collective-permute-start.9
  83.6 2.4 %collective-permute-done.11 = f32[225,112]{1,0:T(8,128)S(1)} collective-permute-done((f32[225,112]{1,0:T(8,128)S(1)}, f32[225,112]{1,0:T(8,128)S(1)}, u32[]{:S(2)}, u32[]{:S(2)}) %collective-permute-start.11) | collective-permute-done | bytes 100832 | tf_op jit(solution)/shard_map/ppermute | solution.py:54
  86.0 3.6 %collective-permute-done.10 = f32[225,112]{1,0:T(8,128)S(1)} collective-permute-done((f32[225,112]{1,0:T(8,128)S(1)}, f32[225,112]{1,0:T(8,128)S(1)}, u32[]{:S(2)}, u32[]{:S(2)}) %collective-permute-start.10) | collective-permute-done | bytes 100832 | tf_op jit(solution)/shard_map/ppermute | solution.py:54
  89.6 0.0 collective-permute-done.9
  89.7 3.7 %collective-permute-start.14 = (f32[225,112]{1,0:T(8,128)S(1)}, f32[225,112]{1,0:T(8,128)S(1)}, u32[]{:S(2)}, u32[]{:S(2)}) collective-permute-start(f32[225,112]{1,0:T(8,128)S(1)} %add_add_fusion.3), channel_id=1, source_target_pairs={{0,24},{8,0},{16,8},{24,16},{1,25},{9,1},{17,9},{25,17},{2,26},{10... | collective-permute-start | bytes 302408 | tf_op jit(solution)/shard_map/ppermute | solution.py:54
  93.3 0.0 collective-permute-start.13
  93.3 1.0 collective-permute-start.12
  94.3 2.7 %collective-permute-done.14 = f32[225,112]{1,0:T(8,128)S(1)} collective-permute-done((f32[225,112]{1,0:T(8,128)S(1)}, f32[225,112]{1,0:T(8,128)S(1)}, u32[]{:S(2)}, u32[]{:S(2)}) %collective-permute-start.14) | collective-permute-done | bytes 100832 | tf_op jit(solution)/shard_map/ppermute | solution.py:54
  97.0 6.2 %collective-permute-done.13 = f32[225,112]{1,0:T(8,128)S(1)} collective-permute-done((f32[225,112]{1,0:T(8,128)S(1)}, f32[225,112]{1,0:T(8,128)S(1)}, u32[]{:S(2)}, u32[]{:S(2)}) %collective-permute-start.13) | collective-permute-done | bytes 100832 | tf_op jit(solution)/shard_map/ppermute | solution.py:54
  103.2 0.0 collective-permute-done.12
  103.3 0.1 copy.25
  103.4 0.1 copy.26
  103.5 0.8 maximum_multiply_fusion.a_ref
  104.3 28.6 %shard_map.18 = f32[256,256]{1,0:T(8,128)} custom-call(f32[224,224]{1,0:T(8,128)} %maximum_multiply_fusion.a_ref), custom_call_target="tpu_custom_call" | custom-call | tf_op jit(solution)/shard_map/pallas_call | solution.py:132
  132.9 10.2 %fusion = f32[32,256]{1,0:T(8,128)S(1)} fusion(f32[32,224,256]{2,1,0:T(8,128)} %get-tuple-element.13, f32[256,256]{1,0:T(8,128)} %shard_map.18), kind=kOutput, calls=%fused_computation.1 | convolution fusion | flops 4936213504 | bytes 14942208 | tf_op jit(solution)/shard_map/pbl,bj->pjl/dot_general | solution.py:287
  143.1 0.6 multiply_bitcast_fusion
  (15 shorter events, 0.4 us)
Async XLA Ops:
  0.0 7.9 %copy-start = (bf16[256,32,224]{0,2,1:T(8,128)(2,1)S(1)}, bf16[256,32,224]{0,2,1:T(8,128)(2,1)}, u32[]{:S(2)}) copy-start(bf16[256,32,224]{0,2,1:T(8,128)(2,1)} %param.1) | copy-start | bytes 11010052
  4.2 53.3 %collective-permute-start.2 = (bf16[15,224,256]{2,1,0:T(8,128)(2,1)}, bf16[15,224,256]{2,1,0:T(8,128)(2,1)S(1)}, u32[]{:S(2)}, u32[]{:S(2)}) collective-permute-start(bf16[15,224,256]{2,1,0:T(8,128)(2,1)} %get-tuple-element.11), channel_id=1, source_target_pairs={{0,1},{1,2},{2,3},{3,4},{4,5},{5,6},{6,7},{8,9},{9,10},{10,11},{11... | collective-permute-start | bytes 5160968 | tf_op jit(solution)/shard_map/ppermute | solution.py:177
  6.6 40.6 %collective-permute-start.6 = (bf16[15,224,256]{2,1,0:T(8,128)(2,1)}, bf16[15,224,256]{2,1,0:T(8,128)(2,1)}, u32[]{:S(2)}, u32[]{:S(2)}) collective-permute-start(bf16[15,224,256]{2,1,0:T(8,128)(2,1)} %get-tuple-element.12), channel_id=1, source_target_pairs={{1,0},{2,1},{3,2},{4,3},{5,4},{6,5},{7,6},{9,8},{10,9},{11,10},{12... | collective-permute-start | bytes 5160968 | tf_op jit(solution)/shard_map/ppermute | solution.py:177
  12.7 14.8 %collective-permute-start = (bf16[32,224,15]{1,0,2:T(8,128)(2,1)}, bf16[32,224,15]{1,0,2:T(8,128)(2,1)}, u32[]{:S(2)}, u32[]{:S(2)}) collective-permute-start(bf16[32,224,15]{1,0,2:T(8,128)(2,1)} %copy.14), channel_id=1, source_target_pairs={{0,8},{8,16},{16,24},{1,9},{9,17},{17,25},{2,10},{10,18},{18,26},{... | collective-permute-start | bytes 645128 | tf_op jit(solution)/shard_map/ppermute | solution.py:180
  19.4 14.5 %collective-permute-start.3 = (bf16[32,224,15]{1,0,2:T(8,128)(2,1)}, bf16[32,224,15]{1,0,2:T(8,128)(2,1)S(1)}, u32[]{:S(2)}, u32[]{:S(2)}) collective-permute-start(bf16[32,224,15]{1,0,2:T(8,128)(2,1)} %copy.16), channel_id=1, source_target_pairs={{8,0},{16,8},{24,16},{9,1},{17,9},{25,17},{10,2},{18,10},{26,18},{... | collective-permute-start | bytes 645128 | tf_op jit(solution)/shard_map/ppermute | solution.py:180
  28.7 18.0 %collective-permute-start.1 = (bf16[15,224,15]{1,2,0:T(8,128)(2,1)S(1)}, bf16[15,224,15]{1,2,0:T(8,128)(2,1)S(1)}, u32[]{:S(2)}, u32[]{:S(2)}) collective-permute-start(bf16[15,224,15]{1,2,0:T(8,128)(2,1)S(1)} %copy.15), channel_id=1, source_target_pairs={{0,1},{1,2},{2,3},{3,4},{4,5},{5,6},{6,7},{8,9},{9,10},{10,11},{11... | collective-permute-start | bytes 302408 | tf_op jit(solution)/shard_map/ppermute | solution.py:177
  32.6 12.3 %collective-permute-start.5 = (bf16[15,224,15]{1,2,0:T(8,128)(2,1)S(1)}, bf16[15,224,15]{1,2,0:T(8,128)(2,1)S(1)}, u32[]{:S(2)}, u32[]{:S(2)}) collective-permute-start(bf16[15,224,15]{1,2,0:T(8,128)(2,1)S(1)} %copy.20), channel_id=1, source_target_pairs={{1,0},{2,1},{3,2},{4,3},{5,4},{6,5},{7,6},{9,8},{10,9},{11,10},{12... | collective-permute-start | bytes 302408 | tf_op jit(solution)/shard_map/ppermute | solution.py:177
  34.0 6.7 %copy-start.1 = (f32[256,32,224]{0,2,1:T(8,128)S(1)}, f32[256,32,224]{0,2,1:T(8,128)}, u32[]{:S(2)}) copy-start(f32[256,32,224]{0,2,1:T(8,128)} %fusion.11) | copy-start | bytes 22020100
  34.0 24.0 %collective-permute-start.4 = (bf16[15,224,15]{1,2,0:T(8,128)(2,1)S(1)}, bf16[15,224,15]{1,2,0:T(8,128)(2,1)S(1)}, u32[]{:S(2)}, u32[]{:S(2)}) collective-permute-start(bf16[15,224,15]{1,2,0:T(8,128)(2,1)S(1)} %copy.17), channel_id=1, source_target_pairs={{0,1},{1,2},{2,3},{3,4},{4,5},{5,6},{6,7},{8,9},{9,10},{10,11},{11... | collective-permute-start | bytes 302408 | tf_op jit(solution)/shard_map/ppermute | solution.py:177
  44.9 10.1 %collective-permute-start.7 = (bf16[15,224,15]{1,2,0:T(8,128)(2,1)S(1)}, bf16[15,224,15]{1,2,0:T(8,128)(2,1)S(1)}, u32[]{:S(2)}, u32[]{:S(2)}) collective-permute-start(bf16[15,224,15]{1,2,0:T(8,128)(2,1)S(1)} %copy.21), channel_id=1, source_target_pairs={{1,0},{2,1},{3,2},{4,3},{5,4},{6,5},{7,6},{9,8},{10,9},{11,10},{12... | collective-permute-start | bytes 302408 | tf_op jit(solution)/shard_map/ppermute | solution.py:177
  75.2 4.5 %collective-permute-start.8 = (f32[225,112]{1,0:T(8,128)S(1)}, f32[225,112]{1,0:T(8,128)S(1)}, u32[]{:S(2)}, u32[]{:S(2)}) collective-permute-start(f32[225,112]{1,0:T(8,128)S(1)} %pad_maximum_fusion), channel_id=1, source_target_pairs={{0,1},{1,0},{2,3},{3,2},{4,5},{5,4},{6,7},{7,6},{8,9},{9,8},{10,11... | collective-permute-start | bytes 302408 | tf_op jit(solution)/shard_map/ppermute | solution.py:283
  79.7 6.3 %collective-permute-start.11 = (f32[225,112]{1,0:T(8,128)S(1)}, f32[225,112]{1,0:T(8,128)S(1)}, u32[]{:S(2)}, u32[]{:S(2)}) collective-permute-start(f32[225,112]{1,0:T(8,128)S(1)} %fusion.44), channel_id=1, source_target_pairs={{0,6},{1,7},{2,0},{3,1},{4,2},{5,3},{6,4},{7,5},{8,14},{9,15},{10,... | collective-permute-start | bytes 302408 | tf_op jit(solution)/shard_map/ppermute | solution.py:54
  79.8 9.9 %collective-permute-start.10 = (f32[225,112]{1,0:T(8,128)S(1)}, f32[225,112]{1,0:T(8,128)S(1)}, u32[]{:S(2)}, u32[]{:S(2)}) collective-permute-start(f32[225,112]{1,0:T(8,128)S(1)} %fusion.44), channel_id=1, source_target_pairs={{0,4},{1,5},{2,6},{3,7},{4,0},{5,1},{6,2},{7,3},{8,12},{9,13},{10,... | collective-permute-start | bytes 302408 | tf_op jit(solution)/shard_map/ppermute | solution.py:54
  83.6 6.0 %collective-permute-start.9 = (f32[225,112]{1,0:T(8,128)S(1)}, f32[225,112]{1,0:T(8,128)S(1)}, u32[]{:S(2)}, u32[]{:S(2)}) collective-permute-start(f32[225,112]{1,0:T(8,128)S(1)} %fusion.44), channel_id=1, source_target_pairs={{0,2},{1,3},{2,4},{3,5},{4,6},{5,7},{6,0},{7,1},{8,10},{9,11},{10,... | collective-permute-start | bytes 302408 | tf_op jit(solution)/shard_map/ppermute | solution.py:54
  89.7 7.4 %collective-permute-start.14 = (f32[225,112]{1,0:T(8,128)S(1)}, f32[225,112]{1,0:T(8,128)S(1)}, u32[]{:S(2)}, u32[]{:S(2)}) collective-permute-start(f32[225,112]{1,0:T(8,128)S(1)} %add_add_fusion.3), channel_id=1, source_target_pairs={{0,24},{8,0},{16,8},{24,16},{1,25},{9,1},{17,9},{25,17},{2,26},{10... | collective-permute-start | bytes 302408 | tf_op jit(solution)/shard_map/ppermute | solution.py:54
  93.3 9.9 %collective-permute-start.13 = (f32[225,112]{1,0:T(8,128)S(1)}, f32[225,112]{1,0:T(8,128)S(1)}, u32[]{:S(2)}, u32[]{:S(2)}) collective-permute-start(f32[225,112]{1,0:T(8,128)S(1)} %add_add_fusion.3), channel_id=1, source_target_pairs={{0,16},{8,24},{16,0},{24,8},{1,17},{9,25},{17,1},{25,9},{2,18},{10... | collective-permute-start | bytes 302408 | tf_op jit(solution)/shard_map/ppermute | solution.py:54
  93.3 9.9 %collective-permute-start.12 = (f32[225,112]{1,0:T(8,128)S(1)}, f32[225,112]{1,0:T(8,128)S(1)}, u32[]{:S(2)}, u32[]{:S(2)}) collective-permute-start(f32[225,112]{1,0:T(8,128)S(1)} %add_add_fusion.3), channel_id=1, source_target_pairs={{0,8},{8,16},{16,24},{24,0},{1,9},{9,17},{17,25},{25,1},{2,10},{10... | collective-permute-start | bytes 302408 | tf_op jit(solution)/shard_map/ppermute | solution.py:54

commit v16 on v15

--- a/solution.py
+++ b/solution.py
@@ -281,7 +281,7 @@
     )
     packed = pack_symmetric(partial_cov)
     packed = packed + lax.ppermute(packed, "cross", [(i, i ^ 1) for i in range(n_cross)])
-    packed = ring_sum(ring_sum(packed, "cross", 2), "track", 1)
+    packed = butterfly_sum(ring_sum(packed, "cross", 2), "track")
     covariance = unpack_symmetric(packed) / (total_lines * total_pix)
     inverse = spd_inverse(covariance, LOAD)
     solved = jnp.einsum(

time: 144 us -> 143 us (level)
    ppermute x6 -> x3, waiting for transfers between devices: 14.9 us -> 6 us  [ring_sum(): total = total + lax.ppermute(x, axis, pairs)]
    ppermute x0 -> x2, waiting for transfers between devices: none -> 7.68 us  [butterfly_sum(): x = x + lax.ppermute(x, axis, pairs)]
    ppermute x6 -> x3, starting transfers between devices: 8.58 us -> 3.91 us  [ring_sum(): total = total + lax.ppermute(x, axis, pairs)]
    ppermute x0 -> x2, starting transfers between devices: none -> 4.29 us  [butterfly_sum(): x = x + lax.ppermute(x, axis, pairs)]
  transfers between devices with their start and end apart: 15 -> 14, of which waited for: 6 -> 6; matrix products, arithmetic and copies ran while one was open for 19% -> 19% of each run, Pallas kernels for 0% -> 0%
where the time goes in v16:
time: 143 us; the launch traced here: 142 us
  Pallas kernels  38.8 us (27%)
  matrix products  35.2 us (25%)
  starting transfers between devices  33.1 us (23%)
  waiting for transfers between devices  20.4 us (14%)
  local copies, waits for them, and re-layouts  12 us (8%)
  other arithmetic  2.41 us (2%)
    pallas_call x1, Pallas kernels, spd_inverse(): pl.pallas_call(functools.partial(sweep_kernel, n, load), out_shape=jax.Sh...  28.6 us
    dot_general x9, matrix products, sum_lines(): jnp.einsum('qbk,kl->qbl', values, w, preferred_element_type=jnp.float32)  20.7 us
    ppermute x6, starting transfers between devices, fetch(): return lax.ppermute(piece, 'cross', pairs)  15.1 us
    pallas_call x1, Pallas kernels, residuals(): pl.pallas_call(residual_kernel, grid=(bands // block,), in_specs=[spec(le...  10.3 us
    dot_general x1, matrix products, shards(): jnp.einsum('pbl,bj->pjl', residual, inverse, precision=highest, preferred...  10.2 us
    ppermute x2, waiting for transfers between devices, butterfly_sum(): x = x + lax.ppermute(x, axis, pairs)  7.68 us
    ppermute x2, starting transfers between devices, fetch(): return lax.ppermute(piece, 'track', pairs)  6.29 us
    ppermute x3, waiting for transfers between devices, ring_sum(): total = total + lax.ppermute(x, axis, pairs)  6 us
  transfers between devices with their start and end apart: 14, of which 6 were waited for; matrix products, arithmetic and copies ran while one was open for 19% of the time, Pallas kernels for 0%

profile of v16, /device:TPU:0, one launch (start us, length us, event | category | flops | bytes accessed | tf_op | source)
XLA Modules:
  0.0 142.2 jit_solution(8597034579936304395)
XLA Ops:
  0.0 0.0 copy-start
  0.0 4.2 %fusion.46 = (bf16[15,224,256]{2,1,0:T(8,128)(2,1)}, bf16[15,224,256]{2,1,0:T(8,128)(2,1)}) fusion(bf16[32,224,256]{2,1,0:T(8,128)(2,1)} %bitcast.59), kind=kLoop, calls=%fused_computation.56 | loop fusion | bytes 6881280 | tf_op jit(solution)/shard_map/slice | solution.py:184
  4.2 2.5 %collective-permute-start.2 = (bf16[15,224,256]{2,1,0:T(8,128)(2,1)}, bf16[15,224,256]{2,1,0:T(8,128)(2,1)S(1)}, u32[]{:S(2)}, u32[]{:S(2)}) collective-permute-start(bf16[15,224,256]{2,1,0:T(8,128)(2,1)} %get-tuple-element.11), channel_id=1, source_target_pairs={{0,1},{1,2},{2,3},{3,4},{4,5},{5,6},{6,7},{8,9},{9,10},{10,11},{11... | collective-permute-start | bytes 5160968 | tf_op jit(solution)/shard_map/ppermute | solution.py:177
  6.6 1.3 collective-permute-start.6
  7.9 0.0 copy-done
  7.9 2.1 %fusion.45 = (bf16[32,224,15]{2,1,0:T(8,128)(2,1)S(1)}, bf16[32,224,15]{2,1,0:T(8,128)(2,1)}) fusion(bf16[32,224,256]{2,1,0:T(8,128)(2,1)S(1)} %bitcast.61), kind=kLoop, calls=%fused_computation.55 | loop fusion | bytes 860160 | tf_op jit(solution)/shard_map/slice | solution.py:190
  10.0 2.7 %copy.14 = bf16[32,224,15]{1,0,2:T(8,128)(2,1)} copy(bf16[32,224,15]{2,1,0:T(8,128)(2,1)} %get-tuple-element.16) | data formatting | bytes 430080 | tf_op jit(solution)/shard_map/slice | solution.py:189
  12.7 5.0 %collective-permute-start = (bf16[32,224,15]{1,0,2:T(8,128)(2,1)}, bf16[32,224,15]{1,0,2:T(8,128)(2,1)}, u32[]{:S(2)}, u32[]{:S(2)}) collective-permute-start(bf16[32,224,15]{1,0,2:T(8,128)(2,1)} %copy.14), channel_id=1, source_target_pairs={{0,8},{8,16},{16,24},{1,9},{9,17},{17,25},{2,10},{10,18},{18,26},{... | collective-permute-start | bytes 645128 | tf_op jit(solution)/shard_map/ppermute | solution.py:180
  17.8 1.7 %copy.16 = bf16[32,224,15]{1,0,2:T(8,128)(2,1)} copy(bf16[32,224,15]{2,1,0:T(8,128)(2,1)S(1)} %get-tuple-element.15) | data formatting | bytes 430080 | tf_op jit(solution)/shard_map/slice | solution.py:190
  19.4 1.3 collective-permute-start.3
  20.7 6.1 %fusion.11 = f32[256,32,224]{0,2,1:T(8,128)} fusion(bf16[256,32,224]{0,2,1:T(8,128)(2,1)} %param.1), kind=kOutput, calls=%fused_computation.14 | convolution fusion | flops 939720704 | bytes 11010048 | tf_op jit(solution)/shard_map/qbk,kl->qbl/dot_general | solution.py:216
  26.9 0.7 broadcast_multiply_fusion.count_ref
  27.6 0.0 collective-permute-done
  27.6 1.0 fusion.48
  28.7 3.9 %collective-permute-start.1 = (bf16[15,224,15]{1,2,0:T(8,128)(2,1)S(1)}, bf16[15,224,15]{1,2,0:T(8,128)(2,1)S(1)}, u32[]{:S(2)}, u32[]{:S(2)}) collective-permute-start(bf16[15,224,15]{1,2,0:T(8,128)(2,1)S(1)} %copy.15), channel_id=1, source_target_pairs={{0,1},{1,2},{2,3},{3,4},{4,5},{5,6},{6,7},{8,9},{9,10},{10,11},{11... | collective-permute-start | bytes 302408 | tf_op jit(solution)/shard_map/ppermute | solution.py:177
  32.6 1.3 collective-permute-start.5
  33.9 0.0 collective-permute-done.3
  34.0 0.0 copy-start.1
  34.0 4.8 %collective-permute-start.4 = (bf16[15,224,15]{1,2,0:T(8,128)(2,1)S(1)}, bf16[15,224,15]{1,2,0:T(8,128)(2,1)S(1)}, u32[]{:S(2)}, u32[]{:S(2)}) collective-permute-start(bf16[15,224,15]{1,2,0:T(8,128)(2,1)S(1)} %copy.17), channel_id=1, source_target_pairs={{0,1},{1,2},{2,3},{3,4},{4,5},{5,6},{6,7},{8,9},{9,10},{10,11},{11... | collective-permute-start | bytes 302408 | tf_op jit(solution)/shard_map/ppermute | solution.py:177
  38.8 1.9 %fusion.6 = f32[32,224,256]{2,1,0:T(8,128)S(1)} fusion(bf16[32,224,15]{1,0,2:T(8,128)(2,1)} %collective-permute-done), kind=kOutput, calls=%fused_computation.9 | convolution fusion | flops 55054080 | bytes 7555072 | tf_op jit(solution)/shard_map/qbk,kl->qbl/dot_general | solution.py:216
  40.7 0.0 copy-done.1
  40.7 4.1 %fusion.1.middle_ref = f32[32,224,256]{2,1,0:T(8,128)} fusion(f32[32,224,256]{2,1,0:T(8,128)S(1)} %fusion.6, f32[256,32,224]{0,2,1:T(8,128)S(1)} %copy-done.1, bf16[32,224,15]{1,0,2:T(8,128)(2,1)S(1)} %collective-permute-done.3, s32[15]{0:T(128)S(1)} %iota_add_fusion), kind=kOutput, calls=%fused_computation.3 | convolution fusion | flops 58724096 | bytes 22235196 | tf_op jit(solution)/shard_map/qbk,kl->qbl/dot_general | solution.py:216
  44.9 0.0 collective-permute-done.5
  44.9 1.3 collective-permute-start.7
  46.2 0.5 fusion.22
  46.7 0.0 collective-permute-done.1
  46.7 0.5 fusion.25
  47.2 0.0 collective-permute-done.6
  47.2 2.1 %fusion.9 = f32[15,224,256]{2,1,0:T(8,128)S(1)} fusion(bf16[15,224,256]{2,1,0:T(8,128)(2,1)} %collective-permute-done.6), kind=kOutput, calls=%fused_computation.13 | convolution fusion | flops 440598528 | bytes 5160960 | tf_op jit(solution)/shard_map/qbk,kl->qbl/dot_general | solution.py:216
  49.3 5.7 %collective-permute-done.7 = bf16[15,224,15]{1,2,0:T(8,128)(2,1)S(1)} collective-permute-done((bf16[15,224,15]{1,2,0:T(8,128)(2,1)S(1)}, bf16[15,224,15]{1,2,0:T(8,128)(2,1)S(1)}, u32[]{:S(2)}, u32[]{:S(2)}) %collective-permute-start.7) | collective-permute-done | bytes 100832 | tf_op jit(solution)/shard_map/ppermute | solution.py:177
  55.0 2.4 %add_add_fusion.right_ref = f32[15,224,256]{2,1,0:T(8,128)} fusion(f32[15,224,256]{2,1,0:T(8,128)S(1)} %fusion.22, f32[15,224,256]{2,1,0:T(8,128)S(1)} %fusion.9, bf16[15,224,15]{1,2,0:T(8,128)(2,1)S(1)} %collective-permute-done.7, s32[15]{0:T(128)S(1)} %iota_add_fusion), kind=kOutput, calls=%fused_computation.4 | convolution fusion | flops 27528960 | bytes 10422780 | tf_op jit(solution)/shard_map/qbk,kl->qbl/dot_general | solution.py:216
  57.4 0.0 collective-permute-done.2
  57.4 0.6 fusion.13
  58.1 0.0 collective-permute-done.4
  58.1 2.4 %add_add_fusion.1.left_ref = f32[15,224,256]{2,1,0:T(8,128)} fusion(f32[15,224,256]{2,1,0:T(8,128)S(1)} %fusion.25, f32[15,224,256]{2,1,0:T(8,128)S(1)} %fusion.13, bf16[15,224,15]{1,2,0:T(8,128)(2,1)S(1)} %collective-permute-done.4, s32[15]{0:T(128)S(1)} %iota_add_fusion), kind=kOutput, calls=%fused_computation.5 | convolution fusion | flops 27528960 | bytes 10422780 | tf_op jit(solution)/shard_map/qbk,kl->qbl/dot_general | solution.py:216
  60.5 10.3 %shard_map.17 = (f32[32,224,256]{2,1,0:T(8,128)}, bf16[32,224,256]{2,1,0:T(8,128)(2,1)}) custom-call(f32[15,224,256]{2,1,0:T(8,128)} %add_add_fusion.1.left_ref, f32[32,224,256]{2,1,0:T(8,128)} %fusion.1.middle_ref, f32[15,224,256]{2,1,0:T(8,128)} %add_add_fusion.right_ref, bf16[32,224,256]{2,1,0:T(8,128)(2,1)} %bitcast.60, ...), custom_call_target="tpu_custom_call" | custom-call | tf_op jit(solution)/shard_map/pallas_call | solution.py:250
  70.8 4.3 %convolution_bitcast_fusion = f32[224,224]{1,0:T(8,128)S(1)} fusion(bf16[32,224,256]{2,1,0:T(8,128)(2,1)} %get-tuple-element.14), kind=kOutput, calls=%fused_computation.6 | convolution fusion | flops 822083584 | bytes 3870720 | tf_op jit(solution)/shard_map/pjl,pkl->jk/dot_general | solution.py:279
  75.1 0.1 fusion.49
  75.2 3.5 %collective-permute-start.8 = (f32[225,112]{1,0:T(8,128)S(1)}, f32[225,112]{1,0:T(8,128)S(1)}, u32[]{:S(2)}, u32[]{:S(2)}) collective-permute-start(f32[225,112]{1,0:T(8,128)S(1)} %pad_maximum_fusion), channel_id=1, source_target_pairs={{0,1},{1,0},{2,3},{3,2},{4,5},{5,4},{6,7},{7,6},{8,9},{9,8},{10,11... | collective-permute-start | bytes 302408 | tf_op jit(solution)/shard_map/ppermute | solution.py:283
  78.7 1.0 collective-permute-done.8
  79.7 0.1 collective-permute-start.11
  79.8 3.9 %collective-permute-start.10 = (f32[225,112]{1,0:T(8,128)S(1)}, f32[225,112]{1,0:T(8,128)S(1)}, u32[]{:S(2)}, u32[]{:S(2)}) collective-permute-start(f32[225,112]{1,0:T(8,128)S(1)} %fusion.44), channel_id=1, source_target_pairs={{0,4},{1,5},{2,6},{3,7},{4,0},{5,1},{6,2},{7,3},{8,12},{9,13},{10,... | collective-permute-start | bytes 302408 | tf_op jit(solution)/shard_map/ppermute | solution.py:54
  83.6 0.0 collective-permute-start.9
  83.6 2.4 %collective-permute-done.11 = f32[225,112]{1,0:T(8,128)S(1)} collective-permute-done((f32[225,112]{1,0:T(8,128)S(1)}, f32[225,112]{1,0:T(8,128)S(1)}, u32[]{:S(2)}, u32[]{:S(2)}) %collective-permute-start.11) | collective-permute-done | bytes 100832 | tf_op jit(solution)/shard_map/ppermute | solution.py:54
  86.0 3.6 %collective-permute-done.10 = f32[225,112]{1,0:T(8,128)S(1)} collective-permute-done((f32[225,112]{1,0:T(8,128)S(1)}, f32[225,112]{1,0:T(8,128)S(1)}, u32[]{:S(2)}, u32[]{:S(2)}) %collective-permute-start.10) | collective-permute-done | bytes 100832 | tf_op jit(solution)/shard_map/ppermute | solution.py:54
  89.6 0.0 collective-permute-done.9
  89.7 1.6 %collective-permute-start.12 = (f32[225,112]{1,0:T(8,128)S(1)}, f32[225,112]{1,0:T(8,128)S(1)}, u32[]{:S(2)}, u32[]{:S(2)}) collective-permute-start(f32[225,112]{1,0:T(8,128)S(1)} %add_add_fusion.2), channel_id=1, source_target_pairs={{0,8},{8,0},{16,24},{24,16},{1,9},{9,1},{17,25},{25,17},{2,10},{10... | collective-permute-start | bytes 302408 | tf_op jit(solution)/shard_map/ppermute | solution.py:41
  91.3 3.3 %collective-permute-done.12 = f32[225,112]{1,0:T(8,128)S(1)} collective-permute-done((f32[225,112]{1,0:T(8,128)S(1)}, f32[225,112]{1,0:T(8,128)S(1)}, u32[]{:S(2)}, u32[]{:S(2)}) %collective-permute-start.12) | collective-permute-done | bytes 100832 | tf_op jit(solution)/shard_map/ppermute | solution.py:41
  94.6 2.6 %collective-permute-start.13 = (f32[225,112]{1,0:T(8,128)S(1)}, f32[225,112]{1,0:T(8,128)S(1)}, u32[]{:S(2)}, u32[]{:S(2)}) collective-permute-start(f32[225,112]{1,0:T(8,128)S(1)} %add.133), channel_id=1, source_target_pairs={{0,16},{8,24},{16,0},{24,8},{1,17},{9,25},{17,1},{25,9},{2,18},{10... | collective-permute-start | bytes 302408 | tf_op jit(solution)/shard_map/ppermute | solution.py:41
  97.2 4.4 %collective-permute-done.13 = f32[225,112]{1,0:T(8,128)S(1)} collective-permute-done((f32[225,112]{1,0:T(8,128)S(1)}, f32[225,112]{1,0:T(8,128)S(1)}, u32[]{:S(2)}, u32[]{:S(2)}) %collective-permute-start.13) | collective-permute-done | bytes 100832 | tf_op jit(solution)/shard_map/ppermute | solution.py:41
  101.7 0.1 copy.25
  101.8 0.1 copy.26
  101.9 0.8 maximum_multiply_fusion.a_ref
  102.7 28.6 %shard_map.18 = f32[256,256]{1,0:T(8,128)} custom-call(f32[224,224]{1,0:T(8,128)} %maximum_multiply_fusion.a_ref), custom_call_target="tpu_custom_call" | custom-call | tf_op jit(solution)/shard_map/pallas_call | solution.py:132
  131.3 10.2 %fusion = f32[32,256]{1,0:T(8,128)S(1)} fusion(f32[32,224,256]{2,1,0:T(8,128)} %get-tuple-element.13, f32[256,256]{1,0:T(8,128)} %shard_map.18), kind=kOutput, calls=%fused_computation.1 | convolution fusion | flops 4936213504 | bytes 14942208 | tf_op jit(solution)/shard_map/pbl,bj->pjl/dot_general | solution.py:287
  141.6 0.6 multiply_bitcast_fusion
  (16 shorter events, 0.4 us)
Async XLA Ops:
  0.0 7.9 %copy-start = (bf16[256,32,224]{0,2,1:T(8,128)(2,1)S(1)}, bf16[256,32,224]{0,2,1:T(8,128)(2,1)}, u32[]{:S(2)}) copy-start(bf16[256,32,224]{0,2,1:T(8,128)(2,1)} %param.1) | copy-start | bytes 11010052
  4.2 53.3 %collective-permute-start.2 = (bf16[15,224,256]{2,1,0:T(8,128)(2,1)}, bf16[15,224,256]{2,1,0:T(8,128)(2,1)S(1)}, u32[]{:S(2)}, u32[]{:S(2)}) collective-permute-start(bf16[15,224,256]{2,1,0:T(8,128)(2,1)} %get-tuple-element.11), channel_id=1, source_target_pairs={{0,1},{1,2},{2,3},{3,4},{4,5},{5,6},{6,7},{8,9},{9,10},{10,11},{11... | collective-permute-start | bytes 5160968 | tf_op jit(solution)/shard_map/ppermute | solution.py:177
  6.6 40.6 %collective-permute-start.6 = (bf16[15,224,256]{2,1,0:T(8,128)(2,1)}, bf16[15,224,256]{2,1,0:T(8,128)(2,1)}, u32[]{:S(2)}, u32[]{:S(2)}) collective-permute-start(bf16[15,224,256]{2,1,0:T(8,128)(2,1)} %get-tuple-element.12), channel_id=1, source_target_pairs={{1,0},{2,1},{3,2},{4,3},{5,4},{6,5},{7,6},{9,8},{10,9},{11,10},{12... | collective-permute-start | bytes 5160968 | tf_op jit(solution)/shard_map/ppermute | solution.py:177
  12.7 14.8 %collective-permute-start = (bf16[32,224,15]{1,0,2:T(8,128)(2,1)}, bf16[32,224,15]{1,0,2:T(8,128)(2,1)}, u32[]{:S(2)}, u32[]{:S(2)}) collective-permute-start(bf16[32,224,15]{1,0,2:T(8,128)(2,1)} %copy.14), channel_id=1, source_target_pairs={{0,8},{8,16},{16,24},{1,9},{9,17},{17,25},{2,10},{10,18},{18,26},{... | collective-permute-start | bytes 645128 | tf_op jit(solution)/shard_map/ppermute | solution.py:180
  19.4 14.5 %collective-permute-start.3 = (bf16[32,224,15]{1,0,2:T(8,128)(2,1)}, bf16[32,224,15]{1,0,2:T(8,128)(2,1)S(1)}, u32[]{:S(2)}, u32[]{:S(2)}) collective-permute-start(bf16[32,224,15]{1,0,2:T(8,128)(2,1)} %copy.16), channel_id=1, source_target_pairs={{8,0},{16,8},{24,16},{9,1},{17,9},{25,17},{10,2},{18,10},{26,18},{... | collective-permute-start | bytes 645128 | tf_op jit(solution)/shard_map/ppermute | solution.py:180
  28.7 18.0 %collective-permute-start.1 = (bf16[15,224,15]{1,2,0:T(8,128)(2,1)S(1)}, bf16[15,224,15]{1,2,0:T(8,128)(2,1)S(1)}, u32[]{:S(2)}, u32[]{:S(2)}) collective-permute-start(bf16[15,224,15]{1,2,0:T(8,128)(2,1)S(1)} %copy.15), channel_id=1, source_target_pairs={{0,1},{1,2},{2,3},{3,4},{4,5},{5,6},{6,7},{8,9},{9,10},{10,11},{11... | collective-permute-start | bytes 302408 | tf_op jit(solution)/shard_map/ppermute | solution.py:177
  32.6 12.3 %collective-permute-start.5 = (bf16[15,224,15]{1,2,0:T(8,128)(2,1)S(1)}, bf16[15,224,15]{1,2,0:T(8,128)(2,1)S(1)}, u32[]{:S(2)}, u32[]{:S(2)}) collective-permute-start(bf16[15,224,15]{1,2,0:T(8,128)(2,1)S(1)} %copy.20), channel_id=1, source_target_pairs={{1,0},{2,1},{3,2},{4,3},{5,4},{6,5},{7,6},{9,8},{10,9},{11,10},{12... | collective-permute-start | bytes 302408 | tf_op jit(solution)/shard_map/ppermute | solution.py:177
  34.0 6.7 %copy-start.1 = (f32[256,32,224]{0,2,1:T(8,128)S(1)}, f32[256,32,224]{0,2,1:T(8,128)}, u32[]{:S(2)}) copy-start(f32[256,32,224]{0,2,1:T(8,128)} %fusion.11) | copy-start | bytes 22020100
  34.0 24.0 %collective-permute-start.4 = (bf16[15,224,15]{1,2,0:T(8,128)(2,1)S(1)}, bf16[15,224,15]{1,2,0:T(8,128)(2,1)S(1)}, u32[]{:S(2)}, u32[]{:S(2)}) collective-permute-start(bf16[15,224,15]{1,2,0:T(8,128)(2,1)S(1)} %copy.17), channel_id=1, source_target_pairs={{0,1},{1,2},{2,3},{3,4},{4,5},{5,6},{6,7},{8,9},{9,10},{10,11},{11... | collective-permute-start | bytes 302408 | tf_op jit(solution)/shard_map/ppermute | solution.py:177
  44.9 10.1 %collective-permute-start.7 = (bf16[15,224,15]{1,2,0:T(8,128)(2,1)S(1)}, bf16[15,224,15]{1,2,0:T(8,128)(2,1)S(1)}, u32[]{:S(2)}, u32[]{:S(2)}) collective-permute-start(bf16[15,224,15]{1,2,0:T(8,128)(2,1)S(1)} %copy.21), channel_id=1, source_target_pairs={{1,0},{2,1},{3,2},{4,3},{5,4},{6,5},{7,6},{9,8},{10,9},{11,10},{12... | collective-permute-start | bytes 302408 | tf_op jit(solution)/shard_map/ppermute | solution.py:177
  75.2 4.5 %collective-permute-start.8 = (f32[225,112]{1,0:T(8,128)S(1)}, f32[225,112]{1,0:T(8,128)S(1)}, u32[]{:S(2)}, u32[]{:S(2)}) collective-permute-start(f32[225,112]{1,0:T(8,128)S(1)} %pad_maximum_fusion), channel_id=1, source_target_pairs={{0,1},{1,0},{2,3},{3,2},{4,5},{5,4},{6,7},{7,6},{8,9},{9,8},{10,11... | collective-permute-start | bytes 302408 | tf_op jit(solution)/shard_map/ppermute | solution.py:283
  79.7 6.3 %collective-permute-start.11 = (f32[225,112]{1,0:T(8,128)S(1)}, f32[225,112]{1,0:T(8,128)S(1)}, u32[]{:S(2)}, u32[]{:S(2)}) collective-permute-start(f32[225,112]{1,0:T(8,128)S(1)} %fusion.44), channel_id=1, source_target_pairs={{0,6},{1,7},{2,0},{3,1},{4,2},{5,3},{6,4},{7,5},{8,14},{9,15},{10,... | collective-permute-start | bytes 302408 | tf_op jit(solution)/shard_map/ppermute | solution.py:54
  79.8 9.9 %collective-permute-start.10 = (f32[225,112]{1,0:T(8,128)S(1)}, f32[225,112]{1,0:T(8,128)S(1)}, u32[]{:S(2)}, u32[]{:S(2)}) collective-permute-start(f32[225,112]{1,0:T(8,128)S(1)} %fusion.44), channel_id=1, source_target_pairs={{0,4},{1,5},{2,6},{3,7},{4,0},{5,1},{6,2},{7,3},{8,12},{9,13},{10,... | collective-permute-start | bytes 302408 | tf_op jit(solution)/shard_map/ppermute | solution.py:54
  83.6 6.0 %collective-permute-start.9 = (f32[225,112]{1,0:T(8,128)S(1)}, f32[225,112]{1,0:T(8,128)S(1)}, u32[]{:S(2)}, u32[]{:S(2)}) collective-permute-start(f32[225,112]{1,0:T(8,128)S(1)} %fusion.44), channel_id=1, source_target_pairs={{0,2},{1,3},{2,4},{3,5},{4,6},{5,7},{6,0},{7,1},{8,10},{9,11},{10,... | collective-permute-start | bytes 302408 | tf_op jit(solution)/shard_map/ppermute | solution.py:54
  89.7 4.9 %collective-permute-start.12 = (f32[225,112]{1,0:T(8,128)S(1)}, f32[225,112]{1,0:T(8,128)S(1)}, u32[]{:S(2)}, u32[]{:S(2)}) collective-permute-start(f32[225,112]{1,0:T(8,128)S(1)} %add_add_fusion.2), channel_id=1, source_target_pairs={{0,8},{8,0},{16,24},{24,16},{1,9},{9,1},{17,25},{25,17},{2,10},{10... | collective-permute-start | bytes 302408 | tf_op jit(solution)/shard_map/ppermute | solution.py:41
  94.6 7.1 %collective-permute-start.13 = (f32[225,112]{1,0:T(8,128)S(1)}, f32[225,112]{1,0:T(8,128)S(1)}, u32[]{:S(2)}, u32[]{:S(2)}) collective-permute-start(f32[225,112]{1,0:T(8,128)S(1)} %add.133), channel_id=1, source_target_pairs={{0,16},{8,24},{16,0},{24,8},{1,17},{9,25},{17,1},{25,9},{2,18},{10... | collective-permute-start | bytes 302408 | tf_op jit(solution)/shard_map/ppermute | solution.py:41

commit v17 on v16

--- a/solution.py
+++ b/solution.py
@@ -279,9 +279,7 @@
     partial_cov = jnp.einsum(
         "pjl,pkl->jk", residual_bf, residual_bf, preferred_element_type=jnp.float32
     )
-    packed = pack_symmetric(partial_cov)
-    packed = packed + lax.ppermute(packed, "cross", [(i, i ^ 1) for i in range(n_cross)])
-    packed = butterfly_sum(ring_sum(packed, "cross", 2), "track")
+    packed = butterfly_sum(butterfly_sum(pack_symmetric(partial_cov), "cross"), "track")
     covariance = unpack_symmetric(packed) / (total_lines * total_pix)
     inverse = spd_inverse(covariance, LOAD)
     solved = jnp.einsum(

time: 143 us -> 144 us (level)
    ppermute x2 -> x5, waiting for transfers between devices: 7.68 us -> 16.3 us  [butterfly_sum(): x = x + lax.ppermute(x, axis, pairs)]
    ppermute x4 -> x0, starting transfers between devices: 7.44 us -> none  [the longest x3 3.91 us: ring_sum(): total = total + lax.ppermute(x, axis, pairs)]
    ppermute x2 -> x5, starting transfers between devices: 4.29 us -> 11.4 us  [butterfly_sum(): x = x + lax.ppermute(x, axis, pairs)]
    ppermute x4 -> x0, waiting for transfers between devices: 6.98 us -> none  [the longest x3 6 us: ring_sum(): total = total + lax.ppermute(x, axis, pairs)]
  transfers between devices with their start and end apart: 14 -> 13, of which waited for: 6 -> 6; matrix products, arithmetic and copies ran while one was open for 19% -> 19% of each run, Pallas kernels for 0% -> 0%
where the time goes in v17:
time: 144 us; the launch traced here: 143 us
  Pallas kernels  38.8 us (27%)
  matrix products  35.1 us (24%)
  starting transfers between devices  33 us (23%)
  waiting for transfers between devices  21.8 us (15%)
  local copies, waits for them, and re-layouts  12 us (8%)
  other arithmetic  2.41 us (2%)
    pallas_call x1, Pallas kernels, spd_inverse(): pl.pallas_call(functools.partial(sweep_kernel, n, load), out_shape=jax.Sh...  28.6 us
    dot_general x9, matrix products, sum_lines(): jnp.einsum('qbk,kl->qbl', values, w, preferred_element_type=jnp.float32)  20.6 us
    ppermute x5, waiting for transfers between devices, butterfly_sum(): x = x + lax.ppermute(x, axis, pairs)  16.3 us
    ppermute x6, starting transfers between devices, fetch(): return lax.ppermute(piece, 'cross', pairs)  15.3 us
    ppermute x5, starting transfers between devices, butterfly_sum(): x = x + lax.ppermute(x, axis, pairs)  11.4 us
    pallas_call x1, Pallas kernels, residuals(): pl.pallas_call(residual_kernel, grid=(bands // block,), in_specs=[spec(le...  10.2 us
    dot_general x1, matrix products, shards(): jnp.einsum('pbl,bj->pjl', residual, inverse, precision=highest, preferred...  10.2 us
    ppermute x2, starting transfers between devices, fetch(): return lax.ppermute(piece, 'track', pairs)  6.3 us
  transfers between devices with their start and end apart: 13, of which 6 were waited for; matrix products, arithmetic and copies ran while one was open for 19% of the time, Pallas kernels for 0%

profile of v17, /device:TPU:0, one launch (start us, length us, event | category | flops | bytes accessed | tf_op | source)
XLA Modules:
  0.0 143.4 jit_solution(17215738440267682344)
XLA Ops:
  0.0 0.0 copy-start
  0.0 4.2 %fusion.46 = (bf16[15,224,256]{2,1,0:T(8,128)(2,1)}, bf16[15,224,256]{2,1,0:T(8,128)(2,1)}) fusion(bf16[32,224,256]{2,1,0:T(8,128)(2,1)} %bitcast.59), kind=kLoop, calls=%fused_computation.55 | loop fusion | bytes 6881280 | tf_op jit(solution)/shard_map/slice | solution.py:184
  4.2 2.5 %collective-permute-start.2 = (bf16[15,224,256]{2,1,0:T(8,128)(2,1)}, bf16[15,224,256]{2,1,0:T(8,128)(2,1)S(1)}, u32[]{:S(2)}, u32[]{:S(2)}) collective-permute-start(bf16[15,224,256]{2,1,0:T(8,128)(2,1)} %get-tuple-element.11), channel_id=1, source_target_pairs={{0,1},{1,2},{2,3},{3,4},{4,5},{5,6},{6,7},{8,9},{9,10},{10,11},{11... | collective-permute-start | bytes 5160968 | tf_op jit(solution)/shard_map/ppermute | solution.py:177
  6.6 1.3 collective-permute-start.6
  7.9 0.0 copy-done
  7.9 2.1 %fusion.45 = (bf16[32,224,15]{2,1,0:T(8,128)(2,1)S(1)}, bf16[32,224,15]{2,1,0:T(8,128)(2,1)}) fusion(bf16[32,224,256]{2,1,0:T(8,128)(2,1)S(1)} %bitcast.61), kind=kLoop, calls=%fused_computation.54 | loop fusion | bytes 860160 | tf_op jit(solution)/shard_map/slice | solution.py:190
  10.0 2.7 %copy.14 = bf16[32,224,15]{1,0,2:T(8,128)(2,1)} copy(bf16[32,224,15]{2,1,0:T(8,128)(2,1)} %get-tuple-element.16) | data formatting | bytes 430080 | tf_op jit(solution)/shard_map/slice | solution.py:189
  12.8 5.0 %collective-permute-start = (bf16[32,224,15]{1,0,2:T(8,128)(2,1)}, bf16[32,224,15]{1,0,2:T(8,128)(2,1)}, u32[]{:S(2)}, u32[]{:S(2)}) collective-permute-start(bf16[32,224,15]{1,0,2:T(8,128)(2,1)} %copy.14), channel_id=1, source_target_pairs={{0,8},{8,16},{16,24},{1,9},{9,17},{17,25},{2,10},{10,18},{18,26},{... | collective-permute-start | bytes 645128 | tf_op jit(solution)/shard_map/ppermute | solution.py:180
  17.8 1.7 %copy.16 = bf16[32,224,15]{1,0,2:T(8,128)(2,1)} copy(bf16[32,224,15]{2,1,0:T(8,128)(2,1)S(1)} %get-tuple-element.15) | data formatting | bytes 430080 | tf_op jit(solution)/shard_map/slice | solution.py:190
  19.4 1.3 collective-permute-start.3
  20.7 6.1 %fusion.11 = f32[256,32,224]{0,2,1:T(8,128)} fusion(bf16[256,32,224]{0,2,1:T(8,128)(2,1)} %param.1), kind=kOutput, calls=%fused_computation.14 | convolution fusion | flops 939720704 | bytes 11010048 | tf_op jit(solution)/shard_map/qbk,kl->qbl/dot_general | solution.py:216
  26.9 0.7 broadcast_multiply_fusion.count_ref
  27.6 0.0 collective-permute-done
  27.6 1.0 fusion.48
  28.7 3.9 %collective-permute-start.1 = (bf16[15,224,15]{1,2,0:T(8,128)(2,1)S(1)}, bf16[15,224,15]{1,2,0:T(8,128)(2,1)S(1)}, u32[]{:S(2)}, u32[]{:S(2)}) collective-permute-start(bf16[15,224,15]{1,2,0:T(8,128)(2,1)S(1)} %copy.15), channel_id=1, source_target_pairs={{0,1},{1,2},{2,3},{3,4},{4,5},{5,6},{6,7},{8,9},{9,10},{10,11},{11... | collective-permute-start | bytes 302408 | tf_op jit(solution)/shard_map/ppermute | solution.py:177
  32.6 1.3 collective-permute-start.5
  33.9 0.0 collective-permute-done.3
  34.0 0.0 copy-start.1
  34.0 4.8 %collective-permute-start.4 = (bf16[15,224,15]{1,2,0:T(8,128)(2,1)S(1)}, bf16[15,224,15]{1,2,0:T(8,128)(2,1)S(1)}, u32[]{:S(2)}, u32[]{:S(2)}) collective-permute-start(bf16[15,224,15]{1,2,0:T(8,128)(2,1)S(1)} %copy.17), channel_id=1, source_target_pairs={{0,1},{1,2},{2,3},{3,4},{4,5},{5,6},{6,7},{8,9},{9,10},{10,11},{11... | collective-permute-start | bytes 302408 | tf_op jit(solution)/shard_map/ppermute | solution.py:177
  38.9 1.9 %fusion.6 = f32[32,224,256]{2,1,0:T(8,128)S(1)} fusion(bf16[32,224,15]{1,0,2:T(8,128)(2,1)} %collective-permute-done), kind=kOutput, calls=%fused_computation.9 | convolution fusion | flops 55054080 | bytes 7555072 | tf_op jit(solution)/shard_map/qbk,kl->qbl/dot_general | solution.py:216
  40.7 0.0 copy-done.1
  40.7 4.1 %fusion.1.middle_ref = f32[32,224,256]{2,1,0:T(8,128)} fusion(f32[32,224,256]{2,1,0:T(8,128)S(1)} %fusion.6, f32[256,32,224]{0,2,1:T(8,128)S(1)} %copy-done.1, bf16[32,224,15]{1,0,2:T(8,128)(2,1)S(1)} %collective-permute-done.3, s32[15]{0:T(128)S(1)} %iota_add_fusion), kind=kOutput, calls=%fused_computation.3 | convolution fusion | flops 58724096 | bytes 22235196 | tf_op jit(solution)/shard_map/qbk,kl->qbl/dot_general | solution.py:216
  44.9 0.0 collective-permute-done.5
  44.9 1.5 %collective-permute-start.7 = (bf16[15,224,15]{1,2,0:T(8,128)(2,1)S(1)}, bf16[15,224,15]{1,2,0:T(8,128)(2,1)S(1)}, u32[]{:S(2)}, u32[]{:S(2)}) collective-permute-start(bf16[15,224,15]{1,2,0:T(8,128)(2,1)S(1)} %copy.21), channel_id=1, source_target_pairs={{1,0},{2,1},{3,2},{4,3},{5,4},{6,5},{7,6},{9,8},{10,9},{11,10},{12... | collective-permute-start | bytes 302408 | tf_op jit(solution)/shard_map/ppermute | solution.py:177
  46.4 0.5 fusion.22
  46.9 0.0 collective-permute-done.1
  46.9 0.5 fusion.25
  47.4 0.0 collective-permute-done.6
  47.4 2.1 %fusion.9 = f32[15,224,256]{2,1,0:T(8,128)S(1)} fusion(bf16[15,224,256]{2,1,0:T(8,128)(2,1)} %collective-permute-done.6), kind=kOutput, calls=%fused_computation.13 | convolution fusion | flops 440598528 | bytes 5160960 | tf_op jit(solution)/shard_map/qbk,kl->qbl/dot_general | solution.py:216
  49.5 5.5 %collective-permute-done.7 = bf16[15,224,15]{1,2,0:T(8,128)(2,1)S(1)} collective-permute-done((bf16[15,224,15]{1,2,0:T(8,128)(2,1)S(1)}, bf16[15,224,15]{1,2,0:T(8,128)(2,1)S(1)}, u32[]{:S(2)}, u32[]{:S(2)}) %collective-permute-start.7) | collective-permute-done | bytes 100832 | tf_op jit(solution)/shard_map/ppermute | solution.py:177
  55.0 2.4 %add_add_fusion.right_ref = f32[15,224,256]{2,1,0:T(8,128)} fusion(f32[15,224,256]{2,1,0:T(8,128)S(1)} %fusion.22, f32[15,224,256]{2,1,0:T(8,128)S(1)} %fusion.9, bf16[15,224,15]{1,2,0:T(8,128)(2,1)S(1)} %collective-permute-done.7, s32[15]{0:T(128)S(1)} %iota_add_fusion), kind=kOutput, calls=%fused_computation.4 | convolution fusion | flops 27528960 | bytes 10422780 | tf_op jit(solution)/shard_map/qbk,kl->qbl/dot_general | solution.py:216
  57.4 0.0 collective-permute-done.2
  57.4 0.6 fusion.13
  58.1 0.0 collective-permute-done.4
  58.1 2.4 %add_add_fusion.1.left_ref = f32[15,224,256]{2,1,0:T(8,128)} fusion(f32[15,224,256]{2,1,0:T(8,128)S(1)} %fusion.25, f32[15,224,256]{2,1,0:T(8,128)S(1)} %fusion.13, bf16[15,224,15]{1,2,0:T(8,128)(2,1)S(1)} %collective-permute-done.4, s32[15]{0:T(128)S(1)} %iota_add_fusion), kind=kOutput, calls=%fused_computation.5 | convolution fusion | flops 27528960 | bytes 10422780 | tf_op jit(solution)/shard_map/qbk,kl->qbl/dot_general | solution.py:216
  60.5 10.2 %shard_map.17 = (f32[32,224,256]{2,1,0:T(8,128)}, bf16[32,224,256]{2,1,0:T(8,128)(2,1)}) custom-call(f32[15,224,256]{2,1,0:T(8,128)} %add_add_fusion.1.left_ref, f32[32,224,256]{2,1,0:T(8,128)} %fusion.1.middle_ref, f32[15,224,256]{2,1,0:T(8,128)} %add_add_fusion.right_ref, bf16[32,224,256]{2,1,0:T(8,128)(2,1)} %bitcast.60, ...), custom_call_target="tpu_custom_call" | custom-call | tf_op jit(solution)/shard_map/pallas_call | solution.py:250
  70.7 4.3 %convolution_bitcast_fusion = f32[224,224]{1,0:T(8,128)S(1)} fusion(bf16[32,224,256]{2,1,0:T(8,128)(2,1)} %get-tuple-element.14), kind=kOutput, calls=%fused_computation.6 | convolution fusion | flops 822083584 | bytes 3870720 | tf_op jit(solution)/shard_map/pjl,pkl->jk/dot_general | solution.py:279
  75.0 0.1 fusion.49
  75.1 3.5 %collective-permute-start.8 = (f32[225,112]{1,0:T(8,128)S(1)}, f32[225,112]{1,0:T(8,128)S(1)}, u32[]{:S(2)}, u32[]{:S(2)}) collective-permute-start(f32[225,112]{1,0:T(8,128)S(1)} %pad_maximum_fusion), channel_id=1, source_target_pairs={{0,1},{1,0},{2,3},{3,2},{4,5},{5,4},{6,7},{7,6},{8,9},{9,8},{10,11... | collective-permute-start | bytes 302408 | tf_op jit(solution)/shard_map/ppermute | solution.py:41
  78.7 1.0 collective-permute-done.8
  79.7 2.5 %collective-permute-start.9 = (f32[225,112]{1,0:T(8,128)S(1)}, f32[225,112]{1,0:T(8,128)S(1)}, u32[]{:S(2)}, u32[]{:S(2)}) collective-permute-start(f32[225,112]{1,0:T(8,128)S(1)} %fusion.44), channel_id=1, source_target_pairs={{0,2},{1,3},{2,0},{3,1},{4,6},{5,7},{6,4},{7,5},{8,10},{9,11},{10,... | collective-permute-start | bytes 302408 | tf_op jit(solution)/shard_map/ppermute | solution.py:41
  82.1 3.7 %collective-permute-done.9 = f32[225,112]{1,0:T(8,128)S(1)} collective-permute-done((f32[225,112]{1,0:T(8,128)S(1)}, f32[225,112]{1,0:T(8,128)S(1)}, u32[]{:S(2)}, u32[]{:S(2)}) %collective-permute-start.9) | collective-permute-done | bytes 100832 | tf_op jit(solution)/shard_map/ppermute | solution.py:41
  85.9 1.1 collective-permute-start.10
  87.0 3.9 %collective-permute-done.10 = f32[225,112]{1,0:T(8,128)S(1)} collective-permute-done((f32[225,112]{1,0:T(8,128)S(1)}, f32[225,112]{1,0:T(8,128)S(1)}, u32[]{:S(2)}, u32[]{:S(2)}) %collective-permute-start.10) | collective-permute-done | bytes 100832 | tf_op jit(solution)/shard_map/ppermute | solution.py:41
  90.9 1.6 %collective-permute-start.11 = (f32[225,112]{1,0:T(8,128)S(1)}, f32[225,112]{1,0:T(8,128)S(1)}, u32[]{:S(2)}, u32[]{:S(2)}) collective-permute-start(f32[225,112]{1,0:T(8,128)S(1)} %add.128), channel_id=1, source_target_pairs={{0,8},{8,0},{16,24},{24,16},{1,9},{9,1},{17,25},{25,17},{2,10},{10... | collective-permute-start | bytes 302408 | tf_op jit(solution)/shard_map/ppermute | solution.py:41
  92.5 3.3 %collective-permute-done.11 = f32[225,112]{1,0:T(8,128)S(1)} collective-permute-done((f32[225,112]{1,0:T(8,128)S(1)}, f32[225,112]{1,0:T(8,128)S(1)}, u32[]{:S(2)}, u32[]{:S(2)}) %collective-permute-start.11) | collective-permute-done | bytes 100832 | tf_op jit(solution)/shard_map/ppermute | solution.py:41
  95.8 2.7 %collective-permute-start.12 = (f32[225,112]{1,0:T(8,128)S(1)}, f32[225,112]{1,0:T(8,128)S(1)}, u32[]{:S(2)}, u32[]{:S(2)}) collective-permute-start(f32[225,112]{1,0:T(8,128)S(1)} %add.129), channel_id=1, source_target_pairs={{0,16},{8,24},{16,0},{24,8},{1,17},{9,25},{17,1},{25,9},{2,18},{10... | collective-permute-start | bytes 302408 | tf_op jit(solution)/shard_map/ppermute | solution.py:41
  98.5 4.4 %collective-permute-done.12 = f32[225,112]{1,0:T(8,128)S(1)} collective-permute-done((f32[225,112]{1,0:T(8,128)S(1)}, f32[225,112]{1,0:T(8,128)S(1)}, u32[]{:S(2)}, u32[]{:S(2)}) %collective-permute-start.12) | collective-permute-done | bytes 100832 | tf_op jit(solution)/shard_map/ppermute | solution.py:41
  102.9 0.1 copy.25
  103.1 0.1 copy.26
  103.1 0.8 maximum_multiply_fusion.a_ref
  104.0 28.6 %shard_map.18 = f32[256,256]{1,0:T(8,128)} custom-call(f32[224,224]{1,0:T(8,128)} %maximum_multiply_fusion.a_ref), custom_call_target="tpu_custom_call" | custom-call | tf_op jit(solution)/shard_map/pallas_call | solution.py:132
  132.5 10.2 %fusion = f32[32,256]{1,0:T(8,128)S(1)} fusion(f32[32,224,256]{2,1,0:T(8,128)} %get-tuple-element.13, f32[256,256]{1,0:T(8,128)} %shard_map.18), kind=kOutput, calls=%fused_computation.1 | convolution fusion | flops 4936213504 | bytes 14942208 | tf_op jit(solution)/shard_map/pbl,bj->pjl/dot_general | solution.py:285
  142.8 0.6 multiply_bitcast_fusion
  (17 shorter events, 0.4 us)
Async XLA Ops:
  0.0 7.9 %copy-start = (bf16[256,32,224]{0,2,1:T(8,128)(2,1)S(1)}, bf16[256,32,224]{0,2,1:T(8,128)(2,1)}, u32[]{:S(2)}) copy-start(bf16[256,32,224]{0,2,1:T(8,128)(2,1)} %param.1) | copy-start | bytes 11010052
  4.2 53.3 %collective-permute-start.2 = (bf16[15,224,256]{2,1,0:T(8,128)(2,1)}, bf16[15,224,256]{2,1,0:T(8,128)(2,1)S(1)}, u32[]{:S(2)}, u32[]{:S(2)}) collective-permute-start(bf16[15,224,256]{2,1,0:T(8,128)(2,1)} %get-tuple-element.11), channel_id=1, source_target_pairs={{0,1},{1,2},{2,3},{3,4},{4,5},{5,6},{6,7},{8,9},{9,10},{10,11},{11... | collective-permute-start | bytes 5160968 | tf_op jit(solution)/shard_map/ppermute | solution.py:177
  6.6 40.8 %collective-permute-start.6 = (bf16[15,224,256]{2,1,0:T(8,128)(2,1)}, bf16[15,224,256]{2,1,0:T(8,128)(2,1)}, u32[]{:S(2)}, u32[]{:S(2)}) collective-permute-start(bf16[15,224,256]{2,1,0:T(8,128)(2,1)} %get-tuple-element.12), channel_id=1, source_target_pairs={{1,0},{2,1},{3,2},{4,3},{5,4},{6,5},{7,6},{9,8},{10,9},{11,10},{12... | collective-permute-start | bytes 5160968 | tf_op jit(solution)/shard_map/ppermute | solution.py:177
  12.8 14.8 %collective-permute-start = (bf16[32,224,15]{1,0,2:T(8,128)(2,1)}, bf16[32,224,15]{1,0,2:T(8,128)(2,1)}, u32[]{:S(2)}, u32[]{:S(2)}) collective-permute-start(bf16[32,224,15]{1,0,2:T(8,128)(2,1)} %copy.14), channel_id=1, source_target_pairs={{0,8},{8,16},{16,24},{1,9},{9,17},{17,25},{2,10},{10,18},{18,26},{... | collective-permute-start | bytes 645128 | tf_op jit(solution)/shard_map/ppermute | solution.py:180
  19.4 14.5 %collective-permute-start.3 = (bf16[32,224,15]{1,0,2:T(8,128)(2,1)}, bf16[32,224,15]{1,0,2:T(8,128)(2,1)S(1)}, u32[]{:S(2)}, u32[]{:S(2)}) collective-permute-start(bf16[32,224,15]{1,0,2:T(8,128)(2,1)} %copy.16), channel_id=1, source_target_pairs={{8,0},{16,8},{24,16},{9,1},{17,9},{25,17},{10,2},{18,10},{26,18},{... | collective-permute-start | bytes 645128 | tf_op jit(solution)/shard_map/ppermute | solution.py:180
  28.7 18.2 %collective-permute-start.1 = (bf16[15,224,15]{1,2,0:T(8,128)(2,1)S(1)}, bf16[15,224,15]{1,2,0:T(8,128)(2,1)S(1)}, u32[]{:S(2)}, u32[]{:S(2)}) collective-permute-start(bf16[15,224,15]{1,2,0:T(8,128)(2,1)S(1)} %copy.15), channel_id=1, source_target_pairs={{0,1},{1,2},{2,3},{3,4},{4,5},{5,6},{6,7},{8,9},{9,10},{10,11},{11... | collective-permute-start | bytes 302408 | tf_op jit(solution)/shard_map/ppermute | solution.py:177
  32.6 12.3 %collective-permute-start.5 = (bf16[15,224,15]{1,2,0:T(8,128)(2,1)S(1)}, bf16[15,224,15]{1,2,0:T(8,128)(2,1)S(1)}, u32[]{:S(2)}, u32[]{:S(2)}) collective-permute-start(bf16[15,224,15]{1,2,0:T(8,128)(2,1)S(1)} %copy.20), channel_id=1, source_target_pairs={{1,0},{2,1},{3,2},{4,3},{5,4},{6,5},{7,6},{9,8},{10,9},{11,10},{12... | collective-permute-start | bytes 302408 | tf_op jit(solution)/shard_map/ppermute | solution.py:177
  34.0 6.7 %copy-start.1 = (f32[256,32,224]{0,2,1:T(8,128)S(1)}, f32[256,32,224]{0,2,1:T(8,128)}, u32[]{:S(2)}) copy-start(f32[256,32,224]{0,2,1:T(8,128)} %fusion.11) | copy-start | bytes 22020100
  34.0 24.0 %collective-permute-start.4 = (bf16[15,224,15]{1,2,0:T(8,128)(2,1)S(1)}, bf16[15,224,15]{1,2,0:T(8,128)(2,1)S(1)}, u32[]{:S(2)}, u32[]{:S(2)}) collective-permute-start(bf16[15,224,15]{1,2,0:T(8,128)(2,1)S(1)} %copy.17), channel_id=1, source_target_pairs={{0,1},{1,2},{2,3},{3,4},{4,5},{5,6},{6,7},{8,9},{9,10},{10,11},{11... | collective-permute-start | bytes 302408 | tf_op jit(solution)/shard_map/ppermute | solution.py:177
  44.9 10.1 %collective-permute-start.7 = (bf16[15,224,15]{1,2,0:T(8,128)(2,1)S(1)}, bf16[15,224,15]{1,2,0:T(8,128)(2,1)S(1)}, u32[]{:S(2)}, u32[]{:S(2)}) collective-permute-start(bf16[15,224,15]{1,2,0:T(8,128)(2,1)S(1)} %copy.21), channel_id=1, source_target_pairs={{1,0},{2,1},{3,2},{4,3},{5,4},{6,5},{7,6},{9,8},{10,9},{11,10},{12... | collective-permute-start | bytes 302408 | tf_op jit(solution)/shard_map/ppermute | solution.py:177
  75.1 4.5 %collective-permute-start.8 = (f32[225,112]{1,0:T(8,128)S(1)}, f32[225,112]{1,0:T(8,128)S(1)}, u32[]{:S(2)}, u32[]{:S(2)}) collective-permute-start(f32[225,112]{1,0:T(8,128)S(1)} %pad_maximum_fusion), channel_id=1, source_target_pairs={{0,1},{1,0},{2,3},{3,2},{4,5},{5,4},{6,7},{7,6},{8,9},{9,8},{10,11... | collective-permute-start | bytes 302408 | tf_op jit(solution)/shard_map/ppermute | solution.py:41
  79.7 6.2 %collective-permute-start.9 = (f32[225,112]{1,0:T(8,128)S(1)}, f32[225,112]{1,0:T(8,128)S(1)}, u32[]{:S(2)}, u32[]{:S(2)}) collective-permute-start(f32[225,112]{1,0:T(8,128)S(1)} %fusion.44), channel_id=1, source_target_pairs={{0,2},{1,3},{2,0},{3,1},{4,6},{5,7},{6,4},{7,5},{8,10},{9,11},{10,... | collective-permute-start | bytes 302408 | tf_op jit(solution)/shard_map/ppermute | solution.py:41
  85.9 5.0 %collective-permute-start.10 = (f32[225,112]{1,0:T(8,128)S(1)}, f32[225,112]{1,0:T(8,128)S(1)}, u32[]{:S(2)}, u32[]{:S(2)}) collective-permute-start(f32[225,112]{1,0:T(8,128)S(1)} %add.127), channel_id=1, source_target_pairs={{0,4},{1,5},{2,6},{3,7},{4,0},{5,1},{6,2},{7,3},{8,12},{9,13},{10,... | collective-permute-start | bytes 302408 | tf_op jit(solution)/shard_map/ppermute | solution.py:41
  90.9 4.9 %collective-permute-start.11 = (f32[225,112]{1,0:T(8,128)S(1)}, f32[225,112]{1,0:T(8,128)S(1)}, u32[]{:S(2)}, u32[]{:S(2)}) collective-permute-start(f32[225,112]{1,0:T(8,128)S(1)} %add.128), channel_id=1, source_target_pairs={{0,8},{8,0},{16,24},{24,16},{1,9},{9,1},{17,25},{25,17},{2,10},{10... | collective-permute-start | bytes 302408 | tf_op jit(solution)/shard_map/ppermute | solution.py:41
  95.8 7.1 %collective-permute-start.12 = (f32[225,112]{1,0:T(8,128)S(1)}, f32[225,112]{1,0:T(8,128)S(1)}, u32[]{:S(2)}, u32[]{:S(2)}) collective-permute-start(f32[225,112]{1,0:T(8,128)S(1)} %add.129), channel_id=1, source_target_pairs={{0,16},{8,24},{16,0},{24,8},{1,17},{9,25},{17,1},{25,9},{2,18},{10... | collective-permute-start | bytes 302408 | tf_op jit(solution)/shard_map/ppermute | solution.py:41

commit v18 on v16

--- a/solution.py
+++ b/solution.py
@@ -285,7 +285,7 @@
     covariance = unpack_symmetric(packed) / (total_lines * total_pix)
     inverse = spd_inverse(covariance, LOAD)
     solved = jnp.einsum(
-        "pbl,bj->pjl", residual, inverse, precision=highest, preferred_element_type=jnp.float32
+        "jb,pbl->pjl", inverse.T, residual, precision=highest, preferred_element_type=jnp.float32
     )
     scores = jnp.sum(residual * solved, axis=1) / bands
     return scores.T

time: 143 us -> 143 us (level)
  no operation moved by 1% of the time
where the time goes in v18:
time: 143 us; the launch traced here: 142 us
  Pallas kernels  38.8 us (27%)
  matrix products  35.4 us (25%)
  starting transfers between devices  33.1 us (23%)
  waiting for transfers between devices  20.4 us (14%)
  local copies, waits for them, and re-layouts  12 us (8%)
  other arithmetic  2.41 us (2%)
    pallas_call x1, Pallas kernels, spd_inverse(): pl.pallas_call(functools.partial(sweep_kernel, n, load), out_shape=jax.Sh...  28.6 us
    dot_general x9, matrix products, sum_lines(): jnp.einsum('qbk,kl->qbl', values, w, preferred_element_type=jnp.float32)  20.7 us
    ppermute x6, starting transfers between devices, fetch(): return lax.ppermute(piece, 'cross', pairs)  15.1 us
    dot_general x1, matrix products, shards(): jnp.einsum('jb,pbl->pjl', inverse.T, residual, precision=highest, preferr...  10.4 us
    pallas_call x1, Pallas kernels, residuals(): pl.pallas_call(residual_kernel, grid=(bands // block,), in_specs=[spec(le...  10.3 us
    ppermute x2, waiting for transfers between devices, butterfly_sum(): x = x + lax.ppermute(x, axis, pairs)  7.68 us
    ppermute x2, starting transfers between devices, fetch(): return lax.ppermute(piece, 'track', pairs)  6.29 us
    ppermute x3, waiting for transfers between devices, ring_sum(): total = total + lax.ppermute(x, axis, pairs)  6 us
  transfers between devices with their start and end apart: 14, of which 6 were waited for; matrix products, arithmetic and copies ran while one was open for 19% of the time, Pallas kernels for 0%

profile of v18, /device:TPU:0, one launch (start us, length us, event | category | flops | bytes accessed | tf_op | source)
XLA Modules:
  0.0 142.4 jit_solution(12428037803042399807)
XLA Ops:
  0.0 0.0 copy-start
  0.0 4.2 %fusion.46 = (bf16[15,224,256]{2,1,0:T(8,128)(2,1)}, bf16[15,224,256]{2,1,0:T(8,128)(2,1)}) fusion(bf16[32,224,256]{2,1,0:T(8,128)(2,1)} %bitcast.59), kind=kLoop, calls=%fused_computation.56 | loop fusion | bytes 6881280 | tf_op jit(solution)/shard_map/slice | solution.py:184
  4.2 2.5 %collective-permute-start.2 = (bf16[15,224,256]{2,1,0:T(8,128)(2,1)}, bf16[15,224,256]{2,1,0:T(8,128)(2,1)S(1)}, u32[]{:S(2)}, u32[]{:S(2)}) collective-permute-start(bf16[15,224,256]{2,1,0:T(8,128)(2,1)} %get-tuple-element.11), channel_id=1, source_target_pairs={{0,1},{1,2},{2,3},{3,4},{4,5},{5,6},{6,7},{8,9},{9,10},{10,11},{11... | collective-permute-start | bytes 5160968 | tf_op jit(solution)/shard_map/ppermute | solution.py:177
  6.6 1.3 collective-permute-start.6
  7.9 0.0 copy-done
  7.9 2.1 %fusion.45 = (bf16[32,224,15]{2,1,0:T(8,128)(2,1)S(1)}, bf16[32,224,15]{2,1,0:T(8,128)(2,1)}) fusion(bf16[32,224,256]{2,1,0:T(8,128)(2,1)S(1)} %bitcast.61), kind=kLoop, calls=%fused_computation.55 | loop fusion | bytes 860160 | tf_op jit(solution)/shard_map/slice | solution.py:190
  10.0 2.7 %copy.14 = bf16[32,224,15]{1,0,2:T(8,128)(2,1)} copy(bf16[32,224,15]{2,1,0:T(8,128)(2,1)} %get-tuple-element.16) | data formatting | bytes 430080 | tf_op jit(solution)/shard_map/slice | solution.py:189
  12.7 5.0 %collective-permute-start = (bf16[32,224,15]{1,0,2:T(8,128)(2,1)}, bf16[32,224,15]{1,0,2:T(8,128)(2,1)}, u32[]{:S(2)}, u32[]{:S(2)}) collective-permute-start(bf16[32,224,15]{1,0,2:T(8,128)(2,1)} %copy.14), channel_id=1, source_target_pairs={{0,8},{8,16},{16,24},{1,9},{9,17},{17,25},{2,10},{10,18},{18,26},{... | collective-permute-start | bytes 645128 | tf_op jit(solution)/shard_map/ppermute | solution.py:180
  17.8 1.7 %copy.16 = bf16[32,224,15]{1,0,2:T(8,128)(2,1)} copy(bf16[32,224,15]{2,1,0:T(8,128)(2,1)S(1)} %get-tuple-element.15) | data formatting | bytes 430080 | tf_op jit(solution)/shard_map/slice | solution.py:190
  19.4 1.3 collective-permute-start.3
  20.7 6.1 %fusion.11 = f32[256,32,224]{0,2,1:T(8,128)} fusion(bf16[256,32,224]{0,2,1:T(8,128)(2,1)} %param.1), kind=kOutput, calls=%fused_computation.14 | convolution fusion | flops 939720704 | bytes 11010048 | tf_op jit(solution)/shard_map/qbk,kl->qbl/dot_general | solution.py:216
  26.9 0.7 broadcast_multiply_fusion.count_ref
  27.6 0.0 collective-permute-done
  27.6 1.0 fusion.48
  28.7 3.9 %collective-permute-start.1 = (bf16[15,224,15]{1,2,0:T(8,128)(2,1)S(1)}, bf16[15,224,15]{1,2,0:T(8,128)(2,1)S(1)}, u32[]{:S(2)}, u32[]{:S(2)}) collective-permute-start(bf16[15,224,15]{1,2,0:T(8,128)(2,1)S(1)} %copy.15), channel_id=1, source_target_pairs={{0,1},{1,2},{2,3},{3,4},{4,5},{5,6},{6,7},{8,9},{9,10},{10,11},{11... | collective-permute-start | bytes 302408 | tf_op jit(solution)/shard_map/ppermute | solution.py:177
  32.6 1.3 collective-permute-start.5
  33.9 0.0 collective-permute-done.3
  34.0 0.0 copy-start.1
  34.0 4.8 %collective-permute-start.4 = (bf16[15,224,15]{1,2,0:T(8,128)(2,1)S(1)}, bf16[15,224,15]{1,2,0:T(8,128)(2,1)S(1)}, u32[]{:S(2)}, u32[]{:S(2)}) collective-permute-start(bf16[15,224,15]{1,2,0:T(8,128)(2,1)S(1)} %copy.17), channel_id=1, source_target_pairs={{0,1},{1,2},{2,3},{3,4},{4,5},{5,6},{6,7},{8,9},{9,10},{10,11},{11... | collective-permute-start | bytes 302408 | tf_op jit(solution)/shard_map/ppermute | solution.py:177
  38.8 1.9 %fusion.6 = f32[32,224,256]{2,1,0:T(8,128)S(1)} fusion(bf16[32,224,15]{1,0,2:T(8,128)(2,1)} %collective-permute-done), kind=kOutput, calls=%fused_computation.9 | convolution fusion | flops 55054080 | bytes 7555072 | tf_op jit(solution)/shard_map/qbk,kl->qbl/dot_general | solution.py:216
  40.7 0.0 copy-done.1
  40.7 4.1 %fusion.1.middle_ref = f32[32,224,256]{2,1,0:T(8,128)} fusion(f32[32,224,256]{2,1,0:T(8,128)S(1)} %fusion.6, f32[256,32,224]{0,2,1:T(8,128)S(1)} %copy-done.1, bf16[32,224,15]{1,0,2:T(8,128)(2,1)S(1)} %collective-permute-done.3, s32[15]{0:T(128)S(1)} %iota_add_fusion), kind=kOutput, calls=%fused_computation.3 | convolution fusion | flops 58724096 | bytes 22235196 | tf_op jit(solution)/shard_map/qbk,kl->qbl/dot_general | solution.py:216
  44.9 0.0 collective-permute-done.5
  44.9 1.3 collective-permute-start.7
  46.2 0.5 fusion.22
  46.7 0.0 collective-permute-done.1
  46.7 0.5 fusion.25
  47.2 0.0 collective-permute-done.6
  47.2 2.1 %fusion.9 = f32[15,224,256]{2,1,0:T(8,128)S(1)} fusion(bf16[15,224,256]{2,1,0:T(8,128)(2,1)} %collective-permute-done.6), kind=kOutput, calls=%fused_computation.13 | convolution fusion | flops 440598528 | bytes 5160960 | tf_op jit(solution)/shard_map/qbk,kl->qbl/dot_general | solution.py:216
  49.3 5.7 %collective-permute-done.7 = bf16[15,224,15]{1,2,0:T(8,128)(2,1)S(1)} collective-permute-done((bf16[15,224,15]{1,2,0:T(8,128)(2,1)S(1)}, bf16[15,224,15]{1,2,0:T(8,128)(2,1)S(1)}, u32[]{:S(2)}, u32[]{:S(2)}) %collective-permute-start.7) | collective-permute-done | bytes 100832 | tf_op jit(solution)/shard_map/ppermute | solution.py:177
  55.0 2.4 %add_add_fusion.right_ref = f32[15,224,256]{2,1,0:T(8,128)} fusion(f32[15,224,256]{2,1,0:T(8,128)S(1)} %fusion.22, f32[15,224,256]{2,1,0:T(8,128)S(1)} %fusion.9, bf16[15,224,15]{1,2,0:T(8,128)(2,1)S(1)} %collective-permute-done.7, s32[15]{0:T(128)S(1)} %iota_add_fusion), kind=kOutput, calls=%fused_computation.4 | convolution fusion | flops 27528960 | bytes 10422780 | tf_op jit(solution)/shard_map/qbk,kl->qbl/dot_general | solution.py:216
  57.4 0.0 collective-permute-done.2
  57.4 0.6 fusion.13
  58.1 0.0 collective-permute-done.4
  58.1 2.4 %add_add_fusion.1.left_ref = f32[15,224,256]{2,1,0:T(8,128)} fusion(f32[15,224,256]{2,1,0:T(8,128)S(1)} %fusion.25, f32[15,224,256]{2,1,0:T(8,128)S(1)} %fusion.13, bf16[15,224,15]{1,2,0:T(8,128)(2,1)S(1)} %collective-permute-done.4, s32[15]{0:T(128)S(1)} %iota_add_fusion), kind=kOutput, calls=%fused_computation.5 | convolution fusion | flops 27528960 | bytes 10422780 | tf_op jit(solution)/shard_map/qbk,kl->qbl/dot_general | solution.py:216
  60.5 10.3 %shard_map.17 = (f32[32,224,256]{2,1,0:T(8,128)}, bf16[32,224,256]{2,1,0:T(8,128)(2,1)}) custom-call(f32[15,224,256]{2,1,0:T(8,128)} %add_add_fusion.1.left_ref, f32[32,224,256]{2,1,0:T(8,128)} %fusion.1.middle_ref, f32[15,224,256]{2,1,0:T(8,128)} %add_add_fusion.right_ref, bf16[32,224,256]{2,1,0:T(8,128)(2,1)} %bitcast.60, ...), custom_call_target="tpu_custom_call" | custom-call | tf_op jit(solution)/shard_map/pallas_call | solution.py:250
  70.8 4.3 %convolution_bitcast_fusion = f32[224,224]{1,0:T(8,128)S(1)} fusion(bf16[32,224,256]{2,1,0:T(8,128)(2,1)} %get-tuple-element.14), kind=kOutput, calls=%fused_computation.6 | convolution fusion | flops 822083584 | bytes 3870720 | tf_op jit(solution)/shard_map/pjl,pkl->jk/dot_general | solution.py:279
  75.1 0.1 fusion.49
  75.2 3.5 %collective-permute-start.8 = (f32[225,112]{1,0:T(8,128)S(1)}, f32[225,112]{1,0:T(8,128)S(1)}, u32[]{:S(2)}, u32[]{:S(2)}) collective-permute-start(f32[225,112]{1,0:T(8,128)S(1)} %pad_maximum_fusion), channel_id=1, source_target_pairs={{0,1},{1,0},{2,3},{3,2},{4,5},{5,4},{6,7},{7,6},{8,9},{9,8},{10,11... | collective-permute-start | bytes 302408 | tf_op jit(solution)/shard_map/ppermute | solution.py:283
  78.7 1.0 collective-permute-done.8
  79.7 0.1 collective-permute-start.11
  79.8 3.9 %collective-permute-start.10 = (f32[225,112]{1,0:T(8,128)S(1)}, f32[225,112]{1,0:T(8,128)S(1)}, u32[]{:S(2)}, u32[]{:S(2)}) collective-permute-start(f32[225,112]{1,0:T(8,128)S(1)} %fusion.44), channel_id=1, source_target_pairs={{0,4},{1,5},{2,6},{3,7},{4,0},{5,1},{6,2},{7,3},{8,12},{9,13},{10,... | collective-permute-start | bytes 302408 | tf_op jit(solution)/shard_map/ppermute | solution.py:54
  83.6 0.0 collective-permute-start.9
  83.6 2.4 %collective-permute-done.11 = f32[225,112]{1,0:T(8,128)S(1)} collective-permute-done((f32[225,112]{1,0:T(8,128)S(1)}, f32[225,112]{1,0:T(8,128)S(1)}, u32[]{:S(2)}, u32[]{:S(2)}) %collective-permute-start.11) | collective-permute-done | bytes 100832 | tf_op jit(solution)/shard_map/ppermute | solution.py:54
  86.0 3.6 %collective-permute-done.10 = f32[225,112]{1,0:T(8,128)S(1)} collective-permute-done((f32[225,112]{1,0:T(8,128)S(1)}, f32[225,112]{1,0:T(8,128)S(1)}, u32[]{:S(2)}, u32[]{:S(2)}) %collective-permute-start.10) | collective-permute-done | bytes 100832 | tf_op jit(solution)/shard_map/ppermute | solution.py:54
  89.6 0.0 collective-permute-done.9
  89.7 1.6 %collective-permute-start.12 = (f32[225,112]{1,0:T(8,128)S(1)}, f32[225,112]{1,0:T(8,128)S(1)}, u32[]{:S(2)}, u32[]{:S(2)}) collective-permute-start(f32[225,112]{1,0:T(8,128)S(1)} %add_add_fusion.2), channel_id=1, source_target_pairs={{0,8},{8,0},{16,24},{24,16},{1,9},{9,1},{17,25},{25,17},{2,10},{10... | collective-permute-start | bytes 302408 | tf_op jit(solution)/shard_map/ppermute | solution.py:41
  91.3 3.3 %collective-permute-done.12 = f32[225,112]{1,0:T(8,128)S(1)} collective-permute-done((f32[225,112]{1,0:T(8,128)S(1)}, f32[225,112]{1,0:T(8,128)S(1)}, u32[]{:S(2)}, u32[]{:S(2)}) %collective-permute-start.12) | collective-permute-done | bytes 100832 | tf_op jit(solution)/shard_map/ppermute | solution.py:41
  94.6 2.6 %collective-permute-start.13 = (f32[225,112]{1,0:T(8,128)S(1)}, f32[225,112]{1,0:T(8,128)S(1)}, u32[]{:S(2)}, u32[]{:S(2)}) collective-permute-start(f32[225,112]{1,0:T(8,128)S(1)} %add.133), channel_id=1, source_target_pairs={{0,16},{8,24},{16,0},{24,8},{1,17},{9,25},{17,1},{25,9},{2,18},{10... | collective-permute-start | bytes 302408 | tf_op jit(solution)/shard_map/ppermute | solution.py:41
  97.2 4.4 %collective-permute-done.13 = f32[225,112]{1,0:T(8,128)S(1)} collective-permute-done((f32[225,112]{1,0:T(8,128)S(1)}, f32[225,112]{1,0:T(8,128)S(1)}, u32[]{:S(2)}, u32[]{:S(2)}) %collective-permute-start.13) | collective-permute-done | bytes 100832 | tf_op jit(solution)/shard_map/ppermute | solution.py:41
  101.7 0.1 copy.25
  101.8 0.1 copy.26
  101.9 0.8 maximum_multiply_fusion.a_ref
  102.7 28.6 %shard_map.18 = f32[256,256]{1,0:T(8,128)} custom-call(f32[224,224]{1,0:T(8,128)} %maximum_multiply_fusion.a_ref), custom_call_target="tpu_custom_call" | custom-call | tf_op jit(solution)/shard_map/pallas_call | solution.py:132
  131.3 10.4 %fusion = f32[32,256]{1,0:T(8,128)S(1)} fusion(f32[32,224,256]{2,1,0:T(8,128)} %get-tuple-element.13, f32[256,256]{1,0:T(8,128)} %shard_map.18), kind=kOutput, calls=%fused_computation.1 | convolution fusion | flops 4936213504 | bytes 14942208 | tf_op jit(solution)/shard_map/jb,pbl->pjl/dot_general | solution.py:287
  141.8 0.6 multiply_bitcast_fusion
  (16 shorter events, 0.4 us)
Async XLA Ops:
  0.0 7.9 %copy-start = (bf16[256,32,224]{0,2,1:T(8,128)(2,1)S(1)}, bf16[256,32,224]{0,2,1:T(8,128)(2,1)}, u32[]{:S(2)}) copy-start(bf16[256,32,224]{0,2,1:T(8,128)(2,1)} %param.1) | copy-start | bytes 11010052
  4.2 53.3 %collective-permute-start.2 = (bf16[15,224,256]{2,1,0:T(8,128)(2,1)}, bf16[15,224,256]{2,1,0:T(8,128)(2,1)S(1)}, u32[]{:S(2)}, u32[]{:S(2)}) collective-permute-start(bf16[15,224,256]{2,1,0:T(8,128)(2,1)} %get-tuple-element.11), channel_id=1, source_target_pairs={{0,1},{1,2},{2,3},{3,4},{4,5},{5,6},{6,7},{8,9},{9,10},{10,11},{11... | collective-permute-start | bytes 5160968 | tf_op jit(solution)/shard_map/ppermute | solution.py:177
  6.6 40.6 %collective-permute-start.6 = (bf16[15,224,256]{2,1,0:T(8,128)(2,1)}, bf16[15,224,256]{2,1,0:T(8,128)(2,1)}, u32[]{:S(2)}, u32[]{:S(2)}) collective-permute-start(bf16[15,224,256]{2,1,0:T(8,128)(2,1)} %get-tuple-element.12), channel_id=1, source_target_pairs={{1,0},{2,1},{3,2},{4,3},{5,4},{6,5},{7,6},{9,8},{10,9},{11,10},{12... | collective-permute-start | bytes 5160968 | tf_op jit(solution)/shard_map/ppermute | solution.py:177
  12.7 14.8 %collective-permute-start = (bf16[32,224,15]{1,0,2:T(8,128)(2,1)}, bf16[32,224,15]{1,0,2:T(8,128)(2,1)}, u32[]{:S(2)}, u32[]{:S(2)}) collective-permute-start(bf16[32,224,15]{1,0,2:T(8,128)(2,1)} %copy.14), channel_id=1, source_target_pairs={{0,8},{8,16},{16,24},{1,9},{9,17},{17,25},{2,10},{10,18},{18,26},{... | collective-permute-start | bytes 645128 | tf_op jit(solution)/shard_map/ppermute | solution.py:180
  19.4 14.5 %collective-permute-start.3 = (bf16[32,224,15]{1,0,2:T(8,128)(2,1)}, bf16[32,224,15]{1,0,2:T(8,128)(2,1)S(1)}, u32[]{:S(2)}, u32[]{:S(2)}) collective-permute-start(bf16[32,224,15]{1,0,2:T(8,128)(2,1)} %copy.16), channel_id=1, source_target_pairs={{8,0},{16,8},{24,16},{9,1},{17,9},{25,17},{10,2},{18,10},{26,18},{... | collective-permute-start | bytes 645128 | tf_op jit(solution)/shard_map/ppermute | solution.py:180
  28.7 18.0 %collective-permute-start.1 = (bf16[15,224,15]{1,2,0:T(8,128)(2,1)S(1)}, bf16[15,224,15]{1,2,0:T(8,128)(2,1)S(1)}, u32[]{:S(2)}, u32[]{:S(2)}) collective-permute-start(bf16[15,224,15]{1,2,0:T(8,128)(2,1)S(1)} %copy.15), channel_id=1, source_target_pairs={{0,1},{1,2},{2,3},{3,4},{4,5},{5,6},{6,7},{8,9},{9,10},{10,11},{11... | collective-permute-start | bytes 302408 | tf_op jit(solution)/shard_map/ppermute | solution.py:177
  32.6 12.3 %collective-permute-start.5 = (bf16[15,224,15]{1,2,0:T(8,128)(2,1)S(1)}, bf16[15,224,15]{1,2,0:T(8,128)(2,1)S(1)}, u32[]{:S(2)}, u32[]{:S(2)}) collective-permute-start(bf16[15,224,15]{1,2,0:T(8,128)(2,1)S(1)} %copy.20), channel_id=1, source_target_pairs={{1,0},{2,1},{3,2},{4,3},{5,4},{6,5},{7,6},{9,8},{10,9},{11,10},{12... | collective-permute-start | bytes 302408 | tf_op jit(solution)/shard_map/ppermute | solution.py:177
  34.0 6.7 %copy-start.1 = (f32[256,32,224]{0,2,1:T(8,128)S(1)}, f32[256,32,224]{0,2,1:T(8,128)}, u32[]{:S(2)}) copy-start(f32[256,32,224]{0,2,1:T(8,128)} %fusion.11) | copy-start | bytes 22020100
  34.0 24.0 %collective-permute-start.4 = (bf16[15,224,15]{1,2,0:T(8,128)(2,1)S(1)}, bf16[15,224,15]{1,2,0:T(8,128)(2,1)S(1)}, u32[]{:S(2)}, u32[]{:S(2)}) collective-permute-start(bf16[15,224,15]{1,2,0:T(8,128)(2,1)S(1)} %copy.17), channel_id=1, source_target_pairs={{0,1},{1,2},{2,3},{3,4},{4,5},{5,6},{6,7},{8,9},{9,10},{10,11},{11... | collective-permute-start | bytes 302408 | tf_op jit(solution)/shard_map/ppermute | solution.py:177
  44.9 10.1 %collective-permute-start.7 = (bf16[15,224,15]{1,2,0:T(8,128)(2,1)S(1)}, bf16[15,224,15]{1,2,0:T(8,128)(2,1)S(1)}, u32[]{:S(2)}, u32[]{:S(2)}) collective-permute-start(bf16[15,224,15]{1,2,0:T(8,128)(2,1)S(1)} %copy.21), channel_id=1, source_target_pairs={{1,0},{2,1},{3,2},{4,3},{5,4},{6,5},{7,6},{9,8},{10,9},{11,10},{12... | collective-permute-start | bytes 302408 | tf_op jit(solution)/shard_map/ppermute | solution.py:177
  75.2 4.5 %collective-permute-start.8 = (f32[225,112]{1,0:T(8,128)S(1)}, f32[225,112]{1,0:T(8,128)S(1)}, u32[]{:S(2)}, u32[]{:S(2)}) collective-permute-start(f32[225,112]{1,0:T(8,128)S(1)} %pad_maximum_fusion), channel_id=1, source_target_pairs={{0,1},{1,0},{2,3},{3,2},{4,5},{5,4},{6,7},{7,6},{8,9},{9,8},{10,11... | collective-permute-start | bytes 302408 | tf_op jit(solution)/shard_map/ppermute | solution.py:283
  79.7 6.3 %collective-permute-start.11 = (f32[225,112]{1,0:T(8,128)S(1)}, f32[225,112]{1,0:T(8,128)S(1)}, u32[]{:S(2)}, u32[]{:S(2)}) collective-permute-start(f32[225,112]{1,0:T(8,128)S(1)} %fusion.44), channel_id=1, source_target_pairs={{0,6},{1,7},{2,0},{3,1},{4,2},{5,3},{6,4},{7,5},{8,14},{9,15},{10,... | collective-permute-start | bytes 302408 | tf_op jit(solution)/shard_map/ppermute | solution.py:54
  79.8 9.9 %collective-permute-start.10 = (f32[225,112]{1,0:T(8,128)S(1)}, f32[225,112]{1,0:T(8,128)S(1)}, u32[]{:S(2)}, u32[]{:S(2)}) collective-permute-start(f32[225,112]{1,0:T(8,128)S(1)} %fusion.44), channel_id=1, source_target_pairs={{0,4},{1,5},{2,6},{3,7},{4,0},{5,1},{6,2},{7,3},{8,12},{9,13},{10,... | collective-permute-start | bytes 302408 | tf_op jit(solution)/shard_map/ppermute | solution.py:54
  83.6 6.0 %collective-permute-start.9 = (f32[225,112]{1,0:T(8,128)S(1)}, f32[225,112]{1,0:T(8,128)S(1)}, u32[]{:S(2)}, u32[]{:S(2)}) collective-permute-start(f32[225,112]{1,0:T(8,128)S(1)} %fusion.44), channel_id=1, source_target_pairs={{0,2},{1,3},{2,4},{3,5},{4,6},{5,7},{6,0},{7,1},{8,10},{9,11},{10,... | collective-permute-start | bytes 302408 | tf_op jit(solution)/shard_map/ppermute | solution.py:54
  89.7 4.9 %collective-permute-start.12 = (f32[225,112]{1,0:T(8,128)S(1)}, f32[225,112]{1,0:T(8,128)S(1)}, u32[]{:S(2)}, u32[]{:S(2)}) collective-permute-start(f32[225,112]{1,0:T(8,128)S(1)} %add_add_fusion.2), channel_id=1, source_target_pairs={{0,8},{8,0},{16,24},{24,16},{1,9},{9,1},{17,25},{25,17},{2,10},{10... | collective-permute-start | bytes 302408 | tf_op jit(solution)/shard_map/ppermute | solution.py:41
  94.6 7.1 %collective-permute-start.13 = (f32[225,112]{1,0:T(8,128)S(1)}, f32[225,112]{1,0:T(8,128)S(1)}, u32[]{:S(2)}, u32[]{:S(2)}) collective-permute-start(f32[225,112]{1,0:T(8,128)S(1)} %add.133), channel_id=1, source_target_pairs={{0,16},{8,24},{16,0},{24,8},{1,17},{9,25},{17,1},{25,9},{2,18},{10... | collective-permute-start | bytes 302408 | tf_op jit(solution)/shard_map/ppermute | solution.py:41

commit v19 on v18

--- a/solution.py
+++ b/solution.py
@@ -218,7 +218,7 @@
     return total
 
 
-def residual_kernel(left_ref, middle_ref, right_ref, x_ref, count_ref, out_ref, out_bf_ref):
+def residual_kernel(left_ref, middle_ref, right_ref, x_ref, count_ref, out_ref):
     refs = [(left_ref, q) for q in range(left_ref.shape[0])]
     refs += [(middle_ref, q) for q in range(middle_ref.shape[0])]
     refs += [(right_ref, q) for q in range(right_ref.shape[0])]
@@ -230,7 +230,6 @@
     def emit(p, running):
         value = x_ref[p].astype(jnp.float32) - running / count_ref[p]
         out_ref[p] = value
-        out_bf_ref[p] = value.astype(jnp.bfloat16)
 
     span = 2 * HALF + 1
     running = plane(0)
@@ -251,11 +250,8 @@
         residual_kernel,
         grid=(bands // block,),
         in_specs=[spec(left.shape[0]), spec(width), spec(right.shape[0]), spec(width), count_spec],
-        out_specs=[spec(width), spec(width)],
-        out_shape=[
-            jax.ShapeDtypeStruct((width, bands, lines), jnp.float32),
-            jax.ShapeDtypeStruct((width, bands, lines), jnp.bfloat16),
-        ],
+        out_specs=spec(width),
+        out_shape=jax.ShapeDtypeStruct((width, bands, lines), jnp.float32),
     )(left, middle, right, planes, count)
 
 
@@ -275,7 +271,8 @@
     line_count = window_count(lax.axis_index("track") * lines_dev, lines_dev, total_lines)
     pixel_count = window_count(lax.axis_index("cross") * pix_dev, pix_dev, total_pix)
     count = pixel_count[:, None, None] * line_count[None, None, :]
-    residual, residual_bf = residuals(left, middle, right, planes, count)
+    residual = residuals(left, middle, right, planes, count)
+    residual_bf = residual.astype(jnp.bfloat16)
     partial_cov = jnp.einsum(
         "pjl,pkl->jk", residual_bf, residual_bf, preferred_element_type=jnp.float32
     )

time: 143 us -> 147 us (1.028)
  starting transfers between devices: 33.1 us -> 39.4 us
  waiting for transfers between devices: 20.4 us -> 16 us
  matrix products: 35.4 us -> 37.4 us
    ppermute x1, starting transfers between devices: 3.53 us -> 12.8 us  [shards(): lax.ppermute(packed, 'cross', [(i, i ^ 1) for i in range(n_cross)])]
    ppermute x6, waiting for transfers between devices: 5.72 us -> 0.02 us  [fetch(): return lax.ppermute(piece, 'cross', pairs)]
    dot_general x1, matrix products: 4.29 us -> 6.3 us  [shards(): jnp.einsum('pjl,pkl->jk', residual_bf, residual_bf, preferred_element_typ...]
  transfers between devices with their start and end apart: 14 -> 14, of which waited for: 6 -> 5; matrix products, arithmetic and copies ran while one was open for 19% -> 16% of each run, Pallas kernels for 0% -> 0%
where the time goes in v19:
time: 147 us; the launch traced here: 146 us
  starting transfers between devices  39.4 us (27%)
  Pallas kernels  37.8 us (26%)
  matrix products  37.4 us (25%)
  waiting for transfers between devices  16 us (11%)
  local copies, waits for them, and re-layouts  13 us (9%)
  other arithmetic  2.4 us (2%)
    pallas_call x1, Pallas kernels, spd_inverse(): pl.pallas_call(functools.partial(sweep_kernel, n, load), out_shape=jax.Sh...  28.6 us
    dot_general x9, matrix products, sum_lines(): jnp.einsum('qbk,kl->qbl', values, w, preferred_element_type=jnp.float32)  20.7 us
    ppermute x6, starting transfers between devices, fetch(): return lax.ppermute(piece, 'cross', pairs)  13.8 us
    ppermute x1, starting transfers between devices, shards(): lax.ppermute(packed, 'cross', [(i, i ^ 1) for i in range(n_cross)])  12.8 us
    dot_general x1, matrix products, shards(): jnp.einsum('jb,pbl->pjl', inverse.T, residual, precision=highest, preferr...  10.4 us
    pallas_call x1, Pallas kernels, residuals(): pl.pallas_call(residual_kernel, grid=(bands // block,), in_specs=[spec(le...  9.22 us
    ppermute x2, waiting for transfers between devices, butterfly_sum(): x = x + lax.ppermute(x, axis, pairs)  9.04 us
    ppermute x2, starting transfers between devices, fetch(): return lax.ppermute(piece, 'track', pairs)  6.9 us
  transfers between devices with their start and end apart: 14, of which 5 were waited for; matrix products, arithmetic and copies ran while one was open for 16% of the time, Pallas kernels for 0%

profile of v19, /device:TPU:0, one launch (start us, length us, event | category | flops | bytes accessed | tf_op | source)
XLA Modules:
  0.0 146.3 jit_solution(4812442108953442986)
XLA Ops:
  0.0 0.0 copy-start
  0.0 4.2 %fusion.51 = (bf16[15,224,256]{2,1,0:T(8,128)(2,1)}, bf16[15,224,256]{2,1,0:T(8,128)(2,1)}) fusion(bf16[32,224,256]{2,1,0:T(8,128)(2,1)} %bitcast.57), kind=kLoop, calls=%fused_computation.58 | loop fusion | bytes 6881280 | tf_op jit(solution)/shard_map/slice | solution.py:184
  4.2 0.0 copy-done
  4.2 2.1 %fusion.50 = (bf16[32,224,15]{2,1,0:T(8,128)(2,1)S(1)}, bf16[32,224,15]{2,1,0:T(8,128)(2,1)}) fusion(bf16[32,224,256]{2,1,0:T(8,128)(2,1)S(1)} %bitcast.59), kind=kLoop, calls=%fused_computation.57 | loop fusion | bytes 860160 | tf_op jit(solution)/shard_map/slice | solution.py:190
  6.3 2.7 %copy.14 = bf16[32,224,15]{1,0,2:T(8,128)(2,1)} copy(bf16[32,224,15]{2,1,0:T(8,128)(2,1)} %get-tuple-element.12) | data formatting | bytes 430080 | tf_op jit(solution)/shard_map/slice | solution.py:189
  9.0 5.6 %collective-permute-start = (bf16[32,224,15]{1,0,2:T(8,128)(2,1)}, bf16[32,224,15]{1,0,2:T(8,128)(2,1)}, u32[]{:S(2)}, u32[]{:S(2)}) collective-permute-start(bf16[32,224,15]{1,0,2:T(8,128)(2,1)} %copy.14), channel_id=1, source_target_pairs={{0,8},{8,16},{16,24},{1,9},{9,17},{17,25},{2,10},{10,18},{18,26},{... | collective-permute-start | bytes 645128 | tf_op jit(solution)/shard_map/ppermute | solution.py:180
  14.6 1.6 %collective-permute-start.2 = (bf16[15,224,256]{2,1,0:T(8,128)(2,1)}, bf16[15,224,256]{2,1,0:T(8,128)(2,1)S(1)}, u32[]{:S(2)}, u32[]{:S(2)}) collective-permute-start(bf16[15,224,256]{2,1,0:T(8,128)(2,1)} %get-tuple-element.9), channel_id=1, source_target_pairs={{0,1},{1,2},{2,3},{3,4},{4,5},{5,6},{6,7},{8,9},{9,10},{10,11},{11... | collective-permute-start | bytes 5160968 | tf_op jit(solution)/shard_map/ppermute | solution.py:177
  16.2 1.7 %copy.16 = bf16[32,224,15]{1,0,2:T(8,128)(2,1)} copy(bf16[32,224,15]{2,1,0:T(8,128)(2,1)S(1)} %get-tuple-element.11) | data formatting | bytes 430080 | tf_op jit(solution)/shard_map/slice | solution.py:190
  17.9 1.3 collective-permute-start.3
  19.1 1.3 collective-permute-start.6
  20.5 6.1 %fusion.16 = f32[256,32,224]{0,2,1:T(8,128)} fusion(bf16[256,32,224]{0,2,1:T(8,128)(2,1)} %param.1), kind=kOutput, calls=%fused_computation.16 | convolution fusion | flops 939720704 | bytes 11010048 | tf_op jit(solution)/shard_map/qbk,kl->qbl/dot_general | solution.py:216
  26.6 0.7 broadcast_multiply_fusion.count_ref
  27.3 0.0 collective-permute-done
  27.3 1.0 fusion.53
  28.4 4.5 %collective-permute-start.1 = (bf16[15,224,15]{1,2,0:T(8,128)(2,1)S(1)}, bf16[15,224,15]{1,2,0:T(8,128)(2,1)S(1)}, u32[]{:S(2)}, u32[]{:S(2)}) collective-permute-start(bf16[15,224,15]{1,2,0:T(8,128)(2,1)S(1)} %copy.15), channel_id=1, source_target_pairs={{0,1},{1,2},{2,3},{3,4},{4,5},{5,6},{6,7},{8,9},{9,10},{10,11},{11... | collective-permute-start | bytes 302408 | tf_op jit(solution)/shard_map/ppermute | solution.py:177
  32.9 0.0 collective-permute-done.3
  32.9 1.0 fusion.52
  33.9 3.6 %collective-permute-start.4 = (bf16[15,224,15]{1,2,0:T(8,128)(2,1)S(1)}, bf16[15,224,15]{1,2,0:T(8,128)(2,1)S(1)}, u32[]{:S(2)}, u32[]{:S(2)}) collective-permute-start(bf16[15,224,15]{1,2,0:T(8,128)(2,1)S(1)} %copy.17), channel_id=1, source_target_pairs={{0,1},{1,2},{2,3},{3,4},{4,5},{5,6},{6,7},{8,9},{9,10},{10,11},{11... | collective-permute-start | bytes 302408 | tf_op jit(solution)/shard_map/ppermute | solution.py:177
  37.6 0.0 copy-start.1
  37.6 1.6 %collective-permute-start.5 = (bf16[15,224,15]{1,2,0:T(8,128)(2,1)S(1)}, bf16[15,224,15]{1,2,0:T(8,128)(2,1)S(1)}, u32[]{:S(2)}, u32[]{:S(2)}) collective-permute-start(bf16[15,224,15]{1,2,0:T(8,128)(2,1)S(1)} %copy.20), channel_id=1, source_target_pairs={{1,0},{2,1},{3,2},{4,3},{5,4},{6,5},{7,6},{9,8},{10,9},{11,10},{12... | collective-permute-start | bytes 302408 | tf_op jit(solution)/shard_map/ppermute | solution.py:177
  39.2 2.4 %fusion.11 = f32[32,224,256]{2,1,0:T(8,128)S(1)} fusion(bf16[32,224,15]{1,0,2:T(8,128)(2,1)} %collective-permute-done), kind=kOutput, calls=%fused_computation.11 | convolution fusion | flops 55054080 | bytes 7555072 | tf_op jit(solution)/shard_map/qbk,kl->qbl/dot_general | solution.py:216
  41.6 0.0 copy-done.1
  41.6 5.1 %fusion.1.middle_ref = f32[32,224,256]{2,1,0:T(8,128)} fusion(f32[32,224,256]{2,1,0:T(8,128)S(1)} %fusion.11, f32[256,32,224]{0,2,1:T(8,128)S(1)} %copy-done.1, bf16[32,224,15]{1,0,2:T(8,128)(2,1)} %collective-permute-done.3, s32[15]{0:T(128)S(1)} %iota_add_fusion), kind=kOutput, calls=%fused_computation.3 | convolution fusion | flops 58724096 | bytes 22235196 | tf_op jit(solution)/shard_map/qbk,kl->qbl/dot_general | solution.py:216
  46.8 0.0 collective-permute-done.1
  46.8 1.3 collective-permute-start.7
  48.1 0.5 fusion.30
  48.6 0.0 collective-permute-done.5
  48.6 0.5 fusion.27
  49.1 0.0 collective-permute-done.2
  49.1 0.6 fusion.18
  49.7 0.0 collective-permute-done.4
  49.7 2.4 %add_add_fusion.1.left_ref = f32[15,224,256]{2,1,0:T(8,128)} fusion(f32[15,224,256]{2,1,0:T(8,128)S(1)} %fusion.30, f32[15,224,256]{2,1,0:T(8,128)S(1)} %fusion.18, bf16[15,224,15]{1,2,0:T(8,128)(2,1)S(1)} %collective-permute-done.4, s32[15]{0:T(128)S(1)} %iota_add_fusion), kind=kOutput, calls=%fused_computation.7 | convolution fusion | flops 27528960 | bytes 10422780 | tf_op jit(solution)/shard_map/qbk,kl->qbl/dot_general | solution.py:216
  52.1 0.0 collective-permute-done.6
  52.1 0.6 fusion.14
  52.8 0.0 collective-permute-done.7
  52.8 2.4 %add_add_fusion.right_ref = f32[15,224,256]{2,1,0:T(8,128)} fusion(f32[15,224,256]{2,1,0:T(8,128)S(1)} %fusion.27, f32[15,224,256]{2,1,0:T(8,128)S(1)} %fusion.14, bf16[15,224,15]{1,2,0:T(8,128)(2,1)S(1)} %collective-permute-done.7, s32[15]{0:T(128)S(1)} %iota_add_fusion), kind=kOutput, calls=%fused_computation.6 | convolution fusion | flops 27528960 | bytes 10422780 | tf_op jit(solution)/shard_map/qbk,kl->qbl/dot_general | solution.py:216
  55.2 9.2 %shard_map.17 = f32[32,224,256]{2,1,0:T(8,128)} custom-call(f32[15,224,256]{2,1,0:T(8,128)} %add_add_fusion.1.left_ref, f32[32,224,256]{2,1,0:T(8,128)} %fusion.1.middle_ref, f32[15,224,256]{2,1,0:T(8,128)} %add_add_fusion.right_ref, bf16[32,224,256]{2,1,0:T(8,128)(2,1)} %bitcast.58, f32[32,1,256]{2,1,0:T(1,128)} %broadcast_multiply_fusion.count_ref), custom_call_target="tpu_custom_call" | custom-call | tf_op jit(solution)/shard_map/pallas_call | solution.py:249
  64.4 6.3 %fusion.4 = f32[224,224]{1,0:T(8,128)S(1)} fusion(f32[32,224,256]{2,1,0:T(8,128)} %shard_map.17), kind=kOutput, calls=%fused_computation.8 | convolution fusion | flops 823918592 | bytes 7540736 | tf_op jit(solution)/shard_map/pjl,pkl->jk/dot_general | solution.py:276
  70.7 0.1 fusion.54
  70.8 12.8 %collective-permute-start.8 = (f32[225,112]{1,0:T(8,128)S(1)}, f32[225,112]{1,0:T(8,128)S(1)}, u32[]{:S(2)}, u32[]{:S(2)}) collective-permute-start(f32[225,112]{1,0:T(8,128)S(1)} %pad_maximum_fusion), channel_id=1, source_target_pairs={{0,1},{1,0},{2,3},{3,2},{4,5},{5,4},{6,7},{7,6},{8,9},{9,8},{10,11... | collective-permute-start | bytes 302408 | tf_op jit(solution)/shard_map/ppermute | solution.py:280
  83.6 1.0 collective-permute-done.8
  84.6 0.1 collective-permute-start.11
  84.6 3.0 %collective-permute-start.10 = (f32[225,112]{1,0:T(8,128)S(1)}, f32[225,112]{1,0:T(8,128)S(1)}, u32[]{:S(2)}, u32[]{:S(2)}) collective-permute-start(f32[225,112]{1,0:T(8,128)S(1)} %fusion.49), channel_id=1, source_target_pairs={{0,4},{1,5},{2,6},{3,7},{4,0},{5,1},{6,2},{7,3},{8,12},{9,13},{10,... | collective-permute-start | bytes 302408 | tf_op jit(solution)/shard_map/ppermute | solution.py:54
  87.6 0.0 collective-permute-start.9
  87.6 2.9 %collective-permute-done.11 = f32[225,112]{1,0:T(8,128)S(1)} collective-permute-done((f32[225,112]{1,0:T(8,128)S(1)}, f32[225,112]{1,0:T(8,128)S(1)}, u32[]{:S(2)}, u32[]{:S(2)}) %collective-permute-start.11) | collective-permute-done | bytes 100832 | tf_op jit(solution)/shard_map/ppermute | solution.py:54
  90.5 3.1 %collective-permute-done.10 = f32[225,112]{1,0:T(8,128)S(1)} collective-permute-done((f32[225,112]{1,0:T(8,128)S(1)}, f32[225,112]{1,0:T(8,128)S(1)}, u32[]{:S(2)}, u32[]{:S(2)}) %collective-permute-start.10) | collective-permute-done | bytes 100832 | tf_op jit(solution)/shard_map/ppermute | solution.py:54
  93.6 0.0 collective-permute-done.9
  93.6 1.0 collective-permute-start.12
  94.6 3.9 %collective-permute-done.12 = f32[225,112]{1,0:T(8,128)S(1)} collective-permute-done((f32[225,112]{1,0:T(8,128)S(1)}, f32[225,112]{1,0:T(8,128)S(1)}, u32[]{:S(2)}, u32[]{:S(2)}) %collective-permute-start.12) | collective-permute-done | bytes 100832 | tf_op jit(solution)/shard_map/ppermute | solution.py:41
  98.6 2.0 %collective-permute-start.13 = (f32[225,112]{1,0:T(8,128)S(1)}, f32[225,112]{1,0:T(8,128)S(1)}, u32[]{:S(2)}, u32[]{:S(2)}) collective-permute-start(f32[225,112]{1,0:T(8,128)S(1)} %add.133), channel_id=1, source_target_pairs={{0,16},{8,24},{16,0},{24,8},{1,17},{9,25},{17,1},{25,9},{2,18},{10... | collective-permute-start | bytes 302408 | tf_op jit(solution)/shard_map/ppermute | solution.py:41
  100.5 5.1 %collective-permute-done.13 = f32[225,112]{1,0:T(8,128)S(1)} collective-permute-done((f32[225,112]{1,0:T(8,128)S(1)}, f32[225,112]{1,0:T(8,128)S(1)}, u32[]{:S(2)}, u32[]{:S(2)}) %collective-permute-start.13) | collective-permute-done | bytes 100832 | tf_op jit(solution)/shard_map/ppermute | solution.py:41
  105.7 0.1 copy.25
  105.8 0.1 copy.26
  105.9 0.8 maximum_multiply_fusion.a_ref
  106.7 28.6 %shard_map.18 = f32[256,256]{1,0:T(8,128)} custom-call(f32[224,224]{1,0:T(8,128)} %maximum_multiply_fusion.a_ref), custom_call_target="tpu_custom_call" | custom-call | tf_op jit(solution)/shard_map/pallas_call | solution.py:132
  135.3 10.4 %fusion = f32[32,256]{1,0:T(8,128)S(1)} fusion(f32[32,224,256]{2,1,0:T(8,128)} %shard_map.17, f32[256,256]{1,0:T(8,128)} %shard_map.18), kind=kOutput, calls=%fused_computation.1 | convolution fusion | flops 4936213504 | bytes 14942208 | tf_op jit(solution)/shard_map/jb,pbl->pjl/dot_general | solution.py:284
  145.7 0.6 multiply_bitcast_fusion
  (15 shorter events, 0.3 us)
Async XLA Ops:
  0.0 4.2 %copy-start = (bf16[256,32,224]{0,2,1:T(8,128)(2,1)S(1)}, bf16[256,32,224]{0,2,1:T(8,128)(2,1)}, u32[]{:S(2)}) copy-start(bf16[256,32,224]{0,2,1:T(8,128)(2,1)} %param.1) | copy-start | bytes 11010052
  9.0 18.3 %collective-permute-start = (bf16[32,224,15]{1,0,2:T(8,128)(2,1)}, bf16[32,224,15]{1,0,2:T(8,128)(2,1)}, u32[]{:S(2)}, u32[]{:S(2)}) collective-permute-start(bf16[32,224,15]{1,0,2:T(8,128)(2,1)} %copy.14), channel_id=1, source_target_pairs={{0,8},{8,16},{16,24},{1,9},{9,17},{17,25},{2,10},{10,18},{18,26},{... | collective-permute-start | bytes 645128 | tf_op jit(solution)/shard_map/ppermute | solution.py:180
  14.6 34.5 %collective-permute-start.2 = (bf16[15,224,256]{2,1,0:T(8,128)(2,1)}, bf16[15,224,256]{2,1,0:T(8,128)(2,1)S(1)}, u32[]{:S(2)}, u32[]{:S(2)}) collective-permute-start(bf16[15,224,256]{2,1,0:T(8,128)(2,1)} %get-tuple-element.9), channel_id=1, source_target_pairs={{0,1},{1,2},{2,3},{3,4},{4,5},{5,6},{6,7},{8,9},{9,10},{10,11},{11... | collective-permute-start | bytes 5160968 | tf_op jit(solution)/shard_map/ppermute | solution.py:177
  17.9 15.0 %collective-permute-start.3 = (bf16[32,224,15]{1,0,2:T(8,128)(2,1)}, bf16[32,224,15]{1,0,2:T(8,128)(2,1)}, u32[]{:S(2)}, u32[]{:S(2)}) collective-permute-start(bf16[32,224,15]{1,0,2:T(8,128)(2,1)} %copy.16), channel_id=1, source_target_pairs={{8,0},{16,8},{24,16},{9,1},{17,9},{25,17},{10,2},{18,10},{26,18},{... | collective-permute-start | bytes 645128 | tf_op jit(solution)/shard_map/ppermute | solution.py:180
  19.1 33.0 %collective-permute-start.6 = (bf16[15,224,256]{2,1,0:T(8,128)(2,1)}, bf16[15,224,256]{2,1,0:T(8,128)(2,1)S(1)}, u32[]{:S(2)}, u32[]{:S(2)}) collective-permute-start(bf16[15,224,256]{2,1,0:T(8,128)(2,1)} %get-tuple-element.10), channel_id=1, source_target_pairs={{1,0},{2,1},{3,2},{4,3},{5,4},{6,5},{7,6},{9,8},{10,9},{11,10},{12... | collective-permute-start | bytes 5160968 | tf_op jit(solution)/shard_map/ppermute | solution.py:177
  28.4 18.4 %collective-permute-start.1 = (bf16[15,224,15]{1,2,0:T(8,128)(2,1)S(1)}, bf16[15,224,15]{1,2,0:T(8,128)(2,1)S(1)}, u32[]{:S(2)}, u32[]{:S(2)}) collective-permute-start(bf16[15,224,15]{1,2,0:T(8,128)(2,1)S(1)} %copy.15), channel_id=1, source_target_pairs={{0,1},{1,2},{2,3},{3,4},{4,5},{5,6},{6,7},{8,9},{9,10},{10,11},{11... | collective-permute-start | bytes 302408 | tf_op jit(solution)/shard_map/ppermute | solution.py:177
  33.9 15.8 %collective-permute-start.4 = (bf16[15,224,15]{1,2,0:T(8,128)(2,1)S(1)}, bf16[15,224,15]{1,2,0:T(8,128)(2,1)S(1)}, u32[]{:S(2)}, u32[]{:S(2)}) collective-permute-start(bf16[15,224,15]{1,2,0:T(8,128)(2,1)S(1)} %copy.17), channel_id=1, source_target_pairs={{0,1},{1,2},{2,3},{3,4},{4,5},{5,6},{6,7},{8,9},{9,10},{10,11},{11... | collective-permute-start | bytes 302408 | tf_op jit(solution)/shard_map/ppermute | solution.py:177
  37.6 4.0 %copy-start.1 = (f32[256,32,224]{0,2,1:T(8,128)S(1)}, f32[256,32,224]{0,2,1:T(8,128)}, u32[]{:S(2)}) copy-start(f32[256,32,224]{0,2,1:T(8,128)} %fusion.16) | copy-start | bytes 22020100
  37.6 11.0 %collective-permute-start.5 = (bf16[15,224,15]{1,2,0:T(8,128)(2,1)S(1)}, bf16[15,224,15]{1,2,0:T(8,128)(2,1)S(1)}, u32[]{:S(2)}, u32[]{:S(2)}) collective-permute-start(bf16[15,224,15]{1,2,0:T(8,128)(2,1)S(1)} %copy.20), channel_id=1, source_target_pairs={{1,0},{2,1},{3,2},{4,3},{5,4},{6,5},{7,6},{9,8},{10,9},{11,10},{12... | collective-permute-start | bytes 302408 | tf_op jit(solution)/shard_map/ppermute | solution.py:177
  46.8 6.0 %collective-permute-start.7 = (bf16[15,224,15]{1,2,0:T(8,128)(2,1)S(1)}, bf16[15,224,15]{1,2,0:T(8,128)(2,1)S(1)}, u32[]{:S(2)}, u32[]{:S(2)}) collective-permute-start(bf16[15,224,15]{1,2,0:T(8,128)(2,1)S(1)} %copy.21), channel_id=1, source_target_pairs={{1,0},{2,1},{3,2},{4,3},{5,4},{6,5},{7,6},{9,8},{10,9},{11,10},{12... | collective-permute-start | bytes 302408 | tf_op jit(solution)/shard_map/ppermute | solution.py:177
  70.8 13.7 %collective-permute-start.8 = (f32[225,112]{1,0:T(8,128)S(1)}, f32[225,112]{1,0:T(8,128)S(1)}, u32[]{:S(2)}, u32[]{:S(2)}) collective-permute-start(f32[225,112]{1,0:T(8,128)S(1)} %pad_maximum_fusion), channel_id=1, source_target_pairs={{0,1},{1,0},{2,3},{3,2},{4,5},{5,4},{6,7},{7,6},{8,9},{9,8},{10,11... | collective-permute-start | bytes 302408 | tf_op jit(solution)/shard_map/ppermute | solution.py:280
  84.6 5.9 %collective-permute-start.11 = (f32[225,112]{1,0:T(8,128)S(1)}, f32[225,112]{1,0:T(8,128)S(1)}, u32[]{:S(2)}, u32[]{:S(2)}) collective-permute-start(f32[225,112]{1,0:T(8,128)S(1)} %fusion.49), channel_id=1, source_target_pairs={{0,6},{1,7},{2,0},{3,1},{4,2},{5,3},{6,4},{7,5},{8,14},{9,15},{10,... | collective-permute-start | bytes 302408 | tf_op jit(solution)/shard_map/ppermute | solution.py:54
  84.6 9.0 %collective-permute-start.10 = (f32[225,112]{1,0:T(8,128)S(1)}, f32[225,112]{1,0:T(8,128)S(1)}, u32[]{:S(2)}, u32[]{:S(2)}) collective-permute-start(f32[225,112]{1,0:T(8,128)S(1)} %fusion.49), channel_id=1, source_target_pairs={{0,4},{1,5},{2,6},{3,7},{4,0},{5,1},{6,2},{7,3},{8,12},{9,13},{10,... | collective-permute-start | bytes 302408 | tf_op jit(solution)/shard_map/ppermute | solution.py:54
  87.6 6.0 %collective-permute-start.9 = (f32[225,112]{1,0:T(8,128)S(1)}, f32[225,112]{1,0:T(8,128)S(1)}, u32[]{:S(2)}, u32[]{:S(2)}) collective-permute-start(f32[225,112]{1,0:T(8,128)S(1)} %fusion.49), channel_id=1, source_target_pairs={{0,2},{1,3},{2,4},{3,5},{4,6},{5,7},{6,0},{7,1},{8,10},{9,11},{10,... | collective-permute-start | bytes 302408 | tf_op jit(solution)/shard_map/ppermute | solution.py:54
  93.6 4.9 %collective-permute-start.12 = (f32[225,112]{1,0:T(8,128)S(1)}, f32[225,112]{1,0:T(8,128)S(1)}, u32[]{:S(2)}, u32[]{:S(2)}) collective-permute-start(f32[225,112]{1,0:T(8,128)S(1)} %add_add_fusion.2), channel_id=1, source_target_pairs={{0,8},{8,0},{16,24},{24,16},{1,9},{9,1},{17,25},{25,17},{2,10},{10... | collective-permute-start | bytes 302408 | tf_op jit(solution)/shard_map/ppermute | solution.py:41
  98.6 7.1 %collective-permute-start.13 = (f32[225,112]{1,0:T(8,128)S(1)}, f32[225,112]{1,0:T(8,128)S(1)}, u32[]{:S(2)}, u32[]{:S(2)}) collective-permute-start(f32[225,112]{1,0:T(8,128)S(1)} %add.133), channel_id=1, source_target_pairs={{0,16},{8,24},{16,0},{24,8},{1,17},{9,25},{17,1},{25,9},{2,18},{10... | collective-permute-start | bytes 302408 | tf_op jit(solution)/shard_map/ppermute | solution.py:41

commit v20 on v18

--- a/solution.py
+++ b/solution.py
@@ -104,8 +104,11 @@
         det = a00 * a11 - a01 * a01
         p00, p01, p11 = a11 / det, -a01 / det, a00 / det
         a = o_ref[...]
-        c0 = jnp.sum(jnp.where(lanes == k, a, 0.0), axis=1, keepdims=True)
-        c1 = jnp.sum(jnp.where(lanes == k + 1, a, 0.0), axis=1, keepdims=True)
+        start = pl.multiple_of((k // 128) * 128, 128)
+        tile = o_ref[:, pl.ds(start, 128)]
+        tile_lanes = lax.broadcasted_iota(jnp.int32, (1, 128), 1) + start
+        c0 = jnp.sum(jnp.where(tile_lanes == k, tile, 0.0), axis=1, keepdims=True)
+        c1 = jnp.sum(jnp.where(tile_lanes == k + 1, tile, 0.0), axis=1, keepdims=True)
         u0 = c0 * p00 + c1 * p01
         u1 = c0 * p01 + c1 * p11
         s0 = r0 * p00 + r1 * p01

time: 143 us -> 143 us (level)
  no operation moved by 1% of the time
where the time goes in v20:
time: 143 us; the launch traced here: 142 us
  Pallas kernels  38.9 us (27%)
  matrix products  35.4 us (25%)
  starting transfers between devices  33.1 us (23%)
  waiting for transfers between devices  20.4 us (14%)
  local copies, waits for them, and re-layouts  12 us (8%)
  other arithmetic  2.41 us (2%)
    pallas_call x1, Pallas kernels, spd_inverse(): pl.pallas_call(functools.partial(sweep_kernel, n, load), out_shape=jax.Sh...  28.7 us
    dot_general x9, matrix products, sum_lines(): jnp.einsum('qbk,kl->qbl', values, w, preferred_element_type=jnp.float32)  20.7 us
    ppermute x6, starting transfers between devices, fetch(): return lax.ppermute(piece, 'cross', pairs)  15.1 us
    dot_general x1, matrix products, shards(): jnp.einsum('jb,pbl->pjl', inverse.T, residual, precision=highest, preferr...  10.4 us
    pallas_call x1, Pallas kernels, residuals(): pl.pallas_call(residual_kernel, grid=(bands // block,), in_specs=[spec(le...  10.3 us
    ppermute x2, waiting for transfers between devices, butterfly_sum(): x = x + lax.ppermute(x, axis, pairs)  7.68 us
    ppermute x2, starting transfers between devices, fetch(): return lax.ppermute(piece, 'track', pairs)  6.29 us
    ppermute x3, waiting for transfers between devices, ring_sum(): total = total + lax.ppermute(x, axis, pairs)  6 us
  transfers between devices with their start and end apart: 14, of which 6 were waited for; matrix products, arithmetic and copies ran while one was open for 19% of the time, Pallas kernels for 0%

profile of v20, /device:TPU:0, one launch (start us, length us, event | category | flops | bytes accessed | tf_op | source)
XLA Modules:
  0.0 142.5 jit_solution(7024996495318669490)
XLA Ops:
  0.0 0.0 copy-start
  0.0 4.2 %fusion.46 = (bf16[15,224,256]{2,1,0:T(8,128)(2,1)}, bf16[15,224,256]{2,1,0:T(8,128)(2,1)}) fusion(bf16[32,224,256]{2,1,0:T(8,128)(2,1)} %bitcast.59), kind=kLoop, calls=%fused_computation.56 | loop fusion | bytes 6881280 | tf_op jit(solution)/shard_map/slice | solution.py:187
  4.2 2.5 %collective-permute-start.2 = (bf16[15,224,256]{2,1,0:T(8,128)(2,1)}, bf16[15,224,256]{2,1,0:T(8,128)(2,1)S(1)}, u32[]{:S(2)}, u32[]{:S(2)}) collective-permute-start(bf16[15,224,256]{2,1,0:T(8,128)(2,1)} %get-tuple-element.11), channel_id=1, source_target_pairs={{0,1},{1,2},{2,3},{3,4},{4,5},{5,6},{6,7},{8,9},{9,10},{10,11},{11... | collective-permute-start | bytes 5160968 | tf_op jit(solution)/shard_map/ppermute | solution.py:180
  6.6 1.3 collective-permute-start.6
  7.9 0.0 copy-done
  7.9 2.1 %fusion.45 = (bf16[32,224,15]{2,1,0:T(8,128)(2,1)S(1)}, bf16[32,224,15]{2,1,0:T(8,128)(2,1)}) fusion(bf16[32,224,256]{2,1,0:T(8,128)(2,1)S(1)} %bitcast.61), kind=kLoop, calls=%fused_computation.55 | loop fusion | bytes 860160 | tf_op jit(solution)/shard_map/slice | solution.py:193
  10.0 2.7 %copy.14 = bf16[32,224,15]{1,0,2:T(8,128)(2,1)} copy(bf16[32,224,15]{2,1,0:T(8,128)(2,1)} %get-tuple-element.16) | data formatting | bytes 430080 | tf_op jit(solution)/shard_map/slice | solution.py:192
  12.7 5.0 %collective-permute-start = (bf16[32,224,15]{1,0,2:T(8,128)(2,1)}, bf16[32,224,15]{1,0,2:T(8,128)(2,1)}, u32[]{:S(2)}, u32[]{:S(2)}) collective-permute-start(bf16[32,224,15]{1,0,2:T(8,128)(2,1)} %copy.14), channel_id=1, source_target_pairs={{0,8},{8,16},{16,24},{1,9},{9,17},{17,25},{2,10},{10,18},{18,26},{... | collective-permute-start | bytes 645128 | tf_op jit(solution)/shard_map/ppermute | solution.py:183
  17.8 1.7 %copy.16 = bf16[32,224,15]{1,0,2:T(8,128)(2,1)} copy(bf16[32,224,15]{2,1,0:T(8,128)(2,1)S(1)} %get-tuple-element.15) | data formatting | bytes 430080 | tf_op jit(solution)/shard_map/slice | solution.py:193
  19.4 1.3 collective-permute-start.3
  20.7 6.1 %fusion.11 = f32[256,32,224]{0,2,1:T(8,128)} fusion(bf16[256,32,224]{0,2,1:T(8,128)(2,1)} %param.1), kind=kOutput, calls=%fused_computation.14 | convolution fusion | flops 939720704 | bytes 11010048 | tf_op jit(solution)/shard_map/qbk,kl->qbl/dot_general | solution.py:219
  26.9 0.7 broadcast_multiply_fusion.count_ref
  27.6 0.0 collective-permute-done
  27.6 1.0 fusion.48
  28.7 3.9 %collective-permute-start.1 = (bf16[15,224,15]{1,2,0:T(8,128)(2,1)S(1)}, bf16[15,224,15]{1,2,0:T(8,128)(2,1)S(1)}, u32[]{:S(2)}, u32[]{:S(2)}) collective-permute-start(bf16[15,224,15]{1,2,0:T(8,128)(2,1)S(1)} %copy.15), channel_id=1, source_target_pairs={{0,1},{1,2},{2,3},{3,4},{4,5},{5,6},{6,7},{8,9},{9,10},{10,11},{11... | collective-permute-start | bytes 302408 | tf_op jit(solution)/shard_map/ppermute | solution.py:180
  32.6 1.3 collective-permute-start.5
  33.9 0.0 collective-permute-done.3
  34.0 0.0 copy-start.1
  34.0 4.8 %collective-permute-start.4 = (bf16[15,224,15]{1,2,0:T(8,128)(2,1)S(1)}, bf16[15,224,15]{1,2,0:T(8,128)(2,1)S(1)}, u32[]{:S(2)}, u32[]{:S(2)}) collective-permute-start(bf16[15,224,15]{1,2,0:T(8,128)(2,1)S(1)} %copy.17), channel_id=1, source_target_pairs={{0,1},{1,2},{2,3},{3,4},{4,5},{5,6},{6,7},{8,9},{9,10},{10,11},{11... | collective-permute-start | bytes 302408 | tf_op jit(solution)/shard_map/ppermute | solution.py:180
  38.8 1.9 %fusion.6 = f32[32,224,256]{2,1,0:T(8,128)S(1)} fusion(bf16[32,224,15]{1,0,2:T(8,128)(2,1)} %collective-permute-done), kind=kOutput, calls=%fused_computation.9 | convolution fusion | flops 55054080 | bytes 7555072 | tf_op jit(solution)/shard_map/qbk,kl->qbl/dot_general | solution.py:219
  40.7 0.0 copy-done.1
  40.7 4.1 %fusion.1.middle_ref = f32[32,224,256]{2,1,0:T(8,128)} fusion(f32[32,224,256]{2,1,0:T(8,128)S(1)} %fusion.6, f32[256,32,224]{0,2,1:T(8,128)S(1)} %copy-done.1, bf16[32,224,15]{1,0,2:T(8,128)(2,1)S(1)} %collective-permute-done.3, s32[15]{0:T(128)S(1)} %iota_add_fusion), kind=kOutput, calls=%fused_computation.3 | convolution fusion | flops 58724096 | bytes 22235196 | tf_op jit(solution)/shard_map/qbk,kl->qbl/dot_general | solution.py:219
  44.9 0.0 collective-permute-done.5
  44.9 1.3 collective-permute-start.7
  46.2 0.5 fusion.22
  46.7 0.0 collective-permute-done.1
  46.7 0.5 fusion.25
  47.2 0.0 collective-permute-done.6
  47.2 2.1 %fusion.9 = f32[15,224,256]{2,1,0:T(8,128)S(1)} fusion(bf16[15,224,256]{2,1,0:T(8,128)(2,1)} %collective-permute-done.6), kind=kOutput, calls=%fused_computation.13 | convolution fusion | flops 440598528 | bytes 5160960 | tf_op jit(solution)/shard_map/qbk,kl->qbl/dot_general | solution.py:219
  49.3 5.7 %collective-permute-done.7 = bf16[15,224,15]{1,2,0:T(8,128)(2,1)S(1)} collective-permute-done((bf16[15,224,15]{1,2,0:T(8,128)(2,1)S(1)}, bf16[15,224,15]{1,2,0:T(8,128)(2,1)S(1)}, u32[]{:S(2)}, u32[]{:S(2)}) %collective-permute-start.7) | collective-permute-done | bytes 100832 | tf_op jit(solution)/shard_map/ppermute | solution.py:180
  55.0 2.4 %add_add_fusion.right_ref = f32[15,224,256]{2,1,0:T(8,128)} fusion(f32[15,224,256]{2,1,0:T(8,128)S(1)} %fusion.22, f32[15,224,256]{2,1,0:T(8,128)S(1)} %fusion.9, bf16[15,224,15]{1,2,0:T(8,128)(2,1)S(1)} %collective-permute-done.7, s32[15]{0:T(128)S(1)} %iota_add_fusion), kind=kOutput, calls=%fused_computation.4 | convolution fusion | flops 27528960 | bytes 10422780 | tf_op jit(solution)/shard_map/qbk,kl->qbl/dot_general | solution.py:219
  57.4 0.0 collective-permute-done.2
  57.4 0.6 fusion.13
  58.1 0.0 collective-permute-done.4
  58.1 2.4 %add_add_fusion.1.left_ref = f32[15,224,256]{2,1,0:T(8,128)} fusion(f32[15,224,256]{2,1,0:T(8,128)S(1)} %fusion.25, f32[15,224,256]{2,1,0:T(8,128)S(1)} %fusion.13, bf16[15,224,15]{1,2,0:T(8,128)(2,1)S(1)} %collective-permute-done.4, s32[15]{0:T(128)S(1)} %iota_add_fusion), kind=kOutput, calls=%fused_computation.5 | convolution fusion | flops 27528960 | bytes 10422780 | tf_op jit(solution)/shard_map/qbk,kl->qbl/dot_general | solution.py:219
  60.5 10.3 %shard_map.17 = (f32[32,224,256]{2,1,0:T(8,128)}, bf16[32,224,256]{2,1,0:T(8,128)(2,1)}) custom-call(f32[15,224,256]{2,1,0:T(8,128)} %add_add_fusion.1.left_ref, f32[32,224,256]{2,1,0:T(8,128)} %fusion.1.middle_ref, f32[15,224,256]{2,1,0:T(8,128)} %add_add_fusion.right_ref, bf16[32,224,256]{2,1,0:T(8,128)(2,1)} %bitcast.60, ...), custom_call_target="tpu_custom_call" | custom-call | tf_op jit(solution)/shard_map/pallas_call | solution.py:253
  70.8 4.3 %convolution_bitcast_fusion = f32[224,224]{1,0:T(8,128)S(1)} fusion(bf16[32,224,256]{2,1,0:T(8,128)(2,1)} %get-tuple-element.14), kind=kOutput, calls=%fused_computation.6 | convolution fusion | flops 822083584 | bytes 3870720 | tf_op jit(solution)/shard_map/pjl,pkl->jk/dot_general | solution.py:282
  75.1 0.1 fusion.49
  75.2 3.5 %collective-permute-start.8 = (f32[225,112]{1,0:T(8,128)S(1)}, f32[225,112]{1,0:T(8,128)S(1)}, u32[]{:S(2)}, u32[]{:S(2)}) collective-permute-start(f32[225,112]{1,0:T(8,128)S(1)} %pad_maximum_fusion), channel_id=1, source_target_pairs={{0,1},{1,0},{2,3},{3,2},{4,5},{5,4},{6,7},{7,6},{8,9},{9,8},{10,11... | collective-permute-start | bytes 302408 | tf_op jit(solution)/shard_map/ppermute | solution.py:286
  78.7 1.0 collective-permute-done.8
  79.7 0.1 collective-permute-start.11
  79.8 3.9 %collective-permute-start.10 = (f32[225,112]{1,0:T(8,128)S(1)}, f32[225,112]{1,0:T(8,128)S(1)}, u32[]{:S(2)}, u32[]{:S(2)}) collective-permute-start(f32[225,112]{1,0:T(8,128)S(1)} %fusion.44), channel_id=1, source_target_pairs={{0,4},{1,5},{2,6},{3,7},{4,0},{5,1},{6,2},{7,3},{8,12},{9,13},{10,... | collective-permute-start | bytes 302408 | tf_op jit(solution)/shard_map/ppermute | solution.py:54
  83.6 0.0 collective-permute-start.9
  83.6 2.4 %collective-permute-done.11 = f32[225,112]{1,0:T(8,128)S(1)} collective-permute-done((f32[225,112]{1,0:T(8,128)S(1)}, f32[225,112]{1,0:T(8,128)S(1)}, u32[]{:S(2)}, u32[]{:S(2)}) %collective-permute-start.11) | collective-permute-done | bytes 100832 | tf_op jit(solution)/shard_map/ppermute | solution.py:54
  86.0 3.6 %collective-permute-done.10 = f32[225,112]{1,0:T(8,128)S(1)} collective-permute-done((f32[225,112]{1,0:T(8,128)S(1)}, f32[225,112]{1,0:T(8,128)S(1)}, u32[]{:S(2)}, u32[]{:S(2)}) %collective-permute-start.10) | collective-permute-done | bytes 100832 | tf_op jit(solution)/shard_map/ppermute | solution.py:54
  89.6 0.0 collective-permute-done.9
  89.7 1.6 %collective-permute-start.12 = (f32[225,112]{1,0:T(8,128)S(1)}, f32[225,112]{1,0:T(8,128)S(1)}, u32[]{:S(2)}, u32[]{:S(2)}) collective-permute-start(f32[225,112]{1,0:T(8,128)S(1)} %add_add_fusion.2), channel_id=1, source_target_pairs={{0,8},{8,0},{16,24},{24,16},{1,9},{9,1},{17,25},{25,17},{2,10},{10... | collective-permute-start | bytes 302408 | tf_op jit(solution)/shard_map/ppermute | solution.py:41
  91.3 3.3 %collective-permute-done.12 = f32[225,112]{1,0:T(8,128)S(1)} collective-permute-done((f32[225,112]{1,0:T(8,128)S(1)}, f32[225,112]{1,0:T(8,128)S(1)}, u32[]{:S(2)}, u32[]{:S(2)}) %collective-permute-start.12) | collective-permute-done | bytes 100832 | tf_op jit(solution)/shard_map/ppermute | solution.py:41
  94.6 2.6 %collective-permute-start.13 = (f32[225,112]{1,0:T(8,128)S(1)}, f32[225,112]{1,0:T(8,128)S(1)}, u32[]{:S(2)}, u32[]{:S(2)}) collective-permute-start(f32[225,112]{1,0:T(8,128)S(1)} %add.133), channel_id=1, source_target_pairs={{0,16},{8,24},{16,0},{24,8},{1,17},{9,25},{17,1},{25,9},{2,18},{10... | collective-permute-start | bytes 302408 | tf_op jit(solution)/shard_map/ppermute | solution.py:41
  97.2 4.4 %collective-permute-done.13 = f32[225,112]{1,0:T(8,128)S(1)} collective-permute-done((f32[225,112]{1,0:T(8,128)S(1)}, f32[225,112]{1,0:T(8,128)S(1)}, u32[]{:S(2)}, u32[]{:S(2)}) %collective-permute-start.13) | collective-permute-done | bytes 100832 | tf_op jit(solution)/shard_map/ppermute | solution.py:41
  101.7 0.1 copy.25
  101.8 0.1 copy.26
  101.9 0.8 maximum_multiply_fusion.a_ref
  102.7 28.7 %shard_map.18 = f32[256,256]{1,0:T(8,128)} custom-call(f32[224,224]{1,0:T(8,128)} %maximum_multiply_fusion.a_ref), custom_call_target="tpu_custom_call" | custom-call | tf_op jit(solution)/shard_map/pallas_call | solution.py:135
  131.4 10.4 %fusion = f32[32,256]{1,0:T(8,128)S(1)} fusion(f32[32,224,256]{2,1,0:T(8,128)} %get-tuple-element.13, f32[256,256]{1,0:T(8,128)} %shard_map.18), kind=kOutput, calls=%fused_computation.1 | convolution fusion | flops 4936213504 | bytes 14942208 | tf_op jit(solution)/shard_map/jb,pbl->pjl/dot_general | solution.py:290
  141.9 0.6 multiply_bitcast_fusion
  (16 shorter events, 0.4 us)
Async XLA Ops:
  0.0 7.9 %copy-start = (bf16[256,32,224]{0,2,1:T(8,128)(2,1)S(1)}, bf16[256,32,224]{0,2,1:T(8,128)(2,1)}, u32[]{:S(2)}) copy-start(bf16[256,32,224]{0,2,1:T(8,128)(2,1)} %param.1) | copy-start | bytes 11010052
  4.2 53.3 %collective-permute-start.2 = (bf16[15,224,256]{2,1,0:T(8,128)(2,1)}, bf16[15,224,256]{2,1,0:T(8,128)(2,1)S(1)}, u32[]{:S(2)}, u32[]{:S(2)}) collective-permute-start(bf16[15,224,256]{2,1,0:T(8,128)(2,1)} %get-tuple-element.11), channel_id=1, source_target_pairs={{0,1},{1,2},{2,3},{3,4},{4,5},{5,6},{6,7},{8,9},{9,10},{10,11},{11... | collective-permute-start | bytes 5160968 | tf_op jit(solution)/shard_map/ppermute | solution.py:180
  6.6 40.6 %collective-permute-start.6 = (bf16[15,224,256]{2,1,0:T(8,128)(2,1)}, bf16[15,224,256]{2,1,0:T(8,128)(2,1)}, u32[]{:S(2)}, u32[]{:S(2)}) collective-permute-start(bf16[15,224,256]{2,1,0:T(8,128)(2,1)} %get-tuple-element.12), channel_id=1, source_target_pairs={{1,0},{2,1},{3,2},{4,3},{5,4},{6,5},{7,6},{9,8},{10,9},{11,10},{12... | collective-permute-start | bytes 5160968 | tf_op jit(solution)/shard_map/ppermute | solution.py:180
  12.7 14.8 %collective-permute-start = (bf16[32,224,15]{1,0,2:T(8,128)(2,1)}, bf16[32,224,15]{1,0,2:T(8,128)(2,1)}, u32[]{:S(2)}, u32[]{:S(2)}) collective-permute-start(bf16[32,224,15]{1,0,2:T(8,128)(2,1)} %copy.14), channel_id=1, source_target_pairs={{0,8},{8,16},{16,24},{1,9},{9,17},{17,25},{2,10},{10,18},{18,26},{... | collective-permute-start | bytes 645128 | tf_op jit(solution)/shard_map/ppermute | solution.py:183
  19.4 14.5 %collective-permute-start.3 = (bf16[32,224,15]{1,0,2:T(8,128)(2,1)}, bf16[32,224,15]{1,0,2:T(8,128)(2,1)S(1)}, u32[]{:S(2)}, u32[]{:S(2)}) collective-permute-start(bf16[32,224,15]{1,0,2:T(8,128)(2,1)} %copy.16), channel_id=1, source_target_pairs={{8,0},{16,8},{24,16},{9,1},{17,9},{25,17},{10,2},{18,10},{26,18},{... | collective-permute-start | bytes 645128 | tf_op jit(solution)/shard_map/ppermute | solution.py:183
  28.7 18.0 %collective-permute-start.1 = (bf16[15,224,15]{1,2,0:T(8,128)(2,1)S(1)}, bf16[15,224,15]{1,2,0:T(8,128)(2,1)S(1)}, u32[]{:S(2)}, u32[]{:S(2)}) collective-permute-start(bf16[15,224,15]{1,2,0:T(8,128)(2,1)S(1)} %copy.15), channel_id=1, source_target_pairs={{0,1},{1,2},{2,3},{3,4},{4,5},{5,6},{6,7},{8,9},{9,10},{10,11},{11... | collective-permute-start | bytes 302408 | tf_op jit(solution)/shard_map/ppermute | solution.py:180
  32.6 12.3 %collective-permute-start.5 = (bf16[15,224,15]{1,2,0:T(8,128)(2,1)S(1)}, bf16[15,224,15]{1,2,0:T(8,128)(2,1)S(1)}, u32[]{:S(2)}, u32[]{:S(2)}) collective-permute-start(bf16[15,224,15]{1,2,0:T(8,128)(2,1)S(1)} %copy.20), channel_id=1, source_target_pairs={{1,0},{2,1},{3,2},{4,3},{5,4},{6,5},{7,6},{9,8},{10,9},{11,10},{12... | collective-permute-start | bytes 302408 | tf_op jit(solution)/shard_map/ppermute | solution.py:180
  34.0 6.7 %copy-start.1 = (f32[256,32,224]{0,2,1:T(8,128)S(1)}, f32[256,32,224]{0,2,1:T(8,128)}, u32[]{:S(2)}) copy-start(f32[256,32,224]{0,2,1:T(8,128)} %fusion.11) | copy-start | bytes 22020100
  34.0 24.0 %collective-permute-start.4 = (bf16[15,224,15]{1,2,0:T(8,128)(2,1)S(1)}, bf16[15,224,15]{1,2,0:T(8,128)(2,1)S(1)}, u32[]{:S(2)}, u32[]{:S(2)}) collective-permute-start(bf16[15,224,15]{1,2,0:T(8,128)(2,1)S(1)} %copy.17), channel_id=1, source_target_pairs={{0,1},{1,2},{2,3},{3,4},{4,5},{5,6},{6,7},{8,9},{9,10},{10,11},{11... | collective-permute-start | bytes 302408 | tf_op jit(solution)/shard_map/ppermute | solution.py:180
  44.9 10.1 %collective-permute-start.7 = (bf16[15,224,15]{1,2,0:T(8,128)(2,1)S(1)}, bf16[15,224,15]{1,2,0:T(8,128)(2,1)S(1)}, u32[]{:S(2)}, u32[]{:S(2)}) collective-permute-start(bf16[15,224,15]{1,2,0:T(8,128)(2,1)S(1)} %copy.21), channel_id=1, source_target_pairs={{1,0},{2,1},{3,2},{4,3},{5,4},{6,5},{7,6},{9,8},{10,9},{11,10},{12... | collective-permute-start | bytes 302408 | tf_op jit(solution)/shard_map/ppermute | solution.py:180
  75.2 4.5 %collective-permute-start.8 = (f32[225,112]{1,0:T(8,128)S(1)}, f32[225,112]{1,0:T(8,128)S(1)}, u32[]{:S(2)}, u32[]{:S(2)}) collective-permute-start(f32[225,112]{1,0:T(8,128)S(1)} %pad_maximum_fusion), channel_id=1, source_target_pairs={{0,1},{1,0},{2,3},{3,2},{4,5},{5,4},{6,7},{7,6},{8,9},{9,8},{10,11... | collective-permute-start | bytes 302408 | tf_op jit(solution)/shard_map/ppermute | solution.py:286
  79.7 6.3 %collective-permute-start.11 = (f32[225,112]{1,0:T(8,128)S(1)}, f32[225,112]{1,0:T(8,128)S(1)}, u32[]{:S(2)}, u32[]{:S(2)}) collective-permute-start(f32[225,112]{1,0:T(8,128)S(1)} %fusion.44), channel_id=1, source_target_pairs={{0,6},{1,7},{2,0},{3,1},{4,2},{5,3},{6,4},{7,5},{8,14},{9,15},{10,... | collective-permute-start | bytes 302408 | tf_op jit(solution)/shard_map/ppermute | solution.py:54
  79.8 9.9 %collective-permute-start.10 = (f32[225,112]{1,0:T(8,128)S(1)}, f32[225,112]{1,0:T(8,128)S(1)}, u32[]{:S(2)}, u32[]{:S(2)}) collective-permute-start(f32[225,112]{1,0:T(8,128)S(1)} %fusion.44), channel_id=1, source_target_pairs={{0,4},{1,5},{2,6},{3,7},{4,0},{5,1},{6,2},{7,3},{8,12},{9,13},{10,... | collective-permute-start | bytes 302408 | tf_op jit(solution)/shard_map/ppermute | solution.py:54
  83.6 6.0 %collective-permute-start.9 = (f32[225,112]{1,0:T(8,128)S(1)}, f32[225,112]{1,0:T(8,128)S(1)}, u32[]{:S(2)}, u32[]{:S(2)}) collective-permute-start(f32[225,112]{1,0:T(8,128)S(1)} %fusion.44), channel_id=1, source_target_pairs={{0,2},{1,3},{2,4},{3,5},{4,6},{5,7},{6,0},{7,1},{8,10},{9,11},{10,... | collective-permute-start | bytes 302408 | tf_op jit(solution)/shard_map/ppermute | solution.py:54
  89.7 4.9 %collective-permute-start.12 = (f32[225,112]{1,0:T(8,128)S(1)}, f32[225,112]{1,0:T(8,128)S(1)}, u32[]{:S(2)}, u32[]{:S(2)}) collective-permute-start(f32[225,112]{1,0:T(8,128)S(1)} %add_add_fusion.2), channel_id=1, source_target_pairs={{0,8},{8,0},{16,24},{24,16},{1,9},{9,1},{17,25},{25,17},{2,10},{10... | collective-permute-start | bytes 302408 | tf_op jit(solution)/shard_map/ppermute | solution.py:41
  94.6 7.1 %collective-permute-start.13 = (f32[225,112]{1,0:T(8,128)S(1)}, f32[225,112]{1,0:T(8,128)S(1)}, u32[]{:S(2)}, u32[]{:S(2)}) collective-permute-start(f32[225,112]{1,0:T(8,128)S(1)} %add.133), channel_id=1, source_target_pairs={{0,16},{8,24},{16,0},{24,8},{1,17},{9,25},{17,1},{25,9},{2,18},{10... | collective-permute-start | bytes 302408 | tf_op jit(solution)/shard_map/ppermute | solution.py:41

commit v21 on v18

--- a/solution.py
+++ b/solution.py
@@ -279,9 +279,9 @@
     partial_cov = jnp.einsum(
         "pjl,pkl->jk", residual_bf, residual_bf, preferred_element_type=jnp.float32
     )
-    packed = pack_symmetric(partial_cov)
+    packed = butterfly_sum(pack_symmetric(partial_cov), "track")
     packed = packed + lax.ppermute(packed, "cross", [(i, i ^ 1) for i in range(n_cross)])
-    packed = butterfly_sum(ring_sum(packed, "cross", 2), "track")
+    packed = ring_sum(packed, "cross", 2)
     covariance = unpack_symmetric(packed) / (total_lines * total_pix)
     inverse = spd_inverse(covariance, LOAD)
     solved = jnp.einsum(

time: 143 us -> 144 us (level)
    ppermute x1, starting transfers between devices: 3.53 us -> 1.04 us  [shards(): lax.ppermute(packed, 'cross', [(i, i ^ 1) for i in range(n_cross)])]
    ppermute x3, starting transfers between devices: 3.91 us -> 6.09 us  [ring_sum(): total = total + lax.ppermute(x, axis, pairs)]
where the time goes in v21:
time: 144 us; the launch traced here: 143 us
  Pallas kernels  38.8 us (27%)
  matrix products  35.4 us (25%)
  starting transfers between devices  32.8 us (23%)
  waiting for transfers between devices  21.6 us (15%)
  local copies, waits for them, and re-layouts  12 us (8%)
  other arithmetic  2.4 us (2%)
    pallas_call x1, Pallas kernels, spd_inverse(): pl.pallas_call(functools.partial(sweep_kernel, n, load), out_shape=jax.Sh...  28.6 us
    dot_general x9, matrix products, sum_lines(): jnp.einsum('qbk,kl->qbl', values, w, preferred_element_type=jnp.float32)  20.7 us
    ppermute x6, starting transfers between devices, fetch(): return lax.ppermute(piece, 'cross', pairs)  15.1 us
    dot_general x1, matrix products, shards(): jnp.einsum('jb,pbl->pjl', inverse.T, residual, precision=highest, preferr...  10.4 us
    pallas_call x1, Pallas kernels, residuals(): pl.pallas_call(residual_kernel, grid=(bands // block,), in_specs=[spec(le...  10.3 us
    ppermute x2, waiting for transfers between devices, butterfly_sum(): x = x + lax.ppermute(x, axis, pairs)  9.08 us
    ppermute x2, starting transfers between devices, fetch(): return lax.ppermute(piece, 'track', pairs)  6.29 us
    ppermute x3, starting transfers between devices, ring_sum(): total = total + lax.ppermute(x, axis, pairs)  6.09 us
  transfers between devices with their start and end apart: 14, of which 6 were waited for; matrix products, arithmetic and copies ran while one was open for 19% of the time, Pallas kernels for 0%

profile of v21, /device:TPU:0, one launch (start us, length us, event | category | flops | bytes accessed | tf_op | source)
XLA Modules:
  0.0 143.3 jit_solution(16331370677940856840)
XLA Ops:
  0.0 0.0 copy-start
  0.0 4.2 %fusion.46 = (bf16[15,224,256]{2,1,0:T(8,128)(2,1)}, bf16[15,224,256]{2,1,0:T(8,128)(2,1)}) fusion(bf16[32,224,256]{2,1,0:T(8,128)(2,1)} %bitcast.59), kind=kLoop, calls=%fused_computation.56 | loop fusion | bytes 6881280 | tf_op jit(solution)/shard_map/slice | solution.py:184
  4.2 2.5 %collective-permute-start.2 = (bf16[15,224,256]{2,1,0:T(8,128)(2,1)}, bf16[15,224,256]{2,1,0:T(8,128)(2,1)S(1)}, u32[]{:S(2)}, u32[]{:S(2)}) collective-permute-start(bf16[15,224,256]{2,1,0:T(8,128)(2,1)} %get-tuple-element.11), channel_id=1, source_target_pairs={{0,1},{1,2},{2,3},{3,4},{4,5},{5,6},{6,7},{8,9},{9,10},{10,11},{11... | collective-permute-start | bytes 5160968 | tf_op jit(solution)/shard_map/ppermute | solution.py:177
  6.6 1.3 collective-permute-start.6
  7.9 0.0 copy-done
  7.9 2.1 %fusion.45 = (bf16[32,224,15]{2,1,0:T(8,128)(2,1)S(1)}, bf16[32,224,15]{2,1,0:T(8,128)(2,1)}) fusion(bf16[32,224,256]{2,1,0:T(8,128)(2,1)S(1)} %bitcast.61), kind=kLoop, calls=%fused_computation.55 | loop fusion | bytes 860160 | tf_op jit(solution)/shard_map/slice | solution.py:190
  10.0 2.7 %copy.14 = bf16[32,224,15]{1,0,2:T(8,128)(2,1)} copy(bf16[32,224,15]{2,1,0:T(8,128)(2,1)} %get-tuple-element.16) | data formatting | bytes 430080 | tf_op jit(solution)/shard_map/slice | solution.py:189
  12.7 5.0 %collective-permute-start = (bf16[32,224,15]{1,0,2:T(8,128)(2,1)}, bf16[32,224,15]{1,0,2:T(8,128)(2,1)}, u32[]{:S(2)}, u32[]{:S(2)}) collective-permute-start(bf16[32,224,15]{1,0,2:T(8,128)(2,1)} %copy.14), channel_id=1, source_target_pairs={{0,8},{8,16},{16,24},{1,9},{9,17},{17,25},{2,10},{10,18},{18,26},{... | collective-permute-start | bytes 645128 | tf_op jit(solution)/shard_map/ppermute | solution.py:180
  17.8 1.7 %copy.16 = bf16[32,224,15]{1,0,2:T(8,128)(2,1)} copy(bf16[32,224,15]{2,1,0:T(8,128)(2,1)S(1)} %get-tuple-element.15) | data formatting | bytes 430080 | tf_op jit(solution)/shard_map/slice | solution.py:190
  19.4 1.3 collective-permute-start.3
  20.7 6.1 %fusion.11 = f32[256,32,224]{0,2,1:T(8,128)} fusion(bf16[256,32,224]{0,2,1:T(8,128)(2,1)} %param.1), kind=kOutput, calls=%fused_computation.14 | convolution fusion | flops 939720704 | bytes 11010048 | tf_op jit(solution)/shard_map/qbk,kl->qbl/dot_general | solution.py:216
  26.9 0.7 broadcast_multiply_fusion.count_ref
  27.6 0.0 collective-permute-done
  27.6 1.0 fusion.48
  28.7 3.9 %collective-permute-start.1 = (bf16[15,224,15]{1,2,0:T(8,128)(2,1)S(1)}, bf16[15,224,15]{1,2,0:T(8,128)(2,1)S(1)}, u32[]{:S(2)}, u32[]{:S(2)}) collective-permute-start(bf16[15,224,15]{1,2,0:T(8,128)(2,1)S(1)} %copy.15), channel_id=1, source_target_pairs={{0,1},{1,2},{2,3},{3,4},{4,5},{5,6},{6,7},{8,9},{9,10},{10,11},{11... | collective-permute-start | bytes 302408 | tf_op jit(solution)/shard_map/ppermute | solution.py:177
  32.6 1.3 collective-permute-start.5
  33.9 0.0 collective-permute-done.3
  34.0 0.0 copy-start.1
  34.0 4.8 %collective-permute-start.4 = (bf16[15,224,15]{1,2,0:T(8,128)(2,1)S(1)}, bf16[15,224,15]{1,2,0:T(8,128)(2,1)S(1)}, u32[]{:S(2)}, u32[]{:S(2)}) collective-permute-start(bf16[15,224,15]{1,2,0:T(8,128)(2,1)S(1)} %copy.17), channel_id=1, source_target_pairs={{0,1},{1,2},{2,3},{3,4},{4,5},{5,6},{6,7},{8,9},{9,10},{10,11},{11... | collective-permute-start | bytes 302408 | tf_op jit(solution)/shard_map/ppermute | solution.py:177
  38.8 1.9 %fusion.6 = f32[32,224,256]{2,1,0:T(8,128)S(1)} fusion(bf16[32,224,15]{1,0,2:T(8,128)(2,1)} %collective-permute-done), kind=kOutput, calls=%fused_computation.9 | convolution fusion | flops 55054080 | bytes 7555072 | tf_op jit(solution)/shard_map/qbk,kl->qbl/dot_general | solution.py:216
  40.7 0.0 copy-done.1
  40.7 4.1 %fusion.1.middle_ref = f32[32,224,256]{2,1,0:T(8,128)} fusion(f32[32,224,256]{2,1,0:T(8,128)S(1)} %fusion.6, f32[256,32,224]{0,2,1:T(8,128)S(1)} %copy-done.1, bf16[32,224,15]{1,0,2:T(8,128)(2,1)S(1)} %collective-permute-done.3, s32[15]{0:T(128)S(1)} %iota_add_fusion), kind=kOutput, calls=%fused_computation.3 | convolution fusion | flops 58724096 | bytes 22235196 | tf_op jit(solution)/shard_map/qbk,kl->qbl/dot_general | solution.py:216
  44.9 0.0 collective-permute-done.5
  44.9 1.3 collective-permute-start.7
  46.2 0.5 fusion.22
  46.7 0.0 collective-permute-done.1
  46.7 0.5 fusion.25
  47.2 0.0 collective-permute-done.6
  47.2 2.1 %fusion.9 = f32[15,224,256]{2,1,0:T(8,128)S(1)} fusion(bf16[15,224,256]{2,1,0:T(8,128)(2,1)} %collective-permute-done.6), kind=kOutput, calls=%fused_computation.13 | convolution fusion | flops 440598528 | bytes 5160960 | tf_op jit(solution)/shard_map/qbk,kl->qbl/dot_general | solution.py:216
  49.3 5.7 %collective-permute-done.7 = bf16[15,224,15]{1,2,0:T(8,128)(2,1)S(1)} collective-permute-done((bf16[15,224,15]{1,2,0:T(8,128)(2,1)S(1)}, bf16[15,224,15]{1,2,0:T(8,128)(2,1)S(1)}, u32[]{:S(2)}, u32[]{:S(2)}) %collective-permute-start.7) | collective-permute-done | bytes 100832 | tf_op jit(solution)/shard_map/ppermute | solution.py:177
  55.0 2.4 %add_add_fusion.right_ref = f32[15,224,256]{2,1,0:T(8,128)} fusion(f32[15,224,256]{2,1,0:T(8,128)S(1)} %fusion.22, f32[15,224,256]{2,1,0:T(8,128)S(1)} %fusion.9, bf16[15,224,15]{1,2,0:T(8,128)(2,1)S(1)} %collective-permute-done.7, s32[15]{0:T(128)S(1)} %iota_add_fusion), kind=kOutput, calls=%fused_computation.4 | convolution fusion | flops 27528960 | bytes 10422780 | tf_op jit(solution)/shard_map/qbk,kl->qbl/dot_general | solution.py:216
  57.4 0.0 collective-permute-done.2
  57.4 0.6 fusion.13
  58.1 0.0 collective-permute-done.4
  58.1 2.4 %add_add_fusion.1.left_ref = f32[15,224,256]{2,1,0:T(8,128)} fusion(f32[15,224,256]{2,1,0:T(8,128)S(1)} %fusion.25, f32[15,224,256]{2,1,0:T(8,128)S(1)} %fusion.13, bf16[15,224,15]{1,2,0:T(8,128)(2,1)S(1)} %collective-permute-done.4, s32[15]{0:T(128)S(1)} %iota_add_fusion), kind=kOutput, calls=%fused_computation.5 | convolution fusion | flops 27528960 | bytes 10422780 | tf_op jit(solution)/shard_map/qbk,kl->qbl/dot_general | solution.py:216
  60.5 10.3 %shard_map.17 = (f32[32,224,256]{2,1,0:T(8,128)}, bf16[32,224,256]{2,1,0:T(8,128)(2,1)}) custom-call(f32[15,224,256]{2,1,0:T(8,128)} %add_add_fusion.1.left_ref, f32[32,224,256]{2,1,0:T(8,128)} %fusion.1.middle_ref, f32[15,224,256]{2,1,0:T(8,128)} %add_add_fusion.right_ref, bf16[32,224,256]{2,1,0:T(8,128)(2,1)} %bitcast.60, ...), custom_call_target="tpu_custom_call" | custom-call | tf_op jit(solution)/shard_map/pallas_call | solution.py:250
  70.8 4.3 %convolution_bitcast_fusion = f32[224,224]{1,0:T(8,128)S(1)} fusion(bf16[32,224,256]{2,1,0:T(8,128)(2,1)} %get-tuple-element.14), kind=kOutput, calls=%fused_computation.6 | convolution fusion | flops 822083584 | bytes 3870720 | tf_op jit(solution)/shard_map/pjl,pkl->jk/dot_general | solution.py:279
  75.1 0.1 fusion.49
  75.2 1.6 %collective-permute-start.8 = (f32[225,112]{1,0:T(8,128)S(1)}, f32[225,112]{1,0:T(8,128)S(1)}, u32[]{:S(2)}, u32[]{:S(2)}) collective-permute-start(f32[225,112]{1,0:T(8,128)S(1)} %pad_maximum_fusion), channel_id=1, source_target_pairs={{0,8},{8,0},{16,24},{24,16},{1,9},{9,1},{17,25},{25,17},{2,10},{10... | collective-permute-start | bytes 302408 | tf_op jit(solution)/shard_map/ppermute | solution.py:41
  76.8 3.3 %collective-permute-done.8 = f32[225,112]{1,0:T(8,128)S(1)} collective-permute-done((f32[225,112]{1,0:T(8,128)S(1)}, f32[225,112]{1,0:T(8,128)S(1)}, u32[]{:S(2)}, u32[]{:S(2)}) %collective-permute-start.8) | collective-permute-done | bytes 100832 | tf_op jit(solution)/shard_map/ppermute | solution.py:41
  80.1 2.7 %collective-permute-start.9 = (f32[225,112]{1,0:T(8,128)S(1)}, f32[225,112]{1,0:T(8,128)S(1)}, u32[]{:S(2)}, u32[]{:S(2)}) collective-permute-start(f32[225,112]{1,0:T(8,128)S(1)} %fusion.44), channel_id=1, source_target_pairs={{0,16},{8,24},{16,0},{24,8},{1,17},{9,25},{17,1},{25,9},{2,18},{10... | collective-permute-start | bytes 302408 | tf_op jit(solution)/shard_map/ppermute | solution.py:41
  82.8 5.8 %collective-permute-done.9 = f32[225,112]{1,0:T(8,128)S(1)} collective-permute-done((f32[225,112]{1,0:T(8,128)S(1)}, f32[225,112]{1,0:T(8,128)S(1)}, u32[]{:S(2)}, u32[]{:S(2)}) %collective-permute-start.9) | collective-permute-done | bytes 100832 | tf_op jit(solution)/shard_map/ppermute | solution.py:41
  88.6 1.0 collective-permute-start.10
  89.6 1.0 collective-permute-done.10
  90.6 0.1 collective-permute-start.13
  90.7 6.0 %collective-permute-start.12 = (f32[225,112]{1,0:T(8,128)S(1)}, f32[225,112]{1,0:T(8,128)S(1)}, u32[]{:S(2)}, u32[]{:S(2)}) collective-permute-start(f32[225,112]{1,0:T(8,128)S(1)} %add.131), channel_id=1, source_target_pairs={{0,4},{1,5},{2,6},{3,7},{4,0},{5,1},{6,2},{7,3},{8,12},{9,13},{10,... | collective-permute-start | bytes 302408 | tf_op jit(solution)/shard_map/ppermute | solution.py:54
  96.7 0.0 collective-permute-start.11
  96.7 2.2 %collective-permute-done.13 = f32[225,112]{1,0:T(8,128)S(1)} collective-permute-done((f32[225,112]{1,0:T(8,128)S(1)}, f32[225,112]{1,0:T(8,128)S(1)}, u32[]{:S(2)}, u32[]{:S(2)}) %collective-permute-start.13) | collective-permute-done | bytes 100832 | tf_op jit(solution)/shard_map/ppermute | solution.py:54
  98.9 3.6 %collective-permute-done.12 = f32[225,112]{1,0:T(8,128)S(1)} collective-permute-done((f32[225,112]{1,0:T(8,128)S(1)}, f32[225,112]{1,0:T(8,128)S(1)}, u32[]{:S(2)}, u32[]{:S(2)}) %collective-permute-start.12) | collective-permute-done | bytes 100832 | tf_op jit(solution)/shard_map/ppermute | solution.py:54
  102.5 0.0 collective-permute-done.11
  102.6 0.1 copy.25
  102.7 0.1 copy.26
  102.8 0.8 maximum_multiply_fusion.a_ref
  103.6 28.6 %shard_map.18 = f32[256,256]{1,0:T(8,128)} custom-call(f32[224,224]{1,0:T(8,128)} %maximum_multiply_fusion.a_ref), custom_call_target="tpu_custom_call" | custom-call | tf_op jit(solution)/shard_map/pallas_call | solution.py:132
  132.2 10.4 %fusion = f32[32,256]{1,0:T(8,128)S(1)} fusion(f32[32,224,256]{2,1,0:T(8,128)} %get-tuple-element.13, f32[256,256]{1,0:T(8,128)} %shard_map.18), kind=kOutput, calls=%fused_computation.1 | convolution fusion | flops 4936213504 | bytes 14942208 | tf_op jit(solution)/shard_map/jb,pbl->pjl/dot_general | solution.py:287
  142.6 0.6 multiply_bitcast_fusion
  (16 shorter events, 0.4 us)
Async XLA Ops:
  0.0 7.9 %copy-start = (bf16[256,32,224]{0,2,1:T(8,128)(2,1)S(1)}, bf16[256,32,224]{0,2,1:T(8,128)(2,1)}, u32[]{:S(2)}) copy-start(bf16[256,32,224]{0,2,1:T(8,128)(2,1)} %param.1) | copy-start | bytes 11010052
  4.2 53.3 %collective-permute-start.2 = (bf16[15,224,256]{2,1,0:T(8,128)(2,1)}, bf16[15,224,256]{2,1,0:T(8,128)(2,1)S(1)}, u32[]{:S(2)}, u32[]{:S(2)}) collective-permute-start(bf16[15,224,256]{2,1,0:T(8,128)(2,1)} %get-tuple-element.11), channel_id=1, source_target_pairs={{0,1},{1,2},{2,3},{3,4},{4,5},{5,6},{6,7},{8,9},{9,10},{10,11},{11... | collective-permute-start | bytes 5160968 | tf_op jit(solution)/shard_map/ppermute | solution.py:177
  6.6 40.6 %collective-permute-start.6 = (bf16[15,224,256]{2,1,0:T(8,128)(2,1)}, bf16[15,224,256]{2,1,0:T(8,128)(2,1)}, u32[]{:S(2)}, u32[]{:S(2)}) collective-permute-start(bf16[15,224,256]{2,1,0:T(8,128)(2,1)} %get-tuple-element.12), channel_id=1, source_target_pairs={{1,0},{2,1},{3,2},{4,3},{5,4},{6,5},{7,6},{9,8},{10,9},{11,10},{12... | collective-permute-start | bytes 5160968 | tf_op jit(solution)/shard_map/ppermute | solution.py:177
  12.7 14.8 %collective-permute-start = (bf16[32,224,15]{1,0,2:T(8,128)(2,1)}, bf16[32,224,15]{1,0,2:T(8,128)(2,1)}, u32[]{:S(2)}, u32[]{:S(2)}) collective-permute-start(bf16[32,224,15]{1,0,2:T(8,128)(2,1)} %copy.14), channel_id=1, source_target_pairs={{0,8},{8,16},{16,24},{1,9},{9,17},{17,25},{2,10},{10,18},{18,26},{... | collective-permute-start | bytes 645128 | tf_op jit(solution)/shard_map/ppermute | solution.py:180
  19.4 14.5 %collective-permute-start.3 = (bf16[32,224,15]{1,0,2:T(8,128)(2,1)}, bf16[32,224,15]{1,0,2:T(8,128)(2,1)S(1)}, u32[]{:S(2)}, u32[]{:S(2)}) collective-permute-start(bf16[32,224,15]{1,0,2:T(8,128)(2,1)} %copy.16), channel_id=1, source_target_pairs={{8,0},{16,8},{24,16},{9,1},{17,9},{25,17},{10,2},{18,10},{26,18},{... | collective-permute-start | bytes 645128 | tf_op jit(solution)/shard_map/ppermute | solution.py:180
  28.7 18.0 %collective-permute-start.1 = (bf16[15,224,15]{1,2,0:T(8,128)(2,1)S(1)}, bf16[15,224,15]{1,2,0:T(8,128)(2,1)S(1)}, u32[]{:S(2)}, u32[]{:S(2)}) collective-permute-start(bf16[15,224,15]{1,2,0:T(8,128)(2,1)S(1)} %copy.15), channel_id=1, source_target_pairs={{0,1},{1,2},{2,3},{3,4},{4,5},{5,6},{6,7},{8,9},{9,10},{10,11},{11... | collective-permute-start | bytes 302408 | tf_op jit(solution)/shard_map/ppermute | solution.py:177
  32.6 12.3 %collective-permute-start.5 = (bf16[15,224,15]{1,2,0:T(8,128)(2,1)S(1)}, bf16[15,224,15]{1,2,0:T(8,128)(2,1)S(1)}, u32[]{:S(2)}, u32[]{:S(2)}) collective-permute-start(bf16[15,224,15]{1,2,0:T(8,128)(2,1)S(1)} %copy.20), channel_id=1, source_target_pairs={{1,0},{2,1},{3,2},{4,3},{5,4},{6,5},{7,6},{9,8},{10,9},{11,10},{12... | collective-permute-start | bytes 302408 | tf_op jit(solution)/shard_map/ppermute | solution.py:177
  34.0 6.7 %copy-start.1 = (f32[256,32,224]{0,2,1:T(8,128)S(1)}, f32[256,32,224]{0,2,1:T(8,128)}, u32[]{:S(2)}) copy-start(f32[256,32,224]{0,2,1:T(8,128)} %fusion.11) | copy-start | bytes 22020100
  34.0 24.0 %collective-permute-start.4 = (bf16[15,224,15]{1,2,0:T(8,128)(2,1)S(1)}, bf16[15,224,15]{1,2,0:T(8,128)(2,1)S(1)}, u32[]{:S(2)}, u32[]{:S(2)}) collective-permute-start(bf16[15,224,15]{1,2,0:T(8,128)(2,1)S(1)} %copy.17), channel_id=1, source_target_pairs={{0,1},{1,2},{2,3},{3,4},{4,5},{5,6},{6,7},{8,9},{9,10},{10,11},{11... | collective-permute-start | bytes 302408 | tf_op jit(solution)/shard_map/ppermute | solution.py:177
  44.9 10.1 %collective-permute-start.7 = (bf16[15,224,15]{1,2,0:T(8,128)(2,1)S(1)}, bf16[15,224,15]{1,2,0:T(8,128)(2,1)S(1)}, u32[]{:S(2)}, u32[]{:S(2)}) collective-permute-start(bf16[15,224,15]{1,2,0:T(8,128)(2,1)S(1)} %copy.21), channel_id=1, source_target_pairs={{1,0},{2,1},{3,2},{4,3},{5,4},{6,5},{7,6},{9,8},{10,9},{11,10},{12... | collective-permute-start | bytes 302408 | tf_op jit(solution)/shard_map/ppermute | solution.py:177
  75.2 4.9 %collective-permute-start.8 = (f32[225,112]{1,0:T(8,128)S(1)}, f32[225,112]{1,0:T(8,128)S(1)}, u32[]{:S(2)}, u32[]{:S(2)}) collective-permute-start(f32[225,112]{1,0:T(8,128)S(1)} %pad_maximum_fusion), channel_id=1, source_target_pairs={{0,8},{8,0},{16,24},{24,16},{1,9},{9,1},{17,25},{25,17},{2,10},{10... | collective-permute-start | bytes 302408 | tf_op jit(solution)/shard_map/ppermute | solution.py:41
  80.1 8.5 %collective-permute-start.9 = (f32[225,112]{1,0:T(8,128)S(1)}, f32[225,112]{1,0:T(8,128)S(1)}, u32[]{:S(2)}, u32[]{:S(2)}) collective-permute-start(f32[225,112]{1,0:T(8,128)S(1)} %fusion.44), channel_id=1, source_target_pairs={{0,16},{8,24},{16,0},{24,8},{1,17},{9,25},{17,1},{25,9},{2,18},{10... | collective-permute-start | bytes 302408 | tf_op jit(solution)/shard_map/ppermute | solution.py:41
  88.6 2.0 %collective-permute-start.10 = (f32[225,112]{1,0:T(8,128)S(1)}, f32[225,112]{1,0:T(8,128)S(1)}, u32[]{:S(2)}, u32[]{:S(2)}) collective-permute-start(f32[225,112]{1,0:T(8,128)S(1)} %add.130), channel_id=1, source_target_pairs={{0,1},{1,0},{2,3},{3,2},{4,5},{5,4},{6,7},{7,6},{8,9},{9,8},{10,11... | collective-permute-start | bytes 302408 | tf_op jit(solution)/shard_map/ppermute | solution.py:283
  90.6 8.3 %collective-permute-start.13 = (f32[225,112]{1,0:T(8,128)S(1)}, f32[225,112]{1,0:T(8,128)S(1)}, u32[]{:S(2)}, u32[]{:S(2)}) collective-permute-start(f32[225,112]{1,0:T(8,128)S(1)} %add.131), channel_id=1, source_target_pairs={{0,6},{1,7},{2,0},{3,1},{4,2},{5,3},{6,4},{7,5},{8,14},{9,15},{10,... | collective-permute-start | bytes 302408 | tf_op jit(solution)/shard_map/ppermute | solution.py:54
  90.7 11.8 %collective-permute-start.12 = (f32[225,112]{1,0:T(8,128)S(1)}, f32[225,112]{1,0:T(8,128)S(1)}, u32[]{:S(2)}, u32[]{:S(2)}) collective-permute-start(f32[225,112]{1,0:T(8,128)S(1)} %add.131), channel_id=1, source_target_pairs={{0,4},{1,5},{2,6},{3,7},{4,0},{5,1},{6,2},{7,3},{8,12},{9,13},{10,... | collective-permute-start | bytes 302408 | tf_op jit(solution)/shard_map/ppermute | solution.py:54
  96.7 5.8 %collective-permute-start.11 = (f32[225,112]{1,0:T(8,128)S(1)}, f32[225,112]{1,0:T(8,128)S(1)}, u32[]{:S(2)}, u32[]{:S(2)}) collective-permute-start(f32[225,112]{1,0:T(8,128)S(1)} %add.131), channel_id=1, source_target_pairs={{0,2},{1,3},{2,4},{3,5},{4,6},{5,7},{6,0},{7,1},{8,10},{9,11},{10,... | collective-permute-start | bytes 302408 | tf_op jit(solution)/shard_map/ppermute | solution.py:54

commit v22 on v18

--- a/solution.py
+++ b/solution.py
@@ -287,8 +287,8 @@
     solved = jnp.einsum(
         "jb,pbl->pjl", inverse.T, residual, precision=highest, preferred_element_type=jnp.float32
     )
-    scores = jnp.sum(residual * solved, axis=1) / bands
-    return scores.T
+    scores = jnp.einsum("pjl,pjl->lp", residual, solved, precision=lax.Precision.HIGHEST)
+    return scores / bands
 
 
 def solution(mesh):

time: 143 us -> 154 us (1.077)
  local copies, waits for them, and re-layouts: 12 us -> 20.5 us
  matrix products: 35.4 us -> 42.7 us
  waiting for transfers between devices: 20.4 us -> 15.8 us
    unnamed x4 -> x5, local copies, waits for them, and re-layouts: 0.01 us -> 8.65 us
    dot_general x1, matrix products: 10.4 us -> 17.6 us  [shards(): jnp.einsum('jb,pbl->pjl', inverse.T, residual, precision=highest, preferr...]
    ppermute x2, waiting for transfers between devices: 7.68 us -> 3.27 us  [butterfly_sum(): x = x + lax.ppermute(x, axis, pairs)]
  transfers between devices with their start and end apart: 14 -> 14, of which waited for: 6 -> 5; matrix products, arithmetic and copies ran while one was open for 19% -> 23% of each run, Pallas kernels for 0% -> 0%
where the time goes in v22:
time: 154 us
  matrix products  42.7 us (28%)
  Pallas kernels  38.9 us (25%)
  starting transfers between devices  33.1 us (21%)
  local copies, waits for them, and re-layouts  20.5 us (13%)
  waiting for transfers between devices  15.8 us (10%)
  other arithmetic  2.4 us (2%)
    pallas_call x1, Pallas kernels, spd_inverse(): pl.pallas_call(functools.partial(sweep_kernel, n, load), out_shape=jax.Sh...  28.6 us
    dot_general x9, matrix products, sum_lines(): jnp.einsum('qbk,kl->qbl', values, w, preferred_element_type=jnp.float32)  20.8 us
    dot_general x1, matrix products, shards(): jnp.einsum('jb,pbl->pjl', inverse.T, residual, precision=highest, preferr...  17.6 us
    ppermute x6, starting transfers between devices, fetch(): return lax.ppermute(piece, 'cross', pairs)  15.1 us
    pallas_call x1, Pallas kernels, residuals(): pl.pallas_call(residual_kernel, grid=(bands // block,), in_specs=[spec(le...  10.3 us
    unnamed x5, local copies, waits for them, and re-layouts  8.65 us
    ppermute x2, starting transfers between devices, fetch(): return lax.ppermute(piece, 'track', pairs)  6.3 us
    ppermute x3, waiting for transfers between devices, ring_sum(): total = total + lax.ppermute(x, axis, pairs)  6 us
  transfers between devices with their start and end apart: 14, of which 5 were waited for; matrix products, arithmetic and copies ran while one was open for 23% of the time, Pallas kernels for 0%

profile of v22, /device:TPU:0, one launch (start us, length us, event | category | flops | bytes accessed | tf_op | source)
XLA Modules:
  0.0 153.7 jit_solution(5813972573058804763)
XLA Ops:
  0.0 0.0 copy-start
  0.0 4.1 %fusion.46 = (bf16[15,224,256]{2,1,0:T(8,128)(2,1)}, bf16[15,224,256]{2,1,0:T(8,128)(2,1)}) fusion(bf16[32,224,256]{2,1,0:T(8,128)(2,1)} %bitcast.60), kind=kLoop, calls=%fused_computation.56 | loop fusion | bytes 6881280 | tf_op jit(solution)/shard_map/slice | solution.py:184
  4.1 2.5 %collective-permute-start.2 = (bf16[15,224,256]{2,1,0:T(8,128)(2,1)}, bf16[15,224,256]{2,1,0:T(8,128)(2,1)S(1)}, u32[]{:S(2)}, u32[]{:S(2)}) collective-permute-start(bf16[15,224,256]{2,1,0:T(8,128)(2,1)} %get-tuple-element.11), channel_id=1, source_target_pairs={{0,1},{1,2},{2,3},{3,4},{4,5},{5,6},{6,7},{8,9},{9,10},{10,11},{11... | collective-permute-start | bytes 5160968 | tf_op jit(solution)/shard_map/ppermute | solution.py:177
  6.6 1.3 collective-permute-start.6
  7.9 0.0 copy-done
  7.9 2.1 %fusion.45 = (bf16[32,224,15]{2,1,0:T(8,128)(2,1)S(1)}, bf16[32,224,15]{2,1,0:T(8,128)(2,1)}) fusion(bf16[32,224,256]{2,1,0:T(8,128)(2,1)S(1)} %bitcast.62), kind=kLoop, calls=%fused_computation.55 | loop fusion | bytes 860160 | tf_op jit(solution)/shard_map/slice | solution.py:190
  9.9 2.7 %copy.13 = bf16[32,224,15]{1,0,2:T(8,128)(2,1)} copy(bf16[32,224,15]{2,1,0:T(8,128)(2,1)} %get-tuple-element.16) | data formatting | bytes 430080 | tf_op jit(solution)/shard_map/slice | solution.py:189
  12.6 5.0 %collective-permute-start = (bf16[32,224,15]{1,0,2:T(8,128)(2,1)}, bf16[32,224,15]{1,0,2:T(8,128)(2,1)}, u32[]{:S(2)}, u32[]{:S(2)}) collective-permute-start(bf16[32,224,15]{1,0,2:T(8,128)(2,1)} %copy.13), channel_id=1, source_target_pairs={{0,8},{8,16},{16,24},{1,9},{9,17},{17,25},{2,10},{10,18},{18,26},{... | collective-permute-start | bytes 645128 | tf_op jit(solution)/shard_map/ppermute | solution.py:180
  17.7 1.7 %copy.15 = bf16[32,224,15]{1,0,2:T(8,128)(2,1)} copy(bf16[32,224,15]{2,1,0:T(8,128)(2,1)S(1)} %get-tuple-element.15) | data formatting | bytes 430080 | tf_op jit(solution)/shard_map/slice | solution.py:190
  19.3 1.3 collective-permute-start.3
  20.6 6.1 %fusion.11 = f32[256,32,224]{0,2,1:T(8,128)} fusion(bf16[256,32,224]{0,2,1:T(8,128)(2,1)} %param.1), kind=kOutput, calls=%fused_computation.14 | convolution fusion | flops 939720704 | bytes 11010048 | tf_op jit(solution)/shard_map/qbk,kl->qbl/dot_general | solution.py:216
  26.8 0.7 broadcast_multiply_fusion.1.count_ref
  27.5 0.0 collective-permute-done
  27.5 1.0 fusion.48
  28.6 3.9 %collective-permute-start.1 = (bf16[15,224,15]{1,2,0:T(8,128)(2,1)S(1)}, bf16[15,224,15]{1,2,0:T(8,128)(2,1)S(1)}, u32[]{:S(2)}, u32[]{:S(2)}) collective-permute-start(bf16[15,224,15]{1,2,0:T(8,128)(2,1)S(1)} %copy.14), channel_id=1, source_target_pairs={{0,1},{1,2},{2,3},{3,4},{4,5},{5,6},{6,7},{8,9},{9,10},{10,11},{11... | collective-permute-start | bytes 302408 | tf_op jit(solution)/shard_map/ppermute | solution.py:177
  32.5 1.3 collective-permute-start.5
  33.8 0.0 collective-permute-done.3
  33.9 0.0 copy-start.1
  33.9 4.8 %collective-permute-start.4 = (bf16[15,224,15]{1,2,0:T(8,128)(2,1)S(1)}, bf16[15,224,15]{1,2,0:T(8,128)(2,1)S(1)}, u32[]{:S(2)}, u32[]{:S(2)}) collective-permute-start(bf16[15,224,15]{1,2,0:T(8,128)(2,1)S(1)} %copy.16), channel_id=1, source_target_pairs={{0,1},{1,2},{2,3},{3,4},{4,5},{5,6},{6,7},{8,9},{9,10},{10,11},{11... | collective-permute-start | bytes 302408 | tf_op jit(solution)/shard_map/ppermute | solution.py:177
  38.8 1.9 %fusion.6 = f32[32,224,256]{2,1,0:T(8,128)S(1)} fusion(bf16[32,224,15]{1,0,2:T(8,128)(2,1)} %collective-permute-done), kind=kOutput, calls=%fused_computation.9 | convolution fusion | flops 55054080 | bytes 7555072 | tf_op jit(solution)/shard_map/qbk,kl->qbl/dot_general | solution.py:216
  40.6 0.0 copy-done.1
  40.7 4.3 %fusion.1.middle_ref = f32[32,224,256]{2,1,0:T(8,128)} fusion(f32[32,224,256]{2,1,0:T(8,128)S(1)} %fusion.6, f32[256,32,224]{0,2,1:T(8,128)S(1)} %copy-done.1, bf16[32,224,15]{1,0,2:T(8,128)(2,1)S(1)} %collective-permute-done.3, s32[15]{0:T(128)S(1)} %iota_add_fusion), kind=kOutput, calls=%fused_computation.3 | convolution fusion | flops 58724096 | bytes 22235196 | tf_op jit(solution)/shard_map/qbk,kl->qbl/dot_general | solution.py:216
  45.0 0.0 collective-permute-done.5
  45.0 1.3 collective-permute-start.7
  46.3 0.5 fusion.22
  46.8 0.0 collective-permute-done.1
  46.8 0.5 fusion.25
  47.3 0.0 collective-permute-done.6
  47.3 2.1 %fusion.9 = f32[15,224,256]{2,1,0:T(8,128)S(1)} fusion(bf16[15,224,256]{2,1,0:T(8,128)(2,1)} %collective-permute-done.6), kind=kOutput, calls=%fused_computation.13 | convolution fusion | flops 440598528 | bytes 5160960 | tf_op jit(solution)/shard_map/qbk,kl->qbl/dot_general | solution.py:216
  49.4 5.6 %collective-permute-done.7 = bf16[15,224,15]{1,2,0:T(8,128)(2,1)S(1)} collective-permute-done((bf16[15,224,15]{1,2,0:T(8,128)(2,1)S(1)}, bf16[15,224,15]{1,2,0:T(8,128)(2,1)S(1)}, u32[]{:S(2)}, u32[]{:S(2)}) %collective-permute-start.7) | collective-permute-done | bytes 100832 | tf_op jit(solution)/shard_map/ppermute | solution.py:177
  54.9 2.4 %add_add_fusion.right_ref = f32[15,224,256]{2,1,0:T(8,128)} fusion(f32[15,224,256]{2,1,0:T(8,128)S(1)} %fusion.22, f32[15,224,256]{2,1,0:T(8,128)S(1)} %fusion.9, bf16[15,224,15]{1,2,0:T(8,128)(2,1)S(1)} %collective-permute-done.7, s32[15]{0:T(128)S(1)} %iota_add_fusion), kind=kOutput, calls=%fused_computation.4 | convolution fusion | flops 27528960 | bytes 10422780 | tf_op jit(solution)/shard_map/qbk,kl->qbl/dot_general | solution.py:216
  57.3 0.0 collective-permute-done.2
  57.3 0.6 fusion.13
  58.0 0.0 collective-permute-done.4
  58.0 2.4 %add_add_fusion.1.left_ref = f32[15,224,256]{2,1,0:T(8,128)} fusion(f32[15,224,256]{2,1,0:T(8,128)S(1)} %fusion.25, f32[15,224,256]{2,1,0:T(8,128)S(1)} %fusion.13, bf16[15,224,15]{1,2,0:T(8,128)(2,1)S(1)} %collective-permute-done.4, s32[15]{0:T(128)S(1)} %iota_add_fusion), kind=kOutput, calls=%fused_computation.5 | convolution fusion | flops 27528960 | bytes 10422780 | tf_op jit(solution)/shard_map/qbk,kl->qbl/dot_general | solution.py:216
  60.4 10.3 %shard_map.17 = (f32[32,224,256]{2,1,0:T(8,128)}, bf16[32,224,256]{2,1,0:T(8,128)(2,1)}) custom-call(f32[15,224,256]{2,1,0:T(8,128)} %add_add_fusion.1.left_ref, f32[32,224,256]{2,1,0:T(8,128)} %fusion.1.middle_ref, f32[15,224,256]{2,1,0:T(8,128)} %add_add_fusion.right_ref, bf16[32,224,256]{2,1,0:T(8,128)(2,1)} %bitcast.61, ...), custom_call_target="tpu_custom_call" | custom-call | tf_op jit(solution)/shard_map/pallas_call | solution.py:250
  70.7 4.3 %convolution_bitcast_fusion = f32[224,224]{1,0:T(8,128)S(1)} fusion(bf16[32,224,256]{2,1,0:T(8,128)(2,1)} %get-tuple-element.14), kind=kOutput, calls=%fused_computation.6 | convolution fusion | flops 822083584 | bytes 3870720 | tf_op jit(solution)/shard_map/pjl,pkl->jk/dot_general | solution.py:279
  75.0 0.1 fusion.49
  75.1 3.5 %collective-permute-start.8 = (f32[225,112]{1,0:T(8,128)S(1)}, f32[225,112]{1,0:T(8,128)S(1)}, u32[]{:S(2)}, u32[]{:S(2)}) collective-permute-start(f32[225,112]{1,0:T(8,128)S(1)} %pad_maximum_fusion), channel_id=1, source_target_pairs={{0,1},{1,0},{2,3},{3,2},{4,5},{5,4},{6,7},{7,6},{8,9},{9,8},{10,11... | collective-permute-start | bytes 302408 | tf_op jit(solution)/shard_map/ppermute | solution.py:283
  78.7 1.0 collective-permute-done.8
  79.6 0.1 collective-permute-start.11
  79.7 3.9 %collective-permute-start.10 = (f32[225,112]{1,0:T(8,128)S(1)}, f32[225,112]{1,0:T(8,128)S(1)}, u32[]{:S(2)}, u32[]{:S(2)}) collective-permute-start(f32[225,112]{1,0:T(8,128)S(1)} %fusion.44), channel_id=1, source_target_pairs={{0,4},{1,5},{2,6},{3,7},{4,0},{5,1},{6,2},{7,3},{8,12},{9,13},{10,... | collective-permute-start | bytes 302408 | tf_op jit(solution)/shard_map/ppermute | solution.py:54
  83.6 0.0 collective-permute-start.9
  83.6 2.4 %collective-permute-done.11 = f32[225,112]{1,0:T(8,128)S(1)} collective-permute-done((f32[225,112]{1,0:T(8,128)S(1)}, f32[225,112]{1,0:T(8,128)S(1)}, u32[]{:S(2)}, u32[]{:S(2)}) %collective-permute-start.11) | collective-permute-done | bytes 100832 | tf_op jit(solution)/shard_map/ppermute | solution.py:54
  86.0 3.6 %collective-permute-done.10 = f32[225,112]{1,0:T(8,128)S(1)} collective-permute-done((f32[225,112]{1,0:T(8,128)S(1)}, f32[225,112]{1,0:T(8,128)S(1)}, u32[]{:S(2)}, u32[]{:S(2)}) %collective-permute-start.10) | collective-permute-done | bytes 100832 | tf_op jit(solution)/shard_map/ppermute | solution.py:54
  89.6 0.0 collective-permute-done.9
  89.6 1.6 %collective-permute-start.12 = (f32[225,112]{1,0:T(8,128)S(1)}, f32[225,112]{1,0:T(8,128)S(1)}, u32[]{:S(2)}, u32[]{:S(2)}) collective-permute-start(f32[225,112]{1,0:T(8,128)S(1)} %add_add_fusion.2), channel_id=1, source_target_pairs={{0,8},{8,0},{16,24},{24,16},{1,9},{9,1},{17,25},{25,17},{2,10},{10... | collective-permute-start | bytes 302408 | tf_op jit(solution)/shard_map/ppermute | solution.py:41
  91.3 3.3 %collective-permute-done.12 = f32[225,112]{1,0:T(8,128)S(1)} collective-permute-done((f32[225,112]{1,0:T(8,128)S(1)}, f32[225,112]{1,0:T(8,128)S(1)}, u32[]{:S(2)}, u32[]{:S(2)}) %collective-permute-start.12) | collective-permute-done | bytes 100832 | tf_op jit(solution)/shard_map/ppermute | solution.py:41
  94.5 2.6 %collective-permute-start.13 = (f32[225,112]{1,0:T(8,128)S(1)}, f32[225,112]{1,0:T(8,128)S(1)}, u32[]{:S(2)}, u32[]{:S(2)}) collective-permute-start(f32[225,112]{1,0:T(8,128)S(1)} %add.133), channel_id=1, source_target_pairs={{0,16},{8,24},{16,0},{24,8},{1,17},{9,25},{17,1},{25,9},{2,18},{10... | collective-permute-start | bytes 302408 | tf_op jit(solution)/shard_map/ppermute | solution.py:41
  97.2 8.6 %copy.32 = f32[256,32,224]{2,0,1:T(8,128)} copy(f32[256,32,224]{0,2,1:T(8,128)} %bitcast.63) | data formatting | bytes 14680064
  105.8 0.0 collective-permute-done.13
  105.9 0.1 copy.24
  106.0 0.1 copy.25
  106.1 0.8 maximum_multiply_fusion.a_ref
  106.9 28.6 %shard_map.18 = f32[256,256]{1,0:T(8,128)} custom-call(f32[224,224]{1,0:T(8,128)} %maximum_multiply_fusion.a_ref), custom_call_target="tpu_custom_call" | custom-call | tf_op jit(solution)/shard_map/pallas_call | solution.py:132
  135.5 17.6 %fusion = f32[256,32]{0,1:T(8,128)S(1)} fusion(f32[256,32,224]{2,0,1:T(8,128)} %copy.32, f32[32,224,256]{2,1,0:T(8,128)} %get-tuple-element.13, f32[256,256]{1,0:T(8,128)} %shard_map.18), kind=kOutput, calls=%fused_computation.1 | convolution fusion | flops 4936213504 | bytes 15990784 | tf_op jit(solution)/shard_map/jb,pbl->pjl/dot_general | solution.py:287
  153.1 0.6 broadcast_multiply_fusion
  (16 shorter events, 0.4 us)
Async XLA Ops:
  0.0 7.9 %copy-start = (bf16[256,32,224]{0,2,1:T(8,128)(2,1)S(1)}, bf16[256,32,224]{0,2,1:T(8,128)(2,1)}, u32[]{:S(2)}) copy-start(bf16[256,32,224]{0,2,1:T(8,128)(2,1)} %param.1) | copy-start | bytes 11010052
  4.1 53.2 %collective-permute-start.2 = (bf16[15,224,256]{2,1,0:T(8,128)(2,1)}, bf16[15,224,256]{2,1,0:T(8,128)(2,1)S(1)}, u32[]{:S(2)}, u32[]{:S(2)}) collective-permute-start(bf16[15,224,256]{2,1,0:T(8,128)(2,1)} %get-tuple-element.11), channel_id=1, source_target_pairs={{0,1},{1,2},{2,3},{3,4},{4,5},{5,6},{6,7},{8,9},{9,10},{10,11},{11... | collective-permute-start | bytes 5160968 | tf_op jit(solution)/shard_map/ppermute | solution.py:177
  6.6 40.7 %collective-permute-start.6 = (bf16[15,224,256]{2,1,0:T(8,128)(2,1)}, bf16[15,224,256]{2,1,0:T(8,128)(2,1)}, u32[]{:S(2)}, u32[]{:S(2)}) collective-permute-start(bf16[15,224,256]{2,1,0:T(8,128)(2,1)} %get-tuple-element.12), channel_id=1, source_target_pairs={{1,0},{2,1},{3,2},{4,3},{5,4},{6,5},{7,6},{9,8},{10,9},{11,10},{12... | collective-permute-start | bytes 5160968 | tf_op jit(solution)/shard_map/ppermute | solution.py:177
  12.6 14.9 %collective-permute-start = (bf16[32,224,15]{1,0,2:T(8,128)(2,1)}, bf16[32,224,15]{1,0,2:T(8,128)(2,1)}, u32[]{:S(2)}, u32[]{:S(2)}) collective-permute-start(bf16[32,224,15]{1,0,2:T(8,128)(2,1)} %copy.13), channel_id=1, source_target_pairs={{0,8},{8,16},{16,24},{1,9},{9,17},{17,25},{2,10},{10,18},{18,26},{... | collective-permute-start | bytes 645128 | tf_op jit(solution)/shard_map/ppermute | solution.py:180
  19.3 14.5 %collective-permute-start.3 = (bf16[32,224,15]{1,0,2:T(8,128)(2,1)}, bf16[32,224,15]{1,0,2:T(8,128)(2,1)S(1)}, u32[]{:S(2)}, u32[]{:S(2)}) collective-permute-start(bf16[32,224,15]{1,0,2:T(8,128)(2,1)} %copy.15), channel_id=1, source_target_pairs={{8,0},{16,8},{24,16},{9,1},{17,9},{25,17},{10,2},{18,10},{26,18},{... | collective-permute-start | bytes 645128 | tf_op jit(solution)/shard_map/ppermute | solution.py:180
  28.6 18.2 %collective-permute-start.1 = (bf16[15,224,15]{1,2,0:T(8,128)(2,1)S(1)}, bf16[15,224,15]{1,2,0:T(8,128)(2,1)S(1)}, u32[]{:S(2)}, u32[]{:S(2)}) collective-permute-start(bf16[15,224,15]{1,2,0:T(8,128)(2,1)S(1)} %copy.14), channel_id=1, source_target_pairs={{0,1},{1,2},{2,3},{3,4},{4,5},{5,6},{6,7},{8,9},{9,10},{10,11},{11... | collective-permute-start | bytes 302408 | tf_op jit(solution)/shard_map/ppermute | solution.py:177
  32.5 12.4 %collective-permute-start.5 = (bf16[15,224,15]{1,2,0:T(8,128)(2,1)S(1)}, bf16[15,224,15]{1,2,0:T(8,128)(2,1)S(1)}, u32[]{:S(2)}, u32[]{:S(2)}) collective-permute-start(bf16[15,224,15]{1,2,0:T(8,128)(2,1)S(1)} %copy.19), channel_id=1, source_target_pairs={{1,0},{2,1},{3,2},{4,3},{5,4},{6,5},{7,6},{9,8},{10,9},{11,10},{12... | collective-permute-start | bytes 302408 | tf_op jit(solution)/shard_map/ppermute | solution.py:177
  33.9 6.7 %copy-start.1 = (f32[256,32,224]{0,2,1:T(8,128)S(1)}, f32[256,32,224]{0,2,1:T(8,128)}, u32[]{:S(2)}) copy-start(f32[256,32,224]{0,2,1:T(8,128)} %fusion.11) | copy-start | bytes 22020100
  33.9 24.0 %collective-permute-start.4 = (bf16[15,224,15]{1,2,0:T(8,128)(2,1)S(1)}, bf16[15,224,15]{1,2,0:T(8,128)(2,1)S(1)}, u32[]{:S(2)}, u32[]{:S(2)}) collective-permute-start(bf16[15,224,15]{1,2,0:T(8,128)(2,1)S(1)} %copy.16), channel_id=1, source_target_pairs={{0,1},{1,2},{2,3},{3,4},{4,5},{5,6},{6,7},{8,9},{9,10},{10,11},{11... | collective-permute-start | bytes 302408 | tf_op jit(solution)/shard_map/ppermute | solution.py:177
  45.0 9.9 %collective-permute-start.7 = (bf16[15,224,15]{1,2,0:T(8,128)(2,1)S(1)}, bf16[15,224,15]{1,2,0:T(8,128)(2,1)S(1)}, u32[]{:S(2)}, u32[]{:S(2)}) collective-permute-start(bf16[15,224,15]{1,2,0:T(8,128)(2,1)S(1)} %copy.20), channel_id=1, source_target_pairs={{1,0},{2,1},{3,2},{4,3},{5,4},{6,5},{7,6},{9,8},{10,9},{11,10},{12... | collective-permute-start | bytes 302408 | tf_op jit(solution)/shard_map/ppermute | solution.py:177
  75.1 4.5 %collective-permute-start.8 = (f32[225,112]{1,0:T(8,128)S(1)}, f32[225,112]{1,0:T(8,128)S(1)}, u32[]{:S(2)}, u32[]{:S(2)}) collective-permute-start(f32[225,112]{1,0:T(8,128)S(1)} %pad_maximum_fusion), channel_id=1, source_target_pairs={{0,1},{1,0},{2,3},{3,2},{4,5},{5,4},{6,7},{7,6},{8,9},{9,8},{10,11... | collective-permute-start | bytes 302408 | tf_op jit(solution)/shard_map/ppermute | solution.py:283
  79.6 6.3 %collective-permute-start.11 = (f32[225,112]{1,0:T(8,128)S(1)}, f32[225,112]{1,0:T(8,128)S(1)}, u32[]{:S(2)}, u32[]{:S(2)}) collective-permute-start(f32[225,112]{1,0:T(8,128)S(1)} %fusion.44), channel_id=1, source_target_pairs={{0,6},{1,7},{2,0},{3,1},{4,2},{5,3},{6,4},{7,5},{8,14},{9,15},{10,... | collective-permute-start | bytes 302408 | tf_op jit(solution)/shard_map/ppermute | solution.py:54
  79.7 9.9 %collective-permute-start.10 = (f32[225,112]{1,0:T(8,128)S(1)}, f32[225,112]{1,0:T(8,128)S(1)}, u32[]{:S(2)}, u32[]{:S(2)}) collective-permute-start(f32[225,112]{1,0:T(8,128)S(1)} %fusion.44), channel_id=1, source_target_pairs={{0,4},{1,5},{2,6},{3,7},{4,0},{5,1},{6,2},{7,3},{8,12},{9,13},{10,... | collective-permute-start | bytes 302408 | tf_op jit(solution)/shard_map/ppermute | solution.py:54
  83.6 6.0 %collective-permute-start.9 = (f32[225,112]{1,0:T(8,128)S(1)}, f32[225,112]{1,0:T(8,128)S(1)}, u32[]{:S(2)}, u32[]{:S(2)}) collective-permute-start(f32[225,112]{1,0:T(8,128)S(1)} %fusion.44), channel_id=1, source_target_pairs={{0,2},{1,3},{2,4},{3,5},{4,6},{5,7},{6,0},{7,1},{8,10},{9,11},{10,... | collective-permute-start | bytes 302408 | tf_op jit(solution)/shard_map/ppermute | solution.py:54
  89.6 4.9 %collective-permute-start.12 = (f32[225,112]{1,0:T(8,128)S(1)}, f32[225,112]{1,0:T(8,128)S(1)}, u32[]{:S(2)}, u32[]{:S(2)}) collective-permute-start(f32[225,112]{1,0:T(8,128)S(1)} %add_add_fusion.2), channel_id=1, source_target_pairs={{0,8},{8,0},{16,24},{24,16},{1,9},{9,1},{17,25},{25,17},{2,10},{10... | collective-permute-start | bytes 302408 | tf_op jit(solution)/shard_map/ppermute | solution.py:41
  94.5 11.3 %collective-permute-start.13 = (f32[225,112]{1,0:T(8,128)S(1)}, f32[225,112]{1,0:T(8,128)S(1)}, u32[]{:S(2)}, u32[]{:S(2)}) collective-permute-start(f32[225,112]{1,0:T(8,128)S(1)} %add.133), channel_id=1, source_target_pairs={{0,16},{8,24},{16,0},{24,8},{1,17},{9,25},{17,1},{25,9},{2,18},{10... | collective-permute-start | bytes 302408 | tf_op jit(solution)/shard_map/ppermute | solution.py:41
